TPU v7x, 32 devices: a whole 2x2x4 slice. The times are simulated.
32 devices in a mesh: src: 8 (over z, core), dst: 4 (over y, x).
Axes of the slice: x: 2, y: 2, z: 4, core: 2. Of those that a mesh axis runs over, the one named last changes fastest.
Arguments:
- teleport: float32 [16, 4, 8192], P(None, 'dst', 'src'), may hold values from 0.1 to 10
- tiles: bfloat16 [4, 8, 128, 256, 256], P('dst', 'src')
- tile_rows: int32 [4, 8, 128], P('dst', 'src'), may hold values from 0 to 31
- tile_cols: int32 [4, 8, 128], P('dst', 'src'), may hold values from 0 to 15
- tile_counts: int32 [4, 8], P('dst', 'src'), may hold values from 32 to 128, as said below
- dangling: int32 [128], replicated, may hold values 0 or 1
- agg_of_block: int32 [128], replicated, may hold values from 0 to 63, as said below
- owner_list: int32 [64], replicated, may hold values from 0 to 63, each once
Outputs:
- fine_out: float32 [16, 4, 8192], P(None, 'dst', 'src')
- coarse_out: float32 [16, 64], P(None, ('src', 'dst'))
Inputs may be any that keep to these rules, and one draw needn't show every extreme that they name: `tile_counts`: slots 0 to count - 1 of a group pair's list hold its tiles, later slots are unused; some group pair fills all 128 slots. `agg_of_block`: every aggregate holds at least one block. `owner_list`: each aggregate appears once.
All inputs are finite; a program needn't handle non-finite values.
Results may differ from a plain program's by a relative error of at most 0.0003.
Values may be sent and summed in bfloat16 or wider, within the bound.
No kernel may reach another device: no remote copies, remote signals or barrier semaphores. Data moves between devices by JAX's collectives and lax.ppermute only.
A program may use at most 192 MiB of HBM per device.

v0:
```python
import functools

import jax
import jax.numpy as jnp
from jax import lax
from jax.experimental import pallas as pl
from jax.experimental.pallas import tpu as pltpu
from jax.sharding import PartitionSpec as P

damping = 0.85
group_size = 32
highest = lax.Precision.HIGHEST


def tile_kernel(mode, blocks_piece, rows_ref, cols_ref, live_ref, nb_ref, x_ref, t_ref, o_ref):
    step = pl.program_id(0)
    vectors = o_ref.shape[1]
    if mode == "image":

        @pl.when(step == 0)
        def _():
            o_ref[...] = jnp.zeros_like(o_ref)

    @pl.when(step < nb_ref[0])
    def _():
        for g in range(group_size):
            slot = step * group_size + g
            col = cols_ref[slot]
            start = pl.multiple_of((col % blocks_piece) * vectors, vectors)
            picked = x_ref[col // blocks_piece, pl.ds(start, vectors), :].astype(jnp.bfloat16)
            weight = jnp.where(live_ref[slot] != 0, 1.0, 0.0).astype(jnp.bfloat16)
            product = jnp.dot(picked * weight, t_ref[g], preferred_element_type=jnp.float32)
            if mode == "image":
                row = rows_ref[slot]
                o_ref[row] = o_ref[row] + product
            else:
                o_ref[g] = product[:, :128] + product[:, 128:]

    if mode == "entries":

        @pl.when(step >= nb_ref[0])
        def _():
            o_ref[...] = jnp.zeros_like(o_ref)


def tile_pass(mode, x_cols, tiles, rows, cols, live, block_count, row_blocks, vectors):
    groups, payload_rows, side = x_cols.shape
    slots = tiles.shape[2]
    steps = slots // group_size

    def tile_index(i, rows_ref, cols_ref, live_ref, nb_ref):
        return (0, 0, jnp.minimum(i, nb_ref[0] - 1), 0, 0)

    if mode == "image":
        out_shape = jax.ShapeDtypeStruct((row_blocks, vectors, side), jnp.float32)
        out_spec = pl.BlockSpec((row_blocks, vectors, side), lambda i, *_: (0, 0, 0))
    else:
        out_shape = jax.ShapeDtypeStruct((slots, vectors, 128), jnp.float32)
        out_spec = pl.BlockSpec((group_size, vectors, 128), lambda i, *_: (i, 0, 0))
    grid_spec = pltpu.PrefetchScalarGridSpec(
        num_scalar_prefetch=4,
        grid=(steps,),
        in_specs=[
            pl.BlockSpec((groups, payload_rows, side), lambda i, *_: (0, 0, 0)),
            pl.BlockSpec((None, None, group_size, side, side), tile_index),
        ],
        out_specs=out_spec,
    )
    return pl.pallas_call(
        functools.partial(tile_kernel, mode, payload_rows // vectors),
        grid_spec=grid_spec,
        out_shape=out_shape,
        compiler_params=pltpu.CompilerParams(dimension_semantics=("arbitrary",)),
    )(rows, cols, live, block_count, x_cols, tiles)


def per_device(
    teleport, tiles, tile_rows, tile_cols, tile_counts, dangling, agg_of_block, owner_list
):
    vectors = teleport.shape[0]
    piece_width = teleport.shape[2]
    slots_total = tiles.shape[2]
    tile_side = tiles.shape[4]
    blocks_piece = piece_width // tile_side
    src_count = lax.axis_size("src")
    dst_count = lax.axis_size("dst")
    row_blocks = blocks_piece * src_count
    col_blocks = blocks_piece * dst_count
    page_total = row_blocks * dst_count * tile_side
    agg_count = owner_list.shape[0]
    src_index = lax.axis_index("src")
    dst_index = lax.axis_index("dst")
    own_rows = jnp.clip(tile_rows[0, 0], 0, row_blocks - 1)
    own_cols = jnp.clip(tile_cols[0, 0], 0, col_blocks - 1)
    own_count = tile_counts[0, 0]
    col_global = (
        own_cols // blocks_piece * (blocks_piece * src_count)
        + src_index * blocks_piece
        + own_cols % blocks_piece
    )
    row_global = dst_index * row_blocks + own_rows
    slot_range = jnp.arange(slots_total, dtype=jnp.int32)
    live_mask = ((slot_range < own_count) & (dangling[col_global] == 0)).astype(jnp.int32)
    steps = slots_total // group_size
    block_count = jnp.clip((own_count + group_size - 1) // group_size, 1, steps).reshape(1)
    block_count = block_count.astype(jnp.int32)
    piece_first = dst_index * row_blocks + src_index * blocks_piece
    piece_dangling = lax.dynamic_slice_in_dim(dangling, piece_first, blocks_piece).astype(
        jnp.float32
    )
    piece_agg = lax.dynamic_slice_in_dim(agg_of_block, piece_first, blocks_piece)
    agg_range = jnp.arange(agg_count, dtype=jnp.int32)
    piece_hot = (piece_agg[:, None] == agg_range[None, :]).astype(jnp.float32)
    tele = jnp.transpose(teleport.reshape(vectors, blocks_piece, tile_side), (1, 0, 2))

    all_axes = ("src", "dst")
    all_count = src_count * dst_count

    def tree_sum(value, axis, size):
        if size & (size - 1):
            return lax.psum(value, axis)
        shift = 1
        while shift < size:
            value = value + lax.ppermute(value, axis, [(i, i ^ shift) for i in range(size)])
            shift *= 2
        return value

    exchange = dst_count & (dst_count - 1) == 0
    if exchange:
        kernel_cols = (
            (own_cols // blocks_piece) ^ dst_index
        ) * blocks_piece + own_cols % blocks_piece
    else:
        kernel_cols = own_cols

    payload_rows = blocks_piece * vectors
    pad_rows = 8

    def with_lost_row(body, lost):
        lead = body.shape[:-2]
        extra = jnp.zeros(lead + (pad_rows, tile_side), jnp.float32)
        extra = extra.at[..., 0, :vectors].set(jnp.broadcast_to(lost, lead + (vectors,)))
        return jnp.concatenate([body, extra], axis=-2)

    def spread_columns(blocks, lost):
        payload = with_lost_row(blocks.reshape(payload_rows, tile_side), lost)[None]
        if exchange:
            shift = 1
            while shift < dst_count:
                got = lax.ppermute(payload, "dst", [(i, i ^ shift) for i in range(dst_count)])
                payload = jnp.concatenate([payload, got], axis=0)
                shift *= 2
        else:
            payload = lax.all_gather(payload, "dst", axis=0, tiled=True)
        lost_dst = jnp.sum(payload[:, payload_rows, :vectors], axis=0)
        return payload, lost_dst

    def reduce_rows(accumulated, lost):
        n = src_count
        chunks = with_lost_row(accumulated.reshape(n, payload_rows, tile_side), lost)
        if n & (n - 1) == 0:
            bit = 0
            while chunks.shape[0] > 1:
                mine = (src_index >> bit) & 1
                paired = chunks.reshape(chunks.shape[0] // 2, 2, *chunks.shape[1:])
                keep = lax.dynamic_index_in_dim(paired, mine, 1, keepdims=False)
                give = lax.dynamic_index_in_dim(paired, 1 - mine, 1, keepdims=False)
                partner = [(i, i ^ (1 << bit)) for i in range(n)]
                chunks = keep + lax.ppermute(give, "src", partner)
                bit += 1
            total = chunks[0]
        else:
            total = lax.dynamic_index_in_dim(chunks, src_index, 0, keepdims=False)
            for shift in range(1, n):
                send = lax.dynamic_index_in_dim(chunks, (src_index + shift) % n, 0, keepdims=False)
                total = total + lax.ppermute(send, "src", [(i, (i + shift) % n) for i in range(n)])
        image = total[:payload_rows].reshape(blocks_piece, vectors, tile_side)
        return image, total[payload_rows, :vectors]

    def lost_partial(blocks):
        return jnp.sum(blocks * piece_dangling[:, None, None], axis=(0, 2))

    def relaxation(blocks, lost_sum=None):
        gathered, lost_dst = spread_columns(blocks, lost_partial(blocks))
        accumulated = tile_pass(
            "image", gathered, tiles, own_rows, kernel_cols, live_mask, block_count,
            row_blocks, vectors,
        )
        image, lost_total = reduce_rows(accumulated, lost_dst)
        if lost_sum is None:
            lost_sum = lost_total
        return (
            damping * (image + (lost_sum / page_total)[None, :, None] * tele)
            + (1.0 - damping) * tele
        )

    tele_sums = jnp.sum(tele, axis=2)
    weight_partial = jnp.einsum("bk,ba->ka", tele_sums, piece_hot, precision=highest)

    relaxed_one = relaxation(tele)
    relaxed_two = relaxation(relaxed_one)

    gathered, _ = spread_columns(relaxed_two, jnp.zeros((vectors,), jnp.float32))
    entries = tile_pass(
        "entries", gathered, tiles, own_rows, kernel_cols, live_mask, block_count,
        row_blocks, vectors,
    ).sum(axis=2)
    block_sums = jnp.sum(relaxed_two, axis=2)
    totals_partial = jnp.einsum("bk,ba->ka", block_sums, piece_hot, precision=highest)
    lost_mass_partial = jnp.einsum(
        "bk,ba->ka", block_sums * piece_dangling[:, None], piece_hot, precision=highest
    )
    row_agg = agg_of_block[row_global]
    col_agg = agg_of_block[col_global]
    row_hot = (row_agg[:, None] == agg_range[None, :]).astype(jnp.float32)
    col_hot = (col_agg[:, None] == agg_range[None, :]).astype(jnp.float32)
    inflow_partial = jnp.einsum("tk,ta->ka", entries, row_hot, precision=highest)
    inflow_one, totals, lost_mass, weight = tree_sum(
        jnp.stack([inflow_partial, totals_partial, lost_mass_partial, weight_partial]),
        all_axes,
        all_count,
    )

    def coarse_sweep(inflow, ratios):
        carried = jnp.sum(lost_mass * ratios, axis=1)
        return (
            damping * (inflow + (carried / page_total)[:, None] * weight)
            + (1.0 - damping) * weight
        )

    level_one = coarse_sweep(inflow_one, jnp.ones((vectors, agg_count), jnp.float32))
    ratios_one = level_one / totals
    ratio_at_tile = jnp.einsum("ka,ta->tk", ratios_one, col_hot, precision=highest)
    inflow_two = tree_sum(
        jnp.einsum("tk,ta->ka", entries * ratio_at_tile, row_hot, precision=highest),
        all_axes,
        all_count,
    )
    level_two = coarse_sweep(inflow_two, ratios_one)
    ratios_two = level_two / totals
    rescale = jnp.einsum("ka,ba->bk", ratios_two, piece_hot, precision=highest)
    corrected = relaxed_two * rescale[:, :, None]
    lost_two = jnp.sum(lost_mass * ratios_two, axis=1)

    position = lax.axis_index(all_axes)
    owned_count = agg_count // (src_count * dst_count)
    owned = lax.dynamic_slice_in_dim(owner_list, position * owned_count, owned_count)
    owned_hot = (owned[:, None] == agg_range[None, :]).astype(jnp.float32)
    coarse_out = jnp.einsum("ka,qa->kq", level_two, owned_hot, precision=highest)

    relaxed_three = relaxation(corrected, lost_two)
    relaxed_four = relaxation(relaxed_three)
    fine_out = jnp.transpose(relaxed_four, (1, 0, 2)).reshape(teleport.shape)
    return fine_out, coarse_out


def solution(mesh):
    placed = (
        P(None, "dst", "src"),
        P("dst", "src", None, None, None),
        P("dst", "src", None),
        P("dst", "src", None),
        P("dst", "src"),
        P(),
        P(),
        P(),
    )
    return jax.shard_map(
        per_device,
        mesh=mesh,
        in_specs=placed,
        out_specs=(P(None, "dst", "src"), P(None, ("src", "dst"))),
        check_vma=False,
    )
```

profile of v0, /device:TPU:0, one launch (start us, length us, event | category | flops | bytes accessed | tf_op | source)
XLA Modules:
  0.0 204.1 jit_solution(8302206800646253008)
XLA Ops:
  2.6 3.0 %collective-permute-start = (f32[1,72,256]{2,1,0:T(8,128)S(1)}, f32[1,72,256]{2,1,0:T(8,128)S(1)}, u32[]{:S(2)}, u32[]{:S(2)}) collective-permute-start(f32[1,72,256]{2,1,0:T(8,128)S(1)} %fusion.24), channel_id=1, source_target_pairs={{0,1},{1,0},{2,3},{3,2},{4,5},{5,4},{6,7},{7,6},{8,9},{9,8},{10,11... | collective-permute-start | bytes 221192 | tf_op jit(solution)/shard_map/ppermute | solution.py:150
  13.1 3.2 %collective-permute-done.1 = f32[2,72,256]{2,1,0:T(8,128)S(1)} collective-permute-done((f32[2,72,256]{2,1,0:T(8,128)S(1)}, f32[2,72,256]{2,1,0:T(8,128)S(1)}, u32[]{:S(2)}, u32[]{:S(2)}) %collective-permute-start.1) | collective-permute-done | bytes 147488 | tf_op jit(solution)/shard_map/ppermute | solution.py:150
  17.1 5.9 %shard_map.95 = f32[32,16,256]{2,1,0:T(8,128)} custom-call(s32[128]{0:T(128)} %clamp_bitcast_fusion.rows_ref, s32[128]{0:T(128)} %fusion.60.cols_ref, s32[128]{0:T(128)} %and_convert_fusion.live_ref, s32[1]{0:T(128)} %bitcast.5.nb_ref, f32[4,72,256]{2,1,0:T(8,128)} %copy-done.1, bf16[1,1,128,256,256]{4,3,2,1,0:T(8,128)(2,1)} %t_ref.9), custom_call_target="tpu_custom_call" | custom-call | tf_op jit(solution)/shard_map/pallas_call | solution.py:69
  28.2 5.9 %collective-permute-done.3 = f32[2,72,256]{2,1,0:T(8,128)S(1)} collective-permute-done((f32[2,72,256]{2,1,0:T(8,128)S(1)}, f32[2,72,256]{2,1,0:T(8,128)S(1)}, u32[]{:S(2)}, u32[]{:S(2)}) %collective-permute-start.3) | collective-permute-done | bytes 147488 | tf_op jit(solution)/shard_map/ppermute | solution.py:169
  35.3 4.9 %collective-permute-done.4 = f32[1,72,256]{2,1,0:T(8,128)S(1)} collective-permute-done((f32[1,72,256]{2,1,0:T(8,128)S(1)}, f32[1,72,256]{2,1,0:T(8,128)S(1)}, u32[]{:S(2)}, u32[]{:S(2)}) %collective-permute-start.4) | collective-permute-done | bytes 73760 | tf_op jit(solution)/shard_map/ppermute | solution.py:169
  42.3 2.6 %collective-permute-done.5 = f32[1,72,256]{2,1,0:T(8,128)S(1)} collective-permute-done((f32[1,72,256]{2,1,0:T(8,128)S(1)}, f32[1,72,256]{2,1,0:T(8,128)S(1)}, u32[]{:S(2)}, u32[]{:S(2)}) %collective-permute-start.5) | collective-permute-done | bytes 73760 | tf_op jit(solution)/shard_map/ppermute | solution.py:150
  44.9 3.2 %collective-permute-start.6 = (f32[2,72,256]{2,1,0:T(8,128)S(1)}, f32[2,72,256]{2,1,0:T(8,128)S(1)}, u32[]{:S(2)}, u32[]{:S(2)}) collective-permute-start(f32[2,72,256]{2,1,0:T(8,128)S(1)} %pad_maximum_fusion.6), channel_id=1, source_target_pairs={{0,2},{1,3},{2,0},{3,1},{4,6},{5,7},{6,4},{7,5},{8,10},{9,11},{10,... | collective-permute-start | bytes 442376 | tf_op jit(solution)/shard_map/ppermute | solution.py:150
  48.1 3.1 %collective-permute-done.6 = f32[2,72,256]{2,1,0:T(8,128)S(1)} collective-permute-done((f32[2,72,256]{2,1,0:T(8,128)S(1)}, f32[2,72,256]{2,1,0:T(8,128)S(1)}, u32[]{:S(2)}, u32[]{:S(2)}) %collective-permute-start.6) | collective-permute-done | bytes 147488 | tf_op jit(solution)/shard_map/ppermute | solution.py:150
  52.0 5.8 %shard_map.96 = f32[32,16,256]{2,1,0:T(8,128)} custom-call(s32[128]{0:T(128)} %clamp_bitcast_fusion.rows_ref, s32[128]{0:T(128)} %fusion.60.cols_ref, s32[128]{0:T(128)} %and_convert_fusion.live_ref, s32[1]{0:T(128)} %bitcast.5.nb_ref, f32[4,72,256]{2,1,0:T(8,128)} %pad_maximum_fusion.1.x_ref, bf16[1,1,128,256,256]{4,3,2,1,0:T(8,128)(2,1)} %t_ref.9), custom_call_target="tpu_custom_call" | custom-call | tf_op jit(solution)/shard_map/pallas_call | solution.py:69
  62.9 5.2 %collective-permute-done.8 = f32[2,72,256]{2,1,0:T(8,128)S(1)} collective-permute-done((f32[2,72,256]{2,1,0:T(8,128)S(1)}, f32[2,72,256]{2,1,0:T(8,128)S(1)}, u32[]{:S(2)}, u32[]{:S(2)}) %collective-permute-start.8) | collective-permute-done | bytes 147488 | tf_op jit(solution)/shard_map/ppermute | solution.py:169
  71.7 2.5 %collective-permute-done.9 = f32[1,72,256]{2,1,0:T(8,128)S(1)} collective-permute-done((f32[1,72,256]{2,1,0:T(8,128)S(1)}, f32[1,72,256]{2,1,0:T(8,128)S(1)}, u32[]{:S(2)}, u32[]{:S(2)}) %collective-permute-start.9) | collective-permute-done | bytes 73760 | tf_op jit(solution)/shard_map/ppermute | solution.py:169
  74.5 3.7 %collective-permute-start.10 = (f32[1,72,256]{2,1,0:T(8,128)S(1)}, f32[1,72,256]{2,1,0:T(8,128)S(1)}, u32[]{:S(2)}, u32[]{:S(2)}) collective-permute-start(f32[1,72,256]{2,1,0:T(8,128)S(1)} %fusion.22), channel_id=1, source_target_pairs={{0,1},{1,0},{2,3},{3,2},{4,5},{5,4},{6,7},{7,6},{8,9},{9,8},{10,11... | collective-permute-start | bytes 221192 | tf_op jit(solution)/shard_map/ppermute | solution.py:150
  80.5 3.5 %collective-permute-start.11 = (f32[2,72,256]{2,1,0:T(8,128)S(1)}, f32[2,72,256]{2,1,0:T(8,128)S(1)}, u32[]{:S(2)}, u32[]{:S(2)}) collective-permute-start(f32[2,72,256]{2,1,0:T(8,128)S(1)} %pad_maximum_fusion.7), channel_id=1, source_target_pairs={{0,2},{1,3},{2,0},{3,1},{4,6},{5,7},{6,4},{7,5},{8,10},{9,11},{10,... | collective-permute-start | bytes 442376 | tf_op jit(solution)/shard_map/ppermute | solution.py:150
  84.4 2.7 %collective-permute-done.11 = f32[2,72,256]{2,1,0:T(8,128)S(1)} collective-permute-done((f32[2,72,256]{2,1,0:T(8,128)S(1)}, f32[2,72,256]{2,1,0:T(8,128)S(1)}, u32[]{:S(2)}, u32[]{:S(2)}) %collective-permute-start.11) | collective-permute-done | bytes 147488 | tf_op jit(solution)/shard_map/ppermute | solution.py:150
  87.8 6.3 %shard_map.97 = f32[128,16,128]{2,1,0:T(8,128)} custom-call(s32[128]{0:T(128)} %clamp_bitcast_fusion.rows_ref, s32[128]{0:T(128)} %fusion.60.cols_ref, s32[128]{0:T(128)} %and_convert_fusion.live_ref, s32[1]{0:T(128)} %bitcast.5.nb_ref, f32[4,72,256]{2,1,0:T(8,128)} %pad_maximum_fusion.2.x_ref, bf16[1,1,128,256,256]{4,3,2,1,0:T(8,128)(2,1)} %t_ref.9), custom_call_target="tpu_custom_call" | custom-call | tf_op jit(solution)/shard_map/pallas_call | solution.py:69
  96.0 3.2 %collective-permute-start.12 = (f32[4,16,64]{2,1,0:T(8,128)S(1)}, f32[4,16,64]{2,1,0:T(8,128)S(1)}, u32[]{:S(2)}, u32[]{:S(2)}) collective-permute-start(f32[4,16,64]{2,1,0:T(8,128)S(1)} %pad_maximum_fusion.10), channel_id=1, source_target_pairs={{0,1},{1,0},{2,3},{3,2},{4,5},{5,4},{6,7},{7,6},{8,9},{9,8},{10,11... | collective-permute-start | bytes 49160 | tf_op jit(solution)/shard_map/ppermute | solution.py:124
  102.1 3.0 %collective-permute-done.13 = f32[4,16,64]{2,1,0:T(8,128)S(1)} collective-permute-done((f32[4,16,64]{2,1,0:T(8,128)S(1)}, f32[4,16,64]{2,1,0:T(8,128)S(1)}, u32[]{:S(2)}, u32[]{:S(2)}) %collective-permute-start.13) | collective-permute-done | bytes 16416 | tf_op jit(solution)/shard_map/ppermute | solution.py:124
  106.4 3.9 %collective-permute-done.15 = f32[4,16,64]{2,1,0:T(8,128)S(1)} collective-permute-done((f32[4,16,64]{2,1,0:T(8,128)S(1)}, f32[4,16,64]{2,1,0:T(8,128)S(1)}, u32[]{:S(2)}, u32[]{:S(2)}) %collective-permute-start.15) | collective-permute-done | bytes 16416 | tf_op jit(solution)/shard_map/ppermute | solution.py:124
  110.3 3.4 %collective-permute-start.16 = (f32[4,16,64]{2,1,0:T(8,128)S(1)}, f32[4,16,64]{2,1,0:T(8,128)S(1)}, u32[]{:S(2)}, u32[]{:S(2)}) collective-permute-start(f32[4,16,64]{2,1,0:T(8,128)S(1)} %add.318), channel_id=1, source_target_pairs={{0,16},{1,17},{2,18},{3,19},{4,20},{5,21},{6,22},{7,23},{8,24},{9,... | collective-permute-start | bytes 49160 | tf_op jit(solution)/shard_map/ppermute | solution.py:124
  128.6 2.8 %collective-permute-start.21 = (f32[16,64]{1,0:T(8,128)S(1)}, f32[16,64]{1,0:T(8,128)S(1)}, u32[]{:S(2)}, u32[]{:S(2)}) collective-permute-start(f32[16,64]{1,0:T(8,128)S(1)} %add.325), channel_id=1, source_target_pairs={{0,16},{1,17},{2,18},{3,19},{4,20},{5,21},{6,22},{7,23},{8,24},{9,... | collective-permute-start | bytes 12296 | tf_op jit(solution)/shard_map/ppermute | solution.py:124
  135.3 2.9 %collective-permute-done.22 = f32[1,72,256]{2,1,0:T(8,128)S(1)} collective-permute-done((f32[1,72,256]{2,1,0:T(8,128)S(1)}, f32[1,72,256]{2,1,0:T(8,128)S(1)}, u32[]{:S(2)}, u32[]{:S(2)}) %collective-permute-start.22) | collective-permute-done | bytes 73760 | tf_op jit(solution)/shard_map/ppermute | solution.py:150
  140.3 3.1 %collective-permute-done.23 = f32[2,72,256]{2,1,0:T(8,128)S(1)} collective-permute-done((f32[2,72,256]{2,1,0:T(8,128)S(1)}, f32[2,72,256]{2,1,0:T(8,128)S(1)}, u32[]{:S(2)}, u32[]{:S(2)}) %collective-permute-start.23) | collective-permute-done | bytes 147488 | tf_op jit(solution)/shard_map/ppermute | solution.py:150
  144.1 5.9 %shard_map.98 = f32[32,16,256]{2,1,0:T(8,128)} custom-call(s32[128]{0:T(128)} %clamp_bitcast_fusion.rows_ref, s32[128]{0:T(128)} %fusion.60.cols_ref, s32[128]{0:T(128)} %and_convert_fusion.live_ref, s32[1]{0:T(128)} %bitcast.5.nb_ref, f32[4,72,256]{2,1,0:T(8,128)} %pad_maximum_fusion.3.x_ref, bf16[1,1,128,256,256]{4,3,2,1,0:T(8,128)(2,1)} %t_ref.9), custom_call_target="tpu_custom_call" | custom-call | tf_op jit(solution)/shard_map/pallas_call | solution.py:69
  156.4 4.2 %collective-permute-done.25 = f32[2,72,256]{2,1,0:T(8,128)S(1)} collective-permute-done((f32[2,72,256]{2,1,0:T(8,128)S(1)}, f32[2,72,256]{2,1,0:T(8,128)S(1)}, u32[]{:S(2)}, u32[]{:S(2)}) %collective-permute-start.25) | collective-permute-done | bytes 147488 | tf_op jit(solution)/shard_map/ppermute | solution.py:169
  160.6 3.0 %collective-permute-start.26 = (f32[1,72,256]{2,1,0:T(8,128)S(1)}, f32[1,72,256]{2,1,0:T(8,128)S(1)}, u32[]{:S(2)}, u32[]{:S(2)}) collective-permute-start(f32[1,72,256]{2,1,0:T(8,128)S(1)} %constant_dynamic-slice_fusion.1), channel_id=1, source_target_pairs={{0,16},{4,20},{8,24},{12,28},{16,0},{20,4},{24,8},{28,12},{1,17},{... | collective-permute-start | bytes 221192 | tf_op jit(solution)/shard_map/ppermute | solution.py:169
  163.6 3.7 %collective-permute-done.26 = f32[1,72,256]{2,1,0:T(8,128)S(1)} collective-permute-done((f32[1,72,256]{2,1,0:T(8,128)S(1)}, f32[1,72,256]{2,1,0:T(8,128)S(1)}, u32[]{:S(2)}, u32[]{:S(2)}) %collective-permute-start.26) | collective-permute-done | bytes 73760 | tf_op jit(solution)/shard_map/ppermute | solution.py:169
  167.5 3.7 %collective-permute-start.27 = (f32[1,72,256]{2,1,0:T(8,128)S(1)}, f32[1,72,256]{2,1,0:T(8,128)S(1)}, u32[]{:S(2)}, u32[]{:S(2)}) collective-permute-start(f32[1,72,256]{2,1,0:T(8,128)S(1)} %fusion.20), channel_id=1, source_target_pairs={{0,1},{1,0},{2,3},{3,2},{4,5},{5,4},{6,7},{7,6},{8,9},{9,8},{10,11... | collective-permute-start | bytes 221192 | tf_op jit(solution)/shard_map/ppermute | solution.py:150
  173.6 3.5 %collective-permute-start.28 = (f32[2,72,256]{2,1,0:T(8,128)S(1)}, f32[2,72,256]{2,1,0:T(8,128)S(1)}, u32[]{:S(2)}, u32[]{:S(2)}) collective-permute-start(f32[2,72,256]{2,1,0:T(8,128)S(1)} %pad_maximum_fusion.9), channel_id=1, source_target_pairs={{0,2},{1,3},{2,0},{3,1},{4,6},{5,7},{6,4},{7,5},{8,10},{9,11},{10,... | collective-permute-start | bytes 442376 | tf_op jit(solution)/shard_map/ppermute | solution.py:150
  177.1 3.1 %collective-permute-done.28 = f32[2,72,256]{2,1,0:T(8,128)S(1)} collective-permute-done((f32[2,72,256]{2,1,0:T(8,128)S(1)}, f32[2,72,256]{2,1,0:T(8,128)S(1)}, u32[]{:S(2)}, u32[]{:S(2)}) %collective-permute-start.28) | collective-permute-done | bytes 147488 | tf_op jit(solution)/shard_map/ppermute | solution.py:150
  180.9 5.8 %shard_map.99 = f32[32,16,256]{2,1,0:T(8,128)} custom-call(s32[128]{0:T(128)} %clamp_bitcast_fusion.rows_ref, s32[128]{0:T(128)} %fusion.60.cols_ref, s32[128]{0:T(128)} %and_convert_fusion.live_ref, s32[1]{0:T(128)} %bitcast.5.nb_ref, f32[4,72,256]{2,1,0:T(8,128)} %pad_maximum_fusion.4.x_ref, bf16[1,1,128,256,256]{4,3,2,1,0:T(8,128)(2,1)} %t_ref.9), custom_call_target="tpu_custom_call" | custom-call | tf_op jit(solution)/shard_map/pallas_call | solution.py:69
  191.9 5.2 %collective-permute-done.30 = f32[2,72,256]{2,1,0:T(8,128)S(1)} collective-permute-done((f32[2,72,256]{2,1,0:T(8,128)S(1)}, f32[2,72,256]{2,1,0:T(8,128)S(1)}, u32[]{:S(2)}, u32[]{:S(2)}) %collective-permute-start.30) | collective-permute-done | bytes 147488 | tf_op jit(solution)/shard_map/ppermute | solution.py:169
  200.2 3.0 %collective-permute-done.31 = f32[1,72,256]{2,1,0:T(8,128)S(1)} collective-permute-done((f32[1,72,256]{2,1,0:T(8,128)S(1)}, f32[1,72,256]{2,1,0:T(8,128)S(1)}, u32[]{:S(2)}, u32[]{:S(2)}) %collective-permute-start.31) | collective-permute-done | bytes 73760 | tf_op jit(solution)/shard_map/ppermute | solution.py:169
  (148 shorter events, 77.6 us)
Async XLA Ops:
  2.6 8.3 %collective-permute-start = (f32[1,72,256]{2,1,0:T(8,128)S(1)}, f32[1,72,256]{2,1,0:T(8,128)S(1)}, u32[]{:S(2)}, u32[]{:S(2)}) collective-permute-start(f32[1,72,256]{2,1,0:T(8,128)S(1)} %fusion.24), channel_id=1, source_target_pairs={{0,1},{1,0},{2,3},{3,2},{4,5},{5,4},{6,7},{7,6},{8,9},{9,8},{10,11... | collective-permute-start | bytes 221192 | tf_op jit(solution)/shard_map/ppermute | solution.py:150
  10.9 5.4 %collective-permute-start.1 = (f32[2,72,256]{2,1,0:T(8,128)S(1)}, f32[2,72,256]{2,1,0:T(8,128)S(1)}, u32[]{:S(2)}, u32[]{:S(2)}) collective-permute-start(f32[2,72,256]{2,1,0:T(8,128)S(1)} %pad_maximum_fusion.5), channel_id=1, source_target_pairs={{0,2},{1,3},{2,0},{3,1},{4,6},{5,7},{6,4},{7,5},{8,10},{9,11},{10,... | collective-permute-start | bytes 442376 | tf_op jit(solution)/shard_map/ppermute | solution.py:150
  23.9 3.0 %collective-permute-start.2 = (f32[4,72,256]{2,1,0:T(8,128)S(1)}, f32[4,72,256]{2,1,0:T(8,128)S(1)}, u32[]{:S(2)}, u32[]{:S(2)}) collective-permute-start(f32[4,72,256]{2,1,0:T(8,128)S(1)} %fusion.16), channel_id=1, source_target_pairs={{0,4},{4,0},{8,12},{12,8},{16,20},{20,16},{24,28},{28,24},{1,5},{5... | collective-permute-start | bytes 884744 | tf_op jit(solution)/shard_map/ppermute | solution.py:169
  27.9 6.2 %collective-permute-start.3 = (f32[2,72,256]{2,1,0:T(8,128)S(1)}, f32[2,72,256]{2,1,0:T(8,128)S(1)}, u32[]{:S(2)}, u32[]{:S(2)}) collective-permute-start(f32[2,72,256]{2,1,0:T(8,128)S(1)} %dynamic-slice_bitcast_fusion.3), channel_id=1, source_target_pairs={{0,8},{4,12},{8,0},{12,4},{16,24},{20,28},{24,16},{28,20},{1,9},{5... | collective-permute-start | bytes 442376 | tf_op jit(solution)/shard_map/ppermute | solution.py:169
  34.2 6.0 %collective-permute-start.4 = (f32[1,72,256]{2,1,0:T(8,128)S(1)}, f32[1,72,256]{2,1,0:T(8,128)S(1)}, u32[]{:S(2)}, u32[]{:S(2)}) collective-permute-start(f32[1,72,256]{2,1,0:T(8,128)S(1)} %constant_dynamic-slice_fusion.3), channel_id=1, source_target_pairs={{0,16},{4,20},{8,24},{12,28},{16,0},{20,4},{24,8},{28,12},{1,17},{... | collective-permute-start | bytes 221192 | tf_op jit(solution)/shard_map/ppermute | solution.py:169
  40.4 4.4 %collective-permute-start.5 = (f32[1,72,256]{2,1,0:T(8,128)S(1)}, f32[1,72,256]{2,1,0:T(8,128)S(1)}, u32[]{:S(2)}, u32[]{:S(2)}) collective-permute-start(f32[1,72,256]{2,1,0:T(8,128)S(1)} %fusion.23), channel_id=1, source_target_pairs={{0,1},{1,0},{2,3},{3,2},{4,5},{5,4},{6,7},{7,6},{8,9},{9,8},{10,11... | collective-permute-start | bytes 221192 | tf_op jit(solution)/shard_map/ppermute | solution.py:150
  44.9 6.4 %collective-permute-start.6 = (f32[2,72,256]{2,1,0:T(8,128)S(1)}, f32[2,72,256]{2,1,0:T(8,128)S(1)}, u32[]{:S(2)}, u32[]{:S(2)}) collective-permute-start(f32[2,72,256]{2,1,0:T(8,128)S(1)} %pad_maximum_fusion.6), channel_id=1, source_target_pairs={{0,2},{1,3},{2,0},{3,1},{4,6},{5,7},{6,4},{7,5},{8,10},{9,11},{10,... | collective-permute-start | bytes 442376 | tf_op jit(solution)/shard_map/ppermute | solution.py:150
  59.5 1.6 collective-permute-start.7
  62.1 6.0 %collective-permute-start.8 = (f32[2,72,256]{2,1,0:T(8,128)S(1)}, f32[2,72,256]{2,1,0:T(8,128)S(1)}, u32[]{:S(2)}, u32[]{:S(2)}) collective-permute-start(f32[2,72,256]{2,1,0:T(8,128)S(1)} %dynamic-slice_bitcast_fusion.2), channel_id=1, source_target_pairs={{0,8},{4,12},{8,0},{12,4},{16,24},{20,28},{24,16},{28,20},{1,9},{5... | collective-permute-start | bytes 442376 | tf_op jit(solution)/shard_map/ppermute | solution.py:169
  68.1 6.1 %collective-permute-start.9 = (f32[1,72,256]{2,1,0:T(8,128)S(1)}, f32[1,72,256]{2,1,0:T(8,128)S(1)}, u32[]{:S(2)}, u32[]{:S(2)}) collective-permute-start(f32[1,72,256]{2,1,0:T(8,128)S(1)} %constant_dynamic-slice_fusion.2), channel_id=1, source_target_pairs={{0,16},{4,20},{8,24},{12,28},{16,0},{20,4},{24,8},{28,12},{1,17},{... | collective-permute-start | bytes 221192 | tf_op jit(solution)/shard_map/ppermute | solution.py:169
  74.5 6.0 %collective-permute-start.10 = (f32[1,72,256]{2,1,0:T(8,128)S(1)}, f32[1,72,256]{2,1,0:T(8,128)S(1)}, u32[]{:S(2)}, u32[]{:S(2)}) collective-permute-start(f32[1,72,256]{2,1,0:T(8,128)S(1)} %fusion.22), channel_id=1, source_target_pairs={{0,1},{1,0},{2,3},{3,2},{4,5},{5,4},{6,7},{7,6},{8,9},{9,8},{10,11... | collective-permute-start | bytes 221192 | tf_op jit(solution)/shard_map/ppermute | solution.py:150
  80.5 6.6 %collective-permute-start.11 = (f32[2,72,256]{2,1,0:T(8,128)S(1)}, f32[2,72,256]{2,1,0:T(8,128)S(1)}, u32[]{:S(2)}, u32[]{:S(2)}) collective-permute-start(f32[2,72,256]{2,1,0:T(8,128)S(1)} %pad_maximum_fusion.7), channel_id=1, source_target_pairs={{0,2},{1,3},{2,0},{3,1},{4,6},{5,7},{6,4},{7,5},{8,10},{9,11},{10,... | collective-permute-start | bytes 442376 | tf_op jit(solution)/shard_map/ppermute | solution.py:150
  96.0 5.1 %collective-permute-start.12 = (f32[4,16,64]{2,1,0:T(8,128)S(1)}, f32[4,16,64]{2,1,0:T(8,128)S(1)}, u32[]{:S(2)}, u32[]{:S(2)}) collective-permute-start(f32[4,16,64]{2,1,0:T(8,128)S(1)} %pad_maximum_fusion.10), channel_id=1, source_target_pairs={{0,1},{1,0},{2,3},{3,2},{4,5},{5,4},{6,7},{7,6},{8,9},{9,8},{10,11... | collective-permute-start | bytes 49160 | tf_op jit(solution)/shard_map/ppermute | solution.py:124
  101.1 4.0 %collective-permute-start.13 = (f32[4,16,64]{2,1,0:T(8,128)S(1)}, f32[4,16,64]{2,1,0:T(8,128)S(1)}, u32[]{:S(2)}, u32[]{:S(2)}) collective-permute-start(f32[4,16,64]{2,1,0:T(8,128)S(1)} %fusion.69), channel_id=1, source_target_pairs={{0,2},{1,3},{2,0},{3,1},{4,6},{5,7},{6,4},{7,5},{8,10},{9,11},{10,... | collective-permute-start | bytes 49160 | tf_op jit(solution)/shard_map/ppermute | solution.py:124
  105.1 1.3 collective-permute-start.14
  106.4 3.9 %collective-permute-start.15 = (f32[4,16,64]{2,1,0:T(8,128)S(1)}, f32[4,16,64]{2,1,0:T(8,128)S(1)}, u32[]{:S(2)}, u32[]{:S(2)}) collective-permute-start(f32[4,16,64]{2,1,0:T(8,128)S(1)} %add.317), channel_id=1, source_target_pairs={{0,8},{1,9},{2,10},{3,11},{4,12},{5,13},{6,14},{7,15},{8,0},{9,1},... | collective-permute-start | bytes 49160 | tf_op jit(solution)/shard_map/ppermute | solution.py:124
  110.3 5.4 %collective-permute-start.16 = (f32[4,16,64]{2,1,0:T(8,128)S(1)}, f32[4,16,64]{2,1,0:T(8,128)S(1)}, u32[]{:S(2)}, u32[]{:S(2)}) collective-permute-start(f32[4,16,64]{2,1,0:T(8,128)S(1)} %add.318), channel_id=1, source_target_pairs={{0,16},{1,17},{2,18},{3,19},{4,20},{5,21},{6,22},{7,23},{8,24},{9,... | collective-permute-start | bytes 49160 | tf_op jit(solution)/shard_map/ppermute | solution.py:124
  116.5 3.7 %collective-permute-start.17 = (f32[16,64]{1,0:T(8,128)S(1)}, f32[16,64]{1,0:T(8,128)S(1)}, u32[]{:S(2)}, u32[]{:S(2)}) collective-permute-start(f32[16,64]{1,0:T(8,128)S(1)} %fusion.39), channel_id=1, source_target_pairs={{0,1},{1,0},{2,3},{3,2},{4,5},{5,4},{6,7},{7,6},{8,9},{9,8},{10,11... | collective-permute-start | bytes 12296 | tf_op jit(solution)/shard_map/ppermute | solution.py:124
  120.1 3.7 %collective-permute-start.18 = (f32[16,64]{1,0:T(8,128)S(1)}, f32[16,64]{1,0:T(8,128)S(1)}, u32[]{:S(2)}, u32[]{:S(2)}) collective-permute-start(f32[16,64]{1,0:T(8,128)S(1)} %add.322), channel_id=1, source_target_pairs={{0,2},{1,3},{2,0},{3,1},{4,6},{5,7},{6,4},{7,5},{8,10},{9,11},{10,... | collective-permute-start | bytes 12296 | tf_op jit(solution)/shard_map/ppermute | solution.py:124
  123.8 1.2 collective-permute-start.19
  125.0 3.7 %collective-permute-start.20 = (f32[16,64]{1,0:T(8,128)S(1)}, f32[16,64]{1,0:T(8,128)S(1)}, u32[]{:S(2)}, u32[]{:S(2)}) collective-permute-start(f32[16,64]{1,0:T(8,128)S(1)} %add.324), channel_id=1, source_target_pairs={{0,8},{1,9},{2,10},{3,11},{4,12},{5,13},{6,14},{7,15},{8,0},{9,1},... | collective-permute-start | bytes 12296 | tf_op jit(solution)/shard_map/ppermute | solution.py:124
  128.6 4.5 %collective-permute-start.21 = (f32[16,64]{1,0:T(8,128)S(1)}, f32[16,64]{1,0:T(8,128)S(1)}, u32[]{:S(2)}, u32[]{:S(2)}) collective-permute-start(f32[16,64]{1,0:T(8,128)S(1)} %add.325), channel_id=1, source_target_pairs={{0,16},{1,17},{2,18},{3,19},{4,20},{5,21},{6,22},{7,23},{8,24},{9,... | collective-permute-start | bytes 12296 | tf_op jit(solution)/shard_map/ppermute | solution.py:124
  133.8 4.4 %collective-permute-start.22 = (f32[1,72,256]{2,1,0:T(8,128)S(1)}, f32[1,72,256]{2,1,0:T(8,128)S(1)}, u32[]{:S(2)}, u32[]{:S(2)}) collective-permute-start(f32[1,72,256]{2,1,0:T(8,128)S(1)} %fusion.21), channel_id=1, source_target_pairs={{0,1},{1,0},{2,3},{3,2},{4,5},{5,4},{6,7},{7,6},{8,9},{9,8},{10,11... | collective-permute-start | bytes 221192 | tf_op jit(solution)/shard_map/ppermute | solution.py:150
  138.2 5.2 %collective-permute-start.23 = (f32[2,72,256]{2,1,0:T(8,128)S(1)}, f32[2,72,256]{2,1,0:T(8,128)S(1)}, u32[]{:S(2)}, u32[]{:S(2)}) collective-permute-start(f32[2,72,256]{2,1,0:T(8,128)S(1)} %pad_maximum_fusion.8), channel_id=1, source_target_pairs={{0,2},{1,3},{2,0},{3,1},{4,6},{5,7},{6,4},{7,5},{8,10},{9,11},{10,... | collective-permute-start | bytes 442376 | tf_op jit(solution)/shard_map/ppermute | solution.py:150
  151.8 1.6 collective-permute-start.24
  154.5 6.1 %collective-permute-start.25 = (f32[2,72,256]{2,1,0:T(8,128)S(1)}, f32[2,72,256]{2,1,0:T(8,128)S(1)}, u32[]{:S(2)}, u32[]{:S(2)}) collective-permute-start(f32[2,72,256]{2,1,0:T(8,128)S(1)} %dynamic-slice_bitcast_fusion.1), channel_id=1, source_target_pairs={{0,8},{4,12},{8,0},{12,4},{16,24},{20,28},{24,16},{28,20},{1,9},{5... | collective-permute-start | bytes 442376 | tf_op jit(solution)/shard_map/ppermute | solution.py:169
  160.6 6.7 %collective-permute-start.26 = (f32[1,72,256]{2,1,0:T(8,128)S(1)}, f32[1,72,256]{2,1,0:T(8,128)S(1)}, u32[]{:S(2)}, u32[]{:S(2)}) collective-permute-start(f32[1,72,256]{2,1,0:T(8,128)S(1)} %constant_dynamic-slice_fusion.1), channel_id=1, source_target_pairs={{0,16},{4,20},{8,24},{12,28},{16,0},{20,4},{24,8},{28,12},{1,17},{... | collective-permute-start | bytes 221192 | tf_op jit(solution)/shard_map/ppermute | solution.py:169
  167.5 6.1 %collective-permute-start.27 = (f32[1,72,256]{2,1,0:T(8,128)S(1)}, f32[1,72,256]{2,1,0:T(8,128)S(1)}, u32[]{:S(2)}, u32[]{:S(2)}) collective-permute-start(f32[1,72,256]{2,1,0:T(8,128)S(1)} %fusion.20), channel_id=1, source_target_pairs={{0,1},{1,0},{2,3},{3,2},{4,5},{5,4},{6,7},{7,6},{8,9},{9,8},{10,11... | collective-permute-start | bytes 221192 | tf_op jit(solution)/shard_map/ppermute | solution.py:150
  173.6 6.6 %collective-permute-start.28 = (f32[2,72,256]{2,1,0:T(8,128)S(1)}, f32[2,72,256]{2,1,0:T(8,128)S(1)}, u32[]{:S(2)}, u32[]{:S(2)}) collective-permute-start(f32[2,72,256]{2,1,0:T(8,128)S(1)} %pad_maximum_fusion.9), channel_id=1, source_target_pairs={{0,2},{1,3},{2,0},{3,1},{4,6},{5,7},{6,4},{7,5},{8,10},{9,11},{10,... | collective-permute-start | bytes 442376 | tf_op jit(solution)/shard_map/ppermute | solution.py:150
  188.4 1.6 collective-permute-start.29
  191.1 6.0 %collective-permute-start.30 = (f32[2,72,256]{2,1,0:T(8,128)S(1)}, f32[2,72,256]{2,1,0:T(8,128)S(1)}, u32[]{:S(2)}, u32[]{:S(2)}) collective-permute-start(f32[2,72,256]{2,1,0:T(8,128)S(1)} %dynamic-slice_bitcast_fusion), channel_id=1, source_target_pairs={{0,8},{4,12},{8,0},{12,4},{16,24},{20,28},{24,16},{28,20},{1,9},{5... | collective-permute-start | bytes 442376 | tf_op jit(solution)/shard_map/ppermute | solution.py:169
  197.1 6.1 %collective-permute-start.31 = (f32[1,72,256]{2,1,0:T(8,128)S(1)}, f32[1,72,256]{2,1,0:T(8,128)S(1)}, u32[]{:S(2)}, u32[]{:S(2)}) collective-permute-start(f32[1,72,256]{2,1,0:T(8,128)S(1)} %constant_dynamic-slice_fusion), channel_id=1, source_target_pairs={{0,16},{4,20},{8,24},{12,28},{16,0},{20,4},{24,8},{28,12},{1,17},{... | collective-permute-start | bytes 221192 | tf_op jit(solution)/shard_map/ppermute | solution.py:169
  (3 other events, 94.1 us)
where the time goes:
time: 208 us; the launch traced here: 204 us
  waiting for transfers between devices  85.1 us (41%)
  starting transfers between devices  57.7 us (28%)
  Pallas kernels  29.7 us (14%)
  other arithmetic  21.9 us (11%)
  local copies, waits for them, and re-layouts  5.83 us (3%)
  matrix products  2.28 us (1%)
    ppermute x12, waiting for transfers between devices, reduce_rows(): chunks = keep + lax.ppermute(give, 'src', partner)  40.6 us
    pallas_call x5, Pallas kernels, tile_pass(): pl.pallas_call(functools.partial(tile_kernel, mode, payload_rows // vecto...  29.7 us
    ppermute x10, starting transfers between devices, spread_columns(): lax.ppermute(payload, 'dst', [(i, i ^ shift) for i in range(dst_count)])  27.6 us
    ppermute x10, waiting for transfers between devices, spread_columns(): lax.ppermute(payload, 'dst', [(i, i ^ shift) for i in range(dst_count)])  25.2 us
    ppermute x10, waiting for transfers between devices, tree_sum(): lax.ppermute(value, axis, [(i, i ^ shift) for i in range(size)])  19.3 us
    ppermute x10, starting transfers between devices, tree_sum(): lax.ppermute(value, axis, [(i, i ^ shift) for i in range(size)])  15.8 us
    ppermute x12, starting transfers between devices, reduce_rows(): chunks = keep + lax.ppermute(give, 'src', partner)  14.3 us
  transfers between devices with their start and end apart: 32, of which 31 were waited for; matrix products, arithmetic and copies ran while one was open for 5% of the time, Pallas kernels for 0%

commit v1 on v0

--- a/solution.py
+++ b/solution.py
@@ -145,11 +145,11 @@
     def spread_columns(blocks, lost):
         payload = with_lost_row(blocks.reshape(payload_rows, tile_side), lost)[None]
         if exchange:
-            shift = 1
-            while shift < dst_count:
-                got = lax.ppermute(payload, "dst", [(i, i ^ shift) for i in range(dst_count)])
-                payload = jnp.concatenate([payload, got], axis=0)
-                shift *= 2
+            pieces = [payload] + [
+                lax.ppermute(payload, "dst", [(i, i ^ v) for i in range(dst_count)])
+                for v in range(1, dst_count)
+            ]
+            payload = jnp.concatenate(pieces, axis=0)
         else:
             payload = lax.all_gather(payload, "dst", axis=0, tiled=True)
         lost_dst = jnp.sum(payload[:, payload_rows, :vectors], axis=0)
@@ -158,17 +158,19 @@
     def reduce_rows(accumulated, lost):
         n = src_count
         chunks = with_lost_row(accumulated.reshape(n, payload_rows, tile_side), lost)
-        if n & (n - 1) == 0:
-            bit = 0
-            while chunks.shape[0] > 1:
-                mine = (src_index >> bit) & 1
-                paired = chunks.reshape(chunks.shape[0] // 2, 2, *chunks.shape[1:])
-                keep = lax.dynamic_index_in_dim(paired, mine, 1, keepdims=False)
-                give = lax.dynamic_index_in_dim(paired, 1 - mine, 1, keepdims=False)
-                partner = [(i, i ^ (1 << bit)) for i in range(n)]
-                chunks = keep + lax.ppermute(give, "src", partner)
-                bit += 1
-            total = chunks[0]
+        if n % 2 == 0:
+            half = n // 2
+            paired = chunks.reshape(half, 2, *chunks.shape[1:])
+            core = src_index % 2
+            keep = lax.dynamic_index_in_dim(paired, core, 1, keepdims=False)
+            give = lax.dynamic_index_in_dim(paired, 1 - core, 1, keepdims=False)
+            part = keep + lax.ppermute(give, "src", [(i, i ^ 1) for i in range(n)])
+            chip = src_index // 2
+            total = lax.dynamic_index_in_dim(part, chip, 0, keepdims=False)
+            for shift in range(1, half):
+                send = lax.dynamic_index_in_dim(part, (chip + shift) % half, 0, keepdims=False)
+                pairs = [(i, ((i // 2 + shift) % half) * 2 + i % 2) for i in range(n)]
+                total = total + lax.ppermute(send, "src", pairs)
         else:
             total = lax.dynamic_index_in_dim(chunks, src_index, 0, keepdims=False)
             for shift in range(1, n):

time: 208 us -> 178 us (0.86)
  waiting for transfers between devices: 85.1 us -> 57.1 us
    ppermute x22 -> x31, waiting for transfers between devices: 65.8 us -> 34 us  [the longest x12 15 us: reduce_rows(): total = total + lax.ppermute(send, 'src', pairs)]
    ppermute x10, starting transfers between devices: 15.8 us -> 11.8 us  [tree_sum(): lax.ppermute(value, axis, [(i, i ^ shift) for i in range(size)])]
    ppermute x10, waiting for transfers between devices: 19.3 us -> 23.1 us  [tree_sum(): lax.ppermute(value, axis, [(i, i ^ shift) for i in range(size)])]
    ppermute x22 -> x31, starting transfers between devices: 41.9 us -> 45 us  [the longest x12 24.2 us: reduce_rows(): total = total + lax.ppermute(send, 'src', pairs)]
  transfers between devices with their start and end apart: 32 -> 41, of which waited for: 31 -> 33; matrix products, arithmetic and copies ran while one was open for 5% -> 5% of each run, Pallas kernels for 0% -> 0%
where the time goes in v1:
time: 178 us; the launch traced here: 175 us
  waiting for transfers between devices  57.1 us (32%)
  starting transfers between devices  56.8 us (32%)
  Pallas kernels  29.7 us (17%)
  other arithmetic  21.8 us (12%)
  local copies, waits for them, and re-layouts  5.86 us (3%)
  matrix products  2.29 us (1%)
    pallas_call x5, Pallas kernels, tile_pass(): pl.pallas_call(functools.partial(tile_kernel, mode, payload_rows // vecto...  29.7 us
    ppermute x12, starting transfers between devices, reduce_rows(): total = total + lax.ppermute(send, 'src', pairs)  24.2 us
    ppermute x10, waiting for transfers between devices, tree_sum(): lax.ppermute(value, axis, [(i, i ^ shift) for i in range(size)])  23.1 us
    ppermute x15, starting transfers between devices, spread_columns(): lax.ppermute(payload, 'dst', [(i, i ^ v) for i in range(dst_count)])  20.5 us
    ppermute x12, waiting for transfers between devices, reduce_rows(): total = total + lax.ppermute(send, 'src', pairs)  15 us
    ppermute x15, waiting for transfers between devices, spread_columns(): lax.ppermute(payload, 'dst', [(i, i ^ v) for i in range(dst_count)])  14.2 us
    ppermute x10, starting transfers between devices, tree_sum(): lax.ppermute(value, axis, [(i, i ^ shift) for i in range(size)])  11.8 us
    ppermute x4, waiting for transfers between devices, reduce_rows(): part = keep + lax.ppermute(give, 'src', [(i, i ^ 1) for i in range(n)])  4.77 us
  transfers between devices with their start and end apart: 41, of which 33 were waited for; matrix products, arithmetic and copies ran while one was open for 5% of the time, Pallas kernels for 0%

profile of v1, /device:TPU:0, one launch (start us, length us, event | category | flops | bytes accessed | tf_op | source)
XLA Modules:
  0.0 175.2 jit_solution(17489466762172926147)
XLA Ops:
  2.6 3.0 %collective-permute-start = (f32[1,72,256]{2,1,0:T(8,128)S(1)}, f32[1,72,256]{2,1,0:T(8,128)S(1)}, u32[]{:S(2)}, u32[]{:S(2)}) collective-permute-start(f32[1,72,256]{2,1,0:T(8,128)S(1)} %fusion.24), channel_id=1, source_target_pairs={{0,1},{1,0},{2,3},{3,2},{4,5},{5,4},{6,7},{7,6},{8,9},{9,8},{10,11... | collective-permute-start | bytes 221192 | tf_op jit(solution)/shard_map/ppermute | solution.py:149
  13.7 5.9 %shard_map.95 = f32[32,16,256]{2,1,0:T(8,128)} custom-call(s32[128]{0:T(128)} %clamp_bitcast_fusion.rows_ref, s32[128]{0:T(128)} %fusion.66.cols_ref, s32[128]{0:T(128)} %and_convert_fusion.live_ref, s32[1]{0:T(128)} %bitcast.5.nb_ref, f32[4,72,256]{2,1,0:T(8,128)} %copy-done.1, bf16[1,1,128,256,256]{4,3,2,1,0:T(8,128)(2,1)} %t_ref.9), custom_call_target="tpu_custom_call" | custom-call | tf_op jit(solution)/shard_map/pallas_call | solution.py:69
  23.3 2.1 %collective-permute-start.4 = (f32[72,256]{1,0:T(8,128)S(1)}, f32[72,256]{1,0:T(8,128)S(1)}, u32[]{:S(2)}, u32[]{:S(2)}) collective-permute-start(f32[72,256]{1,0:T(8,128)S(1)} %get-tuple-element.134), channel_id=1, source_target_pairs={{0,8},{4,12},{8,16},{12,20},{16,24},{20,28},{24,0},{28,4},{1,9},{5... | collective-permute-start | bytes 221192 | tf_op jit(solution)/shard_map/ppermute | solution.py:173
  25.4 2.8 %collective-permute-start.5 = (f32[72,256]{1,0:T(8,128)S(1)}, f32[72,256]{1,0:T(8,128)S(1)}, u32[]{:S(2)}, u32[]{:S(2)}) collective-permute-start(f32[72,256]{1,0:T(8,128)S(1)} %get-tuple-element.136), channel_id=1, source_target_pairs={{0,16},{4,20},{8,24},{12,28},{16,0},{20,4},{24,8},{28,12},{1,17},{... | collective-permute-start | bytes 221192 | tf_op jit(solution)/shard_map/ppermute | solution.py:173
  28.2 2.8 %collective-permute-start.6 = (f32[72,256]{1,0:T(8,128)S(1)}, f32[72,256]{1,0:T(8,128)S(1)}, u32[]{:S(2)}, u32[]{:S(2)}) collective-permute-start(f32[72,256]{1,0:T(8,128)S(1)} %get-tuple-element.135), channel_id=1, source_target_pairs={{0,24},{4,28},{8,0},{12,4},{16,8},{20,12},{24,16},{28,20},{1,25},{... | collective-permute-start | bytes 221192 | tf_op jit(solution)/shard_map/ppermute | solution.py:173
  39.6 2.4 %collective-permute-done.9 = f32[1,72,256]{2,1,0:T(8,128)S(1)} collective-permute-done((f32[1,72,256]{2,1,0:T(8,128)S(1)}, f32[1,72,256]{2,1,0:T(8,128)S(1)}, u32[]{:S(2)}, u32[]{:S(2)}) %collective-permute-start.9) | collective-permute-done | bytes 73760 | tf_op jit(solution)/shard_map/ppermute | solution.py:149
  42.8 5.8 %shard_map.96 = f32[32,16,256]{2,1,0:T(8,128)} custom-call(s32[128]{0:T(128)} %clamp_bitcast_fusion.rows_ref, s32[128]{0:T(128)} %fusion.66.cols_ref, s32[128]{0:T(128)} %and_convert_fusion.live_ref, s32[1]{0:T(128)} %bitcast.5.nb_ref, f32[4,72,256]{2,1,0:T(8,128)} %pad_maximum_fusion.1.x_ref, bf16[1,1,128,256,256]{4,3,2,1,0:T(8,128)(2,1)} %t_ref.9), custom_call_target="tpu_custom_call" | custom-call | tf_op jit(solution)/shard_map/pallas_call | solution.py:69
  53.0 2.1 %collective-permute-start.11 = (f32[72,256]{1,0:T(8,128)S(1)}, f32[72,256]{1,0:T(8,128)S(1)}, u32[]{:S(2)}, u32[]{:S(2)}) collective-permute-start(f32[72,256]{1,0:T(8,128)S(1)} %get-tuple-element.131), channel_id=1, source_target_pairs={{0,8},{4,12},{8,16},{12,20},{16,24},{20,28},{24,0},{28,4},{1,9},{5... | collective-permute-start | bytes 221192 | tf_op jit(solution)/shard_map/ppermute | solution.py:173
  55.1 3.3 %collective-permute-start.12 = (f32[72,256]{1,0:T(8,128)S(1)}, f32[72,256]{1,0:T(8,128)S(1)}, u32[]{:S(2)}, u32[]{:S(2)}) collective-permute-start(f32[72,256]{1,0:T(8,128)S(1)} %get-tuple-element.133), channel_id=1, source_target_pairs={{0,16},{4,20},{8,24},{12,28},{16,0},{20,4},{24,8},{28,12},{1,17},{... | collective-permute-start | bytes 221192 | tf_op jit(solution)/shard_map/ppermute | solution.py:173
  61.0 2.8 %collective-permute-done.12 = f32[72,256]{1,0:T(8,128)S(1)} collective-permute-done((f32[72,256]{1,0:T(8,128)S(1)}, f32[72,256]{1,0:T(8,128)S(1)}, u32[]{:S(2)}, u32[]{:S(2)}) %collective-permute-start.12) | collective-permute-done | bytes 73760 | tf_op jit(solution)/shard_map/ppermute | solution.py:173
  65.7 2.3 %collective-permute-start.16 = (f32[1,72,256]{2,1,0:T(8,128)S(1)}, f32[1,72,256]{2,1,0:T(8,128)S(1)}, u32[]{:S(2)}, u32[]{:S(2)}) collective-permute-start(f32[1,72,256]{2,1,0:T(8,128)S(1)} %fusion.22), channel_id=1, source_target_pairs={{0,3},{1,2},{2,1},{3,0},{4,7},{5,6},{6,5},{7,4},{8,11},{9,10},{10,... | collective-permute-start | bytes 221192 | tf_op jit(solution)/shard_map/ppermute | solution.py:149
  71.7 6.3 %shard_map.97 = f32[128,16,128]{2,1,0:T(8,128)} custom-call(s32[128]{0:T(128)} %clamp_bitcast_fusion.rows_ref, s32[128]{0:T(128)} %fusion.66.cols_ref, s32[128]{0:T(128)} %and_convert_fusion.live_ref, s32[1]{0:T(128)} %bitcast.5.nb_ref, f32[4,72,256]{2,1,0:T(8,128)} %pad_maximum_fusion.2.x_ref, bf16[1,1,128,256,256]{4,3,2,1,0:T(8,128)(2,1)} %t_ref.9), custom_call_target="tpu_custom_call" | custom-call | tf_op jit(solution)/shard_map/pallas_call | solution.py:69
  81.9 2.0 %collective-permute-done.17 = f32[4,16,64]{2,1,0:T(8,128)S(1)} collective-permute-done((f32[4,16,64]{2,1,0:T(8,128)S(1)}, f32[4,16,64]{2,1,0:T(8,128)S(1)}, u32[]{:S(2)}, u32[]{:S(2)}) %collective-permute-start.17) | collective-permute-done | bytes 16416 | tf_op jit(solution)/shard_map/ppermute | solution.py:124
  85.1 2.7 %collective-permute-done.18 = f32[4,16,64]{2,1,0:T(8,128)S(1)} collective-permute-done((f32[4,16,64]{2,1,0:T(8,128)S(1)}, f32[4,16,64]{2,1,0:T(8,128)S(1)}, u32[]{:S(2)}, u32[]{:S(2)}) %collective-permute-start.18) | collective-permute-done | bytes 16416 | tf_op jit(solution)/shard_map/ppermute | solution.py:124
  89.1 3.6 %collective-permute-start.20 = (f32[4,16,64]{2,1,0:T(8,128)S(1)}, f32[4,16,64]{2,1,0:T(8,128)S(1)}, u32[]{:S(2)}, u32[]{:S(2)}) collective-permute-start(f32[4,16,64]{2,1,0:T(8,128)S(1)} %add.379), channel_id=1, source_target_pairs={{0,8},{1,9},{2,10},{3,11},{4,12},{5,13},{6,14},{7,15},{8,0},{9,1},... | collective-permute-start | bytes 49160 | tf_op jit(solution)/shard_map/ppermute | solution.py:124
  96.1 3.3 %collective-permute-done.21 = f32[4,16,64]{2,1,0:T(8,128)S(1)} collective-permute-done((f32[4,16,64]{2,1,0:T(8,128)S(1)}, f32[4,16,64]{2,1,0:T(8,128)S(1)}, u32[]{:S(2)}, u32[]{:S(2)}) %collective-permute-start.21) | collective-permute-done | bytes 16416 | tf_op jit(solution)/shard_map/ppermute | solution.py:124
  100.6 3.2 %collective-permute-done.22 = f32[16,64]{1,0:T(8,128)S(1)} collective-permute-done((f32[16,64]{1,0:T(8,128)S(1)}, f32[16,64]{1,0:T(8,128)S(1)}, u32[]{:S(2)}, u32[]{:S(2)}) %collective-permute-start.22) | collective-permute-done | bytes 4128 | tf_op jit(solution)/shard_map/ppermute | solution.py:124
  103.9 2.0 %collective-permute-start.23 = (f32[16,64]{1,0:T(8,128)S(1)}, f32[16,64]{1,0:T(8,128)S(1)}, u32[]{:S(2)}, u32[]{:S(2)}) collective-permute-start(f32[16,64]{1,0:T(8,128)S(1)} %add.384), channel_id=1, source_target_pairs={{0,2},{1,3},{2,0},{3,1},{4,6},{5,7},{6,4},{7,5},{8,10},{9,11},{10,... | collective-permute-start | bytes 12296 | tf_op jit(solution)/shard_map/ppermute | solution.py:124
  108.7 2.0 %collective-permute-start.25 = (f32[16,64]{1,0:T(8,128)S(1)}, f32[16,64]{1,0:T(8,128)S(1)}, u32[]{:S(2)}, u32[]{:S(2)}) collective-permute-start(f32[16,64]{1,0:T(8,128)S(1)} %add.386), channel_id=1, source_target_pairs={{0,8},{1,9},{2,10},{3,11},{4,12},{5,13},{6,14},{7,15},{8,0},{9,1},... | collective-permute-start | bytes 12296 | tf_op jit(solution)/shard_map/ppermute | solution.py:124
  112.6 4.3 %collective-permute-done.26 = f32[16,64]{1,0:T(8,128)S(1)} collective-permute-done((f32[16,64]{1,0:T(8,128)S(1)}, f32[16,64]{1,0:T(8,128)S(1)}, u32[]{:S(2)}, u32[]{:S(2)}) %collective-permute-start.26) | collective-permute-done | bytes 4128 | tf_op jit(solution)/shard_map/ppermute | solution.py:124
  122.6 2.3 %collective-permute-done.29 = f32[1,72,256]{2,1,0:T(8,128)S(1)} collective-permute-done((f32[1,72,256]{2,1,0:T(8,128)S(1)}, f32[1,72,256]{2,1,0:T(8,128)S(1)}, u32[]{:S(2)}, u32[]{:S(2)}) %collective-permute-start.29) | collective-permute-done | bytes 73760 | tf_op jit(solution)/shard_map/ppermute | solution.py:149
  125.7 5.9 %shard_map.98 = f32[32,16,256]{2,1,0:T(8,128)} custom-call(s32[128]{0:T(128)} %clamp_bitcast_fusion.rows_ref, s32[128]{0:T(128)} %fusion.66.cols_ref, s32[128]{0:T(128)} %and_convert_fusion.live_ref, s32[1]{0:T(128)} %bitcast.5.nb_ref, f32[4,72,256]{2,1,0:T(8,128)} %pad_maximum_fusion.3.x_ref, bf16[1,1,128,256,256]{4,3,2,1,0:T(8,128)(2,1)} %t_ref.9), custom_call_target="tpu_custom_call" | custom-call | tf_op jit(solution)/shard_map/pallas_call | solution.py:69
  136.0 2.1 %collective-permute-start.31 = (f32[72,256]{1,0:T(8,128)S(1)}, f32[72,256]{1,0:T(8,128)S(1)}, u32[]{:S(2)}, u32[]{:S(2)}) collective-permute-start(f32[72,256]{1,0:T(8,128)S(1)} %get-tuple-element.130), channel_id=1, source_target_pairs={{0,8},{4,12},{8,16},{12,20},{16,24},{20,28},{24,0},{28,4},{1,9},{5... | collective-permute-start | bytes 221192 | tf_op jit(solution)/shard_map/ppermute | solution.py:173
  138.2 2.3 %collective-permute-start.33 = (f32[72,256]{1,0:T(8,128)S(1)}, f32[72,256]{1,0:T(8,128)S(1)}, u32[]{:S(2)}, u32[]{:S(2)}) collective-permute-start(f32[72,256]{1,0:T(8,128)S(1)} %get-tuple-element.128), channel_id=1, source_target_pairs={{0,24},{4,28},{8,0},{12,4},{16,8},{20,12},{24,16},{28,20},{1,25},{... | collective-permute-start | bytes 221192 | tf_op jit(solution)/shard_map/ppermute | solution.py:173
  140.5 2.5 %collective-permute-done.31 = f32[72,256]{1,0:T(8,128)S(1)} collective-permute-done((f32[72,256]{1,0:T(8,128)S(1)}, f32[72,256]{1,0:T(8,128)S(1)}, u32[]{:S(2)}, u32[]{:S(2)}) %collective-permute-start.31) | collective-permute-done | bytes 73760 | tf_op jit(solution)/shard_map/ppermute | solution.py:173
  143.0 2.4 %collective-permute-done.32 = f32[72,256]{1,0:T(8,128)S(1)} collective-permute-done((f32[72,256]{1,0:T(8,128)S(1)}, f32[72,256]{1,0:T(8,128)S(1)}, u32[]{:S(2)}, u32[]{:S(2)}) %collective-permute-start.32) | collective-permute-done | bytes 73760 | tf_op jit(solution)/shard_map/ppermute | solution.py:173
  145.6 2.0 %collective-permute-start.34 = (f32[1,72,256]{2,1,0:T(8,128)S(1)}, f32[1,72,256]{2,1,0:T(8,128)S(1)}, u32[]{:S(2)}, u32[]{:S(2)}) collective-permute-start(f32[1,72,256]{2,1,0:T(8,128)S(1)} %fusion.20), channel_id=1, source_target_pairs={{0,1},{1,0},{2,3},{3,2},{4,5},{5,4},{6,7},{7,6},{8,9},{9,8},{10,11... | collective-permute-start | bytes 221192 | tf_op jit(solution)/shard_map/ppermute | solution.py:149
  150.1 2.4 %collective-permute-done.35 = f32[1,72,256]{2,1,0:T(8,128)S(1)} collective-permute-done((f32[1,72,256]{2,1,0:T(8,128)S(1)}, f32[1,72,256]{2,1,0:T(8,128)S(1)}, u32[]{:S(2)}, u32[]{:S(2)}) %collective-permute-start.35) | collective-permute-done | bytes 73760 | tf_op jit(solution)/shard_map/ppermute | solution.py:149
  154.4 5.8 %shard_map.99 = f32[32,16,256]{2,1,0:T(8,128)} custom-call(s32[128]{0:T(128)} %clamp_bitcast_fusion.rows_ref, s32[128]{0:T(128)} %fusion.66.cols_ref, s32[128]{0:T(128)} %and_convert_fusion.live_ref, s32[1]{0:T(128)} %bitcast.5.nb_ref, f32[4,72,256]{2,1,0:T(8,128)} %pad_maximum_fusion.4.x_ref, bf16[1,1,128,256,256]{4,3,2,1,0:T(8,128)(2,1)} %t_ref.9), custom_call_target="tpu_custom_call" | custom-call | tf_op jit(solution)/shard_map/pallas_call | solution.py:69
  164.6 2.1 %collective-permute-start.38 = (f32[72,256]{1,0:T(8,128)S(1)}, f32[72,256]{1,0:T(8,128)S(1)}, u32[]{:S(2)}, u32[]{:S(2)}) collective-permute-start(f32[72,256]{1,0:T(8,128)S(1)} %get-tuple-element.124), channel_id=1, source_target_pairs={{0,8},{4,12},{8,16},{12,20},{16,24},{20,28},{24,0},{28,4},{1,9},{5... | collective-permute-start | bytes 221192 | tf_op jit(solution)/shard_map/ppermute | solution.py:173
  168.5 2.0 %collective-permute-start.40 = (f32[72,256]{1,0:T(8,128)S(1)}, f32[72,256]{1,0:T(8,128)S(1)}, u32[]{:S(2)}, u32[]{:S(2)}) collective-permute-start(f32[72,256]{1,0:T(8,128)S(1)} %get-tuple-element.125), channel_id=1, source_target_pairs={{0,24},{4,28},{8,0},{12,4},{16,8},{20,12},{24,16},{28,20},{1,25},{... | collective-permute-start | bytes 221192 | tf_op jit(solution)/shard_map/ppermute | solution.py:173
  171.2 3.0 %collective-permute-done.39 = f32[72,256]{1,0:T(8,128)S(1)} collective-permute-done((f32[72,256]{1,0:T(8,128)S(1)}, f32[72,256]{1,0:T(8,128)S(1)}, u32[]{:S(2)}, u32[]{:S(2)}) %collective-permute-start.39) | collective-permute-done | bytes 73760 | tf_op jit(solution)/shard_map/ppermute | solution.py:173
  (153 shorter events, 73.7 us)
Async XLA Ops:
  2.6 10.4 %collective-permute-start = (f32[1,72,256]{2,1,0:T(8,128)S(1)}, f32[1,72,256]{2,1,0:T(8,128)S(1)}, u32[]{:S(2)}, u32[]{:S(2)}) collective-permute-start(f32[1,72,256]{2,1,0:T(8,128)S(1)} %fusion.24), channel_id=1, source_target_pairs={{0,1},{1,0},{2,3},{3,2},{4,5},{5,4},{6,7},{7,6},{8,9},{9,8},{10,11... | collective-permute-start | bytes 221192 | tf_op jit(solution)/shard_map/ppermute | solution.py:149
  5.6 7.4 %collective-permute-start.1 = (f32[1,72,256]{2,1,0:T(8,128)S(1)}, f32[1,72,256]{2,1,0:T(8,128)S(1)}, u32[]{:S(2)}, u32[]{:S(2)}) collective-permute-start(f32[1,72,256]{2,1,0:T(8,128)S(1)} %fusion.24), channel_id=1, source_target_pairs={{0,2},{1,3},{2,0},{3,1},{4,6},{5,7},{6,4},{7,5},{8,10},{9,11},{10,... | collective-permute-start | bytes 221192 | tf_op jit(solution)/shard_map/ppermute | solution.py:149
  7.1 5.8 %collective-permute-start.2 = (f32[1,72,256]{2,1,0:T(8,128)S(1)}, f32[1,72,256]{2,1,0:T(8,128)S(1)}, u32[]{:S(2)}, u32[]{:S(2)}) collective-permute-start(f32[1,72,256]{2,1,0:T(8,128)S(1)} %fusion.24), channel_id=1, source_target_pairs={{0,3},{1,2},{2,1},{3,0},{4,7},{5,6},{6,5},{7,4},{8,11},{9,10},{10,... | collective-permute-start | bytes 221192 | tf_op jit(solution)/shard_map/ppermute | solution.py:149
  23.3 7.7 %collective-permute-start.4 = (f32[72,256]{1,0:T(8,128)S(1)}, f32[72,256]{1,0:T(8,128)S(1)}, u32[]{:S(2)}, u32[]{:S(2)}) collective-permute-start(f32[72,256]{1,0:T(8,128)S(1)} %get-tuple-element.134), channel_id=1, source_target_pairs={{0,8},{4,12},{8,16},{12,20},{16,24},{20,28},{24,0},{28,4},{1,9},{5... | collective-permute-start | bytes 221192 | tf_op jit(solution)/shard_map/ppermute | solution.py:173
  25.4 6.3 %collective-permute-start.5 = (f32[72,256]{1,0:T(8,128)S(1)}, f32[72,256]{1,0:T(8,128)S(1)}, u32[]{:S(2)}, u32[]{:S(2)}) collective-permute-start(f32[72,256]{1,0:T(8,128)S(1)} %get-tuple-element.136), channel_id=1, source_target_pairs={{0,16},{4,20},{8,24},{12,28},{16,0},{20,4},{24,8},{28,12},{1,17},{... | collective-permute-start | bytes 221192 | tf_op jit(solution)/shard_map/ppermute | solution.py:173
  28.2 5.0 %collective-permute-start.6 = (f32[72,256]{1,0:T(8,128)S(1)}, f32[72,256]{1,0:T(8,128)S(1)}, u32[]{:S(2)}, u32[]{:S(2)}) collective-permute-start(f32[72,256]{1,0:T(8,128)S(1)} %get-tuple-element.135), channel_id=1, source_target_pairs={{0,24},{4,28},{8,0},{12,4},{16,8},{20,12},{24,16},{28,20},{1,25},{... | collective-permute-start | bytes 221192 | tf_op jit(solution)/shard_map/ppermute | solution.py:173
  33.4 4.7 %collective-permute-start.7 = (f32[1,72,256]{2,1,0:T(8,128)S(1)}, f32[1,72,256]{2,1,0:T(8,128)S(1)}, u32[]{:S(2)}, u32[]{:S(2)}) collective-permute-start(f32[1,72,256]{2,1,0:T(8,128)S(1)} %fusion.23), channel_id=1, source_target_pairs={{0,1},{1,0},{2,3},{3,2},{4,5},{5,4},{6,7},{7,6},{8,9},{9,8},{10,11... | collective-permute-start | bytes 221192 | tf_op jit(solution)/shard_map/ppermute | solution.py:149
  35.3 4.4 %collective-permute-start.8 = (f32[1,72,256]{2,1,0:T(8,128)S(1)}, f32[1,72,256]{2,1,0:T(8,128)S(1)}, u32[]{:S(2)}, u32[]{:S(2)}) collective-permute-start(f32[1,72,256]{2,1,0:T(8,128)S(1)} %fusion.23), channel_id=1, source_target_pairs={{0,2},{1,3},{2,0},{3,1},{4,6},{5,7},{6,4},{7,5},{8,10},{9,11},{10,... | collective-permute-start | bytes 221192 | tf_op jit(solution)/shard_map/ppermute | solution.py:149
  36.8 5.3 %collective-permute-start.9 = (f32[1,72,256]{2,1,0:T(8,128)S(1)}, f32[1,72,256]{2,1,0:T(8,128)S(1)}, u32[]{:S(2)}, u32[]{:S(2)}) collective-permute-start(f32[1,72,256]{2,1,0:T(8,128)S(1)} %fusion.23), channel_id=1, source_target_pairs={{0,3},{1,2},{2,1},{3,0},{4,7},{5,6},{6,5},{7,4},{8,11},{9,10},{10,... | collective-permute-start | bytes 221192 | tf_op jit(solution)/shard_map/ppermute | solution.py:149
  53.0 8.0 %collective-permute-start.11 = (f32[72,256]{1,0:T(8,128)S(1)}, f32[72,256]{1,0:T(8,128)S(1)}, u32[]{:S(2)}, u32[]{:S(2)}) collective-permute-start(f32[72,256]{1,0:T(8,128)S(1)} %get-tuple-element.131), channel_id=1, source_target_pairs={{0,8},{4,12},{8,16},{12,20},{16,24},{20,28},{24,0},{28,4},{1,9},{5... | collective-permute-start | bytes 221192 | tf_op jit(solution)/shard_map/ppermute | solution.py:173
  55.1 8.7 %collective-permute-start.12 = (f32[72,256]{1,0:T(8,128)S(1)}, f32[72,256]{1,0:T(8,128)S(1)}, u32[]{:S(2)}, u32[]{:S(2)}) collective-permute-start(f32[72,256]{1,0:T(8,128)S(1)} %get-tuple-element.133), channel_id=1, source_target_pairs={{0,16},{4,20},{8,24},{12,28},{16,0},{20,4},{24,8},{28,12},{1,17},{... | collective-permute-start | bytes 221192 | tf_op jit(solution)/shard_map/ppermute | solution.py:173
  58.4 5.8 %collective-permute-start.13 = (f32[72,256]{1,0:T(8,128)S(1)}, f32[72,256]{1,0:T(8,128)S(1)}, u32[]{:S(2)}, u32[]{:S(2)}) collective-permute-start(f32[72,256]{1,0:T(8,128)S(1)} %get-tuple-element.132), channel_id=1, source_target_pairs={{0,24},{4,28},{8,0},{12,4},{16,8},{20,12},{24,16},{28,20},{1,25},{... | collective-permute-start | bytes 221192 | tf_op jit(solution)/shard_map/ppermute | solution.py:173
  64.4 5.1 %collective-permute-start.14 = (f32[1,72,256]{2,1,0:T(8,128)S(1)}, f32[1,72,256]{2,1,0:T(8,128)S(1)}, u32[]{:S(2)}, u32[]{:S(2)}) collective-permute-start(f32[1,72,256]{2,1,0:T(8,128)S(1)} %fusion.22), channel_id=1, source_target_pairs={{0,1},{1,0},{2,3},{3,2},{4,5},{5,4},{6,7},{7,6},{8,9},{9,8},{10,11... | collective-permute-start | bytes 221192 | tf_op jit(solution)/shard_map/ppermute | solution.py:149
  64.9 4.8 %collective-permute-start.15 = (f32[1,72,256]{2,1,0:T(8,128)S(1)}, f32[1,72,256]{2,1,0:T(8,128)S(1)}, u32[]{:S(2)}, u32[]{:S(2)}) collective-permute-start(f32[1,72,256]{2,1,0:T(8,128)S(1)} %fusion.22), channel_id=1, source_target_pairs={{0,2},{1,3},{2,0},{3,1},{4,6},{5,7},{6,4},{7,5},{8,10},{9,11},{10,... | collective-permute-start | bytes 221192 | tf_op jit(solution)/shard_map/ppermute | solution.py:149
  65.7 5.3 %collective-permute-start.16 = (f32[1,72,256]{2,1,0:T(8,128)S(1)}, f32[1,72,256]{2,1,0:T(8,128)S(1)}, u32[]{:S(2)}, u32[]{:S(2)}) collective-permute-start(f32[1,72,256]{2,1,0:T(8,128)S(1)} %fusion.22), channel_id=1, source_target_pairs={{0,3},{1,2},{2,1},{3,0},{4,7},{5,6},{6,5},{7,4},{8,11},{9,10},{10,... | collective-permute-start | bytes 221192 | tf_op jit(solution)/shard_map/ppermute | solution.py:149
  79.9 4.0 %collective-permute-start.17 = (f32[4,16,64]{2,1,0:T(8,128)S(1)}, f32[4,16,64]{2,1,0:T(8,128)S(1)}, u32[]{:S(2)}, u32[]{:S(2)}) collective-permute-start(f32[4,16,64]{2,1,0:T(8,128)S(1)} %pad_maximum_fusion.5), channel_id=1, source_target_pairs={{0,1},{1,0},{2,3},{3,2},{4,5},{5,4},{6,7},{7,6},{8,9},{9,8},{10,11... | collective-permute-start | bytes 49160 | tf_op jit(solution)/shard_map/ppermute | solution.py:124
  83.9 4.0 %collective-permute-start.18 = (f32[4,16,64]{2,1,0:T(8,128)S(1)}, f32[4,16,64]{2,1,0:T(8,128)S(1)}, u32[]{:S(2)}, u32[]{:S(2)}) collective-permute-start(f32[4,16,64]{2,1,0:T(8,128)S(1)} %fusion.75), channel_id=1, source_target_pairs={{0,2},{1,3},{2,0},{3,1},{4,6},{5,7},{6,4},{7,5},{8,10},{9,11},{10,... | collective-permute-start | bytes 49160 | tf_op jit(solution)/shard_map/ppermute | solution.py:124
  89.1 5.5 %collective-permute-start.20 = (f32[4,16,64]{2,1,0:T(8,128)S(1)}, f32[4,16,64]{2,1,0:T(8,128)S(1)}, u32[]{:S(2)}, u32[]{:S(2)}) collective-permute-start(f32[4,16,64]{2,1,0:T(8,128)S(1)} %add.379), channel_id=1, source_target_pairs={{0,8},{1,9},{2,10},{3,11},{4,12},{5,13},{6,14},{7,15},{8,0},{9,1},... | collective-permute-start | bytes 49160 | tf_op jit(solution)/shard_map/ppermute | solution.py:124
  94.6 4.8 %collective-permute-start.21 = (f32[4,16,64]{2,1,0:T(8,128)S(1)}, f32[4,16,64]{2,1,0:T(8,128)S(1)}, u32[]{:S(2)}, u32[]{:S(2)}) collective-permute-start(f32[4,16,64]{2,1,0:T(8,128)S(1)} %add.380), channel_id=1, source_target_pairs={{0,16},{1,17},{2,18},{3,19},{4,20},{5,21},{6,22},{7,23},{8,24},{9,... | collective-permute-start | bytes 49160 | tf_op jit(solution)/shard_map/ppermute | solution.py:124
  112.4 4.5 %collective-permute-start.26 = (f32[16,64]{1,0:T(8,128)S(1)}, f32[16,64]{1,0:T(8,128)S(1)}, u32[]{:S(2)}, u32[]{:S(2)}) collective-permute-start(f32[16,64]{1,0:T(8,128)S(1)} %add.387), channel_id=1, source_target_pairs={{0,16},{1,17},{2,18},{3,19},{4,20},{5,21},{6,22},{7,23},{8,24},{9,... | collective-permute-start | bytes 12296 | tf_op jit(solution)/shard_map/ppermute | solution.py:124
  117.5 4.4 %collective-permute-start.27 = (f32[1,72,256]{2,1,0:T(8,128)S(1)}, f32[1,72,256]{2,1,0:T(8,128)S(1)}, u32[]{:S(2)}, u32[]{:S(2)}) collective-permute-start(f32[1,72,256]{2,1,0:T(8,128)S(1)} %fusion.21), channel_id=1, source_target_pairs={{0,1},{1,0},{2,3},{3,2},{4,5},{5,4},{6,7},{7,6},{8,9},{9,8},{10,11... | collective-permute-start | bytes 221192 | tf_op jit(solution)/shard_map/ppermute | solution.py:149
  118.0 4.6 %collective-permute-start.28 = (f32[1,72,256]{2,1,0:T(8,128)S(1)}, f32[1,72,256]{2,1,0:T(8,128)S(1)}, u32[]{:S(2)}, u32[]{:S(2)}) collective-permute-start(f32[1,72,256]{2,1,0:T(8,128)S(1)} %fusion.21), channel_id=1, source_target_pairs={{0,2},{1,3},{2,0},{3,1},{4,6},{5,7},{6,4},{7,5},{8,10},{9,11},{10,... | collective-permute-start | bytes 221192 | tf_op jit(solution)/shard_map/ppermute | solution.py:149
  119.7 5.3 %collective-permute-start.29 = (f32[1,72,256]{2,1,0:T(8,128)S(1)}, f32[1,72,256]{2,1,0:T(8,128)S(1)}, u32[]{:S(2)}, u32[]{:S(2)}) collective-permute-start(f32[1,72,256]{2,1,0:T(8,128)S(1)} %fusion.21), channel_id=1, source_target_pairs={{0,3},{1,2},{2,1},{3,0},{4,7},{5,6},{6,5},{7,4},{8,11},{9,10},{10,... | collective-permute-start | bytes 221192 | tf_op jit(solution)/shard_map/ppermute | solution.py:149
  136.0 7.0 %collective-permute-start.31 = (f32[72,256]{1,0:T(8,128)S(1)}, f32[72,256]{1,0:T(8,128)S(1)}, u32[]{:S(2)}, u32[]{:S(2)}) collective-permute-start(f32[72,256]{1,0:T(8,128)S(1)} %get-tuple-element.130), channel_id=1, source_target_pairs={{0,8},{4,12},{8,16},{12,20},{16,24},{20,28},{24,0},{28,4},{1,9},{5... | collective-permute-start | bytes 221192 | tf_op jit(solution)/shard_map/ppermute | solution.py:173
  138.1 7.3 %collective-permute-start.32 = (f32[72,256]{1,0:T(8,128)S(1)}, f32[72,256]{1,0:T(8,128)S(1)}, u32[]{:S(2)}, u32[]{:S(2)}) collective-permute-start(f32[72,256]{1,0:T(8,128)S(1)} %get-tuple-element.129), channel_id=1, source_target_pairs={{0,16},{4,20},{8,24},{12,28},{16,0},{20,4},{24,8},{28,12},{1,17},{... | collective-permute-start | bytes 221192 | tf_op jit(solution)/shard_map/ppermute | solution.py:173
  138.2 7.2 %collective-permute-start.33 = (f32[72,256]{1,0:T(8,128)S(1)}, f32[72,256]{1,0:T(8,128)S(1)}, u32[]{:S(2)}, u32[]{:S(2)}) collective-permute-start(f32[72,256]{1,0:T(8,128)S(1)} %get-tuple-element.128), channel_id=1, source_target_pairs={{0,24},{4,28},{8,0},{12,4},{16,8},{20,12},{24,16},{28,20},{1,25},{... | collective-permute-start | bytes 221192 | tf_op jit(solution)/shard_map/ppermute | solution.py:173
  145.6 4.4 %collective-permute-start.34 = (f32[1,72,256]{2,1,0:T(8,128)S(1)}, f32[1,72,256]{2,1,0:T(8,128)S(1)}, u32[]{:S(2)}, u32[]{:S(2)}) collective-permute-start(f32[1,72,256]{2,1,0:T(8,128)S(1)} %fusion.20), channel_id=1, source_target_pairs={{0,1},{1,0},{2,3},{3,2},{4,5},{5,4},{6,7},{7,6},{8,9},{9,8},{10,11... | collective-permute-start | bytes 221192 | tf_op jit(solution)/shard_map/ppermute | solution.py:149
  147.7 4.8 %collective-permute-start.35 = (f32[1,72,256]{2,1,0:T(8,128)S(1)}, f32[1,72,256]{2,1,0:T(8,128)S(1)}, u32[]{:S(2)}, u32[]{:S(2)}) collective-permute-start(f32[1,72,256]{2,1,0:T(8,128)S(1)} %fusion.20), channel_id=1, source_target_pairs={{0,2},{1,3},{2,0},{3,1},{4,6},{5,7},{6,4},{7,5},{8,10},{9,11},{10,... | collective-permute-start | bytes 221192 | tf_op jit(solution)/shard_map/ppermute | solution.py:149
  148.4 5.3 %collective-permute-start.36 = (f32[1,72,256]{2,1,0:T(8,128)S(1)}, f32[1,72,256]{2,1,0:T(8,128)S(1)}, u32[]{:S(2)}, u32[]{:S(2)}) collective-permute-start(f32[1,72,256]{2,1,0:T(8,128)S(1)} %fusion.20), channel_id=1, source_target_pairs={{0,3},{1,2},{2,1},{3,0},{4,7},{5,6},{6,5},{7,4},{8,11},{9,10},{10,... | collective-permute-start | bytes 221192 | tf_op jit(solution)/shard_map/ppermute | solution.py:149
  164.6 6.6 %collective-permute-start.38 = (f32[72,256]{1,0:T(8,128)S(1)}, f32[72,256]{1,0:T(8,128)S(1)}, u32[]{:S(2)}, u32[]{:S(2)}) collective-permute-start(f32[72,256]{1,0:T(8,128)S(1)} %get-tuple-element.124), channel_id=1, source_target_pairs={{0,8},{4,12},{8,16},{12,20},{16,24},{20,28},{24,0},{28,4},{1,9},{5... | collective-permute-start | bytes 221192 | tf_op jit(solution)/shard_map/ppermute | solution.py:173
  166.7 7.6 %collective-permute-start.39 = (f32[72,256]{1,0:T(8,128)S(1)}, f32[72,256]{1,0:T(8,128)S(1)}, u32[]{:S(2)}, u32[]{:S(2)}) collective-permute-start(f32[72,256]{1,0:T(8,128)S(1)} %get-tuple-element.126), channel_id=1, source_target_pairs={{0,16},{4,20},{8,24},{12,28},{16,0},{20,4},{24,8},{28,12},{1,17},{... | collective-permute-start | bytes 221192 | tf_op jit(solution)/shard_map/ppermute | solution.py:173
  168.5 5.8 %collective-permute-start.40 = (f32[72,256]{1,0:T(8,128)S(1)}, f32[72,256]{1,0:T(8,128)S(1)}, u32[]{:S(2)}, u32[]{:S(2)}) collective-permute-start(f32[72,256]{1,0:T(8,128)S(1)} %get-tuple-element.125), channel_id=1, source_target_pairs={{0,24},{4,28},{8,0},{12,4},{16,8},{20,12},{24,16},{28,20},{1,25},{... | collective-permute-start | bytes 221192 | tf_op jit(solution)/shard_map/ppermute | solution.py:173
  (12 other events, 93.7 us)

commit v2 on v1

--- a/solution.py
+++ b/solution.py
@@ -197,7 +197,6 @@
         )
 
     tele_sums = jnp.sum(tele, axis=2)
-    weight_partial = jnp.einsum("bk,ba->ka", tele_sums, piece_hot, precision=highest)
 
     relaxed_one = relaxation(tele)
     relaxed_two = relaxation(relaxed_one)
@@ -208,20 +207,47 @@
         row_blocks, vectors,
     ).sum(axis=2)
     block_sums = jnp.sum(relaxed_two, axis=2)
-    totals_partial = jnp.einsum("bk,ba->ka", block_sums, piece_hot, precision=highest)
-    lost_mass_partial = jnp.einsum(
-        "bk,ba->ka", block_sums * piece_dangling[:, None], piece_hot, precision=highest
-    )
     row_agg = agg_of_block[row_global]
     col_agg = agg_of_block[col_global]
-    row_hot = (row_agg[:, None] == agg_range[None, :]).astype(jnp.float32)
-    col_hot = (col_agg[:, None] == agg_range[None, :]).astype(jnp.float32)
-    inflow_partial = jnp.einsum("tk,ta->ka", entries, row_hot, precision=highest)
-    inflow_one, totals, lost_mass, weight = tree_sum(
-        jnp.stack([inflow_partial, totals_partial, lost_mass_partial, weight_partial]),
-        all_axes,
-        all_count,
-    )
+    fields = [
+        entries.reshape(-1),
+        row_agg.astype(jnp.float32),
+        col_agg.astype(jnp.float32),
+        block_sums.reshape(-1),
+        tele_sums.reshape(-1),
+        piece_agg.astype(jnp.float32),
+        piece_dangling,
+    ]
+    sizes = [f.shape[0] for f in fields]
+    shared = jnp.concatenate(fields)[None]
+    if all_count & (all_count - 1) == 0:
+        shift = 1
+        while shift < all_count:
+            got = lax.ppermute(shared, all_axes, [(i, i ^ shift) for i in range(all_count)])
+            shared = jnp.concatenate([shared, got], axis=0)
+            shift *= 2
+    else:
+        shared = lax.all_gather(shared[0], all_axes, axis=0, tiled=False)
+    offsets = [0]
+    for size in sizes:
+        offsets.append(offsets[-1] + size)
+    every = [shared[:, offsets[i]:offsets[i + 1]] for i in range(len(sizes))]
+    all_entries = every[0].reshape(-1, vectors)
+    all_row_hot = (every[1].reshape(-1)[:, None] == agg_range[None, :].astype(jnp.float32))
+    all_col_hot = (every[2].reshape(-1)[:, None] == agg_range[None, :].astype(jnp.float32))
+    all_row_hot = all_row_hot.astype(jnp.float32)
+    all_col_hot = all_col_hot.astype(jnp.float32)
+    all_block_sums = every[3].reshape(-1, vectors)
+    all_tele_sums = every[4].reshape(-1, vectors)
+    all_block_hot = (every[5].reshape(-1)[:, None] == agg_range[None, :].astype(jnp.float32))
+    all_block_hot = all_block_hot.astype(jnp.float32)
+    all_dangling = every[6].reshape(-1)
+    totals = jnp.einsum("bk,ba->ka", all_block_sums, all_block_hot, precision=highest)
+    lost_mass = jnp.einsum(
+        "bk,ba->ka", all_block_sums * all_dangling[:, None], all_block_hot, precision=highest
+    )
+    weight = jnp.einsum("bk,ba->ka", all_tele_sums, all_block_hot, precision=highest)
+    inflow_one = jnp.einsum("tk,ta->ka", all_entries, all_row_hot, precision=highest)
 
     def coarse_sweep(inflow, ratios):
         carried = jnp.sum(lost_mass * ratios, axis=1)
@@ -232,11 +258,9 @@
 
     level_one = coarse_sweep(inflow_one, jnp.ones((vectors, agg_count), jnp.float32))
     ratios_one = level_one / totals
-    ratio_at_tile = jnp.einsum("ka,ta->tk", ratios_one, col_hot, precision=highest)
-    inflow_two = tree_sum(
-        jnp.einsum("tk,ta->ka", entries * ratio_at_tile, row_hot, precision=highest),
-        all_axes,
-        all_count,
+    ratio_at_tile = jnp.einsum("ka,ta->tk", ratios_one, all_col_hot, precision=highest)
+    inflow_two = jnp.einsum(
+        "tk,ta->ka", all_entries * ratio_at_tile, all_row_hot, precision=highest
     )
     level_two = coarse_sweep(inflow_two, ratios_one)
     ratios_two = level_two / totals

time: 178 us -> 175 us (0.983); the launches traced: 175 us -> 179 us
  matrix products: 2.29 us -> 8.05 us
  other arithmetic: 21.8 us -> 17.1 us
  starting transfers between devices: 56.8 us -> 52.8 us
  local copies, waits for them, and re-layouts: 5.86 us -> 9.56 us
  waiting for transfers between devices: 57.1 us -> 59.6 us
    ppermute x12, waiting for transfers between devices: 15 us -> 23 us  [reduce_rows(): total = total + lax.ppermute(send, 'src', pairs)]
    dot_general x6, matrix products: 1.36 us -> 7.11 us  [the longest x1 2.45 us: per_device(): jnp.einsum('tk,ta->ka', all_entries * ratio_at_tile, all_row_hot, precisi...]
    ppermute x10 -> x5, starting transfers between devices: 11.8 us -> 6.07 us  [per_device(): lax.ppermute(shared, all_axes, [(i, i ^ shift) for i in range(all_count)])]
    ppermute x10 -> x5, waiting for transfers between devices: 23.1 us -> 18.4 us  [per_device(): lax.ppermute(shared, all_axes, [(i, i ^ shift) for i in range(all_count)])]
    ppermute x12, starting transfers between devices: 24.2 us -> 27.7 us  [reduce_rows(): total = total + lax.ppermute(send, 'src', pairs)]
    reduce_sum x4, other arithmetic: 2.23 us -> 0.09 us  [spread_columns(): lost_dst = jnp.sum(payload[:, payload_rows, :vectors], axis=0)]
    concatenate x5, other arithmetic: 3.02 us -> 0.88 us  [spread_columns(): payload = jnp.concatenate(pieces, axis=0)]
    ppermute x15, waiting for transfers between devices: 14.2 us -> 12.1 us  [spread_columns(): lax.ppermute(payload, 'dst', [(i, i ^ v) for i in range(dst_count)])]
  transfers between devices with their start and end apart: 41 -> 36, of which waited for: 33 -> 30; matrix products, arithmetic and copies ran while one was open for 5% -> 5% of each run, Pallas kernels for 0% -> 0%
where the time goes in v2:
time: 175 us; the launch traced here: 179 us
  waiting for transfers between devices  59.6 us (34%)
  starting transfers between devices  52.8 us (30%)
  Pallas kernels  29.6 us (17%)
  other arithmetic  17.1 us (10%)
  local copies, waits for them, and re-layouts  9.56 us (5%)
  matrix products  8.05 us (5%)
  between operations  1.8 us (1%)
    pallas_call x5, Pallas kernels, tile_pass(): pl.pallas_call(functools.partial(tile_kernel, mode, payload_rows // vecto...  29.6 us
    ppermute x12, starting transfers between devices, reduce_rows(): total = total + lax.ppermute(send, 'src', pairs)  27.7 us
    ppermute x12, waiting for transfers between devices, reduce_rows(): total = total + lax.ppermute(send, 'src', pairs)  23 us
    ppermute x15, starting transfers between devices, spread_columns(): lax.ppermute(payload, 'dst', [(i, i ^ v) for i in range(dst_count)])  18.8 us
    ppermute x5, waiting for transfers between devices, per_device(): lax.ppermute(shared, all_axes, [(i, i ^ shift) for i in range(all_count)])  18.4 us
    ppermute x15, waiting for transfers between devices, spread_columns(): lax.ppermute(payload, 'dst', [(i, i ^ v) for i in range(dst_count)])  12.1 us
    ppermute x4, waiting for transfers between devices, reduce_rows(): part = keep + lax.ppermute(give, 'src', [(i, i ^ 1) for i in range(n)])  6.1 us
    ppermute x5, starting transfers between devices, per_device(): lax.ppermute(shared, all_axes, [(i, i ^ shift) for i in range(all_count)])  6.07 us
  transfers between devices with their start and end apart: 36, of which 30 were waited for; matrix products, arithmetic and copies ran while one was open for 5% of the time, Pallas kernels for 0%

profile of v2, /device:TPU:0, one launch (start us, length us, event | category | flops | bytes accessed | tf_op | source)
XLA Modules:
  0.0 178.6 jit_solution(15182892258763668529)
XLA Ops:
  2.6 4.0 %collective-permute-start.2 = (f32[1,72,256]{2,1,0:T(8,128)S(1)}, f32[1,72,256]{2,1,0:T(8,128)S(1)}, u32[]{:S(2)}, u32[]{:S(2)}) collective-permute-start(f32[1,72,256]{2,1,0:T(8,128)S(1)} %fusion.62), channel_id=1, source_target_pairs={{0,3},{1,2},{2,1},{3,0},{4,7},{5,6},{6,5},{7,4},{8,11},{9,10},{10,... | collective-permute-start | bytes 221192 | tf_op jit(solution)/shard_map/ppermute | solution.py:149
  13.9 5.8 %shard_map.95 = f32[32,16,256]{2,1,0:T(8,128)} custom-call(s32[128]{0:T(128)} %clamp_bitcast_fusion.rows_ref, s32[128]{0:T(128)} %fusion.96.cols_ref, s32[128]{0:T(128)} %and_convert_fusion.live_ref, s32[1]{0:T(128)} %bitcast.5.nb_ref, f32[4,72,256]{2,1,0:T(8,128)} %copy-done.2, bf16[1,1,128,256,256]{4,3,2,1,0:T(8,128)(2,1)} %t_ref.9), custom_call_target="tpu_custom_call" | custom-call | tf_op jit(solution)/shard_map/pallas_call | solution.py:69
  23.3 2.0 %collective-permute-start.4 = (f32[72,256]{1,0:T(8,128)S(1)}, f32[72,256]{1,0:T(8,128)S(1)}, u32[]{:S(2)}, u32[]{:S(2)}) collective-permute-start(f32[72,256]{1,0:T(8,128)S(1)} %get-tuple-element.138), channel_id=1, source_target_pairs={{0,8},{4,12},{8,16},{12,20},{16,24},{20,28},{24,0},{28,4},{1,9},{5... | collective-permute-start | bytes 221192 | tf_op jit(solution)/shard_map/ppermute | solution.py:173
  25.3 5.1 %collective-permute-start.6 = (f32[72,256]{1,0:T(8,128)S(1)}, f32[72,256]{1,0:T(8,128)S(1)}, u32[]{:S(2)}, u32[]{:S(2)}) collective-permute-start(f32[72,256]{1,0:T(8,128)S(1)} %get-tuple-element.139), channel_id=1, source_target_pairs={{0,24},{4,28},{8,0},{12,4},{16,8},{20,12},{24,16},{28,20},{1,25},{... | collective-permute-start | bytes 221192 | tf_op jit(solution)/shard_map/ppermute | solution.py:173
  31.4 1.7 collective-permute-done.4
  33.8 3.9 %collective-permute-done.5 = f32[72,256]{1,0:T(8,128)S(1)} collective-permute-done((f32[72,256]{1,0:T(8,128)S(1)}, f32[72,256]{1,0:T(8,128)S(1)}, u32[]{:S(2)}, u32[]{:S(2)}) %collective-permute-start.5) | collective-permute-done | bytes 73760 | tf_op jit(solution)/shard_map/ppermute | solution.py:173
  38.0 2.5 %collective-permute-start.9 = (f32[1,72,256]{2,1,0:T(8,128)S(1)}, f32[1,72,256]{2,1,0:T(8,128)S(1)}, u32[]{:S(2)}, u32[]{:S(2)}) collective-permute-start(f32[1,72,256]{2,1,0:T(8,128)S(1)} %fusion.61), channel_id=1, source_target_pairs={{0,3},{1,2},{2,1},{3,0},{4,7},{5,6},{6,5},{7,4},{8,11},{9,10},{10,... | collective-permute-start | bytes 221192 | tf_op jit(solution)/shard_map/ppermute | solution.py:149
  41.5 1.8 %collective-permute-done.9 = f32[1,72,256]{2,1,0:T(8,128)S(1)} collective-permute-done((f32[1,72,256]{2,1,0:T(8,128)S(1)}, f32[1,72,256]{2,1,0:T(8,128)S(1)}, u32[]{:S(2)}, u32[]{:S(2)}) %collective-permute-start.9) | collective-permute-done | bytes 73760 | tf_op jit(solution)/shard_map/ppermute | solution.py:149
  45.7 5.8 %shard_map.96 = f32[32,16,256]{2,1,0:T(8,128)} custom-call(s32[128]{0:T(128)} %clamp_bitcast_fusion.rows_ref, s32[128]{0:T(128)} %fusion.96.cols_ref, s32[128]{0:T(128)} %and_convert_fusion.live_ref, s32[1]{0:T(128)} %bitcast.5.nb_ref, f32[4,72,256]{2,1,0:T(8,128)} %copy-done.3, bf16[1,1,128,256,256]{4,3,2,1,0:T(8,128)(2,1)} %t_ref.9), custom_call_target="tpu_custom_call" | custom-call | tf_op jit(solution)/shard_map/pallas_call | solution.py:69
  55.2 5.3 %collective-permute-start.13 = (f32[72,256]{1,0:T(8,128)S(1)}, f32[72,256]{1,0:T(8,128)S(1)}, u32[]{:S(2)}, u32[]{:S(2)}) collective-permute-start(f32[72,256]{1,0:T(8,128)S(1)} %get-tuple-element.136), channel_id=1, source_target_pairs={{0,24},{4,28},{8,0},{12,4},{16,8},{20,12},{24,16},{28,20},{1,25},{... | collective-permute-start | bytes 221192 | tf_op jit(solution)/shard_map/ppermute | solution.py:173
  63.2 4.4 %collective-permute-done.12 = f32[72,256]{1,0:T(8,128)S(1)} collective-permute-done((f32[72,256]{1,0:T(8,128)S(1)}, f32[72,256]{1,0:T(8,128)S(1)}, u32[]{:S(2)}, u32[]{:S(2)}) %collective-permute-start.12) | collective-permute-done | bytes 73760 | tf_op jit(solution)/shard_map/ppermute | solution.py:173
  67.8 2.0 %collective-permute-start.16 = (f32[1,72,256]{2,1,0:T(8,128)S(1)}, f32[1,72,256]{2,1,0:T(8,128)S(1)}, u32[]{:S(2)}, u32[]{:S(2)}) collective-permute-start(f32[1,72,256]{2,1,0:T(8,128)S(1)} %fusion.60), channel_id=1, source_target_pairs={{0,3},{1,2},{2,1},{3,0},{4,7},{5,6},{6,5},{7,4},{8,11},{9,10},{10,... | collective-permute-start | bytes 221192 | tf_op jit(solution)/shard_map/ppermute | solution.py:149
  75.8 6.4 %shard_map.97 = f32[128,16,128]{2,1,0:T(8,128)} custom-call(s32[128]{0:T(128)} %clamp_bitcast_fusion.rows_ref, s32[128]{0:T(128)} %fusion.96.cols_ref, s32[128]{0:T(128)} %and_convert_fusion.live_ref, s32[1]{0:T(128)} %bitcast.5.nb_ref, f32[4,72,256]{2,1,0:T(8,128)} %pad_maximum_fusion.2.x_ref, bf16[1,1,128,256,256]{4,3,2,1,0:T(8,128)(2,1)} %t_ref.9), custom_call_target="tpu_custom_call" | custom-call | tf_op jit(solution)/shard_map/pallas_call | solution.py:69
  84.7 3.0 %collective-permute-done.17 = f32[1,2440]{1,0:T(1,128)S(1)} collective-permute-done((f32[1,2440]{1,0:T(1,128)S(1)}, f32[1,2440]{1,0:T(1,128)S(1)}, u32[]{:S(2)}, u32[]{:S(2)}) %collective-permute-start.17) | collective-permute-done | bytes 9792 | tf_op jit(solution)/shard_map/ppermute | solution.py:226
  88.9 2.7 %collective-permute-done.18 = f32[2,2440]{1,0:T(2,128)S(1)} collective-permute-done((f32[2,2440]{1,0:T(2,128)S(1)}, f32[2,2440]{1,0:T(2,128)S(1)}, u32[]{:S(2)}, u32[]{:S(2)}) %collective-permute-start.18) | collective-permute-done | bytes 19552 | tf_op jit(solution)/shard_map/ppermute | solution.py:226
  93.4 4.1 %collective-permute-done.20 = f32[8,2440]{1,0:T(8,128)S(1)} collective-permute-done((f32[8,2440]{1,0:T(8,128)S(1)}, f32[8,2440]{1,0:T(8,128)S(1)}, u32[]{:S(2)}, u32[]{:S(2)}) %collective-permute-start.20) | collective-permute-done | bytes 78112 | tf_op jit(solution)/shard_map/ppermute | solution.py:226
  97.5 3.6 %collective-permute-start.21 = (f32[16,2440]{1,0:T(8,128)S(1)}, f32[16,2440]{1,0:T(8,128)S(1)}, u32[]{:S(2)}, u32[]{:S(2)}) collective-permute-start(f32[16,2440]{1,0:T(8,128)S(1)} %concatenate.118), channel_id=1, source_target_pairs={{0,16},{1,17},{2,18},{3,19},{4,20},{5,21},{6,22},{7,23},{8,24},{9,... | collective-permute-start | bytes 468488 | tf_op jit(solution)/shard_map/ppermute | solution.py:226
  101.1 7.5 %collective-permute-done.21 = f32[16,2440]{1,0:T(8,128)S(1)} collective-permute-done((f32[16,2440]{1,0:T(8,128)S(1)}, f32[16,2440]{1,0:T(8,128)S(1)}, u32[]{:S(2)}, u32[]{:S(2)}) %collective-permute-start.21) | collective-permute-done | bytes 156192 | tf_op jit(solution)/shard_map/ppermute | solution.py:226
  110.9 2.4 %multiply_reduce_fusion.4 = (f32[16]{0:T(128)S(1)}, f32[16,64]{1,0:T(8,128)S(1)}) fusion(f32[16,64]{1,0:T(8,128)S(1)} %get-tuple-element.142, f32[16,64]{1,0:T(8,128)S(1)} %fusion.52, f32[16,64]{1,0:T(8,128)S(1)} %fusion.54, f32[16]{0:T(128)S(1)} %broadcast_multiply_fusion.3, f32[4096,16]{1,0:T(8,128)S(1)} %reshape.536, f32[64]{0:T(128)S(1)} %iota_convert_fusion, ...), kind=kOutput, calls=%fused_computation.145 | convolution fusion | flops 50601968 | bytes 295296 | tf_op jit(solution)/shard_map/tk,ta->ka/dot_general | solution.py:250
  114.7 2.5 %multiply_reduce_fusion.3 = (f32[16]{0:T(128)S(1)}, f32[16,64]{1,0:T(8,128)S(1)}) fusion(f32[16,64]{1,0:T(8,128)S(1)} %get-tuple-element.142, f32[16,64]{1,0:T(8,128)S(1)} %fusion.52, f32[16,64]{1,0:T(8,128)S(1)} %fusion.54, f32[16]{0:T(128)S(1)} %broadcast_multiply_fusion.2, f32[4096,16]{1,0:T(8,128)S(1)} %convolution_multiply_fusion, ...), kind=kOutput, calls=%fused_computation.144 | convolution fusion | flops 50601968 | bytes 295296 | tf_op jit(solution)/shard_map/tk,ta->ka/dot_general | solution.py:262
  117.5 2.1 %collective-permute-start.24 = (f32[1,72,256]{2,1,0:T(8,128)S(1)}, f32[1,72,256]{2,1,0:T(8,128)S(1)}, u32[]{:S(2)}, u32[]{:S(2)}) collective-permute-start(f32[1,72,256]{2,1,0:T(8,128)S(1)} %fusion.59), channel_id=1, source_target_pairs={{0,3},{1,2},{2,1},{3,0},{4,7},{5,6},{6,5},{7,4},{8,11},{9,10},{10,... | collective-permute-start | bytes 221192 | tf_op jit(solution)/shard_map/ppermute | solution.py:149
  121.1 2.3 %collective-permute-done.24 = f32[1,72,256]{2,1,0:T(8,128)S(1)} collective-permute-done((f32[1,72,256]{2,1,0:T(8,128)S(1)}, f32[1,72,256]{2,1,0:T(8,128)S(1)}, u32[]{:S(2)}, u32[]{:S(2)}) %collective-permute-start.24) | collective-permute-done | bytes 73760 | tf_op jit(solution)/shard_map/ppermute | solution.py:149
  124.8 5.8 %shard_map.98 = f32[32,16,256]{2,1,0:T(8,128)} custom-call(s32[128]{0:T(128)} %clamp_bitcast_fusion.rows_ref, s32[128]{0:T(128)} %fusion.96.cols_ref, s32[128]{0:T(128)} %and_convert_fusion.live_ref, s32[1]{0:T(128)} %bitcast.5.nb_ref, f32[4,72,256]{2,1,0:T(8,128)} %copy-done.4, bf16[1,1,128,256,256]{4,3,2,1,0:T(8,128)(2,1)} %t_ref.9), custom_call_target="tpu_custom_call" | custom-call | tf_op jit(solution)/shard_map/pallas_call | solution.py:69
  134.3 6.8 %collective-permute-start.28 = (f32[72,256]{1,0:T(8,128)S(1)}, f32[72,256]{1,0:T(8,128)S(1)}, u32[]{:S(2)}, u32[]{:S(2)}) collective-permute-start(f32[72,256]{1,0:T(8,128)S(1)} %get-tuple-element.132), channel_id=1, source_target_pairs={{0,24},{4,28},{8,0},{12,4},{16,8},{20,12},{24,16},{28,20},{1,25},{... | collective-permute-start | bytes 221192 | tf_op jit(solution)/shard_map/ppermute | solution.py:173
  141.8 2.0 %collective-permute-done.28 = f32[72,256]{1,0:T(8,128)S(1)} collective-permute-done((f32[72,256]{1,0:T(8,128)S(1)}, f32[72,256]{1,0:T(8,128)S(1)}, u32[]{:S(2)}, u32[]{:S(2)}) %collective-permute-start.28) | collective-permute-done | bytes 73760 | tf_op jit(solution)/shard_map/ppermute | solution.py:173
  143.8 4.6 %collective-permute-done.27 = f32[72,256]{1,0:T(8,128)S(1)} collective-permute-done((f32[72,256]{1,0:T(8,128)S(1)}, f32[72,256]{1,0:T(8,128)S(1)}, u32[]{:S(2)}, u32[]{:S(2)}) %collective-permute-start.27) | collective-permute-done | bytes 73760 | tf_op jit(solution)/shard_map/ppermute | solution.py:173
  148.7 1.8 collective-permute-start.31
  152.2 1.9 %collective-permute-done.31 = f32[1,72,256]{2,1,0:T(8,128)S(1)} collective-permute-done((f32[1,72,256]{2,1,0:T(8,128)S(1)}, f32[1,72,256]{2,1,0:T(8,128)S(1)}, u32[]{:S(2)}, u32[]{:S(2)}) %collective-permute-start.31) | collective-permute-done | bytes 73760 | tf_op jit(solution)/shard_map/ppermute | solution.py:149
  156.4 5.9 %shard_map.99 = f32[32,16,256]{2,1,0:T(8,128)} custom-call(s32[128]{0:T(128)} %clamp_bitcast_fusion.rows_ref, s32[128]{0:T(128)} %fusion.96.cols_ref, s32[128]{0:T(128)} %and_convert_fusion.live_ref, s32[1]{0:T(128)} %bitcast.5.nb_ref, f32[4,72,256]{2,1,0:T(8,128)} %copy-done.1, bf16[1,1,128,256,256]{4,3,2,1,0:T(8,128)(2,1)} %t_ref.9), custom_call_target="tpu_custom_call" | custom-call | tf_op jit(solution)/shard_map/pallas_call | solution.py:69
  166.0 4.3 %collective-permute-start.35 = (f32[72,256]{1,0:T(8,128)S(1)}, f32[72,256]{1,0:T(8,128)S(1)}, u32[]{:S(2)}, u32[]{:S(2)}) collective-permute-start(f32[72,256]{1,0:T(8,128)S(1)} %get-tuple-element.129), channel_id=1, source_target_pairs={{0,24},{4,28},{8,0},{12,4},{16,8},{20,12},{24,16},{28,20},{1,25},{... | collective-permute-start | bytes 221192 | tf_op jit(solution)/shard_map/ppermute | solution.py:173
  170.4 2.0 %collective-permute-start.34 = (f32[72,256]{1,0:T(8,128)S(1)}, f32[72,256]{1,0:T(8,128)S(1)}, u32[]{:S(2)}, u32[]{:S(2)}) collective-permute-start(f32[72,256]{1,0:T(8,128)S(1)} %get-tuple-element.130), channel_id=1, source_target_pairs={{0,16},{4,20},{8,24},{12,28},{16,0},{20,4},{24,8},{28,12},{1,17},{... | collective-permute-start | bytes 221192 | tf_op jit(solution)/shard_map/ppermute | solution.py:173
  174.7 3.0 %collective-permute-done.34 = f32[72,256]{1,0:T(8,128)S(1)} collective-permute-done((f32[72,256]{1,0:T(8,128)S(1)}, f32[72,256]{1,0:T(8,128)S(1)}, u32[]{:S(2)}, u32[]{:S(2)}) %collective-permute-start.34) | collective-permute-done | bytes 73760 | tf_op jit(solution)/shard_map/ppermute | solution.py:173
  (157 shorter events, 57.9 us)
Async XLA Ops:
  2.6 10.5 %collective-permute-start.2 = (f32[1,72,256]{2,1,0:T(8,128)S(1)}, f32[1,72,256]{2,1,0:T(8,128)S(1)}, u32[]{:S(2)}, u32[]{:S(2)}) collective-permute-start(f32[1,72,256]{2,1,0:T(8,128)S(1)} %fusion.62), channel_id=1, source_target_pairs={{0,3},{1,2},{2,1},{3,0},{4,7},{5,6},{6,5},{7,4},{8,11},{9,10},{10,... | collective-permute-start | bytes 221192 | tf_op jit(solution)/shard_map/ppermute | solution.py:149
  6.6 6.5 %collective-permute-start.1 = (f32[1,72,256]{2,1,0:T(8,128)S(1)}, f32[1,72,256]{2,1,0:T(8,128)S(1)}, u32[]{:S(2)}, u32[]{:S(2)}) collective-permute-start(f32[1,72,256]{2,1,0:T(8,128)S(1)} %fusion.62), channel_id=1, source_target_pairs={{0,2},{1,3},{2,0},{3,1},{4,6},{5,7},{6,4},{7,5},{8,10},{9,11},{10,... | collective-permute-start | bytes 221192 | tf_op jit(solution)/shard_map/ppermute | solution.py:149
  7.1 6.0 %collective-permute-start = (f32[1,72,256]{2,1,0:T(8,128)S(1)}, f32[1,72,256]{2,1,0:T(8,128)S(1)}, u32[]{:S(2)}, u32[]{:S(2)}) collective-permute-start(f32[1,72,256]{2,1,0:T(8,128)S(1)} %fusion.62), channel_id=1, source_target_pairs={{0,1},{1,0},{2,3},{3,2},{4,5},{5,4},{6,7},{7,6},{8,9},{9,8},{10,11... | collective-permute-start | bytes 221192 | tf_op jit(solution)/shard_map/ppermute | solution.py:149
  20.6 1.6 collective-permute-start.3
  23.3 9.8 %collective-permute-start.4 = (f32[72,256]{1,0:T(8,128)S(1)}, f32[72,256]{1,0:T(8,128)S(1)}, u32[]{:S(2)}, u32[]{:S(2)}) collective-permute-start(f32[72,256]{1,0:T(8,128)S(1)} %get-tuple-element.138), channel_id=1, source_target_pairs={{0,8},{4,12},{8,16},{12,20},{16,24},{20,28},{24,0},{28,4},{1,9},{5... | collective-permute-start | bytes 221192 | tf_op jit(solution)/shard_map/ppermute | solution.py:173
  25.3 8.5 %collective-permute-start.6 = (f32[72,256]{1,0:T(8,128)S(1)}, f32[72,256]{1,0:T(8,128)S(1)}, u32[]{:S(2)}, u32[]{:S(2)}) collective-permute-start(f32[72,256]{1,0:T(8,128)S(1)} %get-tuple-element.139), channel_id=1, source_target_pairs={{0,24},{4,28},{8,0},{12,4},{16,8},{20,12},{24,16},{28,20},{1,25},{... | collective-permute-start | bytes 221192 | tf_op jit(solution)/shard_map/ppermute | solution.py:173
  30.5 7.2 %collective-permute-start.5 = (f32[72,256]{1,0:T(8,128)S(1)}, f32[72,256]{1,0:T(8,128)S(1)}, u32[]{:S(2)}, u32[]{:S(2)}) collective-permute-start(f32[72,256]{1,0:T(8,128)S(1)} %get-tuple-element.140), channel_id=1, source_target_pairs={{0,16},{4,20},{8,24},{12,28},{16,0},{20,4},{24,8},{28,12},{1,17},{... | collective-permute-start | bytes 221192 | tf_op jit(solution)/shard_map/ppermute | solution.py:173
  38.0 5.4 %collective-permute-start.9 = (f32[1,72,256]{2,1,0:T(8,128)S(1)}, f32[1,72,256]{2,1,0:T(8,128)S(1)}, u32[]{:S(2)}, u32[]{:S(2)}) collective-permute-start(f32[1,72,256]{2,1,0:T(8,128)S(1)} %fusion.61), channel_id=1, source_target_pairs={{0,3},{1,2},{2,1},{3,0},{4,7},{5,6},{6,5},{7,4},{8,11},{9,10},{10,... | collective-permute-start | bytes 221192 | tf_op jit(solution)/shard_map/ppermute | solution.py:149
  40.5 4.4 %collective-permute-start.8 = (f32[1,72,256]{2,1,0:T(8,128)S(1)}, f32[1,72,256]{2,1,0:T(8,128)S(1)}, u32[]{:S(2)}, u32[]{:S(2)}) collective-permute-start(f32[1,72,256]{2,1,0:T(8,128)S(1)} %fusion.61), channel_id=1, source_target_pairs={{0,2},{1,3},{2,0},{3,1},{4,6},{5,7},{6,4},{7,5},{8,10},{9,11},{10,... | collective-permute-start | bytes 221192 | tf_op jit(solution)/shard_map/ppermute | solution.py:149
  40.5 4.4 %collective-permute-start.7 = (f32[1,72,256]{2,1,0:T(8,128)S(1)}, f32[1,72,256]{2,1,0:T(8,128)S(1)}, u32[]{:S(2)}, u32[]{:S(2)}) collective-permute-start(f32[1,72,256]{2,1,0:T(8,128)S(1)} %fusion.61), channel_id=1, source_target_pairs={{0,1},{1,0},{2,3},{3,2},{4,5},{5,4},{6,7},{7,6},{8,9},{9,8},{10,11... | collective-permute-start | bytes 221192 | tf_op jit(solution)/shard_map/ppermute | solution.py:149
  55.1 7.8 %collective-permute-start.11 = (f32[72,256]{1,0:T(8,128)S(1)}, f32[72,256]{1,0:T(8,128)S(1)}, u32[]{:S(2)}, u32[]{:S(2)}) collective-permute-start(f32[72,256]{1,0:T(8,128)S(1)} %get-tuple-element.135), channel_id=1, source_target_pairs={{0,8},{4,12},{8,16},{12,20},{16,24},{20,28},{24,0},{28,4},{1,9},{5... | collective-permute-start | bytes 221192 | tf_op jit(solution)/shard_map/ppermute | solution.py:173
  55.2 8.0 %collective-permute-start.13 = (f32[72,256]{1,0:T(8,128)S(1)}, f32[72,256]{1,0:T(8,128)S(1)}, u32[]{:S(2)}, u32[]{:S(2)}) collective-permute-start(f32[72,256]{1,0:T(8,128)S(1)} %get-tuple-element.136), channel_id=1, source_target_pairs={{0,24},{4,28},{8,0},{12,4},{16,8},{20,12},{24,16},{28,20},{1,25},{... | collective-permute-start | bytes 221192 | tf_op jit(solution)/shard_map/ppermute | solution.py:173
  60.5 7.1 %collective-permute-start.12 = (f32[72,256]{1,0:T(8,128)S(1)}, f32[72,256]{1,0:T(8,128)S(1)}, u32[]{:S(2)}, u32[]{:S(2)}) collective-permute-start(f32[72,256]{1,0:T(8,128)S(1)} %get-tuple-element.137), channel_id=1, source_target_pairs={{0,16},{4,20},{8,24},{12,28},{16,0},{20,4},{24,8},{28,12},{1,17},{... | collective-permute-start | bytes 221192 | tf_op jit(solution)/shard_map/ppermute | solution.py:173
  67.8 5.4 %collective-permute-start.16 = (f32[1,72,256]{2,1,0:T(8,128)S(1)}, f32[1,72,256]{2,1,0:T(8,128)S(1)}, u32[]{:S(2)}, u32[]{:S(2)}) collective-permute-start(f32[1,72,256]{2,1,0:T(8,128)S(1)} %fusion.60), channel_id=1, source_target_pairs={{0,3},{1,2},{2,1},{3,0},{4,7},{5,6},{6,5},{7,4},{8,11},{9,10},{10,... | collective-permute-start | bytes 221192 | tf_op jit(solution)/shard_map/ppermute | solution.py:149
  69.8 4.8 %collective-permute-start.15 = (f32[1,72,256]{2,1,0:T(8,128)S(1)}, f32[1,72,256]{2,1,0:T(8,128)S(1)}, u32[]{:S(2)}, u32[]{:S(2)}) collective-permute-start(f32[1,72,256]{2,1,0:T(8,128)S(1)} %fusion.60), channel_id=1, source_target_pairs={{0,2},{1,3},{2,0},{3,1},{4,6},{5,7},{6,4},{7,5},{8,10},{9,11},{10,... | collective-permute-start | bytes 221192 | tf_op jit(solution)/shard_map/ppermute | solution.py:149
  69.9 5.1 %collective-permute-start.14 = (f32[1,72,256]{2,1,0:T(8,128)S(1)}, f32[1,72,256]{2,1,0:T(8,128)S(1)}, u32[]{:S(2)}, u32[]{:S(2)}) collective-permute-start(f32[1,72,256]{2,1,0:T(8,128)S(1)} %fusion.60), channel_id=1, source_target_pairs={{0,1},{1,0},{2,3},{3,2},{4,5},{5,4},{6,7},{7,6},{8,9},{9,8},{10,11... | collective-permute-start | bytes 221192 | tf_op jit(solution)/shard_map/ppermute | solution.py:149
  83.9 3.7 %collective-permute-start.17 = (f32[1,2440]{1,0:T(1,128)S(1)}, f32[1,2440]{1,0:T(1,128)S(1)}, u32[]{:S(2)}, u32[]{:S(2)}) collective-permute-start(f32[1,2440]{1,0:T(1,128)S(1)} %broadcast_in_dim.15), channel_id=1, source_target_pairs={{0,1},{1,0},{2,3},{3,2},{4,5},{5,4},{6,7},{7,6},{8,9},{9,8},{10,11... | collective-permute-start | bytes 29288 | tf_op jit(solution)/shard_map/ppermute | solution.py:226
  87.7 3.8 %collective-permute-start.18 = (f32[2,2440]{1,0:T(2,128)S(1)}, f32[2,2440]{1,0:T(2,128)S(1)}, u32[]{:S(2)}, u32[]{:S(2)}) collective-permute-start(f32[2,2440]{1,0:T(2,128)S(1)} %pad_maximum_fusion.7), channel_id=1, source_target_pairs={{0,2},{1,3},{2,0},{3,1},{4,6},{5,7},{6,4},{7,5},{8,10},{9,11},{10,... | collective-permute-start | bytes 58568 | tf_op jit(solution)/shard_map/ppermute | solution.py:226
  92.9 4.6 %collective-permute-start.20 = (f32[8,2440]{1,0:T(8,128)S(1)}, f32[8,2440]{1,0:T(8,128)S(1)}, u32[]{:S(2)}, u32[]{:S(2)}) collective-permute-start(f32[8,2440]{1,0:T(8,128)S(1)} %pad_maximum_fusion.5), channel_id=1, source_target_pairs={{0,8},{1,9},{2,10},{3,11},{4,12},{5,13},{6,14},{7,15},{8,0},{9,1},... | collective-permute-start | bytes 234248 | tf_op jit(solution)/shard_map/ppermute | solution.py:226
  97.5 11.1 %collective-permute-start.21 = (f32[16,2440]{1,0:T(8,128)S(1)}, f32[16,2440]{1,0:T(8,128)S(1)}, u32[]{:S(2)}, u32[]{:S(2)}) collective-permute-start(f32[16,2440]{1,0:T(8,128)S(1)} %concatenate.118), channel_id=1, source_target_pairs={{0,16},{1,17},{2,18},{3,19},{4,20},{5,21},{6,22},{7,23},{8,24},{9,... | collective-permute-start | bytes 468488 | tf_op jit(solution)/shard_map/ppermute | solution.py:226
  117.5 5.8 %collective-permute-start.24 = (f32[1,72,256]{2,1,0:T(8,128)S(1)}, f32[1,72,256]{2,1,0:T(8,128)S(1)}, u32[]{:S(2)}, u32[]{:S(2)}) collective-permute-start(f32[1,72,256]{2,1,0:T(8,128)S(1)} %fusion.59), channel_id=1, source_target_pairs={{0,3},{1,2},{2,1},{3,0},{4,7},{5,6},{6,5},{7,4},{8,11},{9,10},{10,... | collective-permute-start | bytes 221192 | tf_op jit(solution)/shard_map/ppermute | solution.py:149
  119.7 4.4 %collective-permute-start.23 = (f32[1,72,256]{2,1,0:T(8,128)S(1)}, f32[1,72,256]{2,1,0:T(8,128)S(1)}, u32[]{:S(2)}, u32[]{:S(2)}) collective-permute-start(f32[1,72,256]{2,1,0:T(8,128)S(1)} %fusion.59), channel_id=1, source_target_pairs={{0,2},{1,3},{2,0},{3,1},{4,6},{5,7},{6,4},{7,5},{8,10},{9,11},{10,... | collective-permute-start | bytes 221192 | tf_op jit(solution)/shard_map/ppermute | solution.py:149
  119.7 4.4 %collective-permute-start.22 = (f32[1,72,256]{2,1,0:T(8,128)S(1)}, f32[1,72,256]{2,1,0:T(8,128)S(1)}, u32[]{:S(2)}, u32[]{:S(2)}) collective-permute-start(f32[1,72,256]{2,1,0:T(8,128)S(1)} %fusion.59), channel_id=1, source_target_pairs={{0,1},{1,0},{2,3},{3,2},{4,5},{5,4},{6,7},{7,6},{8,9},{9,8},{10,11... | collective-permute-start | bytes 221192 | tf_op jit(solution)/shard_map/ppermute | solution.py:149
  134.3 9.5 %collective-permute-start.28 = (f32[72,256]{1,0:T(8,128)S(1)}, f32[72,256]{1,0:T(8,128)S(1)}, u32[]{:S(2)}, u32[]{:S(2)}) collective-permute-start(f32[72,256]{1,0:T(8,128)S(1)} %get-tuple-element.132), channel_id=1, source_target_pairs={{0,24},{4,28},{8,0},{12,4},{16,8},{20,12},{24,16},{28,20},{1,25},{... | collective-permute-start | bytes 221192 | tf_op jit(solution)/shard_map/ppermute | solution.py:173
  141.1 7.3 %collective-permute-start.27 = (f32[72,256]{1,0:T(8,128)S(1)}, f32[72,256]{1,0:T(8,128)S(1)}, u32[]{:S(2)}, u32[]{:S(2)}) collective-permute-start(f32[72,256]{1,0:T(8,128)S(1)} %get-tuple-element.133), channel_id=1, source_target_pairs={{0,16},{4,20},{8,24},{12,28},{16,0},{20,4},{24,8},{28,12},{1,17},{... | collective-permute-start | bytes 221192 | tf_op jit(solution)/shard_map/ppermute | solution.py:173
  141.1 7.3 %collective-permute-start.26 = (f32[72,256]{1,0:T(8,128)S(1)}, f32[72,256]{1,0:T(8,128)S(1)}, u32[]{:S(2)}, u32[]{:S(2)}) collective-permute-start(f32[72,256]{1,0:T(8,128)S(1)} %get-tuple-element.134), channel_id=1, source_target_pairs={{0,8},{4,12},{8,16},{12,20},{16,24},{20,28},{24,0},{28,4},{1,9},{5... | collective-permute-start | bytes 221192 | tf_op jit(solution)/shard_map/ppermute | solution.py:173
  148.7 5.4 %collective-permute-start.31 = (f32[1,72,256]{2,1,0:T(8,128)S(1)}, f32[1,72,256]{2,1,0:T(8,128)S(1)}, u32[]{:S(2)}, u32[]{:S(2)}) collective-permute-start(f32[1,72,256]{2,1,0:T(8,128)S(1)} %fusion.58), channel_id=1, source_target_pairs={{0,3},{1,2},{2,1},{3,0},{4,7},{5,6},{6,5},{7,4},{8,11},{9,10},{10,... | collective-permute-start | bytes 221192 | tf_op jit(solution)/shard_map/ppermute | solution.py:149
  150.4 5.0 %collective-permute-start.30 = (f32[1,72,256]{2,1,0:T(8,128)S(1)}, f32[1,72,256]{2,1,0:T(8,128)S(1)}, u32[]{:S(2)}, u32[]{:S(2)}) collective-permute-start(f32[1,72,256]{2,1,0:T(8,128)S(1)} %fusion.58), channel_id=1, source_target_pairs={{0,2},{1,3},{2,0},{3,1},{4,6},{5,7},{6,4},{7,5},{8,10},{9,11},{10,... | collective-permute-start | bytes 221192 | tf_op jit(solution)/shard_map/ppermute | solution.py:149
  150.5 5.1 %collective-permute-start.29 = (f32[1,72,256]{2,1,0:T(8,128)S(1)}, f32[1,72,256]{2,1,0:T(8,128)S(1)}, u32[]{:S(2)}, u32[]{:S(2)}) collective-permute-start(f32[1,72,256]{2,1,0:T(8,128)S(1)} %fusion.58), channel_id=1, source_target_pairs={{0,1},{1,0},{2,3},{3,2},{4,5},{5,4},{6,7},{7,6},{8,9},{9,8},{10,11... | collective-permute-start | bytes 221192 | tf_op jit(solution)/shard_map/ppermute | solution.py:149
  166.0 7.2 %collective-permute-start.33 = (f32[72,256]{1,0:T(8,128)S(1)}, f32[72,256]{1,0:T(8,128)S(1)}, u32[]{:S(2)}, u32[]{:S(2)}) collective-permute-start(f32[72,256]{1,0:T(8,128)S(1)} %get-tuple-element.128), channel_id=1, source_target_pairs={{0,8},{4,12},{8,16},{12,20},{16,24},{20,28},{24,0},{28,4},{1,9},{5... | collective-permute-start | bytes 221192 | tf_op jit(solution)/shard_map/ppermute | solution.py:173
  166.0 8.6 %collective-permute-start.35 = (f32[72,256]{1,0:T(8,128)S(1)}, f32[72,256]{1,0:T(8,128)S(1)}, u32[]{:S(2)}, u32[]{:S(2)}) collective-permute-start(f32[72,256]{1,0:T(8,128)S(1)} %get-tuple-element.129), channel_id=1, source_target_pairs={{0,24},{4,28},{8,0},{12,4},{16,8},{20,12},{24,16},{28,20},{1,25},{... | collective-permute-start | bytes 221192 | tf_op jit(solution)/shard_map/ppermute | solution.py:173
  170.4 7.3 %collective-permute-start.34 = (f32[72,256]{1,0:T(8,128)S(1)}, f32[72,256]{1,0:T(8,128)S(1)}, u32[]{:S(2)}, u32[]{:S(2)}) collective-permute-start(f32[72,256]{1,0:T(8,128)S(1)} %get-tuple-element.130), channel_id=1, source_target_pairs={{0,16},{4,20},{8,24},{12,28},{16,0},{20,4},{24,8},{28,12},{1,17},{... | collective-permute-start | bytes 221192 | tf_op jit(solution)/shard_map/ppermute | solution.py:173
  (10 other events, 25.5 us)

commit v3 on v2

--- a/solution.py
+++ b/solution.py
@@ -12,9 +12,10 @@
 highest = lax.Precision.HIGHEST
 
 
-def tile_kernel(mode, blocks_piece, rows_ref, cols_ref, live_ref, nb_ref, x_ref, t_ref, o_ref):
+def tile_kernel(
+    mode, blocks_piece, vectors, rows_ref, cols_ref, live_ref, nb_ref, x_ref, t_ref, o_ref
+):
     step = pl.program_id(0)
-    vectors = o_ref.shape[1]
     if mode == "image":
 
         @pl.when(step == 0)
@@ -32,7 +33,9 @@
             product = jnp.dot(picked * weight, t_ref[g], preferred_element_type=jnp.float32)
             if mode == "image":
                 row = rows_ref[slot]
-                o_ref[row] = o_ref[row] + product
+                at = pl.multiple_of((row % blocks_piece) * vectors, vectors)
+                window = (row // blocks_piece, pl.ds(at, vectors), slice(None))
+                o_ref[window] = o_ref[window] + product
             else:
                 o_ref[g] = product[:, :128] + product[:, 128:]
 
@@ -44,7 +47,9 @@
 
 
 def tile_pass(mode, x_cols, tiles, rows, cols, live, block_count, row_blocks, vectors):
-    groups, payload_rows, side = x_cols.shape
+    groups, padded_rows, side = x_cols.shape
+    blocks_piece = padded_rows // vectors
+    owners = row_blocks // blocks_piece
     slots = tiles.shape[2]
     steps = slots // group_size
 
@@ -52,8 +57,8 @@
         return (0, 0, jnp.minimum(i, nb_ref[0] - 1), 0, 0)
 
     if mode == "image":
-        out_shape = jax.ShapeDtypeStruct((row_blocks, vectors, side), jnp.float32)
-        out_spec = pl.BlockSpec((row_blocks, vectors, side), lambda i, *_: (0, 0, 0))
+        out_shape = jax.ShapeDtypeStruct((owners, padded_rows, side), jnp.float32)
+        out_spec = pl.BlockSpec((owners, padded_rows, side), lambda i, *_: (0, 0, 0))
     else:
         out_shape = jax.ShapeDtypeStruct((slots, vectors, 128), jnp.float32)
         out_spec = pl.BlockSpec((group_size, vectors, 128), lambda i, *_: (i, 0, 0))
@@ -61,13 +66,13 @@
         num_scalar_prefetch=4,
         grid=(steps,),
         in_specs=[
-            pl.BlockSpec((groups, payload_rows, side), lambda i, *_: (0, 0, 0)),
+            pl.BlockSpec((groups, padded_rows, side), lambda i, *_: (0, 0, 0)),
             pl.BlockSpec((None, None, group_size, side, side), tile_index),
         ],
         out_specs=out_spec,
     )
     return pl.pallas_call(
-        functools.partial(tile_kernel, mode, payload_rows // vectors),
+        functools.partial(tile_kernel, mode, blocks_piece, vectors),
         grid_spec=grid_spec,
         out_shape=out_shape,
         compiler_params=pltpu.CompilerParams(dimension_semantics=("arbitrary",)),
@@ -157,7 +162,9 @@
 
     def reduce_rows(accumulated, lost):
         n = src_count
-        chunks = with_lost_row(accumulated.reshape(n, payload_rows, tile_side), lost)
+        chunks = accumulated.at[:, payload_rows, :vectors].set(
+            jnp.broadcast_to(lost, (n, vectors))
+        )
         if n % 2 == 0:
             half = n // 2
             paired = chunks.reshape(half, 2, *chunks.shape[1:])
@@ -220,12 +227,24 @@
     ]
     sizes = [f.shape[0] for f in fields]
     shared = jnp.concatenate(fields)[None]
-    if all_count & (all_count - 1) == 0:
-        shift = 1
-        while shift < all_count:
-            got = lax.ppermute(shared, all_axes, [(i, i ^ shift) for i in range(all_count)])
-            shared = jnp.concatenate([shared, got], axis=0)
-            shift *= 2
+    if exchange and src_count % 2 == 0:
+        shared = jnp.concatenate(
+            [shared]
+            + [
+                lax.ppermute(shared, "dst", [(i, i ^ v) for i in range(dst_count)])
+                for v in range(1, dst_count)
+            ],
+            axis=0,
+        )
+        shared = jnp.concatenate(
+            [shared, lax.ppermute(shared, "src", [(i, i ^ 1) for i in range(src_count)])], axis=0
+        )
+        half = src_count // 2
+        pieces = [shared]
+        for shift in range(1, half):
+            pairs = [(i, ((i // 2 + shift) % half) * 2 + i % 2) for i in range(src_count)]
+            pieces.append(lax.ppermute(shared, "src", pairs))
+        shared = jnp.concatenate(pieces, axis=0)
     else:
         shared = lax.all_gather(shared[0], all_axes, axis=0, tiled=False)
     offsets = [0]

time: 175 us -> 173 us (0.989); the launches traced: 179 us -> 170 us
  local copies, waits for them, and re-layouts: 9.56 us -> 19.5 us
  starting transfers between devices: 52.8 us -> 43.7 us
  waiting for transfers between devices: 59.6 us -> 53.6 us
  other arithmetic: 17.1 us -> 13.2 us
    ppermute x12, starting transfers between devices: 27.7 us -> 16.4 us  [reduce_rows(): total = total + lax.ppermute(send, 'src', pairs)]
    ppermute x5 -> x7, waiting for transfers between devices: 18.4 us -> 11.6 us  [the longest x3 7.49 us: per_device(): pieces.append(lax.ppermute(shared, 'src', pairs))]
    scatter x4, local copies, waits for them, and re-layouts: 0.02 us -> 6 us  [reduce_rows(): accumulated.at[:, payload_rows, :vectors]]
    squeeze x0 -> x4, local copies, waits for them, and re-layouts: none -> 3.92 us  [reduce_rows(): give = lax.dynamic_index_in_dim(paired, 1 - core, 1, keepdims=False)]
    squeeze x4 -> x0, other arithmetic: 3.92 us -> none  [reduce_rows(): give = lax.dynamic_index_in_dim(paired, 1 - core, 1, keepdims=False)]
    ppermute x15, starting transfers between devices: 18.8 us -> 20.7 us  [spread_columns(): lax.ppermute(payload, 'dst', [(i, i ^ v) for i in range(dst_count)])]
    ppermute x5 -> x7, starting transfers between devices: 6.07 us -> 6.28 us  [the longest x3 3.55 us: per_device(): lax.ppermute(shared, 'dst', [(i, i ^ v) for i in range(dst_count)])]
  transfers between devices with their start and end apart: 36 -> 38, of which waited for: 30 -> 31; matrix products, arithmetic and copies ran while one was open for 5% -> 5% of each run, Pallas kernels for 0% -> 0%
where the time goes in v3:
time: 173 us; the launch traced here: 170 us
  waiting for transfers between devices  53.6 us (31%)
  starting transfers between devices  43.7 us (25%)
  Pallas kernels  29.9 us (17%)
  local copies, waits for them, and re-layouts  19.5 us (11%)
  other arithmetic  13.2 us (8%)
  matrix products  8.05 us (5%)
  between operations  1.77 us (1%)
    pallas_call x5, Pallas kernels, tile_pass(): pl.pallas_call(functools.partial(tile_kernel, mode, blocks_piece, vectors...  29.9 us
    ppermute x12, waiting for transfers between devices, reduce_rows(): total = total + lax.ppermute(send, 'src', pairs)  23.6 us
    ppermute x15, starting transfers between devices, spread_columns(): lax.ppermute(payload, 'dst', [(i, i ^ v) for i in range(dst_count)])  20.7 us
    ppermute x12, starting transfers between devices, reduce_rows(): total = total + lax.ppermute(send, 'src', pairs)  16.4 us
    ppermute x15, waiting for transfers between devices, spread_columns(): lax.ppermute(payload, 'dst', [(i, i ^ v) for i in range(dst_count)])  12.4 us
    ppermute x3, waiting for transfers between devices, per_device(): pieces.append(lax.ppermute(shared, 'src', pairs))  7.49 us
    ppermute x4, waiting for transfers between devices, reduce_rows(): part = keep + lax.ppermute(give, 'src', [(i, i ^ 1) for i in range(n)])  6.1 us
    scatter x4, local copies, waits for them, and re-layouts, reduce_rows(): accumulated.at[:, payload_rows, :vectors]  6 us
  transfers between devices with their start and end apart: 38, of which 31 were waited for; matrix products, arithmetic and copies ran while one was open for 5% of the time, Pallas kernels for 0%

profile of v3, /device:TPU:0, one launch (start us, length us, event | category | flops | bytes accessed | tf_op | source)
XLA Modules:
  0.0 169.7 jit_solution(7146314289963304917)
XLA Ops:
  2.6 4.0 %collective-permute-start.2 = (f32[1,72,256]{2,1,0:T(8,128)S(1)}, f32[1,72,256]{2,1,0:T(8,128)S(1)}, u32[]{:S(2)}, u32[]{:S(2)}) collective-permute-start(f32[1,72,256]{2,1,0:T(8,128)S(1)} %fusion.42), channel_id=1, source_target_pairs={{0,3},{1,2},{2,1},{3,0},{4,7},{5,6},{6,5},{7,4},{8,11},{9,10},{10,... | collective-permute-start | bytes 221192 | tf_op jit(solution)/shard_map/ppermute | solution.py:154
  13.9 5.9 %shard_map.95 = f32[8,72,256]{2,1,0:T(8,128)} custom-call(s32[128]{0:T(128)} %clamp_bitcast_fusion.rows_ref, s32[128]{0:T(128)} %fusion.76.cols_ref, s32[128]{0:T(128)} %and_convert_fusion.live_ref, s32[1]{0:T(128)} %bitcast.5.nb_ref, f32[4,72,256]{2,1,0:T(8,128)} %copy-done.2, bf16[1,1,128,256,256]{4,3,2,1,0:T(8,128)(2,1)} %t_ref.9), custom_call_target="tpu_custom_call" | custom-call | tf_op jit(solution)/shard_map/pallas_call | solution.py:74
  24.9 3.8 %collective-permute-start.4 = (f32[72,256]{1,0:T(8,128)S(1)}, f32[72,256]{1,0:T(8,128)S(1)}, u32[]{:S(2)}, u32[]{:S(2)}) collective-permute-start(f32[72,256]{1,0:T(8,128)S(1)} %get-tuple-element.138), channel_id=1, source_target_pairs={{0,8},{4,12},{8,16},{12,20},{16,24},{20,28},{24,0},{28,4},{1,9},{5... | collective-permute-start | bytes 221192 | tf_op jit(solution)/shard_map/ppermute | solution.py:180
  31.7 1.7 %collective-permute-done.6 = f32[72,256]{1,0:T(8,128)S(1)} collective-permute-done((f32[72,256]{1,0:T(8,128)S(1)}, f32[72,256]{1,0:T(8,128)S(1)}, u32[]{:S(2)}, u32[]{:S(2)}) %collective-permute-start.6) | collective-permute-done | bytes 73760 | tf_op jit(solution)/shard_map/ppermute | solution.py:180
  33.4 2.9 %collective-permute-done.5 = f32[72,256]{1,0:T(8,128)S(1)} collective-permute-done((f32[72,256]{1,0:T(8,128)S(1)}, f32[72,256]{1,0:T(8,128)S(1)}, u32[]{:S(2)}, u32[]{:S(2)}) %collective-permute-start.5) | collective-permute-done | bytes 73760 | tf_op jit(solution)/shard_map/ppermute | solution.py:180
  36.5 3.4 %collective-permute-start.9 = (f32[1,72,256]{2,1,0:T(8,128)S(1)}, f32[1,72,256]{2,1,0:T(8,128)S(1)}, u32[]{:S(2)}, u32[]{:S(2)}) collective-permute-start(f32[1,72,256]{2,1,0:T(8,128)S(1)} %fusion.41), channel_id=1, source_target_pairs={{0,3},{1,2},{2,1},{3,0},{4,7},{5,6},{6,5},{7,4},{8,11},{9,10},{10,... | collective-permute-start | bytes 221192 | tf_op jit(solution)/shard_map/ppermute | solution.py:154
  42.3 1.9 %collective-permute-done.8 = f32[1,72,256]{2,1,0:T(8,128)S(1)} collective-permute-done((f32[1,72,256]{2,1,0:T(8,128)S(1)}, f32[1,72,256]{2,1,0:T(8,128)S(1)}, u32[]{:S(2)}, u32[]{:S(2)}) %collective-permute-start.8) | collective-permute-done | bytes 73760 | tf_op jit(solution)/shard_map/ppermute | solution.py:154
  45.9 5.9 %shard_map.96 = f32[8,72,256]{2,1,0:T(8,128)} custom-call(s32[128]{0:T(128)} %clamp_bitcast_fusion.rows_ref, s32[128]{0:T(128)} %fusion.76.cols_ref, s32[128]{0:T(128)} %and_convert_fusion.live_ref, s32[1]{0:T(128)} %bitcast.5.nb_ref, f32[4,72,256]{2,1,0:T(8,128)} %copy-done.3, bf16[1,1,128,256,256]{4,3,2,1,0:T(8,128)(2,1)} %t_ref.9), custom_call_target="tpu_custom_call" | custom-call | tf_op jit(solution)/shard_map/pallas_call | solution.py:74
  58.5 2.3 %collective-permute-start.13 = (f32[72,256]{1,0:T(8,128)S(1)}, f32[72,256]{1,0:T(8,128)S(1)}, u32[]{:S(2)}, u32[]{:S(2)}) collective-permute-start(f32[72,256]{1,0:T(8,128)S(1)} %get-tuple-element.136), channel_id=1, source_target_pairs={{0,24},{4,28},{8,0},{12,4},{16,8},{20,12},{24,16},{28,20},{1,25},{... | collective-permute-start | bytes 221192 | tf_op jit(solution)/shard_map/ppermute | solution.py:180
  62.1 1.8 %collective-permute-done.11 = f32[72,256]{1,0:T(8,128)S(1)} collective-permute-done((f32[72,256]{1,0:T(8,128)S(1)}, f32[72,256]{1,0:T(8,128)S(1)}, u32[]{:S(2)}, u32[]{:S(2)}) %collective-permute-start.11) | collective-permute-done | bytes 73760 | tf_op jit(solution)/shard_map/ppermute | solution.py:180
  64.4 2.8 %collective-permute-done.12 = f32[72,256]{1,0:T(8,128)S(1)} collective-permute-done((f32[72,256]{1,0:T(8,128)S(1)}, f32[72,256]{1,0:T(8,128)S(1)}, u32[]{:S(2)}, u32[]{:S(2)}) %collective-permute-start.12) | collective-permute-done | bytes 73760 | tf_op jit(solution)/shard_map/ppermute | solution.py:180
  67.5 2.0 %collective-permute-start.16 = (f32[1,72,256]{2,1,0:T(8,128)S(1)}, f32[1,72,256]{2,1,0:T(8,128)S(1)}, u32[]{:S(2)}, u32[]{:S(2)}) collective-permute-start(f32[1,72,256]{2,1,0:T(8,128)S(1)} %fusion.40), channel_id=1, source_target_pairs={{0,3},{1,2},{2,1},{3,0},{4,7},{5,6},{6,5},{7,4},{8,11},{9,10},{10,... | collective-permute-start | bytes 221192 | tf_op jit(solution)/shard_map/ppermute | solution.py:154
  75.2 6.3 %shard_map.97 = f32[128,16,128]{2,1,0:T(8,128)} custom-call(s32[128]{0:T(128)} %clamp_bitcast_fusion.rows_ref, s32[128]{0:T(128)} %fusion.76.cols_ref, s32[128]{0:T(128)} %and_convert_fusion.live_ref, s32[1]{0:T(128)} %bitcast.5.nb_ref, f32[4,72,256]{2,1,0:T(8,128)} %pad_maximum_fusion.2.x_ref, bf16[1,1,128,256,256]{4,3,2,1,0:T(8,128)(2,1)} %t_ref.9), custom_call_target="tpu_custom_call" | custom-call | tf_op jit(solution)/shard_map/pallas_call | solution.py:74
  83.3 2.8 %collective-permute-start.19 = (f32[1,2440]{1,0:T(1,128)S(1)}, f32[1,2440]{1,0:T(1,128)S(1)}, u32[]{:S(2)}, u32[]{:S(2)}) collective-permute-start(f32[1,2440]{1,0:T(1,128)S(1)} %broadcast_in_dim.15), channel_id=1, source_target_pairs={{0,3},{1,2},{2,1},{3,0},{4,7},{5,6},{6,5},{7,4},{8,11},{9,10},{10,... | collective-permute-start | bytes 29288 | tf_op jit(solution)/shard_map/ppermute | solution.py:234
  87.9 1.8 %collective-permute-done.18 = f32[1,2440]{1,0:T(1,128)S(1)} collective-permute-done((f32[1,2440]{1,0:T(1,128)S(1)}, f32[1,2440]{1,0:T(1,128)S(1)}, u32[]{:S(2)}, u32[]{:S(2)}) %collective-permute-start.18) | collective-permute-done | bytes 9792 | tf_op jit(solution)/shard_map/ppermute | solution.py:234
  91.1 2.0 %collective-permute-start.23 = (f32[8,2440]{1,0:T(8,128)S(1)}, f32[8,2440]{1,0:T(8,128)S(1)}, u32[]{:S(2)}, u32[]{:S(2)}) collective-permute-start(f32[8,2440]{1,0:T(8,128)S(1)} %concatenate.71), channel_id=1, source_target_pairs={{0,24},{4,28},{8,0},{12,4},{16,8},{20,12},{24,16},{28,20},{1,25},{... | collective-permute-start | bytes 234248 | tf_op jit(solution)/shard_map/ppermute | solution.py:246
  93.8 2.2 %collective-permute-done.23 = f32[8,2440]{1,0:T(8,128)S(1)} collective-permute-done((f32[8,2440]{1,0:T(8,128)S(1)}, f32[8,2440]{1,0:T(8,128)S(1)}, u32[]{:S(2)}, u32[]{:S(2)}) %collective-permute-start.23) | collective-permute-done | bytes 78112 | tf_op jit(solution)/shard_map/ppermute | solution.py:246
  96.0 5.3 %collective-permute-done.22 = f32[8,2440]{1,0:T(8,128)S(1)} collective-permute-done((f32[8,2440]{1,0:T(8,128)S(1)}, f32[8,2440]{1,0:T(8,128)S(1)}, u32[]{:S(2)}, u32[]{:S(2)}) %collective-permute-start.22) | collective-permute-done | bytes 78112 | tf_op jit(solution)/shard_map/ppermute | solution.py:246
  103.6 2.4 %multiply_reduce_fusion.4 = (f32[16]{0:T(128)S(1)}, f32[16,64]{1,0:T(8,128)S(1)}) fusion(f32[16,64]{1,0:T(8,128)S(1)} %get-tuple-element.142, f32[16,64]{1,0:T(8,128)S(1)} %fusion.32, f32[16,64]{1,0:T(8,128)S(1)} %fusion.34, f32[16]{0:T(128)S(1)} %broadcast_multiply_fusion.3, f32[4096,16]{1,0:T(8,128)S(1)} %reshape.497, f32[64]{0:T(128)S(1)} %iota_convert_fusion, ...), kind=kOutput, calls=%fused_computation.115 | convolution fusion | flops 50601968 | bytes 295296 | tf_op jit(solution)/shard_map/tk,ta->ka/dot_general | solution.py:269
  107.4 2.5 %multiply_reduce_fusion.3 = (f32[16]{0:T(128)S(1)}, f32[16,64]{1,0:T(8,128)S(1)}) fusion(f32[16,64]{1,0:T(8,128)S(1)} %get-tuple-element.142, f32[16,64]{1,0:T(8,128)S(1)} %fusion.32, f32[16,64]{1,0:T(8,128)S(1)} %fusion.34, f32[16]{0:T(128)S(1)} %broadcast_multiply_fusion.2, f32[4096,16]{1,0:T(8,128)S(1)} %convolution_multiply_fusion, ...), kind=kOutput, calls=%fused_computation.114 | convolution fusion | flops 50601968 | bytes 295296 | tf_op jit(solution)/shard_map/tk,ta->ka/dot_general | solution.py:281
  110.2 1.8 %collective-permute-start.26 = (f32[1,72,256]{2,1,0:T(8,128)S(1)}, f32[1,72,256]{2,1,0:T(8,128)S(1)}, u32[]{:S(2)}, u32[]{:S(2)}) collective-permute-start(f32[1,72,256]{2,1,0:T(8,128)S(1)} %fusion.39), channel_id=1, source_target_pairs={{0,3},{1,2},{2,1},{3,0},{4,7},{5,6},{6,5},{7,4},{8,11},{9,10},{10,... | collective-permute-start | bytes 221192 | tf_op jit(solution)/shard_map/ppermute | solution.py:154
  113.8 1.9 %collective-permute-done.26 = f32[1,72,256]{2,1,0:T(8,128)S(1)} collective-permute-done((f32[1,72,256]{2,1,0:T(8,128)S(1)}, f32[1,72,256]{2,1,0:T(8,128)S(1)}, u32[]{:S(2)}, u32[]{:S(2)}) %collective-permute-start.26) | collective-permute-done | bytes 73760 | tf_op jit(solution)/shard_map/ppermute | solution.py:154
  118.1 5.9 %shard_map.98 = f32[8,72,256]{2,1,0:T(8,128)} custom-call(s32[128]{0:T(128)} %clamp_bitcast_fusion.rows_ref, s32[128]{0:T(128)} %fusion.76.cols_ref, s32[128]{0:T(128)} %and_convert_fusion.live_ref, s32[1]{0:T(128)} %bitcast.5.nb_ref, f32[4,72,256]{2,1,0:T(8,128)} %copy-done.4, bf16[1,1,128,256,256]{4,3,2,1,0:T(8,128)(2,1)} %t_ref.9), custom_call_target="tpu_custom_call" | custom-call | tf_op jit(solution)/shard_map/pallas_call | solution.py:74
  133.6 5.0 %collective-permute-done.29 = f32[72,256]{1,0:T(8,128)S(1)} collective-permute-done((f32[72,256]{1,0:T(8,128)S(1)}, f32[72,256]{1,0:T(8,128)S(1)}, u32[]{:S(2)}, u32[]{:S(2)}) %collective-permute-start.29) | collective-permute-done | bytes 73760 | tf_op jit(solution)/shard_map/ppermute | solution.py:180
  138.8 2.8 %collective-permute-start.33 = (f32[1,72,256]{2,1,0:T(8,128)S(1)}, f32[1,72,256]{2,1,0:T(8,128)S(1)}, u32[]{:S(2)}, u32[]{:S(2)}) collective-permute-start(f32[1,72,256]{2,1,0:T(8,128)S(1)} %fusion.38), channel_id=1, source_target_pairs={{0,3},{1,2},{2,1},{3,0},{4,7},{5,6},{6,5},{7,4},{8,11},{9,10},{10,... | collective-permute-start | bytes 221192 | tf_op jit(solution)/shard_map/ppermute | solution.py:154
  142.6 1.6 collective-permute-done.33
  144.3 1.7 %collective-permute-done.32 = f32[1,72,256]{2,1,0:T(8,128)S(1)} collective-permute-done((f32[1,72,256]{2,1,0:T(8,128)S(1)}, f32[1,72,256]{2,1,0:T(8,128)S(1)}, u32[]{:S(2)}, u32[]{:S(2)}) %collective-permute-start.32) | collective-permute-done | bytes 73760 | tf_op jit(solution)/shard_map/ppermute | solution.py:154
  146.8 6.0 %shard_map.99 = f32[8,72,256]{2,1,0:T(8,128)} custom-call(s32[128]{0:T(128)} %clamp_bitcast_fusion.rows_ref, s32[128]{0:T(128)} %fusion.76.cols_ref, s32[128]{0:T(128)} %and_convert_fusion.live_ref, s32[1]{0:T(128)} %bitcast.5.nb_ref, f32[4,72,256]{2,1,0:T(8,128)} %copy-done.1, bf16[1,1,128,256,256]{4,3,2,1,0:T(8,128)(2,1)} %t_ref.9), custom_call_target="tpu_custom_call" | custom-call | tf_op jit(solution)/shard_map/pallas_call | solution.py:74
  157.9 2.1 %collective-permute-start.35 = (f32[72,256]{1,0:T(8,128)S(1)}, f32[72,256]{1,0:T(8,128)S(1)}, u32[]{:S(2)}, u32[]{:S(2)}) collective-permute-start(f32[72,256]{1,0:T(8,128)S(1)} %get-tuple-element.128), channel_id=1, source_target_pairs={{0,8},{4,12},{8,16},{12,20},{16,24},{20,28},{24,0},{28,4},{1,9},{5... | collective-permute-start | bytes 221192 | tf_op jit(solution)/shard_map/ppermute | solution.py:180
  160.0 1.8 %collective-permute-start.37 = (f32[72,256]{1,0:T(8,128)S(1)}, f32[72,256]{1,0:T(8,128)S(1)}, u32[]{:S(2)}, u32[]{:S(2)}) collective-permute-start(f32[72,256]{1,0:T(8,128)S(1)} %get-tuple-element.129), channel_id=1, source_target_pairs={{0,24},{4,28},{8,0},{12,4},{16,8},{20,12},{24,16},{28,20},{1,25},{... | collective-permute-start | bytes 221192 | tf_op jit(solution)/shard_map/ppermute | solution.py:180
  162.5 2.3 %collective-permute-done.35 = f32[72,256]{1,0:T(8,128)S(1)} collective-permute-done((f32[72,256]{1,0:T(8,128)S(1)}, f32[72,256]{1,0:T(8,128)S(1)}, u32[]{:S(2)}, u32[]{:S(2)}) %collective-permute-start.35) | collective-permute-done | bytes 73760 | tf_op jit(solution)/shard_map/ppermute | solution.py:180
  165.8 3.0 %collective-permute-done.36 = f32[72,256]{1,0:T(8,128)S(1)} collective-permute-done((f32[72,256]{1,0:T(8,128)S(1)}, f32[72,256]{1,0:T(8,128)S(1)}, u32[]{:S(2)}, u32[]{:S(2)}) %collective-permute-start.36) | collective-permute-done | bytes 73760 | tf_op jit(solution)/shard_map/ppermute | solution.py:180
  (159 shorter events, 68.2 us)
Async XLA Ops:
  2.6 10.5 %collective-permute-start.2 = (f32[1,72,256]{2,1,0:T(8,128)S(1)}, f32[1,72,256]{2,1,0:T(8,128)S(1)}, u32[]{:S(2)}, u32[]{:S(2)}) collective-permute-start(f32[1,72,256]{2,1,0:T(8,128)S(1)} %fusion.42), channel_id=1, source_target_pairs={{0,3},{1,2},{2,1},{3,0},{4,7},{5,6},{6,5},{7,4},{8,11},{9,10},{10,... | collective-permute-start | bytes 221192 | tf_op jit(solution)/shard_map/ppermute | solution.py:154
  6.6 6.5 %collective-permute-start.1 = (f32[1,72,256]{2,1,0:T(8,128)S(1)}, f32[1,72,256]{2,1,0:T(8,128)S(1)}, u32[]{:S(2)}, u32[]{:S(2)}) collective-permute-start(f32[1,72,256]{2,1,0:T(8,128)S(1)} %fusion.42), channel_id=1, source_target_pairs={{0,2},{1,3},{2,0},{3,1},{4,6},{5,7},{6,4},{7,5},{8,10},{9,11},{10,... | collective-permute-start | bytes 221192 | tf_op jit(solution)/shard_map/ppermute | solution.py:154
  7.1 6.0 %collective-permute-start = (f32[1,72,256]{2,1,0:T(8,128)S(1)}, f32[1,72,256]{2,1,0:T(8,128)S(1)}, u32[]{:S(2)}, u32[]{:S(2)}) collective-permute-start(f32[1,72,256]{2,1,0:T(8,128)S(1)} %fusion.42), channel_id=1, source_target_pairs={{0,1},{1,0},{2,3},{3,2},{4,5},{5,4},{6,7},{7,6},{8,9},{9,8},{10,11... | collective-permute-start | bytes 221192 | tf_op jit(solution)/shard_map/ppermute | solution.py:154
  24.9 6.8 %collective-permute-start.4 = (f32[72,256]{1,0:T(8,128)S(1)}, f32[72,256]{1,0:T(8,128)S(1)}, u32[]{:S(2)}, u32[]{:S(2)}) collective-permute-start(f32[72,256]{1,0:T(8,128)S(1)} %get-tuple-element.138), channel_id=1, source_target_pairs={{0,8},{4,12},{8,16},{12,20},{16,24},{20,28},{24,0},{28,4},{1,9},{5... | collective-permute-start | bytes 221192 | tf_op jit(solution)/shard_map/ppermute | solution.py:180
  28.7 4.7 %collective-permute-start.6 = (f32[72,256]{1,0:T(8,128)S(1)}, f32[72,256]{1,0:T(8,128)S(1)}, u32[]{:S(2)}, u32[]{:S(2)}) collective-permute-start(f32[72,256]{1,0:T(8,128)S(1)} %get-tuple-element.139), channel_id=1, source_target_pairs={{0,24},{4,28},{8,0},{12,4},{16,8},{20,12},{24,16},{28,20},{1,25},{... | collective-permute-start | bytes 221192 | tf_op jit(solution)/shard_map/ppermute | solution.py:180
  29.0 7.2 %collective-permute-start.5 = (f32[72,256]{1,0:T(8,128)S(1)}, f32[72,256]{1,0:T(8,128)S(1)}, u32[]{:S(2)}, u32[]{:S(2)}) collective-permute-start(f32[72,256]{1,0:T(8,128)S(1)} %get-tuple-element.140), channel_id=1, source_target_pairs={{0,16},{4,20},{8,24},{12,28},{16,0},{20,4},{24,8},{28,12},{1,17},{... | collective-permute-start | bytes 221192 | tf_op jit(solution)/shard_map/ppermute | solution.py:180
  36.5 5.8 %collective-permute-start.9 = (f32[1,72,256]{2,1,0:T(8,128)S(1)}, f32[1,72,256]{2,1,0:T(8,128)S(1)}, u32[]{:S(2)}, u32[]{:S(2)}) collective-permute-start(f32[1,72,256]{2,1,0:T(8,128)S(1)} %fusion.41), channel_id=1, source_target_pairs={{0,3},{1,2},{2,1},{3,0},{4,7},{5,6},{6,5},{7,4},{8,11},{9,10},{10,... | collective-permute-start | bytes 221192 | tf_op jit(solution)/shard_map/ppermute | solution.py:154
  39.9 4.4 %collective-permute-start.8 = (f32[1,72,256]{2,1,0:T(8,128)S(1)}, f32[1,72,256]{2,1,0:T(8,128)S(1)}, u32[]{:S(2)}, u32[]{:S(2)}) collective-permute-start(f32[1,72,256]{2,1,0:T(8,128)S(1)} %fusion.41), channel_id=1, source_target_pairs={{0,2},{1,3},{2,0},{3,1},{4,6},{5,7},{6,4},{7,5},{8,10},{9,11},{10,... | collective-permute-start | bytes 221192 | tf_op jit(solution)/shard_map/ppermute | solution.py:154
  40.1 5.0 %collective-permute-start.7 = (f32[1,72,256]{2,1,0:T(8,128)S(1)}, f32[1,72,256]{2,1,0:T(8,128)S(1)}, u32[]{:S(2)}, u32[]{:S(2)}) collective-permute-start(f32[1,72,256]{2,1,0:T(8,128)S(1)} %fusion.41), channel_id=1, source_target_pairs={{0,1},{1,0},{2,3},{3,2},{4,5},{5,4},{6,7},{7,6},{8,9},{9,8},{10,11... | collective-permute-start | bytes 221192 | tf_op jit(solution)/shard_map/ppermute | solution.py:154
  56.9 7.0 %collective-permute-start.11 = (f32[72,256]{1,0:T(8,128)S(1)}, f32[72,256]{1,0:T(8,128)S(1)}, u32[]{:S(2)}, u32[]{:S(2)}) collective-permute-start(f32[72,256]{1,0:T(8,128)S(1)} %get-tuple-element.135), channel_id=1, source_target_pairs={{0,8},{4,12},{8,16},{12,20},{16,24},{20,28},{24,0},{28,4},{1,9},{5... | collective-permute-start | bytes 221192 | tf_op jit(solution)/shard_map/ppermute | solution.py:180
  58.5 5.9 %collective-permute-start.13 = (f32[72,256]{1,0:T(8,128)S(1)}, f32[72,256]{1,0:T(8,128)S(1)}, u32[]{:S(2)}, u32[]{:S(2)}) collective-permute-start(f32[72,256]{1,0:T(8,128)S(1)} %get-tuple-element.136), channel_id=1, source_target_pairs={{0,24},{4,28},{8,0},{12,4},{16,8},{20,12},{24,16},{28,20},{1,25},{... | collective-permute-start | bytes 221192 | tf_op jit(solution)/shard_map/ppermute | solution.py:180
  60.8 6.4 %collective-permute-start.12 = (f32[72,256]{1,0:T(8,128)S(1)}, f32[72,256]{1,0:T(8,128)S(1)}, u32[]{:S(2)}, u32[]{:S(2)}) collective-permute-start(f32[72,256]{1,0:T(8,128)S(1)} %get-tuple-element.137), channel_id=1, source_target_pairs={{0,16},{4,20},{8,24},{12,28},{16,0},{20,4},{24,8},{28,12},{1,17},{... | collective-permute-start | bytes 221192 | tf_op jit(solution)/shard_map/ppermute | solution.py:180
  67.5 5.8 %collective-permute-start.16 = (f32[1,72,256]{2,1,0:T(8,128)S(1)}, f32[1,72,256]{2,1,0:T(8,128)S(1)}, u32[]{:S(2)}, u32[]{:S(2)}) collective-permute-start(f32[1,72,256]{2,1,0:T(8,128)S(1)} %fusion.40), channel_id=1, source_target_pairs={{0,3},{1,2},{2,1},{3,0},{4,7},{5,6},{6,5},{7,4},{8,11},{9,10},{10,... | collective-permute-start | bytes 221192 | tf_op jit(solution)/shard_map/ppermute | solution.py:154
  69.5 4.5 %collective-permute-start.15 = (f32[1,72,256]{2,1,0:T(8,128)S(1)}, f32[1,72,256]{2,1,0:T(8,128)S(1)}, u32[]{:S(2)}, u32[]{:S(2)}) collective-permute-start(f32[1,72,256]{2,1,0:T(8,128)S(1)} %fusion.40), channel_id=1, source_target_pairs={{0,2},{1,3},{2,0},{3,1},{4,6},{5,7},{6,4},{7,5},{8,10},{9,11},{10,... | collective-permute-start | bytes 221192 | tf_op jit(solution)/shard_map/ppermute | solution.py:154
  69.9 4.5 %collective-permute-start.14 = (f32[1,72,256]{2,1,0:T(8,128)S(1)}, f32[1,72,256]{2,1,0:T(8,128)S(1)}, u32[]{:S(2)}, u32[]{:S(2)}) collective-permute-start(f32[1,72,256]{2,1,0:T(8,128)S(1)} %fusion.40), channel_id=1, source_target_pairs={{0,1},{1,0},{2,3},{3,2},{4,5},{5,4},{6,7},{7,6},{8,9},{9,8},{10,11... | collective-permute-start | bytes 221192 | tf_op jit(solution)/shard_map/ppermute | solution.py:154
  83.3 4.6 %collective-permute-start.19 = (f32[1,2440]{1,0:T(1,128)S(1)}, f32[1,2440]{1,0:T(1,128)S(1)}, u32[]{:S(2)}, u32[]{:S(2)}) collective-permute-start(f32[1,2440]{1,0:T(1,128)S(1)} %broadcast_in_dim.15), channel_id=1, source_target_pairs={{0,3},{1,2},{2,1},{3,0},{4,7},{5,6},{6,5},{7,4},{8,11},{9,10},{10,... | collective-permute-start | bytes 29288 | tf_op jit(solution)/shard_map/ppermute | solution.py:234
  86.0 3.7 %collective-permute-start.18 = (f32[1,2440]{1,0:T(1,128)S(1)}, f32[1,2440]{1,0:T(1,128)S(1)}, u32[]{:S(2)}, u32[]{:S(2)}) collective-permute-start(f32[1,2440]{1,0:T(1,128)S(1)} %broadcast_in_dim.15), channel_id=1, source_target_pairs={{0,2},{1,3},{2,0},{3,1},{4,6},{5,7},{6,4},{7,5},{8,10},{9,11},{10,... | collective-permute-start | bytes 29288 | tf_op jit(solution)/shard_map/ppermute | solution.py:234
  91.1 4.9 %collective-permute-start.23 = (f32[8,2440]{1,0:T(8,128)S(1)}, f32[8,2440]{1,0:T(8,128)S(1)}, u32[]{:S(2)}, u32[]{:S(2)}) collective-permute-start(f32[8,2440]{1,0:T(8,128)S(1)} %concatenate.71), channel_id=1, source_target_pairs={{0,24},{4,28},{8,0},{12,4},{16,8},{20,12},{24,16},{28,20},{1,25},{... | collective-permute-start | bytes 234248 | tf_op jit(solution)/shard_map/ppermute | solution.py:246
  93.1 8.1 %collective-permute-start.22 = (f32[8,2440]{1,0:T(8,128)S(1)}, f32[8,2440]{1,0:T(8,128)S(1)}, u32[]{:S(2)}, u32[]{:S(2)}) collective-permute-start(f32[8,2440]{1,0:T(8,128)S(1)} %concatenate.71), channel_id=1, source_target_pairs={{0,16},{4,20},{8,24},{12,28},{16,0},{20,4},{24,8},{28,12},{1,17},{... | collective-permute-start | bytes 234248 | tf_op jit(solution)/shard_map/ppermute | solution.py:246
  93.1 8.1 %collective-permute-start.21 = (f32[8,2440]{1,0:T(8,128)S(1)}, f32[8,2440]{1,0:T(8,128)S(1)}, u32[]{:S(2)}, u32[]{:S(2)}) collective-permute-start(f32[8,2440]{1,0:T(8,128)S(1)} %concatenate.71), channel_id=1, source_target_pairs={{0,8},{4,12},{8,16},{12,20},{16,24},{20,28},{24,0},{28,4},{1,9},{5... | collective-permute-start | bytes 234248 | tf_op jit(solution)/shard_map/ppermute | solution.py:246
  110.2 5.5 %collective-permute-start.26 = (f32[1,72,256]{2,1,0:T(8,128)S(1)}, f32[1,72,256]{2,1,0:T(8,128)S(1)}, u32[]{:S(2)}, u32[]{:S(2)}) collective-permute-start(f32[1,72,256]{2,1,0:T(8,128)S(1)} %fusion.39), channel_id=1, source_target_pairs={{0,3},{1,2},{2,1},{3,0},{4,7},{5,6},{6,5},{7,4},{8,11},{9,10},{10,... | collective-permute-start | bytes 221192 | tf_op jit(solution)/shard_map/ppermute | solution.py:154
  112.0 4.9 %collective-permute-start.25 = (f32[1,72,256]{2,1,0:T(8,128)S(1)}, f32[1,72,256]{2,1,0:T(8,128)S(1)}, u32[]{:S(2)}, u32[]{:S(2)}) collective-permute-start(f32[1,72,256]{2,1,0:T(8,128)S(1)} %fusion.39), channel_id=1, source_target_pairs={{0,2},{1,3},{2,0},{3,1},{4,6},{5,7},{6,4},{7,5},{8,10},{9,11},{10,... | collective-permute-start | bytes 221192 | tf_op jit(solution)/shard_map/ppermute | solution.py:154
  112.5 4.9 %collective-permute-start.24 = (f32[1,72,256]{2,1,0:T(8,128)S(1)}, f32[1,72,256]{2,1,0:T(8,128)S(1)}, u32[]{:S(2)}, u32[]{:S(2)}) collective-permute-start(f32[1,72,256]{2,1,0:T(8,128)S(1)} %fusion.39), channel_id=1, source_target_pairs={{0,1},{1,0},{2,3},{3,2},{4,5},{5,4},{6,7},{7,6},{8,9},{9,8},{10,11... | collective-permute-start | bytes 221192 | tf_op jit(solution)/shard_map/ppermute | solution.py:154
  129.2 4.4 %collective-permute-start.30 = (f32[72,256]{1,0:T(8,128)S(1)}, f32[72,256]{1,0:T(8,128)S(1)}, u32[]{:S(2)}, u32[]{:S(2)}) collective-permute-start(f32[72,256]{1,0:T(8,128)S(1)} %get-tuple-element.132), channel_id=1, source_target_pairs={{0,24},{4,28},{8,0},{12,4},{16,8},{20,12},{24,16},{28,20},{1,25},{... | collective-permute-start | bytes 221192 | tf_op jit(solution)/shard_map/ppermute | solution.py:180
  130.4 8.3 %collective-permute-start.29 = (f32[72,256]{1,0:T(8,128)S(1)}, f32[72,256]{1,0:T(8,128)S(1)}, u32[]{:S(2)}, u32[]{:S(2)}) collective-permute-start(f32[72,256]{1,0:T(8,128)S(1)} %get-tuple-element.133), channel_id=1, source_target_pairs={{0,16},{4,20},{8,24},{12,28},{16,0},{20,4},{24,8},{28,12},{1,17},{... | collective-permute-start | bytes 221192 | tf_op jit(solution)/shard_map/ppermute | solution.py:180
  131.4 7.2 %collective-permute-start.28 = (f32[72,256]{1,0:T(8,128)S(1)}, f32[72,256]{1,0:T(8,128)S(1)}, u32[]{:S(2)}, u32[]{:S(2)}) collective-permute-start(f32[72,256]{1,0:T(8,128)S(1)} %get-tuple-element.134), channel_id=1, source_target_pairs={{0,8},{4,12},{8,16},{12,20},{16,24},{20,28},{24,0},{28,4},{1,9},{5... | collective-permute-start | bytes 221192 | tf_op jit(solution)/shard_map/ppermute | solution.py:180
  138.8 5.4 %collective-permute-start.33 = (f32[1,72,256]{2,1,0:T(8,128)S(1)}, f32[1,72,256]{2,1,0:T(8,128)S(1)}, u32[]{:S(2)}, u32[]{:S(2)}) collective-permute-start(f32[1,72,256]{2,1,0:T(8,128)S(1)} %fusion.38), channel_id=1, source_target_pairs={{0,3},{1,2},{2,1},{3,0},{4,7},{5,6},{6,5},{7,4},{8,11},{9,10},{10,... | collective-permute-start | bytes 221192 | tf_op jit(solution)/shard_map/ppermute | solution.py:154
  141.7 4.4 %collective-permute-start.32 = (f32[1,72,256]{2,1,0:T(8,128)S(1)}, f32[1,72,256]{2,1,0:T(8,128)S(1)}, u32[]{:S(2)}, u32[]{:S(2)}) collective-permute-start(f32[1,72,256]{2,1,0:T(8,128)S(1)} %fusion.38), channel_id=1, source_target_pairs={{0,2},{1,3},{2,0},{3,1},{4,6},{5,7},{6,4},{7,5},{8,10},{9,11},{10,... | collective-permute-start | bytes 221192 | tf_op jit(solution)/shard_map/ppermute | solution.py:154
  141.7 4.4 %collective-permute-start.31 = (f32[1,72,256]{2,1,0:T(8,128)S(1)}, f32[1,72,256]{2,1,0:T(8,128)S(1)}, u32[]{:S(2)}, u32[]{:S(2)}) collective-permute-start(f32[1,72,256]{2,1,0:T(8,128)S(1)} %fusion.38), channel_id=1, source_target_pairs={{0,1},{1,0},{2,3},{3,2},{4,5},{5,4},{6,7},{7,6},{8,9},{9,8},{10,11... | collective-permute-start | bytes 221192 | tf_op jit(solution)/shard_map/ppermute | solution.py:154
  157.9 7.0 %collective-permute-start.35 = (f32[72,256]{1,0:T(8,128)S(1)}, f32[72,256]{1,0:T(8,128)S(1)}, u32[]{:S(2)}, u32[]{:S(2)}) collective-permute-start(f32[72,256]{1,0:T(8,128)S(1)} %get-tuple-element.128), channel_id=1, source_target_pairs={{0,8},{4,12},{8,16},{12,20},{16,24},{20,28},{24,0},{28,4},{1,9},{5... | collective-permute-start | bytes 221192 | tf_op jit(solution)/shard_map/ppermute | solution.py:180
  160.0 5.8 %collective-permute-start.37 = (f32[72,256]{1,0:T(8,128)S(1)}, f32[72,256]{1,0:T(8,128)S(1)}, u32[]{:S(2)}, u32[]{:S(2)}) collective-permute-start(f32[72,256]{1,0:T(8,128)S(1)} %get-tuple-element.129), channel_id=1, source_target_pairs={{0,24},{4,28},{8,0},{12,4},{16,8},{20,12},{24,16},{28,20},{1,25},{... | collective-permute-start | bytes 221192 | tf_op jit(solution)/shard_map/ppermute | solution.py:180
  161.8 7.0 %collective-permute-start.36 = (f32[72,256]{1,0:T(8,128)S(1)}, f32[72,256]{1,0:T(8,128)S(1)}, u32[]{:S(2)}, u32[]{:S(2)}) collective-permute-start(f32[72,256]{1,0:T(8,128)S(1)} %get-tuple-element.130), channel_id=1, source_target_pairs={{0,16},{4,20},{8,24},{12,28},{16,0},{20,4},{24,8},{28,12},{1,17},{... | collective-permute-start | bytes 221192 | tf_op jit(solution)/shard_map/ppermute | solution.py:180
  (12 other events, 32.0 us)

commit v4 on v3

--- a/solution.py
+++ b/solution.py
@@ -189,8 +189,11 @@
     def lost_partial(blocks):
         return jnp.sum(blocks * piece_dangling[:, None, None], axis=(0, 2))
 
-    def relaxation(blocks, lost_sum=None):
-        gathered, lost_dst = spread_columns(blocks, lost_partial(blocks))
+    def relaxation(blocks, lost_sum=None, gathered=None):
+        if gathered is None:
+            gathered, lost_dst = spread_columns(blocks, lost_partial(blocks))
+        else:
+            lost_dst = jnp.zeros((vectors,), jnp.float32)
         accumulated = tile_pass(
             "image", gathered, tiles, own_rows, kernel_cols, live_mask, block_count,
             row_blocks, vectors,
@@ -283,8 +286,24 @@
     )
     level_two = coarse_sweep(inflow_two, ratios_one)
     ratios_two = level_two / totals
-    rescale = jnp.einsum("ka,ba->bk", ratios_two, piece_hot, precision=highest)
-    corrected = relaxed_two * rescale[:, :, None]
+    groups = gathered.shape[0]
+    group_ids = jnp.arange(groups, dtype=jnp.int32)
+    if exchange:
+        group_ids = group_ids ^ dst_index
+    block_ids = (
+        group_ids[:, None] * row_blocks
+        + src_index * blocks_piece
+        + jnp.arange(blocks_piece, dtype=jnp.int32)[None, :]
+    )
+    block_scale = jnp.take(ratios_two, agg_of_block[block_ids.reshape(-1)], axis=1)
+    block_scale = block_scale.T.reshape(groups, payload_rows, 1)
+    corrected_cols = jnp.concatenate(
+        [
+            gathered[:, :payload_rows, :] * block_scale,
+            jnp.zeros((groups, pad_rows, tile_side), jnp.float32),
+        ],
+        axis=1,
+    )
     lost_two = jnp.sum(lost_mass * ratios_two, axis=1)
 
     position = lax.axis_index(all_axes)
@@ -293,7 +312,7 @@
     owned_hot = (owned[:, None] == agg_range[None, :]).astype(jnp.float32)
     coarse_out = jnp.einsum("ka,qa->kq", level_two, owned_hot, precision=highest)
 
-    relaxed_three = relaxation(corrected, lost_two)
+    relaxed_three = relaxation(None, lost_two, corrected_cols)
     relaxed_four = relaxation(relaxed_three)
     fine_out = jnp.transpose(relaxed_four, (1, 0, 2)).reshape(teleport.shape)
     return fine_out, coarse_out

time: 173 us -> 168 us (0.971); the launches traced: 170 us -> 168 us
  waiting for transfers between devices: 53.6 us -> 49.7 us
    ppermute x15 -> x12, starting transfers between devices: 20.7 us -> 15.7 us  [spread_columns(): lax.ppermute(payload, 'dst', [(i, i ^ v) for i in range(dst_count)])]
    ppermute x12, starting transfers between devices: 16.4 us -> 20.8 us  [reduce_rows(): total = total + lax.ppermute(send, 'src', pairs)]
    ppermute x15 -> x12, waiting for transfers between devices: 12.4 us -> 8.76 us  [spread_columns(): lax.ppermute(payload, 'dst', [(i, i ^ v) for i in range(dst_count)])]
    ppermute x3, starting transfers between devices: 3.55 us -> 5.35 us  [per_device(): lax.ppermute(shared, 'dst', [(i, i ^ v) for i in range(dst_count)])]
  transfers between devices with their start and end apart: 38 -> 35, of which waited for: 31 -> 29; matrix products, arithmetic and copies ran while one was open for 5% -> 6% of each run, Pallas kernels for 0% -> 0%
where the time goes in v4:
time: 168 us
  waiting for transfers between devices  49.7 us (30%)
  starting transfers between devices  44.2 us (26%)
  Pallas kernels  30.1 us (18%)
  local copies, waits for them, and re-layouts  21 us (12%)
  other arithmetic  13.2 us (8%)
  matrix products  7.86 us (5%)
  between operations  1.81 us (1%)
    pallas_call x5, Pallas kernels, tile_pass(): pl.pallas_call(functools.partial(tile_kernel, mode, blocks_piece, vectors...  30.1 us
    ppermute x12, waiting for transfers between devices, reduce_rows(): total = total + lax.ppermute(send, 'src', pairs)  24.7 us
    ppermute x12, starting transfers between devices, reduce_rows(): total = total + lax.ppermute(send, 'src', pairs)  20.8 us
    ppermute x12, starting transfers between devices, spread_columns(): lax.ppermute(payload, 'dst', [(i, i ^ v) for i in range(dst_count)])  15.7 us
    ppermute x12, waiting for transfers between devices, spread_columns(): lax.ppermute(payload, 'dst', [(i, i ^ v) for i in range(dst_count)])  8.76 us
    ppermute x3, waiting for transfers between devices, per_device(): pieces.append(lax.ppermute(shared, 'src', pairs))  7.37 us
    scatter x4, local copies, waits for them, and re-layouts, reduce_rows(): accumulated.at[:, payload_rows, :vectors]  6.04 us
    ppermute x4, waiting for transfers between devices, reduce_rows(): part = keep + lax.ppermute(give, 'src', [(i, i ^ 1) for i in range(n)])  5.4 us
  transfers between devices with their start and end apart: 35, of which 29 were waited for; matrix products, arithmetic and copies ran while one was open for 6% of the time, Pallas kernels for 0%

profile of v4, /device:TPU:0, one launch (start us, length us, event | category | flops | bytes accessed | tf_op | source)
XLA Modules:
  0.0 167.9 jit_solution(4814294147656284574)
XLA Ops:
  2.6 4.0 %collective-permute-start.2 = (f32[1,72,256]{2,1,0:T(8,128)S(1)}, f32[1,72,256]{2,1,0:T(8,128)S(1)}, u32[]{:S(2)}, u32[]{:S(2)}) collective-permute-start(f32[1,72,256]{2,1,0:T(8,128)S(1)} %fusion.41), channel_id=1, source_target_pairs={{0,3},{1,2},{2,1},{3,0},{4,7},{5,6},{6,5},{7,4},{8,11},{9,10},{10,... | collective-permute-start | bytes 221192 | tf_op jit(solution)/shard_map/ppermute | solution.py:154
  10.9 1.6 gather_fusion
  13.9 5.9 %shard_map.95 = f32[8,72,256]{2,1,0:T(8,128)} custom-call(s32[128]{0:T(128)} %clamp_bitcast_fusion.rows_ref, s32[128]{0:T(128)} %fusion.73.cols_ref, s32[128]{0:T(128)} %and_convert_fusion.live_ref, s32[1]{0:T(128)} %bitcast.5.nb_ref, f32[4,72,256]{2,1,0:T(8,128)} %copy-done.3, bf16[1,1,128,256,256]{4,3,2,1,0:T(8,128)(2,1)} %t_ref.9), custom_call_target="tpu_custom_call" | custom-call | tf_op jit(solution)/shard_map/pallas_call | solution.py:74
  24.9 5.2 %collective-permute-start.4 = (f32[72,256]{1,0:T(8,128)S(1)}, f32[72,256]{1,0:T(8,128)S(1)}, u32[]{:S(2)}, u32[]{:S(2)}) collective-permute-start(f32[72,256]{1,0:T(8,128)S(1)} %get-tuple-element.124), channel_id=1, source_target_pairs={{0,8},{4,12},{8,16},{12,20},{16,24},{20,28},{24,0},{28,4},{1,9},{5... | collective-permute-start | bytes 221192 | tf_op jit(solution)/shard_map/ppermute | solution.py:180
  31.6 2.1 %collective-permute-done.4 = f32[72,256]{1,0:T(8,128)S(1)} collective-permute-done((f32[72,256]{1,0:T(8,128)S(1)}, f32[72,256]{1,0:T(8,128)S(1)}, u32[]{:S(2)}, u32[]{:S(2)}) %collective-permute-start.4) | collective-permute-done | bytes 73760 | tf_op jit(solution)/shard_map/ppermute | solution.py:180
  35.2 3.1 %collective-permute-done.5 = f32[72,256]{1,0:T(8,128)S(1)} collective-permute-done((f32[72,256]{1,0:T(8,128)S(1)}, f32[72,256]{1,0:T(8,128)S(1)}, u32[]{:S(2)}, u32[]{:S(2)}) %collective-permute-start.5) | collective-permute-done | bytes 73760 | tf_op jit(solution)/shard_map/ppermute | solution.py:180
  38.6 1.7 collective-permute-start.9
  42.3 2.1 %collective-permute-done.9 = f32[1,72,256]{2,1,0:T(8,128)S(1)} collective-permute-done((f32[1,72,256]{2,1,0:T(8,128)S(1)}, f32[1,72,256]{2,1,0:T(8,128)S(1)}, u32[]{:S(2)}, u32[]{:S(2)}) %collective-permute-start.9) | collective-permute-done | bytes 73760 | tf_op jit(solution)/shard_map/ppermute | solution.py:154
  46.7 6.0 %shard_map.96 = f32[8,72,256]{2,1,0:T(8,128)} custom-call(s32[128]{0:T(128)} %clamp_bitcast_fusion.rows_ref, s32[128]{0:T(128)} %fusion.73.cols_ref, s32[128]{0:T(128)} %and_convert_fusion.live_ref, s32[1]{0:T(128)} %bitcast.5.nb_ref, f32[4,72,256]{2,1,0:T(8,128)} %copy-done.4, bf16[1,1,128,256,256]{4,3,2,1,0:T(8,128)(2,1)} %t_ref.9), custom_call_target="tpu_custom_call" | custom-call | tf_op jit(solution)/shard_map/pallas_call | solution.py:74
  57.9 2.5 %collective-permute-start.11 = (f32[72,256]{1,0:T(8,128)S(1)}, f32[72,256]{1,0:T(8,128)S(1)}, u32[]{:S(2)}, u32[]{:S(2)}) collective-permute-start(f32[72,256]{1,0:T(8,128)S(1)} %get-tuple-element.121), channel_id=1, source_target_pairs={{0,8},{4,12},{8,16},{12,20},{16,24},{20,28},{24,0},{28,4},{1,9},{5... | collective-permute-start | bytes 221192 | tf_op jit(solution)/shard_map/ppermute | solution.py:180
  60.3 1.6 collective-permute-start.13
  65.9 3.4 %collective-permute-done.12 = f32[72,256]{1,0:T(8,128)S(1)} collective-permute-done((f32[72,256]{1,0:T(8,128)S(1)}, f32[72,256]{1,0:T(8,128)S(1)}, u32[]{:S(2)}, u32[]{:S(2)}) %collective-permute-start.12) | collective-permute-done | bytes 73760 | tf_op jit(solution)/shard_map/ppermute | solution.py:180
  69.6 2.0 %collective-permute-start.16 = (f32[1,72,256]{2,1,0:T(8,128)S(1)}, f32[1,72,256]{2,1,0:T(8,128)S(1)}, u32[]{:S(2)}, u32[]{:S(2)}) collective-permute-start(f32[1,72,256]{2,1,0:T(8,128)S(1)} %fusion.39), channel_id=1, source_target_pairs={{0,3},{1,2},{2,1},{3,0},{4,7},{5,6},{6,5},{7,4},{8,11},{9,10},{10,... | collective-permute-start | bytes 221192 | tf_op jit(solution)/shard_map/ppermute | solution.py:154
  77.4 6.3 %shard_map.97 = f32[128,16,128]{2,1,0:T(8,128)} custom-call(s32[128]{0:T(128)} %clamp_bitcast_fusion.rows_ref, s32[128]{0:T(128)} %fusion.73.cols_ref, s32[128]{0:T(128)} %and_convert_fusion.live_ref, s32[1]{0:T(128)} %bitcast.5.nb_ref, f32[4,72,256]{2,1,0:T(8,128)} %pad_maximum_fusion.2.x_ref, bf16[1,1,128,256,256]{4,3,2,1,0:T(8,128)(2,1)} %t_ref.9), custom_call_target="tpu_custom_call" | custom-call | tf_op jit(solution)/shard_map/pallas_call | solution.py:74
  83.8 1.6 reduce_sum.112
  85.5 2.8 %collective-permute-start.19 = (f32[1,2440]{1,0:T(1,128)S(1)}, f32[1,2440]{1,0:T(1,128)S(1)}, u32[]{:S(2)}, u32[]{:S(2)}) collective-permute-start(f32[1,2440]{1,0:T(1,128)S(1)} %broadcast_in_dim.21), channel_id=1, source_target_pairs={{0,3},{1,2},{2,1},{3,0},{4,7},{5,6},{6,5},{7,4},{8,11},{9,10},{10,... | collective-permute-start | bytes 29288 | tf_op jit(solution)/shard_map/ppermute | solution.py:237
  96.6 3.3 %collective-permute-done.23 = f32[8,2440]{1,0:T(8,128)S(1)} collective-permute-done((f32[8,2440]{1,0:T(8,128)S(1)}, f32[8,2440]{1,0:T(8,128)S(1)}, u32[]{:S(2)}, u32[]{:S(2)}) %collective-permute-start.23) | collective-permute-done | bytes 78112 | tf_op jit(solution)/shard_map/ppermute | solution.py:249
  99.9 4.1 %collective-permute-done.22 = f32[8,2440]{1,0:T(8,128)S(1)} collective-permute-done((f32[8,2440]{1,0:T(8,128)S(1)}, f32[8,2440]{1,0:T(8,128)S(1)}, u32[]{:S(2)}, u32[]{:S(2)}) %collective-permute-start.22) | collective-permute-done | bytes 78112 | tf_op jit(solution)/shard_map/ppermute | solution.py:249
  106.3 2.4 %multiply_reduce_fusion.3 = (f32[16]{0:T(128)S(1)}, f32[16,64]{1,0:T(8,128)S(1)}) fusion(f32[16,64]{1,0:T(8,128)S(1)} %get-tuple-element.128, f32[16,64]{1,0:T(8,128)S(1)} %fusion.32, f32[16,64]{1,0:T(8,128)S(1)} %fusion.34, f32[16]{0:T(128)S(1)} %broadcast_multiply_fusion.2, f32[4096,16]{1,0:T(8,128)S(1)} %reshape.524, f32[64]{0:T(128)S(1)} %iota_convert_fusion, ...), kind=kOutput, calls=%fused_computation.113 | convolution fusion | flops 50601968 | bytes 295296 | tf_op jit(solution)/shard_map/tk,ta->ka/dot_general | solution.py:272
  110.1 2.5 %multiply_reduce_fusion.2 = (f32[16]{0:T(128)S(1)}, f32[16,64]{1,0:T(8,128)S(1)}, f32[16,64]{1,0:T(8,128)S(1)}) fusion(f32[16,64]{1,0:T(8,128)S(1)} %get-tuple-element.128, f32[16,64]{1,0:T(8,128)S(1)} %fusion.32, f32[16,64]{1,0:T(8,128)S(1)} %fusion.34, f32[16]{0:T(128)S(1)} %broadcast_multiply_fusion.1, f32[4096,16]{1,0:T(8,128)S(1)} %convolution_multiply_fusion, ...), kind=kOutput, calls=%fused_computation.112 | convolution fusion | flops 50601968 | bytes 299392 | tf_op jit(solution)/shard_map/tk,ta->ka/dot_general | solution.py:284
  114.2 5.9 %shard_map.98 = f32[8,72,256]{2,1,0:T(8,128)} custom-call(s32[128]{0:T(128)} %clamp_bitcast_fusion.rows_ref, s32[128]{0:T(128)} %fusion.73.cols_ref, s32[128]{0:T(128)} %and_convert_fusion.live_ref, s32[1]{0:T(128)} %bitcast.5.nb_ref, f32[4,72,256]{2,1,0:T(8,128)} %concatenate.68.x_ref, bf16[1,1,128,256,256]{4,3,2,1,0:T(8,128)(2,1)} %t_ref.9), custom_call_target="tpu_custom_call" | custom-call | tf_op jit(solution)/shard_map/pallas_call | solution.py:74
  120.1 1.5 scatter.35
  122.7 1.6 collective-permute-done.24
  125.3 3.6 %collective-permute-start.27 = (f32[72,256]{1,0:T(8,128)S(1)}, f32[72,256]{1,0:T(8,128)S(1)}, u32[]{:S(2)}, u32[]{:S(2)}) collective-permute-start(f32[72,256]{1,0:T(8,128)S(1)} %get-tuple-element.118), channel_id=1, source_target_pairs={{0,24},{4,28},{8,0},{12,4},{16,8},{20,12},{24,16},{28,20},{1,25},{... | collective-permute-start | bytes 221192 | tf_op jit(solution)/shard_map/ppermute | solution.py:180
  129.9 1.7 %collective-permute-done.27 = f32[72,256]{1,0:T(8,128)S(1)} collective-permute-done((f32[72,256]{1,0:T(8,128)S(1)}, f32[72,256]{1,0:T(8,128)S(1)}, u32[]{:S(2)}, u32[]{:S(2)}) %collective-permute-start.27) | collective-permute-done | bytes 73760 | tf_op jit(solution)/shard_map/ppermute | solution.py:180
  131.6 5.4 %collective-permute-done.26 = f32[72,256]{1,0:T(8,128)S(1)} collective-permute-done((f32[72,256]{1,0:T(8,128)S(1)}, f32[72,256]{1,0:T(8,128)S(1)}, u32[]{:S(2)}, u32[]{:S(2)}) %collective-permute-start.26) | collective-permute-done | bytes 73760 | tf_op jit(solution)/shard_map/ppermute | solution.py:180
  138.0 1.7 collective-permute-start.29
  140.8 2.3 %collective-permute-done.30 = f32[1,72,256]{2,1,0:T(8,128)S(1)} collective-permute-done((f32[1,72,256]{2,1,0:T(8,128)S(1)}, f32[1,72,256]{2,1,0:T(8,128)S(1)}, u32[]{:S(2)}, u32[]{:S(2)}) %collective-permute-start.30) | collective-permute-done | bytes 73760 | tf_op jit(solution)/shard_map/ppermute | solution.py:154
  144.9 6.0 %shard_map.99 = f32[8,72,256]{2,1,0:T(8,128)} custom-call(s32[128]{0:T(128)} %clamp_bitcast_fusion.rows_ref, s32[128]{0:T(128)} %fusion.73.cols_ref, s32[128]{0:T(128)} %and_convert_fusion.live_ref, s32[1]{0:T(128)} %bitcast.5.nb_ref, f32[4,72,256]{2,1,0:T(8,128)} %copy-done.2, bf16[1,1,128,256,256]{4,3,2,1,0:T(8,128)(2,1)} %t_ref.9), custom_call_target="tpu_custom_call" | custom-call | tf_op jit(solution)/shard_map/pallas_call | solution.py:74
  150.9 1.5 scatter.39
  156.1 3.4 %collective-permute-start.32 = (f32[72,256]{1,0:T(8,128)S(1)}, f32[72,256]{1,0:T(8,128)S(1)}, u32[]{:S(2)}, u32[]{:S(2)}) collective-permute-start(f32[72,256]{1,0:T(8,128)S(1)} %get-tuple-element.114), channel_id=1, source_target_pairs={{0,8},{4,12},{8,16},{12,20},{16,24},{20,28},{24,0},{28,4},{1,9},{5... | collective-permute-start | bytes 221192 | tf_op jit(solution)/shard_map/ppermute | solution.py:180
  164.3 2.7 %collective-permute-done.33 = f32[72,256]{1,0:T(8,128)S(1)} collective-permute-done((f32[72,256]{1,0:T(8,128)S(1)}, f32[72,256]{1,0:T(8,128)S(1)}, u32[]{:S(2)}, u32[]{:S(2)}) %collective-permute-start.33) | collective-permute-done | bytes 73760 | tf_op jit(solution)/shard_map/ppermute | solution.py:180
  (163 shorter events, 64.8 us)
Async XLA Ops:
  2.6 10.5 %collective-permute-start.2 = (f32[1,72,256]{2,1,0:T(8,128)S(1)}, f32[1,72,256]{2,1,0:T(8,128)S(1)}, u32[]{:S(2)}, u32[]{:S(2)}) collective-permute-start(f32[1,72,256]{2,1,0:T(8,128)S(1)} %fusion.41), channel_id=1, source_target_pairs={{0,3},{1,2},{2,1},{3,0},{4,7},{5,6},{6,5},{7,4},{8,11},{9,10},{10,... | collective-permute-start | bytes 221192 | tf_op jit(solution)/shard_map/ppermute | solution.py:154
  6.6 6.5 %collective-permute-start.1 = (f32[1,72,256]{2,1,0:T(8,128)S(1)}, f32[1,72,256]{2,1,0:T(8,128)S(1)}, u32[]{:S(2)}, u32[]{:S(2)}) collective-permute-start(f32[1,72,256]{2,1,0:T(8,128)S(1)} %fusion.41), channel_id=1, source_target_pairs={{0,2},{1,3},{2,0},{3,1},{4,6},{5,7},{6,4},{7,5},{8,10},{9,11},{10,... | collective-permute-start | bytes 221192 | tf_op jit(solution)/shard_map/ppermute | solution.py:154
  7.1 6.0 %collective-permute-start = (f32[1,72,256]{2,1,0:T(8,128)S(1)}, f32[1,72,256]{2,1,0:T(8,128)S(1)}, u32[]{:S(2)}, u32[]{:S(2)}) collective-permute-start(f32[1,72,256]{2,1,0:T(8,128)S(1)} %fusion.41), channel_id=1, source_target_pairs={{0,1},{1,0},{2,3},{3,2},{4,5},{5,4},{6,7},{7,6},{8,9},{9,8},{10,11... | collective-permute-start | bytes 221192 | tf_op jit(solution)/shard_map/ppermute | solution.py:154
  22.3 1.6 collective-permute-start.3
  24.9 8.8 %collective-permute-start.4 = (f32[72,256]{1,0:T(8,128)S(1)}, f32[72,256]{1,0:T(8,128)S(1)}, u32[]{:S(2)}, u32[]{:S(2)}) collective-permute-start(f32[72,256]{1,0:T(8,128)S(1)} %get-tuple-element.124), channel_id=1, source_target_pairs={{0,8},{4,12},{8,16},{12,20},{16,24},{20,28},{24,0},{28,4},{1,9},{5... | collective-permute-start | bytes 221192 | tf_op jit(solution)/shard_map/ppermute | solution.py:180
  30.1 5.0 %collective-permute-start.6 = (f32[72,256]{1,0:T(8,128)S(1)}, f32[72,256]{1,0:T(8,128)S(1)}, u32[]{:S(2)}, u32[]{:S(2)}) collective-permute-start(f32[72,256]{1,0:T(8,128)S(1)} %get-tuple-element.125), channel_id=1, source_target_pairs={{0,24},{4,28},{8,0},{12,4},{16,8},{20,12},{24,16},{28,20},{1,25},{... | collective-permute-start | bytes 221192 | tf_op jit(solution)/shard_map/ppermute | solution.py:180
  30.8 7.5 %collective-permute-start.5 = (f32[72,256]{1,0:T(8,128)S(1)}, f32[72,256]{1,0:T(8,128)S(1)}, u32[]{:S(2)}, u32[]{:S(2)}) collective-permute-start(f32[72,256]{1,0:T(8,128)S(1)} %get-tuple-element.126), channel_id=1, source_target_pairs={{0,16},{4,20},{8,24},{12,28},{16,0},{20,4},{24,8},{28,12},{1,17},{... | collective-permute-start | bytes 221192 | tf_op jit(solution)/shard_map/ppermute | solution.py:180
  38.6 5.8 %collective-permute-start.9 = (f32[1,72,256]{2,1,0:T(8,128)S(1)}, f32[1,72,256]{2,1,0:T(8,128)S(1)}, u32[]{:S(2)}, u32[]{:S(2)}) collective-permute-start(f32[1,72,256]{2,1,0:T(8,128)S(1)} %fusion.40), channel_id=1, source_target_pairs={{0,3},{1,2},{2,1},{3,0},{4,7},{5,6},{6,5},{7,4},{8,11},{9,10},{10,... | collective-permute-start | bytes 221192 | tf_op jit(solution)/shard_map/ppermute | solution.py:154
  40.2 5.1 %collective-permute-start.8 = (f32[1,72,256]{2,1,0:T(8,128)S(1)}, f32[1,72,256]{2,1,0:T(8,128)S(1)}, u32[]{:S(2)}, u32[]{:S(2)}) collective-permute-start(f32[1,72,256]{2,1,0:T(8,128)S(1)} %fusion.40), channel_id=1, source_target_pairs={{0,2},{1,3},{2,0},{3,1},{4,6},{5,7},{6,4},{7,5},{8,10},{9,11},{10,... | collective-permute-start | bytes 221192 | tf_op jit(solution)/shard_map/ppermute | solution.py:154
  41.6 4.4 %collective-permute-start.7 = (f32[1,72,256]{2,1,0:T(8,128)S(1)}, f32[1,72,256]{2,1,0:T(8,128)S(1)}, u32[]{:S(2)}, u32[]{:S(2)}) collective-permute-start(f32[1,72,256]{2,1,0:T(8,128)S(1)} %fusion.40), channel_id=1, source_target_pairs={{0,1},{1,0},{2,3},{3,2},{4,5},{5,4},{6,7},{7,6},{8,9},{9,8},{10,11... | collective-permute-start | bytes 221192 | tf_op jit(solution)/shard_map/ppermute | solution.py:154
  55.2 1.6 collective-permute-start.10
  57.9 6.9 %collective-permute-start.11 = (f32[72,256]{1,0:T(8,128)S(1)}, f32[72,256]{1,0:T(8,128)S(1)}, u32[]{:S(2)}, u32[]{:S(2)}) collective-permute-start(f32[72,256]{1,0:T(8,128)S(1)} %get-tuple-element.121), channel_id=1, source_target_pairs={{0,8},{4,12},{8,16},{12,20},{16,24},{20,28},{24,0},{28,4},{1,9},{5... | collective-permute-start | bytes 221192 | tf_op jit(solution)/shard_map/ppermute | solution.py:180
  60.3 5.6 %collective-permute-start.13 = (f32[72,256]{1,0:T(8,128)S(1)}, f32[72,256]{1,0:T(8,128)S(1)}, u32[]{:S(2)}, u32[]{:S(2)}) collective-permute-start(f32[72,256]{1,0:T(8,128)S(1)} %get-tuple-element.122), channel_id=1, source_target_pairs={{0,24},{4,28},{8,0},{12,4},{16,8},{20,12},{24,16},{28,20},{1,25},{... | collective-permute-start | bytes 221192 | tf_op jit(solution)/shard_map/ppermute | solution.py:180
  61.9 7.5 %collective-permute-start.12 = (f32[72,256]{1,0:T(8,128)S(1)}, f32[72,256]{1,0:T(8,128)S(1)}, u32[]{:S(2)}, u32[]{:S(2)}) collective-permute-start(f32[72,256]{1,0:T(8,128)S(1)} %get-tuple-element.123), channel_id=1, source_target_pairs={{0,16},{4,20},{8,24},{12,28},{16,0},{20,4},{24,8},{28,12},{1,17},{... | collective-permute-start | bytes 221192 | tf_op jit(solution)/shard_map/ppermute | solution.py:180
  69.6 5.7 %collective-permute-start.16 = (f32[1,72,256]{2,1,0:T(8,128)S(1)}, f32[1,72,256]{2,1,0:T(8,128)S(1)}, u32[]{:S(2)}, u32[]{:S(2)}) collective-permute-start(f32[1,72,256]{2,1,0:T(8,128)S(1)} %fusion.39), channel_id=1, source_target_pairs={{0,3},{1,2},{2,1},{3,0},{4,7},{5,6},{6,5},{7,4},{8,11},{9,10},{10,... | collective-permute-start | bytes 221192 | tf_op jit(solution)/shard_map/ppermute | solution.py:154
  71.6 4.4 %collective-permute-start.15 = (f32[1,72,256]{2,1,0:T(8,128)S(1)}, f32[1,72,256]{2,1,0:T(8,128)S(1)}, u32[]{:S(2)}, u32[]{:S(2)}) collective-permute-start(f32[1,72,256]{2,1,0:T(8,128)S(1)} %fusion.39), channel_id=1, source_target_pairs={{0,2},{1,3},{2,0},{3,1},{4,6},{5,7},{6,4},{7,5},{8,10},{9,11},{10,... | collective-permute-start | bytes 221192 | tf_op jit(solution)/shard_map/ppermute | solution.py:154
  72.2 4.5 %collective-permute-start.14 = (f32[1,72,256]{2,1,0:T(8,128)S(1)}, f32[1,72,256]{2,1,0:T(8,128)S(1)}, u32[]{:S(2)}, u32[]{:S(2)}) collective-permute-start(f32[1,72,256]{2,1,0:T(8,128)S(1)} %fusion.39), channel_id=1, source_target_pairs={{0,1},{1,0},{2,3},{3,2},{4,5},{5,4},{6,7},{7,6},{8,9},{9,8},{10,11... | collective-permute-start | bytes 221192 | tf_op jit(solution)/shard_map/ppermute | solution.py:154
  85.5 5.4 %collective-permute-start.19 = (f32[1,2440]{1,0:T(1,128)S(1)}, f32[1,2440]{1,0:T(1,128)S(1)}, u32[]{:S(2)}, u32[]{:S(2)}) collective-permute-start(f32[1,2440]{1,0:T(1,128)S(1)} %broadcast_in_dim.21), channel_id=1, source_target_pairs={{0,3},{1,2},{2,1},{3,0},{4,7},{5,6},{6,5},{7,4},{8,11},{9,10},{10,... | collective-permute-start | bytes 29288 | tf_op jit(solution)/shard_map/ppermute | solution.py:237
  88.3 3.7 %collective-permute-start.18 = (f32[1,2440]{1,0:T(1,128)S(1)}, f32[1,2440]{1,0:T(1,128)S(1)}, u32[]{:S(2)}, u32[]{:S(2)}) collective-permute-start(f32[1,2440]{1,0:T(1,128)S(1)} %broadcast_in_dim.21), channel_id=1, source_target_pairs={{0,2},{1,3},{2,0},{3,1},{4,6},{5,7},{6,4},{7,5},{8,10},{9,11},{10,... | collective-permute-start | bytes 29288 | tf_op jit(solution)/shard_map/ppermute | solution.py:237
  89.5 3.7 %collective-permute-start.17 = (f32[1,2440]{1,0:T(1,128)S(1)}, f32[1,2440]{1,0:T(1,128)S(1)}, u32[]{:S(2)}, u32[]{:S(2)}) collective-permute-start(f32[1,2440]{1,0:T(1,128)S(1)} %broadcast_in_dim.21), channel_id=1, source_target_pairs={{0,1},{1,0},{2,3},{3,2},{4,5},{5,4},{6,7},{7,6},{8,9},{9,8},{10,11... | collective-permute-start | bytes 29288 | tf_op jit(solution)/shard_map/ppermute | solution.py:237
  94.6 5.4 %collective-permute-start.23 = (f32[8,2440]{1,0:T(8,128)S(1)}, f32[8,2440]{1,0:T(8,128)S(1)}, u32[]{:S(2)}, u32[]{:S(2)}) collective-permute-start(f32[8,2440]{1,0:T(8,128)S(1)} %concatenate.66), channel_id=1, source_target_pairs={{0,24},{4,28},{8,0},{12,4},{16,8},{20,12},{24,16},{28,20},{1,25},{... | collective-permute-start | bytes 234248 | tf_op jit(solution)/shard_map/ppermute | solution.py:249
  95.4 8.6 %collective-permute-start.22 = (f32[8,2440]{1,0:T(8,128)S(1)}, f32[8,2440]{1,0:T(8,128)S(1)}, u32[]{:S(2)}, u32[]{:S(2)}) collective-permute-start(f32[8,2440]{1,0:T(8,128)S(1)} %concatenate.66), channel_id=1, source_target_pairs={{0,16},{4,20},{8,24},{12,28},{16,0},{20,4},{24,8},{28,12},{1,17},{... | collective-permute-start | bytes 234248 | tf_op jit(solution)/shard_map/ppermute | solution.py:249
  95.9 8.1 %collective-permute-start.21 = (f32[8,2440]{1,0:T(8,128)S(1)}, f32[8,2440]{1,0:T(8,128)S(1)}, u32[]{:S(2)}, u32[]{:S(2)}) collective-permute-start(f32[8,2440]{1,0:T(8,128)S(1)} %concatenate.66), channel_id=1, source_target_pairs={{0,8},{4,12},{8,16},{12,20},{16,24},{20,28},{24,0},{28,4},{1,9},{5... | collective-permute-start | bytes 234248 | tf_op jit(solution)/shard_map/ppermute | solution.py:249
  125.3 6.3 %collective-permute-start.27 = (f32[72,256]{1,0:T(8,128)S(1)}, f32[72,256]{1,0:T(8,128)S(1)}, u32[]{:S(2)}, u32[]{:S(2)}) collective-permute-start(f32[72,256]{1,0:T(8,128)S(1)} %get-tuple-element.118), channel_id=1, source_target_pairs={{0,24},{4,28},{8,0},{12,4},{16,8},{20,12},{24,16},{28,20},{1,25},{... | collective-permute-start | bytes 221192 | tf_op jit(solution)/shard_map/ppermute | solution.py:180
  128.9 8.0 %collective-permute-start.26 = (f32[72,256]{1,0:T(8,128)S(1)}, f32[72,256]{1,0:T(8,128)S(1)}, u32[]{:S(2)}, u32[]{:S(2)}) collective-permute-start(f32[72,256]{1,0:T(8,128)S(1)} %get-tuple-element.119), channel_id=1, source_target_pairs={{0,16},{4,20},{8,24},{12,28},{16,0},{20,4},{24,8},{28,12},{1,17},{... | collective-permute-start | bytes 221192 | tf_op jit(solution)/shard_map/ppermute | solution.py:180
  129.8 7.1 %collective-permute-start.25 = (f32[72,256]{1,0:T(8,128)S(1)}, f32[72,256]{1,0:T(8,128)S(1)}, u32[]{:S(2)}, u32[]{:S(2)}) collective-permute-start(f32[72,256]{1,0:T(8,128)S(1)} %get-tuple-element.120), channel_id=1, source_target_pairs={{0,8},{4,12},{8,16},{12,20},{16,24},{20,28},{24,0},{28,4},{1,9},{5... | collective-permute-start | bytes 221192 | tf_op jit(solution)/shard_map/ppermute | solution.py:180
  137.1 5.9 %collective-permute-start.30 = (f32[1,72,256]{2,1,0:T(8,128)S(1)}, f32[1,72,256]{2,1,0:T(8,128)S(1)}, u32[]{:S(2)}, u32[]{:S(2)}) collective-permute-start(f32[1,72,256]{2,1,0:T(8,128)S(1)} %fusion.38), channel_id=1, source_target_pairs={{0,3},{1,2},{2,1},{3,0},{4,7},{5,6},{6,5},{7,4},{8,11},{9,10},{10,... | collective-permute-start | bytes 221192 | tf_op jit(solution)/shard_map/ppermute | solution.py:154
  138.0 5.5 %collective-permute-start.29 = (f32[1,72,256]{2,1,0:T(8,128)S(1)}, f32[1,72,256]{2,1,0:T(8,128)S(1)}, u32[]{:S(2)}, u32[]{:S(2)}) collective-permute-start(f32[1,72,256]{2,1,0:T(8,128)S(1)} %fusion.38), channel_id=1, source_target_pairs={{0,2},{1,3},{2,0},{3,1},{4,6},{5,7},{6,4},{7,5},{8,10},{9,11},{10,... | collective-permute-start | bytes 221192 | tf_op jit(solution)/shard_map/ppermute | solution.py:154
  139.6 4.5 %collective-permute-start.28 = (f32[1,72,256]{2,1,0:T(8,128)S(1)}, f32[1,72,256]{2,1,0:T(8,128)S(1)}, u32[]{:S(2)}, u32[]{:S(2)}) collective-permute-start(f32[1,72,256]{2,1,0:T(8,128)S(1)} %fusion.38), channel_id=1, source_target_pairs={{0,1},{1,0},{2,3},{3,2},{4,5},{5,4},{6,7},{7,6},{8,9},{9,8},{10,11... | collective-permute-start | bytes 221192 | tf_op jit(solution)/shard_map/ppermute | solution.py:154
  156.1 6.8 %collective-permute-start.32 = (f32[72,256]{1,0:T(8,128)S(1)}, f32[72,256]{1,0:T(8,128)S(1)}, u32[]{:S(2)}, u32[]{:S(2)}) collective-permute-start(f32[72,256]{1,0:T(8,128)S(1)} %get-tuple-element.114), channel_id=1, source_target_pairs={{0,8},{4,12},{8,16},{12,20},{16,24},{20,28},{24,0},{28,4},{1,9},{5... | collective-permute-start | bytes 221192 | tf_op jit(solution)/shard_map/ppermute | solution.py:180
  159.5 4.8 %collective-permute-start.34 = (f32[72,256]{1,0:T(8,128)S(1)}, f32[72,256]{1,0:T(8,128)S(1)}, u32[]{:S(2)}, u32[]{:S(2)}) collective-permute-start(f32[72,256]{1,0:T(8,128)S(1)} %get-tuple-element.115), channel_id=1, source_target_pairs={{0,24},{4,28},{8,0},{12,4},{16,8},{20,12},{24,16},{28,20},{1,25},{... | collective-permute-start | bytes 221192 | tf_op jit(solution)/shard_map/ppermute | solution.py:180
  160.0 7.1 %collective-permute-start.33 = (f32[72,256]{1,0:T(8,128)S(1)}, f32[72,256]{1,0:T(8,128)S(1)}, u32[]{:S(2)}, u32[]{:S(2)}) collective-permute-start(f32[72,256]{1,0:T(8,128)S(1)} %get-tuple-element.116), channel_id=1, source_target_pairs={{0,16},{4,20},{8,24},{12,28},{16,0},{20,4},{24,8},{28,12},{1,17},{... | collective-permute-start | bytes 221192 | tf_op jit(solution)/shard_map/ppermute | solution.py:180
  (9 other events, 27.2 us)

commit v5 on v4

--- a/solution.py
+++ b/solution.py
@@ -13,14 +13,21 @@
 
 
 def tile_kernel(
-    mode, blocks_piece, vectors, rows_ref, cols_ref, live_ref, nb_ref, x_ref, t_ref, o_ref
+    mode, blocks_piece, vectors, rows_ref, cols_ref, live_ref, nb_ref, x_ref, t_ref, *refs
 ):
     step = pl.program_id(0)
     if mode == "image":
+        lost_ref, o_ref = refs
+        body_rows = blocks_piece * vectors
 
         @pl.when(step == 0)
         def _():
-            o_ref[...] = jnp.zeros_like(o_ref)
+            o_ref[:, :body_rows, :] = jnp.zeros((o_ref.shape[0], body_rows, o_ref.shape[2]), o_ref.dtype)
+            o_ref[:, body_rows:, :] = jnp.broadcast_to(
+                lost_ref[...][None], (o_ref.shape[0],) + lost_ref.shape
+            )
+    else:
+        (o_ref,) = refs
 
     @pl.when(step < nb_ref[0])
     def _():
@@ -46,7 +53,7 @@
             o_ref[...] = jnp.zeros_like(o_ref)
 
 
-def tile_pass(mode, x_cols, tiles, rows, cols, live, block_count, row_blocks, vectors):
+def tile_pass(mode, x_cols, tiles, rows, cols, live, block_count, row_blocks, vectors, lost=None):
     groups, padded_rows, side = x_cols.shape
     blocks_piece = padded_rows // vectors
     owners = row_blocks // blocks_piece
@@ -62,13 +69,20 @@
     else:
         out_shape = jax.ShapeDtypeStruct((slots, vectors, 128), jnp.float32)
         out_spec = pl.BlockSpec((group_size, vectors, 128), lambda i, *_: (i, 0, 0))
+    in_specs = [
+        pl.BlockSpec((groups, padded_rows, side), lambda i, *_: (0, 0, 0)),
+        pl.BlockSpec((None, None, group_size, side, side), tile_index),
+    ]
+    operands = [x_cols, tiles]
+    if mode == "image":
+        pad = padded_rows - blocks_piece * vectors
+        lost_block = jnp.zeros((pad, side), jnp.float32).at[0, :vectors].set(lost)
+        in_specs.append(pl.BlockSpec((pad, side), lambda i, *_: (0, 0)))
+        operands.append(lost_block)
     grid_spec = pltpu.PrefetchScalarGridSpec(
         num_scalar_prefetch=4,
         grid=(steps,),
-        in_specs=[
-            pl.BlockSpec((groups, padded_rows, side), lambda i, *_: (0, 0, 0)),
-            pl.BlockSpec((None, None, group_size, side, side), tile_index),
-        ],
+        in_specs=in_specs,
         out_specs=out_spec,
     )
     return pl.pallas_call(
@@ -76,7 +90,7 @@
         grid_spec=grid_spec,
         out_shape=out_shape,
         compiler_params=pltpu.CompilerParams(dimension_semantics=("arbitrary",)),
-    )(rows, cols, live, block_count, x_cols, tiles)
+    )(rows, cols, live, block_count, *operands)
 
 
 def per_device(
@@ -147,6 +161,15 @@
         extra = extra.at[..., 0, :vectors].set(jnp.broadcast_to(lost, lead + (vectors,)))
         return jnp.concatenate([body, extra], axis=-2)
 
+    row_owner = own_rows // blocks_piece
+    if src_count % 2 == 0:
+        half = src_count // 2
+        chip = src_index // 2
+        position = ((row_owner % 2) ^ (src_index % 2)) * half + (row_owner // 2 - chip) % half
+    else:
+        position = (row_owner - src_index) % src_count
+    kernel_rows = position * blocks_piece + own_rows % blocks_piece
+
     def spread_columns(blocks, lost):
         payload = with_lost_row(blocks.reshape(payload_rows, tile_side), lost)[None]
         if exchange:
@@ -160,29 +183,20 @@
         lost_dst = jnp.sum(payload[:, payload_rows, :vectors], axis=0)
         return payload, lost_dst
 
-    def reduce_rows(accumulated, lost):
+    def reduce_rows(chunks):
         n = src_count
-        chunks = accumulated.at[:, payload_rows, :vectors].set(
-            jnp.broadcast_to(lost, (n, vectors))
-        )
         if n % 2 == 0:
             half = n // 2
-            paired = chunks.reshape(half, 2, *chunks.shape[1:])
-            core = src_index % 2
-            keep = lax.dynamic_index_in_dim(paired, core, 1, keepdims=False)
-            give = lax.dynamic_index_in_dim(paired, 1 - core, 1, keepdims=False)
-            part = keep + lax.ppermute(give, "src", [(i, i ^ 1) for i in range(n)])
-            chip = src_index // 2
-            total = lax.dynamic_index_in_dim(part, chip, 0, keepdims=False)
+            part = chunks[:half] + lax.ppermute(chunks[half:], "src", [(i, i ^ 1) for i in range(n)])
+            total = part[0]
             for shift in range(1, half):
-                send = lax.dynamic_index_in_dim(part, (chip + shift) % half, 0, keepdims=False)
                 pairs = [(i, ((i // 2 + shift) % half) * 2 + i % 2) for i in range(n)]
-                total = total + lax.ppermute(send, "src", pairs)
+                total = total + lax.ppermute(part[shift], "src", pairs)
         else:
-            total = lax.dynamic_index_in_dim(chunks, src_index, 0, keepdims=False)
+            total = chunks[0]
             for shift in range(1, n):
-                send = lax.dynamic_index_in_dim(chunks, (src_index + shift) % n, 0, keepdims=False)
-                total = total + lax.ppermute(send, "src", [(i, (i + shift) % n) for i in range(n)])
+                pairs = [(i, (i + shift) % n) for i in range(n)]
+                total = total + lax.ppermute(chunks[shift], "src", pairs)
         image = total[:payload_rows].reshape(blocks_piece, vectors, tile_side)
         return image, total[payload_rows, :vectors]
 
@@ -195,10 +209,10 @@
         else:
             lost_dst = jnp.zeros((vectors,), jnp.float32)
         accumulated = tile_pass(
-            "image", gathered, tiles, own_rows, kernel_cols, live_mask, block_count,
-            row_blocks, vectors,
-        )
-        image, lost_total = reduce_rows(accumulated, lost_dst)
+            "image", gathered, tiles, kernel_rows, kernel_cols, live_mask, block_count,
+            row_blocks, vectors, lost_dst,
+        )
+        image, lost_total = reduce_rows(accumulated)
         if lost_sum is None:
             lost_sum = lost_total
         return (

time: 168 us -> 167 us (level)
  local copies, waits for them, and re-layouts: 21 us -> 14.9 us
  starting transfers between devices: 44.2 us -> 47.7 us
    ppermute x16, starting transfers between devices: 21.1 us -> 25.6 us  [the longest x12 25.3 us: reduce_rows(): total = total + lax.ppermute(part[shift], 'src', pairs)]
    scatter x4, local copies, waits for them, and re-layouts: 6.04 us -> 2.03 us  [the longest x3 2.03 us: tile_pass(): lost_block = jnp.zeros((pad, side), jnp.float32).at[0, :vectors].set(lost)]
    squeeze x8 -> x4, local copies, waits for them, and re-layouts: 4.06 us -> 0.07 us  [the longest x3 0.05 us: reduce_rows(): total = total + lax.ppermute(part[shift], 'src', pairs)]
    slice x0 -> x4, local copies, waits for them, and re-layouts: none -> 3.92 us  [reduce_rows(): chunks[half:]]
    unnamed x12 -> x16, local copies, waits for them, and re-layouts: 2.06 us -> 0.05 us
  transfers between devices with their start and end apart: 35 -> 35, of which waited for: 29 -> 26; matrix products, arithmetic and copies ran while one was open for 6% -> 5% of each run, Pallas kernels for 0% -> 0%
where the time goes in v5:
time: 167 us; the launch traced here: 166 us
  waiting for transfers between devices  50.6 us (30%)
  starting transfers between devices  47.7 us (29%)
  Pallas kernels  30.3 us (18%)
  local copies, waits for them, and re-layouts  14.9 us (9%)
  other arithmetic  12.6 us (8%)
  matrix products  7.86 us (5%)
  between operations  1.78 us (1%)
    pallas_call x5, Pallas kernels, tile_pass(): pl.pallas_call(functools.partial(tile_kernel, mode, blocks_piece, vectors...  30.3 us
    ppermute x12, starting transfers between devices, reduce_rows(): total = total + lax.ppermute(part[shift], 'src', pairs)  25.3 us
    ppermute x12, waiting for transfers between devices, reduce_rows(): total = total + lax.ppermute(part[shift], 'src', pairs)  24.1 us
    ppermute x12, starting transfers between devices, spread_columns(): lax.ppermute(payload, 'dst', [(i, i ^ v) for i in range(dst_count)])  15.4 us
    ppermute x12, waiting for transfers between devices, spread_columns(): lax.ppermute(payload, 'dst', [(i, i ^ v) for i in range(dst_count)])  9.36 us
    ppermute x3, waiting for transfers between devices, per_device(): pieces.append(lax.ppermute(shared, 'src', pairs))  7.49 us
    ppermute x4, waiting for transfers between devices, reduce_rows(): lax.ppermute(chunks[half:], 'src', [(i, i ^ 1) for i in range(n)])  4.83 us
    ppermute x3, starting transfers between devices, per_device(): lax.ppermute(shared, 'dst', [(i, i ^ v) for i in range(dst_count)])  4.02 us
  transfers between devices with their start and end apart: 35, of which 26 were waited for; matrix products, arithmetic and copies ran while one was open for 5% of the time, Pallas kernels for 0%

profile of v5, /device:TPU:0, one launch (start us, length us, event | category | flops | bytes accessed | tf_op | source)
XLA Modules:
  0.0 165.9 jit_solution(537274427551797582)
XLA Ops:
  2.6 4.0 %collective-permute-start.2 = (f32[1,72,256]{2,1,0:T(8,128)S(1)}, f32[1,72,256]{2,1,0:T(8,128)S(1)}, u32[]{:S(2)}, u32[]{:S(2)}) collective-permute-start(f32[1,72,256]{2,1,0:T(8,128)S(1)} %fusion.49), channel_id=1, source_target_pairs={{0,3},{1,2},{2,1},{3,0},{4,7},{5,6},{6,5},{7,4},{8,11},{9,10},{10,... | collective-permute-start | bytes 221192 | tf_op jit(solution)/shard_map/ppermute | solution.py:177
  8.6 1.6 gather_fusion
  12.7 6.0 %shard_map.95 = f32[8,72,256]{2,1,0:T(8,128)} custom-call(s32[128]{0:T(128)} %get-tuple-element.130.rows_ref, s32[128]{0:T(128)} %get-tuple-element.131.cols_ref, s32[128]{0:T(128)} %and_convert_fusion.live_ref, s32[1]{0:T(128)} %bitcast.5.nb_ref, f32[4,72,256]{2,1,0:T(8,128)} %copy-done.3, bf16[1,1,128,256,256]{4,3,2,1,0:T(8,128)(2,1)} %t_ref.9, ...), custom_call_target="tpu_custom_call" | custom-call | tf_op jit(solution)/shard_map/pallas_call | solution.py:88
  22.4 2.0 %collective-permute-start.4 = (f32[72,256]{1,0:T(8,128)S(1)}, f32[72,256]{1,0:T(8,128)S(1)}, u32[]{:S(2)}, u32[]{:S(2)}) collective-permute-start(f32[72,256]{1,0:T(8,128)S(1)} %get-tuple-element.120), channel_id=1, source_target_pairs={{0,8},{4,12},{8,16},{12,20},{16,24},{20,28},{24,0},{28,4},{1,9},{5... | collective-permute-start | bytes 221192 | tf_op jit(solution)/shard_map/ppermute | solution.py:194
  24.5 5.2 %collective-permute-start.6 = (f32[72,256]{1,0:T(8,128)S(1)}, f32[72,256]{1,0:T(8,128)S(1)}, u32[]{:S(2)}, u32[]{:S(2)}) collective-permute-start(f32[72,256]{1,0:T(8,128)S(1)} %get-tuple-element.121), channel_id=1, source_target_pairs={{0,24},{4,28},{8,0},{12,4},{16,8},{20,12},{24,16},{28,20},{1,25},{... | collective-permute-start | bytes 221192 | tf_op jit(solution)/shard_map/ppermute | solution.py:194
  30.3 2.0 %collective-permute-done.4 = f32[72,256]{1,0:T(8,128)S(1)} collective-permute-done((f32[72,256]{1,0:T(8,128)S(1)}, f32[72,256]{1,0:T(8,128)S(1)}, u32[]{:S(2)}, u32[]{:S(2)}) %collective-permute-start.4) | collective-permute-done | bytes 73760 | tf_op jit(solution)/shard_map/ppermute | solution.py:194
  32.4 4.6 %collective-permute-done.5 = f32[72,256]{1,0:T(8,128)S(1)} collective-permute-done((f32[72,256]{1,0:T(8,128)S(1)}, f32[72,256]{1,0:T(8,128)S(1)}, u32[]{:S(2)}, u32[]{:S(2)}) %collective-permute-start.5) | collective-permute-done | bytes 73760 | tf_op jit(solution)/shard_map/ppermute | solution.py:194
  37.7 1.6 collective-permute-start.8
  40.7 2.4 %collective-permute-done.9 = f32[1,72,256]{2,1,0:T(8,128)S(1)} collective-permute-done((f32[1,72,256]{2,1,0:T(8,128)S(1)}, f32[1,72,256]{2,1,0:T(8,128)S(1)}, u32[]{:S(2)}, u32[]{:S(2)}) %collective-permute-start.9) | collective-permute-done | bytes 73760 | tf_op jit(solution)/shard_map/ppermute | solution.py:177
  44.4 6.0 %shard_map.96 = f32[8,72,256]{2,1,0:T(8,128)} custom-call(s32[128]{0:T(128)} %get-tuple-element.130.rows_ref, s32[128]{0:T(128)} %get-tuple-element.131.cols_ref, s32[128]{0:T(128)} %and_convert_fusion.live_ref, s32[1]{0:T(128)} %bitcast.5.nb_ref, f32[4,72,256]{2,1,0:T(8,128)} %copy-done.4, bf16[1,1,128,256,256]{4,3,2,1,0:T(8,128)(2,1)} %t_ref.9, ...), custom_call_target="tpu_custom_call" | custom-call | tf_op jit(solution)/shard_map/pallas_call | solution.py:88
  54.2 5.1 %collective-permute-start.13 = (f32[72,256]{1,0:T(8,128)S(1)}, f32[72,256]{1,0:T(8,128)S(1)}, u32[]{:S(2)}, u32[]{:S(2)}) collective-permute-start(f32[72,256]{1,0:T(8,128)S(1)} %get-tuple-element.118), channel_id=1, source_target_pairs={{0,24},{4,28},{8,0},{12,4},{16,8},{20,12},{24,16},{28,20},{1,25},{... | collective-permute-start | bytes 221192 | tf_op jit(solution)/shard_map/ppermute | solution.py:194
  62.0 4.6 %collective-permute-done.12 = f32[72,256]{1,0:T(8,128)S(1)} collective-permute-done((f32[72,256]{1,0:T(8,128)S(1)}, f32[72,256]{1,0:T(8,128)S(1)}, u32[]{:S(2)}, u32[]{:S(2)}) %collective-permute-start.12) | collective-permute-done | bytes 73760 | tf_op jit(solution)/shard_map/ppermute | solution.py:194
  68.0 2.5 %collective-permute-start.15 = (f32[1,72,256]{2,1,0:T(8,128)S(1)}, f32[1,72,256]{2,1,0:T(8,128)S(1)}, u32[]{:S(2)}, u32[]{:S(2)}) collective-permute-start(f32[1,72,256]{2,1,0:T(8,128)S(1)} %maximum_bitcast_fusion), channel_id=1, source_target_pairs={{0,2},{1,3},{2,0},{3,1},{4,6},{5,7},{6,4},{7,5},{8,10},{9,11},{10,... | collective-permute-start | bytes 221192 | tf_op jit(solution)/shard_map/ppermute | solution.py:177
  73.3 1.6 collective-permute-done.14
  75.7 6.3 %shard_map.97 = f32[128,16,128]{2,1,0:T(8,128)} custom-call(s32[128]{0:T(128)} %clamp_bitcast_fusion.rows_ref, s32[128]{0:T(128)} %get-tuple-element.131.cols_ref, s32[128]{0:T(128)} %and_convert_fusion.live_ref, s32[1]{0:T(128)} %bitcast.5.nb_ref, f32[4,72,256]{2,1,0:T(8,128)} %pad_maximum_fusion.2.x_ref, bf16[1,1,128,256,256]{4,3,2,1,0:T(8,128)(2,1)} %t_ref.9), custom_call_target="tpu_custom_call" | custom-call | tf_op jit(solution)/shard_map/pallas_call | solution.py:88
  82.0 1.6 reduce_sum.112
  84.0 3.7 %collective-permute-start.18 = (f32[1,2440]{1,0:T(1,128)S(1)}, f32[1,2440]{1,0:T(1,128)S(1)}, u32[]{:S(2)}, u32[]{:S(2)}) collective-permute-start(f32[1,2440]{1,0:T(1,128)S(1)} %broadcast_in_dim.21), channel_id=1, source_target_pairs={{0,2},{1,3},{2,0},{3,1},{4,6},{5,7},{6,4},{7,5},{8,10},{9,11},{10,... | collective-permute-start | bytes 29288 | tf_op jit(solution)/shard_map/ppermute | solution.py:251
  89.4 2.0 %collective-permute-done.17 = f32[1,2440]{1,0:T(1,128)S(1)} collective-permute-done((f32[1,2440]{1,0:T(1,128)S(1)}, f32[1,2440]{1,0:T(1,128)S(1)}, u32[]{:S(2)}, u32[]{:S(2)}) %collective-permute-start.17) | collective-permute-done | bytes 9792 | tf_op jit(solution)/shard_map/ppermute | solution.py:251
  92.9 2.0 %collective-permute-start.23 = (f32[8,2440]{1,0:T(8,128)S(1)}, f32[8,2440]{1,0:T(8,128)S(1)}, u32[]{:S(2)}, u32[]{:S(2)}) collective-permute-start(f32[8,2440]{1,0:T(8,128)S(1)} %concatenate.64), channel_id=1, source_target_pairs={{0,24},{4,28},{8,0},{12,4},{16,8},{20,12},{24,16},{28,20},{1,25},{... | collective-permute-start | bytes 234248 | tf_op jit(solution)/shard_map/ppermute | solution.py:263
  95.5 2.2 %collective-permute-done.23 = f32[8,2440]{1,0:T(8,128)S(1)} collective-permute-done((f32[8,2440]{1,0:T(8,128)S(1)}, f32[8,2440]{1,0:T(8,128)S(1)}, u32[]{:S(2)}, u32[]{:S(2)}) %collective-permute-start.23) | collective-permute-done | bytes 78112 | tf_op jit(solution)/shard_map/ppermute | solution.py:263
  97.7 5.3 %collective-permute-done.22 = f32[8,2440]{1,0:T(8,128)S(1)} collective-permute-done((f32[8,2440]{1,0:T(8,128)S(1)}, f32[8,2440]{1,0:T(8,128)S(1)}, u32[]{:S(2)}, u32[]{:S(2)}) %collective-permute-start.22) | collective-permute-done | bytes 78112 | tf_op jit(solution)/shard_map/ppermute | solution.py:263
  105.3 2.4 %multiply_reduce_fusion.3 = (f32[16]{0:T(128)S(1)}, f32[16,64]{1,0:T(8,128)S(1)}) fusion(f32[16,64]{1,0:T(8,128)S(1)} %get-tuple-element.124, f32[16,64]{1,0:T(8,128)S(1)} %fusion.32, f32[16,64]{1,0:T(8,128)S(1)} %fusion.34, f32[16]{0:T(128)S(1)} %broadcast_multiply_fusion.2, f32[4096,16]{1,0:T(8,128)S(1)} %reshape.490, f32[64]{0:T(128)S(1)} %iota_convert_fusion, ...), kind=kOutput, calls=%fused_computation.111 | convolution fusion | flops 50601968 | bytes 295296 | tf_op jit(solution)/shard_map/tk,ta->ka/dot_general | solution.py:286
  109.1 2.5 %multiply_reduce_fusion.2 = (f32[16]{0:T(128)S(1)}, f32[16,64]{1,0:T(8,128)S(1)}, f32[16,64]{1,0:T(8,128)S(1)}) fusion(f32[16,64]{1,0:T(8,128)S(1)} %get-tuple-element.124, f32[16,64]{1,0:T(8,128)S(1)} %fusion.32, f32[16,64]{1,0:T(8,128)S(1)} %fusion.34, f32[16]{0:T(128)S(1)} %broadcast_multiply_fusion.1, f32[4096,16]{1,0:T(8,128)S(1)} %convolution_multiply_fusion, ...), kind=kOutput, calls=%fused_computation.110 | convolution fusion | flops 50601968 | bytes 299392 | tf_op jit(solution)/shard_map/tk,ta->ka/dot_general | solution.py:298
  113.2 5.9 %shard_map.98 = f32[8,72,256]{2,1,0:T(8,128)} custom-call(s32[128]{0:T(128)} %get-tuple-element.130.rows_ref, s32[128]{0:T(128)} %get-tuple-element.131.cols_ref, s32[128]{0:T(128)} %and_convert_fusion.live_ref, s32[1]{0:T(128)} %bitcast.5.nb_ref, f32[4,72,256]{2,1,0:T(8,128)} %concatenate.66.x_ref, bf16[1,1,128,256,256]{4,3,2,1,0:T(8,128)(2,1)} %t_ref.9, ...), custom_call_target="tpu_custom_call" | custom-call | tf_op jit(solution)/shard_map/pallas_call | solution.py:88
  122.8 4.8 %collective-permute-start.27 = (f32[72,256]{1,0:T(8,128)S(1)}, f32[72,256]{1,0:T(8,128)S(1)}, u32[]{:S(2)}, u32[]{:S(2)}) collective-permute-start(f32[72,256]{1,0:T(8,128)S(1)} %get-tuple-element.114), channel_id=1, source_target_pairs={{0,24},{4,28},{8,0},{12,4},{16,8},{20,12},{24,16},{28,20},{1,25},{... | collective-permute-start | bytes 221192 | tf_op jit(solution)/shard_map/ppermute | solution.py:194
  128.7 1.6 collective-permute-done.27
  130.3 5.0 %collective-permute-done.26 = f32[72,256]{1,0:T(8,128)S(1)} collective-permute-done((f32[72,256]{1,0:T(8,128)S(1)}, f32[72,256]{1,0:T(8,128)S(1)}, u32[]{:S(2)}, u32[]{:S(2)}) %collective-permute-start.26) | collective-permute-done | bytes 73760 | tf_op jit(solution)/shard_map/ppermute | solution.py:194
  136.0 2.1 %collective-permute-start.29 = (f32[1,72,256]{2,1,0:T(8,128)S(1)}, f32[1,72,256]{2,1,0:T(8,128)S(1)}, u32[]{:S(2)}, u32[]{:S(2)}) collective-permute-start(f32[1,72,256]{2,1,0:T(8,128)S(1)} %fusion.41), channel_id=1, source_target_pairs={{0,2},{1,3},{2,0},{3,1},{4,6},{5,7},{6,4},{7,5},{8,10},{9,11},{10,... | collective-permute-start | bytes 221192 | tf_op jit(solution)/shard_map/ppermute | solution.py:177
  139.0 2.3 %collective-permute-done.30 = f32[1,72,256]{2,1,0:T(8,128)S(1)} collective-permute-done((f32[1,72,256]{2,1,0:T(8,128)S(1)}, f32[1,72,256]{2,1,0:T(8,128)S(1)}, u32[]{:S(2)}, u32[]{:S(2)}) %collective-permute-start.30) | collective-permute-done | bytes 73760 | tf_op jit(solution)/shard_map/ppermute | solution.py:177
  143.2 6.0 %shard_map.99 = f32[8,72,256]{2,1,0:T(8,128)} custom-call(s32[128]{0:T(128)} %get-tuple-element.130.rows_ref, s32[128]{0:T(128)} %get-tuple-element.131.cols_ref, s32[128]{0:T(128)} %and_convert_fusion.live_ref, s32[1]{0:T(128)} %bitcast.5.nb_ref, f32[4,72,256]{2,1,0:T(8,128)} %copy-done.2, bf16[1,1,128,256,256]{4,3,2,1,0:T(8,128)(2,1)} %t_ref.9, ...), custom_call_target="tpu_custom_call" | custom-call | tf_op jit(solution)/shard_map/pallas_call | solution.py:88
  153.0 4.8 %collective-permute-start.34 = (f32[72,256]{1,0:T(8,128)S(1)}, f32[72,256]{1,0:T(8,128)S(1)}, u32[]{:S(2)}, u32[]{:S(2)}) collective-permute-start(f32[72,256]{1,0:T(8,128)S(1)} %get-tuple-element.111), channel_id=1, source_target_pairs={{0,24},{4,28},{8,0},{12,4},{16,8},{20,12},{24,16},{28,20},{1,25},{... | collective-permute-start | bytes 221192 | tf_op jit(solution)/shard_map/ppermute | solution.py:194
  161.5 3.5 %collective-permute-done.33 = f32[72,256]{1,0:T(8,128)S(1)} collective-permute-done((f32[72,256]{1,0:T(8,128)S(1)}, f32[72,256]{1,0:T(8,128)S(1)}, u32[]{:S(2)}, u32[]{:S(2)}) %collective-permute-start.33) | collective-permute-done | bytes 73760 | tf_op jit(solution)/shard_map/ppermute | solution.py:194
  (164 shorter events, 50.7 us)
Async XLA Ops:
  2.6 9.3 %collective-permute-start.2 = (f32[1,72,256]{2,1,0:T(8,128)S(1)}, f32[1,72,256]{2,1,0:T(8,128)S(1)}, u32[]{:S(2)}, u32[]{:S(2)}) collective-permute-start(f32[1,72,256]{2,1,0:T(8,128)S(1)} %fusion.49), channel_id=1, source_target_pairs={{0,3},{1,2},{2,1},{3,0},{4,7},{5,6},{6,5},{7,4},{8,11},{9,10},{10,... | collective-permute-start | bytes 221192 | tf_op jit(solution)/shard_map/ppermute | solution.py:177
  6.6 5.4 %collective-permute-start.1 = (f32[1,72,256]{2,1,0:T(8,128)S(1)}, f32[1,72,256]{2,1,0:T(8,128)S(1)}, u32[]{:S(2)}, u32[]{:S(2)}) collective-permute-start(f32[1,72,256]{2,1,0:T(8,128)S(1)} %fusion.49), channel_id=1, source_target_pairs={{0,2},{1,3},{2,0},{3,1},{4,6},{5,7},{6,4},{7,5},{8,10},{9,11},{10,... | collective-permute-start | bytes 221192 | tf_op jit(solution)/shard_map/ppermute | solution.py:177
  7.1 4.9 %collective-permute-start = (f32[1,72,256]{2,1,0:T(8,128)S(1)}, f32[1,72,256]{2,1,0:T(8,128)S(1)}, u32[]{:S(2)}, u32[]{:S(2)}) collective-permute-start(f32[1,72,256]{2,1,0:T(8,128)S(1)} %fusion.49), channel_id=1, source_target_pairs={{0,1},{1,0},{2,3},{3,2},{4,5},{5,4},{6,7},{7,6},{8,9},{9,8},{10,11... | collective-permute-start | bytes 221192 | tf_op jit(solution)/shard_map/ppermute | solution.py:177
  19.7 1.6 collective-permute-start.3
  22.4 9.9 %collective-permute-start.4 = (f32[72,256]{1,0:T(8,128)S(1)}, f32[72,256]{1,0:T(8,128)S(1)}, u32[]{:S(2)}, u32[]{:S(2)}) collective-permute-start(f32[72,256]{1,0:T(8,128)S(1)} %get-tuple-element.120), channel_id=1, source_target_pairs={{0,8},{4,12},{8,16},{12,20},{16,24},{20,28},{24,0},{28,4},{1,9},{5... | collective-permute-start | bytes 221192 | tf_op jit(solution)/shard_map/ppermute | solution.py:194
  24.5 7.9 %collective-permute-start.6 = (f32[72,256]{1,0:T(8,128)S(1)}, f32[72,256]{1,0:T(8,128)S(1)}, u32[]{:S(2)}, u32[]{:S(2)}) collective-permute-start(f32[72,256]{1,0:T(8,128)S(1)} %get-tuple-element.121), channel_id=1, source_target_pairs={{0,24},{4,28},{8,0},{12,4},{16,8},{20,12},{24,16},{28,20},{1,25},{... | collective-permute-start | bytes 221192 | tf_op jit(solution)/shard_map/ppermute | solution.py:194
  29.7 7.2 %collective-permute-start.5 = (f32[72,256]{1,0:T(8,128)S(1)}, f32[72,256]{1,0:T(8,128)S(1)}, u32[]{:S(2)}, u32[]{:S(2)}) collective-permute-start(f32[72,256]{1,0:T(8,128)S(1)} %get-tuple-element.122), channel_id=1, source_target_pairs={{0,16},{4,20},{8,24},{12,28},{16,0},{20,4},{24,8},{28,12},{1,17},{... | collective-permute-start | bytes 221192 | tf_op jit(solution)/shard_map/ppermute | solution.py:194
  37.2 6.0 %collective-permute-start.9 = (f32[1,72,256]{2,1,0:T(8,128)S(1)}, f32[1,72,256]{2,1,0:T(8,128)S(1)}, u32[]{:S(2)}, u32[]{:S(2)}) collective-permute-start(f32[1,72,256]{2,1,0:T(8,128)S(1)} %fusion.45), channel_id=1, source_target_pairs={{0,3},{1,2},{2,1},{3,0},{4,7},{5,6},{6,5},{7,4},{8,11},{9,10},{10,... | collective-permute-start | bytes 221192 | tf_op jit(solution)/shard_map/ppermute | solution.py:177
  37.7 5.4 %collective-permute-start.8 = (f32[1,72,256]{2,1,0:T(8,128)S(1)}, f32[1,72,256]{2,1,0:T(8,128)S(1)}, u32[]{:S(2)}, u32[]{:S(2)}) collective-permute-start(f32[1,72,256]{2,1,0:T(8,128)S(1)} %fusion.45), channel_id=1, source_target_pairs={{0,2},{1,3},{2,0},{3,1},{4,6},{5,7},{6,4},{7,5},{8,10},{9,11},{10,... | collective-permute-start | bytes 221192 | tf_op jit(solution)/shard_map/ppermute | solution.py:177
  39.3 4.4 %collective-permute-start.7 = (f32[1,72,256]{2,1,0:T(8,128)S(1)}, f32[1,72,256]{2,1,0:T(8,128)S(1)}, u32[]{:S(2)}, u32[]{:S(2)}) collective-permute-start(f32[1,72,256]{2,1,0:T(8,128)S(1)} %fusion.45), channel_id=1, source_target_pairs={{0,1},{1,0},{2,3},{3,2},{4,5},{5,4},{6,7},{7,6},{8,9},{9,8},{10,11... | collective-permute-start | bytes 221192 | tf_op jit(solution)/shard_map/ppermute | solution.py:177
  51.5 1.6 collective-permute-start.10
  54.1 7.9 %collective-permute-start.11 = (f32[72,256]{1,0:T(8,128)S(1)}, f32[72,256]{1,0:T(8,128)S(1)}, u32[]{:S(2)}, u32[]{:S(2)}) collective-permute-start(f32[72,256]{1,0:T(8,128)S(1)} %get-tuple-element.117), channel_id=1, source_target_pairs={{0,8},{4,12},{8,16},{12,20},{16,24},{20,28},{24,0},{28,4},{1,9},{5... | collective-permute-start | bytes 221192 | tf_op jit(solution)/shard_map/ppermute | solution.py:194
  54.2 7.8 %collective-permute-start.13 = (f32[72,256]{1,0:T(8,128)S(1)}, f32[72,256]{1,0:T(8,128)S(1)}, u32[]{:S(2)}, u32[]{:S(2)}) collective-permute-start(f32[72,256]{1,0:T(8,128)S(1)} %get-tuple-element.118), channel_id=1, source_target_pairs={{0,24},{4,28},{8,0},{12,4},{16,8},{20,12},{24,16},{28,20},{1,25},{... | collective-permute-start | bytes 221192 | tf_op jit(solution)/shard_map/ppermute | solution.py:194
  59.4 7.3 %collective-permute-start.12 = (f32[72,256]{1,0:T(8,128)S(1)}, f32[72,256]{1,0:T(8,128)S(1)}, u32[]{:S(2)}, u32[]{:S(2)}) collective-permute-start(f32[72,256]{1,0:T(8,128)S(1)} %get-tuple-element.119), channel_id=1, source_target_pairs={{0,16},{4,20},{8,24},{12,28},{16,0},{20,4},{24,8},{28,12},{1,17},{... | collective-permute-start | bytes 221192 | tf_op jit(solution)/shard_map/ppermute | solution.py:194
  66.9 6.0 %collective-permute-start.16 = (f32[1,72,256]{2,1,0:T(8,128)S(1)}, f32[1,72,256]{2,1,0:T(8,128)S(1)}, u32[]{:S(2)}, u32[]{:S(2)}) collective-permute-start(f32[1,72,256]{2,1,0:T(8,128)S(1)} %maximum_bitcast_fusion), channel_id=1, source_target_pairs={{0,3},{1,2},{2,1},{3,0},{4,7},{5,6},{6,5},{7,4},{8,11},{9,10},{10,... | collective-permute-start | bytes 221192 | tf_op jit(solution)/shard_map/ppermute | solution.py:177
  68.0 5.3 %collective-permute-start.15 = (f32[1,72,256]{2,1,0:T(8,128)S(1)}, f32[1,72,256]{2,1,0:T(8,128)S(1)}, u32[]{:S(2)}, u32[]{:S(2)}) collective-permute-start(f32[1,72,256]{2,1,0:T(8,128)S(1)} %maximum_bitcast_fusion), channel_id=1, source_target_pairs={{0,2},{1,3},{2,0},{3,1},{4,6},{5,7},{6,4},{7,5},{8,10},{9,11},{10,... | collective-permute-start | bytes 221192 | tf_op jit(solution)/shard_map/ppermute | solution.py:177
  70.6 4.4 %collective-permute-start.14 = (f32[1,72,256]{2,1,0:T(8,128)S(1)}, f32[1,72,256]{2,1,0:T(8,128)S(1)}, u32[]{:S(2)}, u32[]{:S(2)}) collective-permute-start(f32[1,72,256]{2,1,0:T(8,128)S(1)} %maximum_bitcast_fusion), channel_id=1, source_target_pairs={{0,1},{1,0},{2,3},{3,2},{4,5},{5,4},{6,7},{7,6},{8,9},{9,8},{10,11... | collective-permute-start | bytes 221192 | tf_op jit(solution)/shard_map/ppermute | solution.py:177
  83.7 4.6 %collective-permute-start.19 = (f32[1,2440]{1,0:T(1,128)S(1)}, f32[1,2440]{1,0:T(1,128)S(1)}, u32[]{:S(2)}, u32[]{:S(2)}) collective-permute-start(f32[1,2440]{1,0:T(1,128)S(1)} %broadcast_in_dim.21), channel_id=1, source_target_pairs={{0,3},{1,2},{2,1},{3,0},{4,7},{5,6},{6,5},{7,4},{8,11},{9,10},{10,... | collective-permute-start | bytes 29288 | tf_op jit(solution)/shard_map/ppermute | solution.py:251
  84.0 5.4 %collective-permute-start.18 = (f32[1,2440]{1,0:T(1,128)S(1)}, f32[1,2440]{1,0:T(1,128)S(1)}, u32[]{:S(2)}, u32[]{:S(2)}) collective-permute-start(f32[1,2440]{1,0:T(1,128)S(1)} %broadcast_in_dim.21), channel_id=1, source_target_pairs={{0,2},{1,3},{2,0},{3,1},{4,6},{5,7},{6,4},{7,5},{8,10},{9,11},{10,... | collective-permute-start | bytes 29288 | tf_op jit(solution)/shard_map/ppermute | solution.py:251
  87.8 3.7 %collective-permute-start.17 = (f32[1,2440]{1,0:T(1,128)S(1)}, f32[1,2440]{1,0:T(1,128)S(1)}, u32[]{:S(2)}, u32[]{:S(2)}) collective-permute-start(f32[1,2440]{1,0:T(1,128)S(1)} %broadcast_in_dim.21), channel_id=1, source_target_pairs={{0,1},{1,0},{2,3},{3,2},{4,5},{5,4},{6,7},{7,6},{8,9},{9,8},{10,11... | collective-permute-start | bytes 29288 | tf_op jit(solution)/shard_map/ppermute | solution.py:251
  92.9 4.9 %collective-permute-start.23 = (f32[8,2440]{1,0:T(8,128)S(1)}, f32[8,2440]{1,0:T(8,128)S(1)}, u32[]{:S(2)}, u32[]{:S(2)}) collective-permute-start(f32[8,2440]{1,0:T(8,128)S(1)} %concatenate.64), channel_id=1, source_target_pairs={{0,24},{4,28},{8,0},{12,4},{16,8},{20,12},{24,16},{28,20},{1,25},{... | collective-permute-start | bytes 234248 | tf_op jit(solution)/shard_map/ppermute | solution.py:263
  94.9 8.1 %collective-permute-start.22 = (f32[8,2440]{1,0:T(8,128)S(1)}, f32[8,2440]{1,0:T(8,128)S(1)}, u32[]{:S(2)}, u32[]{:S(2)}) collective-permute-start(f32[8,2440]{1,0:T(8,128)S(1)} %concatenate.64), channel_id=1, source_target_pairs={{0,16},{4,20},{8,24},{12,28},{16,0},{20,4},{24,8},{28,12},{1,17},{... | collective-permute-start | bytes 234248 | tf_op jit(solution)/shard_map/ppermute | solution.py:263
  94.9 8.1 %collective-permute-start.21 = (f32[8,2440]{1,0:T(8,128)S(1)}, f32[8,2440]{1,0:T(8,128)S(1)}, u32[]{:S(2)}, u32[]{:S(2)}) collective-permute-start(f32[8,2440]{1,0:T(8,128)S(1)} %concatenate.64), channel_id=1, source_target_pairs={{0,8},{4,12},{8,16},{12,20},{16,24},{20,28},{24,0},{28,4},{1,9},{5... | collective-permute-start | bytes 234248 | tf_op jit(solution)/shard_map/ppermute | solution.py:263
  122.8 7.5 %collective-permute-start.27 = (f32[72,256]{1,0:T(8,128)S(1)}, f32[72,256]{1,0:T(8,128)S(1)}, u32[]{:S(2)}, u32[]{:S(2)}) collective-permute-start(f32[72,256]{1,0:T(8,128)S(1)} %get-tuple-element.114), channel_id=1, source_target_pairs={{0,24},{4,28},{8,0},{12,4},{16,8},{20,12},{24,16},{28,20},{1,25},{... | collective-permute-start | bytes 221192 | tf_op jit(solution)/shard_map/ppermute | solution.py:194
  127.6 7.6 %collective-permute-start.26 = (f32[72,256]{1,0:T(8,128)S(1)}, f32[72,256]{1,0:T(8,128)S(1)}, u32[]{:S(2)}, u32[]{:S(2)}) collective-permute-start(f32[72,256]{1,0:T(8,128)S(1)} %get-tuple-element.115), channel_id=1, source_target_pairs={{0,16},{4,20},{8,24},{12,28},{16,0},{20,4},{24,8},{28,12},{1,17},{... | collective-permute-start | bytes 221192 | tf_op jit(solution)/shard_map/ppermute | solution.py:194
  127.6 7.6 %collective-permute-start.25 = (f32[72,256]{1,0:T(8,128)S(1)}, f32[72,256]{1,0:T(8,128)S(1)}, u32[]{:S(2)}, u32[]{:S(2)}) collective-permute-start(f32[72,256]{1,0:T(8,128)S(1)} %get-tuple-element.116), channel_id=1, source_target_pairs={{0,8},{4,12},{8,16},{12,20},{16,24},{20,28},{24,0},{28,4},{1,9},{5... | collective-permute-start | bytes 221192 | tf_op jit(solution)/shard_map/ppermute | solution.py:194
  135.5 5.8 %collective-permute-start.30 = (f32[1,72,256]{2,1,0:T(8,128)S(1)}, f32[1,72,256]{2,1,0:T(8,128)S(1)}, u32[]{:S(2)}, u32[]{:S(2)}) collective-permute-start(f32[1,72,256]{2,1,0:T(8,128)S(1)} %fusion.41), channel_id=1, source_target_pairs={{0,3},{1,2},{2,1},{3,0},{4,7},{5,6},{6,5},{7,4},{8,11},{9,10},{10,... | collective-permute-start | bytes 221192 | tf_op jit(solution)/shard_map/ppermute | solution.py:177
  136.0 5.3 %collective-permute-start.29 = (f32[1,72,256]{2,1,0:T(8,128)S(1)}, f32[1,72,256]{2,1,0:T(8,128)S(1)}, u32[]{:S(2)}, u32[]{:S(2)}) collective-permute-start(f32[1,72,256]{2,1,0:T(8,128)S(1)} %fusion.41), channel_id=1, source_target_pairs={{0,2},{1,3},{2,0},{3,1},{4,6},{5,7},{6,4},{7,5},{8,10},{9,11},{10,... | collective-permute-start | bytes 221192 | tf_op jit(solution)/shard_map/ppermute | solution.py:177
  138.1 4.4 %collective-permute-start.28 = (f32[1,72,256]{2,1,0:T(8,128)S(1)}, f32[1,72,256]{2,1,0:T(8,128)S(1)}, u32[]{:S(2)}, u32[]{:S(2)}) collective-permute-start(f32[1,72,256]{2,1,0:T(8,128)S(1)} %fusion.41), channel_id=1, source_target_pairs={{0,1},{1,0},{2,3},{3,2},{4,5},{5,4},{6,7},{7,6},{8,9},{9,8},{10,11... | collective-permute-start | bytes 221192 | tf_op jit(solution)/shard_map/ppermute | solution.py:177
  152.9 7.5 %collective-permute-start.32 = (f32[72,256]{1,0:T(8,128)S(1)}, f32[72,256]{1,0:T(8,128)S(1)}, u32[]{:S(2)}, u32[]{:S(2)}) collective-permute-start(f32[72,256]{1,0:T(8,128)S(1)} %get-tuple-element.110), channel_id=1, source_target_pairs={{0,8},{4,12},{8,16},{12,20},{16,24},{20,28},{24,0},{28,4},{1,9},{5... | collective-permute-start | bytes 221192 | tf_op jit(solution)/shard_map/ppermute | solution.py:194
  153.0 8.5 %collective-permute-start.34 = (f32[72,256]{1,0:T(8,128)S(1)}, f32[72,256]{1,0:T(8,128)S(1)}, u32[]{:S(2)}, u32[]{:S(2)}) collective-permute-start(f32[72,256]{1,0:T(8,128)S(1)} %get-tuple-element.111), channel_id=1, source_target_pairs={{0,24},{4,28},{8,0},{12,4},{16,8},{20,12},{24,16},{28,20},{1,25},{... | collective-permute-start | bytes 221192 | tf_op jit(solution)/shard_map/ppermute | solution.py:194
  157.7 7.2 %collective-permute-start.33 = (f32[72,256]{1,0:T(8,128)S(1)}, f32[72,256]{1,0:T(8,128)S(1)}, u32[]{:S(2)}, u32[]{:S(2)}) collective-permute-start(f32[72,256]{1,0:T(8,128)S(1)} %get-tuple-element.112), channel_id=1, source_target_pairs={{0,16},{4,20},{8,24},{12,28},{16,0},{20,4},{24,8},{28,12},{1,17},{... | collective-permute-start | bytes 221192 | tf_op jit(solution)/shard_map/ppermute | solution.py:194
  (11 other events, 62.5 us)

commit v6 on v5

--- a/solution.py
+++ b/solution.py
@@ -91,6 +91,25 @@
         out_shape=out_shape,
         compiler_params=pltpu.CompilerParams(dimension_semantics=("arbitrary",)),
     )(rows, cols, live, block_count, *operands)
+
+
+def split_three(value):
+    high = lax.reduce_precision(value, exponent_bits=8, mantissa_bits=7)
+    rest = value - high
+    middle = lax.reduce_precision(rest, exponent_bits=8, mantissa_bits=7)
+    low = lax.reduce_precision(rest - middle, exponent_bits=8, mantissa_bits=7)
+    return jnp.stack([high, middle, low]).astype(jnp.bfloat16)
+
+
+def select_dot(spec, value, one_hot):
+    parts = jnp.einsum(
+        "p" + spec.split(",")[0] + "," + spec.split(",")[1].split("->")[0] + "->p"
+        + spec.split("->")[1],
+        split_three(value),
+        one_hot,
+        preferred_element_type=jnp.float32,
+    )
+    return jnp.sum(parts, axis=0)
 
 
 def per_device(
@@ -269,10 +288,10 @@
         offsets.append(offsets[-1] + size)
     every = [shared[:, offsets[i]:offsets[i + 1]] for i in range(len(sizes))]
     all_entries = every[0].reshape(-1, vectors)
-    all_row_hot = (every[1].reshape(-1)[:, None] == agg_range[None, :].astype(jnp.float32))
-    all_col_hot = (every[2].reshape(-1)[:, None] == agg_range[None, :].astype(jnp.float32))
-    all_row_hot = all_row_hot.astype(jnp.float32)
-    all_col_hot = all_col_hot.astype(jnp.float32)
+    all_row_hot = every[1].reshape(-1)[:, None] == agg_range[None, :].astype(jnp.float32)
+    all_col_hot = every[2].reshape(-1)[:, None] == agg_range[None, :].astype(jnp.float32)
+    all_row_hot = all_row_hot.astype(jnp.bfloat16)
+    all_col_hot = all_col_hot.astype(jnp.bfloat16)
     all_block_sums = every[3].reshape(-1, vectors)
     all_tele_sums = every[4].reshape(-1, vectors)
     all_block_hot = (every[5].reshape(-1)[:, None] == agg_range[None, :].astype(jnp.float32))
@@ -283,7 +302,7 @@
         "bk,ba->ka", all_block_sums * all_dangling[:, None], all_block_hot, precision=highest
     )
     weight = jnp.einsum("bk,ba->ka", all_tele_sums, all_block_hot, precision=highest)
-    inflow_one = jnp.einsum("tk,ta->ka", all_entries, all_row_hot, precision=highest)
+    inflow_one = select_dot("tk,ta->ka", all_entries, all_row_hot)
 
     def coarse_sweep(inflow, ratios):
         carried = jnp.sum(lost_mass * ratios, axis=1)
@@ -294,10 +313,8 @@
 
     level_one = coarse_sweep(inflow_one, jnp.ones((vectors, agg_count), jnp.float32))
     ratios_one = level_one / totals
-    ratio_at_tile = jnp.einsum("ka,ta->tk", ratios_one, all_col_hot, precision=highest)
-    inflow_two = jnp.einsum(
-        "tk,ta->ka", all_entries * ratio_at_tile, all_row_hot, precision=highest
-    )
+    ratio_at_tile = select_dot("ka,ta->tk", ratios_one, all_col_hot)
+    inflow_two = select_dot("tk,ta->ka", all_entries * ratio_at_tile, all_row_hot)
     level_two = coarse_sweep(inflow_two, ratios_one)
     ratios_two = level_two / totals
     groups = gathered.shape[0]

time: 167 us -> 155 us (0.928)
  waiting for transfers between devices: 50.6 us -> 45.5 us
  matrix products: 7.86 us -> 3 us
    ppermute x12, starting transfers between devices: 25.3 us -> 13.2 us  [reduce_rows(): total = total + lax.ppermute(part[shift], 'src', pairs)]
    ppermute x4, starting transfers between devices: 0.28 us -> 9.29 us  [reduce_rows(): lax.ppermute(chunks[half:], 'src', [(i, i ^ 1) for i in range(n)])]
    dot_general x3, matrix products: 6.21 us -> 1.24 us  [select_dot(): jnp.einsum('p' + spec.split(',')[0] + ',' + spec.split(',')[1].split('->'...]
    ppermute x3, waiting for transfers between devices: 7.49 us -> 4.89 us  [per_device(): pieces.append(lax.ppermute(shared, 'src', pairs))]
    ppermute x3, starting transfers between devices: 2.66 us -> 5.07 us  [per_device(): pieces.append(lax.ppermute(shared, 'src', pairs))]
  transfers between devices with their start and end apart: 35 -> 35, of which waited for: 26 -> 26; matrix products, arithmetic and copies ran while one was open for 5% -> 6% of each run, Pallas kernels for 0% -> 0%
where the time goes in v6:
time: 155 us
  starting transfers between devices  46.4 us (30%)
  waiting for transfers between devices  45.5 us (29%)
  Pallas kernels  30.3 us (20%)
  local copies, waits for them, and re-layouts  15.5 us (10%)
  other arithmetic  12.9 us (8%)
  matrix products  3 us (2%)
  between operations  1.77 us (1%)
    pallas_call x5, Pallas kernels, tile_pass(): pl.pallas_call(functools.partial(tile_kernel, mode, blocks_piece, vectors...  30.3 us
    ppermute x12, waiting for transfers between devices, reduce_rows(): total = total + lax.ppermute(part[shift], 'src', pairs)  24.6 us
    ppermute x12, starting transfers between devices, spread_columns(): lax.ppermute(payload, 'dst', [(i, i ^ v) for i in range(dst_count)])  15.3 us
    ppermute x12, starting transfers between devices, reduce_rows(): total = total + lax.ppermute(part[shift], 'src', pairs)  13.2 us
    ppermute x4, starting transfers between devices, reduce_rows(): lax.ppermute(chunks[half:], 'src', [(i, i ^ 1) for i in range(n)])  9.29 us
    ppermute x12, waiting for transfers between devices, spread_columns(): lax.ppermute(payload, 'dst', [(i, i ^ v) for i in range(dst_count)])  7.81 us
    ppermute x3, starting transfers between devices, per_device(): pieces.append(lax.ppermute(shared, 'src', pairs))  5.07 us
    ppermute x3, waiting for transfers between devices, per_device(): pieces.append(lax.ppermute(shared, 'src', pairs))  4.89 us
  transfers between devices with their start and end apart: 35, of which 26 were waited for; matrix products, arithmetic and copies ran while one was open for 6% of the time, Pallas kernels for 0%

profile of v6, /device:TPU:0, one launch (start us, length us, event | category | flops | bytes accessed | tf_op | source)
XLA Modules:
  0.0 155.4 jit_solution(3241202040128422713)
XLA Ops:
  2.6 4.0 %collective-permute-start.2 = (f32[1,72,256]{2,1,0:T(8,128)S(1)}, f32[1,72,256]{2,1,0:T(8,128)S(1)}, u32[]{:S(2)}, u32[]{:S(2)}) collective-permute-start(f32[1,72,256]{2,1,0:T(8,128)S(1)} %fusion.43), channel_id=1, source_target_pairs={{0,3},{1,2},{2,1},{3,0},{4,7},{5,6},{6,5},{7,4},{8,11},{9,10},{10,... | collective-permute-start | bytes 221192 | tf_op jit(solution)/shard_map/ppermute | solution.py:196
  12.8 6.0 %shard_map.95 = f32[8,72,256]{2,1,0:T(8,128)} custom-call(s32[128]{0:T(128)} %get-tuple-element.139.rows_ref, s32[128]{0:T(128)} %get-tuple-element.140.cols_ref, s32[128]{0:T(128)} %and_convert_fusion.live_ref, s32[1]{0:T(128)} %bitcast.5.nb_ref, f32[4,72,256]{2,1,0:T(8,128)} %copy-done.3, bf16[1,1,128,256,256]{4,3,2,1,0:T(8,128)(2,1)} %t_ref.9, ...), custom_call_target="tpu_custom_call" | custom-call | tf_op jit(solution)/shard_map/pallas_call | solution.py:88
  19.8 2.5 %collective-permute-start.3 = (f32[4,72,256]{2,1,0:T(8,128)S(1)}, f32[4,72,256]{2,1,0:T(8,128)S(1)}, u32[]{:S(2)}, u32[]{:S(2)}) collective-permute-start(f32[4,72,256]{2,1,0:T(8,128)S(1)} %slice.302), channel_id=1, source_target_pairs={{0,4},{4,0},{8,12},{12,8},{16,20},{20,16},{24,28},{28,24},{1,5},{5... | collective-permute-start | bytes 884744 | tf_op jit(solution)/shard_map/ppermute | solution.py:209
  24.5 3.8 %collective-permute-start.6 = (f32[72,256]{1,0:T(8,128)S(1)}, f32[72,256]{1,0:T(8,128)S(1)}, u32[]{:S(2)}, u32[]{:S(2)}) collective-permute-start(f32[72,256]{1,0:T(8,128)S(1)} %get-tuple-element.126), channel_id=1, source_target_pairs={{0,24},{4,28},{8,0},{12,4},{16,8},{20,12},{24,16},{28,20},{1,25},{... | collective-permute-start | bytes 221192 | tf_op jit(solution)/shard_map/ppermute | solution.py:213
  30.9 4.9 %collective-permute-done.5 = f32[72,256]{1,0:T(8,128)S(1)} collective-permute-done((f32[72,256]{1,0:T(8,128)S(1)}, f32[72,256]{1,0:T(8,128)S(1)}, u32[]{:S(2)}, u32[]{:S(2)}) %collective-permute-start.5) | collective-permute-done | bytes 73760 | tf_op jit(solution)/shard_map/ppermute | solution.py:213
  36.1 1.7 %collective-permute-start.9 = (f32[1,72,256]{2,1,0:T(8,128)S(1)}, f32[1,72,256]{2,1,0:T(8,128)S(1)}, u32[]{:S(2)}, u32[]{:S(2)}) collective-permute-start(f32[1,72,256]{2,1,0:T(8,128)S(1)} %fusion.39), channel_id=1, source_target_pairs={{0,3},{1,2},{2,1},{3,0},{4,7},{5,6},{6,5},{7,4},{8,11},{9,10},{10,... | collective-permute-start | bytes 221192 | tf_op jit(solution)/shard_map/ppermute | solution.py:196
  37.7 1.9 %collective-permute-start.7 = (f32[1,72,256]{2,1,0:T(8,128)S(1)}, f32[1,72,256]{2,1,0:T(8,128)S(1)}, u32[]{:S(2)}, u32[]{:S(2)}) collective-permute-start(f32[1,72,256]{2,1,0:T(8,128)S(1)} %fusion.39), channel_id=1, source_target_pairs={{0,1},{1,0},{2,3},{3,2},{4,5},{5,4},{6,7},{7,6},{8,9},{9,8},{10,11... | collective-permute-start | bytes 221192 | tf_op jit(solution)/shard_map/ppermute | solution.py:196
  39.6 2.3 %collective-permute-done.9 = f32[1,72,256]{2,1,0:T(8,128)S(1)} collective-permute-done((f32[1,72,256]{2,1,0:T(8,128)S(1)}, f32[1,72,256]{2,1,0:T(8,128)S(1)}, u32[]{:S(2)}, u32[]{:S(2)}) %collective-permute-start.9) | collective-permute-done | bytes 73760 | tf_op jit(solution)/shard_map/ppermute | solution.py:196
  43.6 5.9 %shard_map.96 = f32[8,72,256]{2,1,0:T(8,128)} custom-call(s32[128]{0:T(128)} %get-tuple-element.139.rows_ref, s32[128]{0:T(128)} %get-tuple-element.140.cols_ref, s32[128]{0:T(128)} %and_convert_fusion.live_ref, s32[1]{0:T(128)} %bitcast.5.nb_ref, f32[4,72,256]{2,1,0:T(8,128)} %copy-done.4, bf16[1,1,128,256,256]{4,3,2,1,0:T(8,128)(2,1)} %t_ref.9, ...), custom_call_target="tpu_custom_call" | custom-call | tf_op jit(solution)/shard_map/pallas_call | solution.py:88
  50.5 2.8 %collective-permute-start.10 = (f32[4,72,256]{2,1,0:T(8,128)S(1)}, f32[4,72,256]{2,1,0:T(8,128)S(1)}, u32[]{:S(2)}, u32[]{:S(2)}) collective-permute-start(f32[4,72,256]{2,1,0:T(8,128)S(1)} %slice.311), channel_id=1, source_target_pairs={{0,4},{4,0},{8,12},{12,8},{16,20},{20,16},{24,28},{28,24},{1,5},{5... | collective-permute-start | bytes 884744 | tf_op jit(solution)/shard_map/ppermute | solution.py:209
  55.7 2.0 %collective-permute-start.11 = (f32[72,256]{1,0:T(8,128)S(1)}, f32[72,256]{1,0:T(8,128)S(1)}, u32[]{:S(2)}, u32[]{:S(2)}) collective-permute-start(f32[72,256]{1,0:T(8,128)S(1)} %get-tuple-element.122), channel_id=1, source_target_pairs={{0,8},{4,12},{8,16},{12,20},{16,24},{20,28},{24,0},{28,4},{1,9},{5... | collective-permute-start | bytes 221192 | tf_op jit(solution)/shard_map/ppermute | solution.py:213
  58.9 2.4 %collective-permute-done.13 = f32[72,256]{1,0:T(8,128)S(1)} collective-permute-done((f32[72,256]{1,0:T(8,128)S(1)}, f32[72,256]{1,0:T(8,128)S(1)}, u32[]{:S(2)}, u32[]{:S(2)}) %collective-permute-start.13) | collective-permute-done | bytes 73760 | tf_op jit(solution)/shard_map/ppermute | solution.py:213
  61.3 3.0 %collective-permute-done.12 = f32[72,256]{1,0:T(8,128)S(1)} collective-permute-done((f32[72,256]{1,0:T(8,128)S(1)}, f32[72,256]{1,0:T(8,128)S(1)}, u32[]{:S(2)}, u32[]{:S(2)}) %collective-permute-start.12) | collective-permute-done | bytes 73760 | tf_op jit(solution)/shard_map/ppermute | solution.py:213
  65.7 2.4 %collective-permute-start.14 = (f32[1,72,256]{2,1,0:T(8,128)S(1)}, f32[1,72,256]{2,1,0:T(8,128)S(1)}, u32[]{:S(2)}, u32[]{:S(2)}) collective-permute-start(f32[1,72,256]{2,1,0:T(8,128)S(1)} %maximum_bitcast_fusion), channel_id=1, source_target_pairs={{0,1},{1,0},{2,3},{3,2},{4,5},{5,4},{6,7},{7,6},{8,9},{9,8},{10,11... | collective-permute-start | bytes 221192 | tf_op jit(solution)/shard_map/ppermute | solution.py:196
  71.3 6.5 %shard_map.97 = f32[128,16,128]{2,1,0:T(8,128)} custom-call(s32[128]{0:T(128)} %clamp_bitcast_fusion.rows_ref, s32[128]{0:T(128)} %get-tuple-element.140.cols_ref, s32[128]{0:T(128)} %and_convert_fusion.live_ref, s32[1]{0:T(128)} %bitcast.5.nb_ref, f32[4,72,256]{2,1,0:T(8,128)} %pad_maximum_fusion.2.x_ref, bf16[1,1,128,256,256]{4,3,2,1,0:T(8,128)(2,1)} %t_ref.9), custom_call_target="tpu_custom_call" | custom-call | tf_op jit(solution)/shard_map/pallas_call | solution.py:88
  79.6 2.0 %collective-permute-start.17 = (f32[1,2440]{1,0:T(1,128)S(1)}, f32[1,2440]{1,0:T(1,128)S(1)}, u32[]{:S(2)}, u32[]{:S(2)}) collective-permute-start(f32[1,2440]{1,0:T(1,128)S(1)} %broadcast_in_dim.21), channel_id=1, source_target_pairs={{0,1},{1,0},{2,3},{3,2},{4,5},{5,4},{6,7},{7,6},{8,9},{9,8},{10,11... | collective-permute-start | bytes 29288 | tf_op jit(solution)/shard_map/ppermute | solution.py:270
  83.3 1.9 %collective-permute-done.18 = f32[1,2440]{1,0:T(1,128)S(1)} collective-permute-done((f32[1,2440]{1,0:T(1,128)S(1)}, f32[1,2440]{1,0:T(1,128)S(1)}, u32[]{:S(2)}, u32[]{:S(2)}) %collective-permute-start.18) | collective-permute-done | bytes 9792 | tf_op jit(solution)/shard_map/ppermute | solution.py:270
  87.8 2.0 %collective-permute-start.22 = (f32[8,2440]{1,0:T(8,128)S(1)}, f32[8,2440]{1,0:T(8,128)S(1)}, u32[]{:S(2)}, u32[]{:S(2)}) collective-permute-start(f32[8,2440]{1,0:T(8,128)S(1)} %concatenate.64), channel_id=1, source_target_pairs={{0,16},{4,20},{8,24},{12,28},{16,0},{20,4},{24,8},{28,12},{1,17},{... | collective-permute-start | bytes 234248 | tf_op jit(solution)/shard_map/ppermute | solution.py:282
  89.8 2.8 %collective-permute-start.23 = (f32[8,2440]{1,0:T(8,128)S(1)}, f32[8,2440]{1,0:T(8,128)S(1)}, u32[]{:S(2)}, u32[]{:S(2)}) collective-permute-start(f32[8,2440]{1,0:T(8,128)S(1)} %concatenate.64), channel_id=1, source_target_pairs={{0,24},{4,28},{8,0},{12,4},{16,8},{20,12},{24,16},{28,20},{1,25},{... | collective-permute-start | bytes 234248 | tf_op jit(solution)/shard_map/ppermute | solution.py:282
  92.7 2.2 %collective-permute-done.21 = f32[8,2440]{1,0:T(8,128)S(1)} collective-permute-done((f32[8,2440]{1,0:T(8,128)S(1)}, f32[8,2440]{1,0:T(8,128)S(1)}, u32[]{:S(2)}, u32[]{:S(2)}) %collective-permute-start.21) | collective-permute-done | bytes 78112 | tf_op jit(solution)/shard_map/ppermute | solution.py:282
  94.8 2.7 %collective-permute-done.22 = f32[8,2440]{1,0:T(8,128)S(1)} collective-permute-done((f32[8,2440]{1,0:T(8,128)S(1)}, f32[8,2440]{1,0:T(8,128)S(1)}, u32[]{:S(2)}, u32[]{:S(2)}) %collective-permute-start.22) | collective-permute-done | bytes 78112 | tf_op jit(solution)/shard_map/ppermute | solution.py:282
  103.8 6.0 %shard_map.98 = f32[8,72,256]{2,1,0:T(8,128)} custom-call(s32[128]{0:T(128)} %get-tuple-element.139.rows_ref, s32[128]{0:T(128)} %get-tuple-element.140.cols_ref, s32[128]{0:T(128)} %and_convert_fusion.live_ref, s32[1]{0:T(128)} %bitcast.5.nb_ref, f32[4,72,256]{2,1,0:T(8,128)} %concatenate.66.x_ref, bf16[1,1,128,256,256]{4,3,2,1,0:T(8,128)(2,1)} %t_ref.9, ...), custom_call_target="tpu_custom_call" | custom-call | tf_op jit(solution)/shard_map/pallas_call | solution.py:88
  110.8 1.6 %collective-permute-start.24 = (f32[4,72,256]{2,1,0:T(8,128)S(1)}, f32[4,72,256]{2,1,0:T(8,128)S(1)}, u32[]{:S(2)}, u32[]{:S(2)}) collective-permute-start(f32[4,72,256]{2,1,0:T(8,128)S(1)} %slice.327), channel_id=1, source_target_pairs={{0,4},{4,0},{8,12},{12,8},{16,20},{20,16},{24,28},{28,24},{1,5},{5... | collective-permute-start | bytes 884744 | tf_op jit(solution)/shard_map/ppermute | solution.py:209
  114.6 4.0 %collective-permute-start.27 = (f32[72,256]{1,0:T(8,128)S(1)}, f32[72,256]{1,0:T(8,128)S(1)}, u32[]{:S(2)}, u32[]{:S(2)}) collective-permute-start(f32[72,256]{1,0:T(8,128)S(1)} %get-tuple-element.119), channel_id=1, source_target_pairs={{0,24},{4,28},{8,0},{12,4},{16,8},{20,12},{24,16},{28,20},{1,25},{... | collective-permute-start | bytes 221192 | tf_op jit(solution)/shard_map/ppermute | solution.py:213
  119.2 2.0 %collective-permute-done.27 = f32[72,256]{1,0:T(8,128)S(1)} collective-permute-done((f32[72,256]{1,0:T(8,128)S(1)}, f32[72,256]{1,0:T(8,128)S(1)}, u32[]{:S(2)}, u32[]{:S(2)}) %collective-permute-start.27) | collective-permute-done | bytes 73760 | tf_op jit(solution)/shard_map/ppermute | solution.py:213
  121.2 4.9 %collective-permute-done.26 = f32[72,256]{1,0:T(8,128)S(1)} collective-permute-done((f32[72,256]{1,0:T(8,128)S(1)}, f32[72,256]{1,0:T(8,128)S(1)}, u32[]{:S(2)}, u32[]{:S(2)}) %collective-permute-start.26) | collective-permute-done | bytes 73760 | tf_op jit(solution)/shard_map/ppermute | solution.py:213
  129.9 2.0 %collective-permute-done.30 = f32[1,72,256]{2,1,0:T(8,128)S(1)} collective-permute-done((f32[1,72,256]{2,1,0:T(8,128)S(1)}, f32[1,72,256]{2,1,0:T(8,128)S(1)}, u32[]{:S(2)}, u32[]{:S(2)}) %collective-permute-start.30) | collective-permute-done | bytes 73760 | tf_op jit(solution)/shard_map/ppermute | solution.py:196
  134.2 5.9 %shard_map.99 = f32[8,72,256]{2,1,0:T(8,128)} custom-call(s32[128]{0:T(128)} %get-tuple-element.139.rows_ref, s32[128]{0:T(128)} %get-tuple-element.140.cols_ref, s32[128]{0:T(128)} %and_convert_fusion.live_ref, s32[1]{0:T(128)} %bitcast.5.nb_ref, f32[4,72,256]{2,1,0:T(8,128)} %copy-done.2, bf16[1,1,128,256,256]{4,3,2,1,0:T(8,128)(2,1)} %t_ref.9, ...), custom_call_target="tpu_custom_call" | custom-call | tf_op jit(solution)/shard_map/pallas_call | solution.py:88
  141.1 2.4 %collective-permute-start.31 = (f32[4,72,256]{2,1,0:T(8,128)S(1)}, f32[4,72,256]{2,1,0:T(8,128)S(1)}, u32[]{:S(2)}, u32[]{:S(2)}) collective-permute-start(f32[4,72,256]{2,1,0:T(8,128)S(1)} %slice.338), channel_id=1, source_target_pairs={{0,4},{4,0},{8,12},{12,8},{16,20},{20,16},{24,28},{28,24},{1,5},{5... | collective-permute-start | bytes 884744 | tf_op jit(solution)/shard_map/ppermute | solution.py:209
  145.9 2.0 %collective-permute-start.32 = (f32[72,256]{1,0:T(8,128)S(1)}, f32[72,256]{1,0:T(8,128)S(1)}, u32[]{:S(2)}, u32[]{:S(2)}) collective-permute-start(f32[72,256]{1,0:T(8,128)S(1)} %get-tuple-element.115), channel_id=1, source_target_pairs={{0,8},{4,12},{8,16},{12,20},{16,24},{20,28},{24,0},{28,4},{1,9},{5... | collective-permute-start | bytes 221192 | tf_op jit(solution)/shard_map/ppermute | solution.py:213
  148.6 2.9 %collective-permute-done.34 = f32[72,256]{1,0:T(8,128)S(1)} collective-permute-done((f32[72,256]{1,0:T(8,128)S(1)}, f32[72,256]{1,0:T(8,128)S(1)}, u32[]{:S(2)}, u32[]{:S(2)}) %collective-permute-start.34) | collective-permute-done | bytes 73760 | tf_op jit(solution)/shard_map/ppermute | solution.py:213
  151.5 3.0 %collective-permute-done.33 = f32[72,256]{1,0:T(8,128)S(1)} collective-permute-done((f32[72,256]{1,0:T(8,128)S(1)}, f32[72,256]{1,0:T(8,128)S(1)}, u32[]{:S(2)}, u32[]{:S(2)}) %collective-permute-start.33) | collective-permute-done | bytes 73760 | tf_op jit(solution)/shard_map/ppermute | solution.py:213
  (169 shorter events, 51.6 us)
Async XLA Ops:
  2.6 9.4 %collective-permute-start.2 = (f32[1,72,256]{2,1,0:T(8,128)S(1)}, f32[1,72,256]{2,1,0:T(8,128)S(1)}, u32[]{:S(2)}, u32[]{:S(2)}) collective-permute-start(f32[1,72,256]{2,1,0:T(8,128)S(1)} %fusion.43), channel_id=1, source_target_pairs={{0,3},{1,2},{2,1},{3,0},{4,7},{5,6},{6,5},{7,4},{8,11},{9,10},{10,... | collective-permute-start | bytes 221192 | tf_op jit(solution)/shard_map/ppermute | solution.py:196
  6.6 5.4 %collective-permute-start.1 = (f32[1,72,256]{2,1,0:T(8,128)S(1)}, f32[1,72,256]{2,1,0:T(8,128)S(1)}, u32[]{:S(2)}, u32[]{:S(2)}) collective-permute-start(f32[1,72,256]{2,1,0:T(8,128)S(1)} %fusion.43), channel_id=1, source_target_pairs={{0,2},{1,3},{2,0},{3,1},{4,6},{5,7},{6,4},{7,5},{8,10},{9,11},{10,... | collective-permute-start | bytes 221192 | tf_op jit(solution)/shard_map/ppermute | solution.py:196
  7.1 4.9 %collective-permute-start = (f32[1,72,256]{2,1,0:T(8,128)S(1)}, f32[1,72,256]{2,1,0:T(8,128)S(1)}, u32[]{:S(2)}, u32[]{:S(2)}) collective-permute-start(f32[1,72,256]{2,1,0:T(8,128)S(1)} %fusion.43), channel_id=1, source_target_pairs={{0,1},{1,0},{2,3},{3,2},{4,5},{5,4},{6,7},{7,6},{8,9},{9,8},{10,11... | collective-permute-start | bytes 221192 | tf_op jit(solution)/shard_map/ppermute | solution.py:196
  19.8 3.7 %collective-permute-start.3 = (f32[4,72,256]{2,1,0:T(8,128)S(1)}, f32[4,72,256]{2,1,0:T(8,128)S(1)}, u32[]{:S(2)}, u32[]{:S(2)}) collective-permute-start(f32[4,72,256]{2,1,0:T(8,128)S(1)} %slice.302), channel_id=1, source_target_pairs={{0,4},{4,0},{8,12},{12,8},{16,20},{20,16},{24,28},{28,24},{1,5},{5... | collective-permute-start | bytes 884744 | tf_op jit(solution)/shard_map/ppermute | solution.py:209
  24.5 6.4 %collective-permute-start.6 = (f32[72,256]{1,0:T(8,128)S(1)}, f32[72,256]{1,0:T(8,128)S(1)}, u32[]{:S(2)}, u32[]{:S(2)}) collective-permute-start(f32[72,256]{1,0:T(8,128)S(1)} %get-tuple-element.126), channel_id=1, source_target_pairs={{0,24},{4,28},{8,0},{12,4},{16,8},{20,12},{24,16},{28,20},{1,25},{... | collective-permute-start | bytes 221192 | tf_op jit(solution)/shard_map/ppermute | solution.py:213
  28.3 7.5 %collective-permute-start.5 = (f32[72,256]{1,0:T(8,128)S(1)}, f32[72,256]{1,0:T(8,128)S(1)}, u32[]{:S(2)}, u32[]{:S(2)}) collective-permute-start(f32[72,256]{1,0:T(8,128)S(1)} %get-tuple-element.127), channel_id=1, source_target_pairs={{0,16},{4,20},{8,24},{12,28},{16,0},{20,4},{24,8},{28,12},{1,17},{... | collective-permute-start | bytes 221192 | tf_op jit(solution)/shard_map/ppermute | solution.py:213
  28.3 7.5 %collective-permute-start.4 = (f32[72,256]{1,0:T(8,128)S(1)}, f32[72,256]{1,0:T(8,128)S(1)}, u32[]{:S(2)}, u32[]{:S(2)}) collective-permute-start(f32[72,256]{1,0:T(8,128)S(1)} %get-tuple-element.125), channel_id=1, source_target_pairs={{0,8},{4,12},{8,16},{12,20},{16,24},{20,28},{24,0},{28,4},{1,9},{5... | collective-permute-start | bytes 221192 | tf_op jit(solution)/shard_map/ppermute | solution.py:213
  36.1 5.8 %collective-permute-start.9 = (f32[1,72,256]{2,1,0:T(8,128)S(1)}, f32[1,72,256]{2,1,0:T(8,128)S(1)}, u32[]{:S(2)}, u32[]{:S(2)}) collective-permute-start(f32[1,72,256]{2,1,0:T(8,128)S(1)} %fusion.39), channel_id=1, source_target_pairs={{0,3},{1,2},{2,1},{3,0},{4,7},{5,6},{6,5},{7,4},{8,11},{9,10},{10,... | collective-permute-start | bytes 221192 | tf_op jit(solution)/shard_map/ppermute | solution.py:196
  37.7 5.1 %collective-permute-start.8 = (f32[1,72,256]{2,1,0:T(8,128)S(1)}, f32[1,72,256]{2,1,0:T(8,128)S(1)}, u32[]{:S(2)}, u32[]{:S(2)}) collective-permute-start(f32[1,72,256]{2,1,0:T(8,128)S(1)} %fusion.39), channel_id=1, source_target_pairs={{0,2},{1,3},{2,0},{3,1},{4,6},{5,7},{6,4},{7,5},{8,10},{9,11},{10,... | collective-permute-start | bytes 221192 | tf_op jit(solution)/shard_map/ppermute | solution.py:196
  37.7 5.1 %collective-permute-start.7 = (f32[1,72,256]{2,1,0:T(8,128)S(1)}, f32[1,72,256]{2,1,0:T(8,128)S(1)}, u32[]{:S(2)}, u32[]{:S(2)}) collective-permute-start(f32[1,72,256]{2,1,0:T(8,128)S(1)} %fusion.39), channel_id=1, source_target_pairs={{0,1},{1,0},{2,3},{3,2},{4,5},{5,4},{6,7},{7,6},{8,9},{9,8},{10,11... | collective-permute-start | bytes 221192 | tf_op jit(solution)/shard_map/ppermute | solution.py:196
  50.5 4.0 %collective-permute-start.10 = (f32[4,72,256]{2,1,0:T(8,128)S(1)}, f32[4,72,256]{2,1,0:T(8,128)S(1)}, u32[]{:S(2)}, u32[]{:S(2)}) collective-permute-start(f32[4,72,256]{2,1,0:T(8,128)S(1)} %slice.311), channel_id=1, source_target_pairs={{0,4},{4,0},{8,12},{12,8},{16,20},{20,16},{24,28},{28,24},{1,5},{5... | collective-permute-start | bytes 884744 | tf_op jit(solution)/shard_map/ppermute | solution.py:209
  55.5 5.8 %collective-permute-start.13 = (f32[72,256]{1,0:T(8,128)S(1)}, f32[72,256]{1,0:T(8,128)S(1)}, u32[]{:S(2)}, u32[]{:S(2)}) collective-permute-start(f32[72,256]{1,0:T(8,128)S(1)} %get-tuple-element.123), channel_id=1, source_target_pairs={{0,24},{4,28},{8,0},{12,4},{16,8},{20,12},{24,16},{28,20},{1,25},{... | collective-permute-start | bytes 221192 | tf_op jit(solution)/shard_map/ppermute | solution.py:213
  55.6 8.7 %collective-permute-start.12 = (f32[72,256]{1,0:T(8,128)S(1)}, f32[72,256]{1,0:T(8,128)S(1)}, u32[]{:S(2)}, u32[]{:S(2)}) collective-permute-start(f32[72,256]{1,0:T(8,128)S(1)} %get-tuple-element.124), channel_id=1, source_target_pairs={{0,16},{4,20},{8,24},{12,28},{16,0},{20,4},{24,8},{28,12},{1,17},{... | collective-permute-start | bytes 221192 | tf_op jit(solution)/shard_map/ppermute | solution.py:213
  55.7 8.6 %collective-permute-start.11 = (f32[72,256]{1,0:T(8,128)S(1)}, f32[72,256]{1,0:T(8,128)S(1)}, u32[]{:S(2)}, u32[]{:S(2)}) collective-permute-start(f32[72,256]{1,0:T(8,128)S(1)} %get-tuple-element.122), channel_id=1, source_target_pairs={{0,8},{4,12},{8,16},{12,20},{16,24},{20,28},{24,0},{28,4},{1,9},{5... | collective-permute-start | bytes 221192 | tf_op jit(solution)/shard_map/ppermute | solution.py:213
  64.6 5.7 %collective-permute-start.16 = (f32[1,72,256]{2,1,0:T(8,128)S(1)}, f32[1,72,256]{2,1,0:T(8,128)S(1)}, u32[]{:S(2)}, u32[]{:S(2)}) collective-permute-start(f32[1,72,256]{2,1,0:T(8,128)S(1)} %maximum_bitcast_fusion), channel_id=1, source_target_pairs={{0,3},{1,2},{2,1},{3,0},{4,7},{5,6},{6,5},{7,4},{8,11},{9,10},{10,... | collective-permute-start | bytes 221192 | tf_op jit(solution)/shard_map/ppermute | solution.py:196
  65.4 5.1 %collective-permute-start.15 = (f32[1,72,256]{2,1,0:T(8,128)S(1)}, f32[1,72,256]{2,1,0:T(8,128)S(1)}, u32[]{:S(2)}, u32[]{:S(2)}) collective-permute-start(f32[1,72,256]{2,1,0:T(8,128)S(1)} %maximum_bitcast_fusion), channel_id=1, source_target_pairs={{0,2},{1,3},{2,0},{3,1},{4,6},{5,7},{6,4},{7,5},{8,10},{9,11},{10,... | collective-permute-start | bytes 221192 | tf_op jit(solution)/shard_map/ppermute | solution.py:196
  65.7 4.8 %collective-permute-start.14 = (f32[1,72,256]{2,1,0:T(8,128)S(1)}, f32[1,72,256]{2,1,0:T(8,128)S(1)}, u32[]{:S(2)}, u32[]{:S(2)}) collective-permute-start(f32[1,72,256]{2,1,0:T(8,128)S(1)} %maximum_bitcast_fusion), channel_id=1, source_target_pairs={{0,1},{1,0},{2,3},{3,2},{4,5},{5,4},{6,7},{7,6},{8,9},{9,8},{10,11... | collective-permute-start | bytes 221192 | tf_op jit(solution)/shard_map/ppermute | solution.py:196
  79.6 3.8 %collective-permute-start.17 = (f32[1,2440]{1,0:T(1,128)S(1)}, f32[1,2440]{1,0:T(1,128)S(1)}, u32[]{:S(2)}, u32[]{:S(2)}) collective-permute-start(f32[1,2440]{1,0:T(1,128)S(1)} %broadcast_in_dim.21), channel_id=1, source_target_pairs={{0,1},{1,0},{2,3},{3,2},{4,5},{5,4},{6,7},{7,6},{8,9},{9,8},{10,11... | collective-permute-start | bytes 29288 | tf_op jit(solution)/shard_map/ppermute | solution.py:270
  81.5 3.7 %collective-permute-start.18 = (f32[1,2440]{1,0:T(1,128)S(1)}, f32[1,2440]{1,0:T(1,128)S(1)}, u32[]{:S(2)}, u32[]{:S(2)}) collective-permute-start(f32[1,2440]{1,0:T(1,128)S(1)} %broadcast_in_dim.21), channel_id=1, source_target_pairs={{0,2},{1,3},{2,0},{3,1},{4,6},{5,7},{6,4},{7,5},{8,10},{9,11},{10,... | collective-permute-start | bytes 29288 | tf_op jit(solution)/shard_map/ppermute | solution.py:270
  81.6 4.6 %collective-permute-start.19 = (f32[1,2440]{1,0:T(1,128)S(1)}, f32[1,2440]{1,0:T(1,128)S(1)}, u32[]{:S(2)}, u32[]{:S(2)}) collective-permute-start(f32[1,2440]{1,0:T(1,128)S(1)} %broadcast_in_dim.21), channel_id=1, source_target_pairs={{0,3},{1,2},{2,1},{3,0},{4,7},{5,6},{6,5},{7,4},{8,11},{9,10},{10,... | collective-permute-start | bytes 29288 | tf_op jit(solution)/shard_map/ppermute | solution.py:270
  87.6 7.2 %collective-permute-start.21 = (f32[8,2440]{1,0:T(8,128)S(1)}, f32[8,2440]{1,0:T(8,128)S(1)}, u32[]{:S(2)}, u32[]{:S(2)}) collective-permute-start(f32[8,2440]{1,0:T(8,128)S(1)} %concatenate.64), channel_id=1, source_target_pairs={{0,8},{4,12},{8,16},{12,20},{16,24},{20,28},{24,0},{28,4},{1,9},{5... | collective-permute-start | bytes 234248 | tf_op jit(solution)/shard_map/ppermute | solution.py:282
  87.8 9.7 %collective-permute-start.22 = (f32[8,2440]{1,0:T(8,128)S(1)}, f32[8,2440]{1,0:T(8,128)S(1)}, u32[]{:S(2)}, u32[]{:S(2)}) collective-permute-start(f32[8,2440]{1,0:T(8,128)S(1)} %concatenate.64), channel_id=1, source_target_pairs={{0,16},{4,20},{8,24},{12,28},{16,0},{20,4},{24,8},{28,12},{1,17},{... | collective-permute-start | bytes 234248 | tf_op jit(solution)/shard_map/ppermute | solution.py:282
  89.8 7.7 %collective-permute-start.23 = (f32[8,2440]{1,0:T(8,128)S(1)}, f32[8,2440]{1,0:T(8,128)S(1)}, u32[]{:S(2)}, u32[]{:S(2)}) collective-permute-start(f32[8,2440]{1,0:T(8,128)S(1)} %concatenate.64), channel_id=1, source_target_pairs={{0,24},{4,28},{8,0},{12,4},{16,8},{20,12},{24,16},{28,20},{1,25},{... | collective-permute-start | bytes 234248 | tf_op jit(solution)/shard_map/ppermute | solution.py:282
  114.6 6.6 %collective-permute-start.27 = (f32[72,256]{1,0:T(8,128)S(1)}, f32[72,256]{1,0:T(8,128)S(1)}, u32[]{:S(2)}, u32[]{:S(2)}) collective-permute-start(f32[72,256]{1,0:T(8,128)S(1)} %get-tuple-element.119), channel_id=1, source_target_pairs={{0,24},{4,28},{8,0},{12,4},{16,8},{20,12},{24,16},{28,20},{1,25},{... | collective-permute-start | bytes 221192 | tf_op jit(solution)/shard_map/ppermute | solution.py:213
  118.6 7.5 %collective-permute-start.26 = (f32[72,256]{1,0:T(8,128)S(1)}, f32[72,256]{1,0:T(8,128)S(1)}, u32[]{:S(2)}, u32[]{:S(2)}) collective-permute-start(f32[72,256]{1,0:T(8,128)S(1)} %get-tuple-element.120), channel_id=1, source_target_pairs={{0,16},{4,20},{8,24},{12,28},{16,0},{20,4},{24,8},{28,12},{1,17},{... | collective-permute-start | bytes 221192 | tf_op jit(solution)/shard_map/ppermute | solution.py:213
  118.6 7.5 %collective-permute-start.25 = (f32[72,256]{1,0:T(8,128)S(1)}, f32[72,256]{1,0:T(8,128)S(1)}, u32[]{:S(2)}, u32[]{:S(2)}) collective-permute-start(f32[72,256]{1,0:T(8,128)S(1)} %get-tuple-element.121), channel_id=1, source_target_pairs={{0,8},{4,12},{8,16},{12,20},{16,24},{20,28},{24,0},{28,4},{1,9},{5... | collective-permute-start | bytes 221192 | tf_op jit(solution)/shard_map/ppermute | solution.py:213
  126.4 5.5 %collective-permute-start.30 = (f32[1,72,256]{2,1,0:T(8,128)S(1)}, f32[1,72,256]{2,1,0:T(8,128)S(1)}, u32[]{:S(2)}, u32[]{:S(2)}) collective-permute-start(f32[1,72,256]{2,1,0:T(8,128)S(1)} %fusion.35), channel_id=1, source_target_pairs={{0,3},{1,2},{2,1},{3,0},{4,7},{5,6},{6,5},{7,4},{8,11},{9,10},{10,... | collective-permute-start | bytes 221192 | tf_op jit(solution)/shard_map/ppermute | solution.py:196
  127.5 5.0 %collective-permute-start.29 = (f32[1,72,256]{2,1,0:T(8,128)S(1)}, f32[1,72,256]{2,1,0:T(8,128)S(1)}, u32[]{:S(2)}, u32[]{:S(2)}) collective-permute-start(f32[1,72,256]{2,1,0:T(8,128)S(1)} %fusion.35), channel_id=1, source_target_pairs={{0,2},{1,3},{2,0},{3,1},{4,6},{5,7},{6,4},{7,5},{8,10},{9,11},{10,... | collective-permute-start | bytes 221192 | tf_op jit(solution)/shard_map/ppermute | solution.py:196
  128.3 5.1 %collective-permute-start.28 = (f32[1,72,256]{2,1,0:T(8,128)S(1)}, f32[1,72,256]{2,1,0:T(8,128)S(1)}, u32[]{:S(2)}, u32[]{:S(2)}) collective-permute-start(f32[1,72,256]{2,1,0:T(8,128)S(1)} %fusion.35), channel_id=1, source_target_pairs={{0,1},{1,0},{2,3},{3,2},{4,5},{5,4},{6,7},{7,6},{8,9},{9,8},{10,11... | collective-permute-start | bytes 221192 | tf_op jit(solution)/shard_map/ppermute | solution.py:196
  145.7 5.8 %collective-permute-start.34 = (f32[72,256]{1,0:T(8,128)S(1)}, f32[72,256]{1,0:T(8,128)S(1)}, u32[]{:S(2)}, u32[]{:S(2)}) collective-permute-start(f32[72,256]{1,0:T(8,128)S(1)} %get-tuple-element.116), channel_id=1, source_target_pairs={{0,24},{4,28},{8,0},{12,4},{16,8},{20,12},{24,16},{28,20},{1,25},{... | collective-permute-start | bytes 221192 | tf_op jit(solution)/shard_map/ppermute | solution.py:213
  145.8 8.7 %collective-permute-start.33 = (f32[72,256]{1,0:T(8,128)S(1)}, f32[72,256]{1,0:T(8,128)S(1)}, u32[]{:S(2)}, u32[]{:S(2)}) collective-permute-start(f32[72,256]{1,0:T(8,128)S(1)} %get-tuple-element.117), channel_id=1, source_target_pairs={{0,16},{4,20},{8,24},{12,28},{16,0},{20,4},{24,8},{28,12},{1,17},{... | collective-permute-start | bytes 221192 | tf_op jit(solution)/shard_map/ppermute | solution.py:213
  145.9 8.6 %collective-permute-start.32 = (f32[72,256]{1,0:T(8,128)S(1)}, f32[72,256]{1,0:T(8,128)S(1)}, u32[]{:S(2)}, u32[]{:S(2)}) collective-permute-start(f32[72,256]{1,0:T(8,128)S(1)} %get-tuple-element.115), channel_id=1, source_target_pairs={{0,8},{4,12},{8,16},{12,20},{16,24},{20,28},{24,0},{28,4},{1,9},{5... | collective-permute-start | bytes 221192 | tf_op jit(solution)/shard_map/ppermute | solution.py:213
  (11 other events, 193.2 us)

commit v7 on v6

--- a/solution.py
+++ b/solution.py
@@ -17,15 +17,18 @@
 ):
     step = pl.program_id(0)
     if mode == "image":
-        lost_ref, o_ref = refs
+        lost_ref = refs[0]
+        outs = refs[1:]
         body_rows = blocks_piece * vectors
 
         @pl.when(step == 0)
         def _():
-            o_ref[:, :body_rows, :] = jnp.zeros((o_ref.shape[0], body_rows, o_ref.shape[2]), o_ref.dtype)
-            o_ref[:, body_rows:, :] = jnp.broadcast_to(
-                lost_ref[...][None], (o_ref.shape[0],) + lost_ref.shape
-            )
+            for out_ref in outs:
+                count = out_ref.shape[0]
+                out_ref[:, :body_rows, :] = jnp.zeros((count, body_rows, out_ref.shape[2]), jnp.float32)
+                out_ref[:, body_rows:, :] = jnp.broadcast_to(
+                    lost_ref[...][None], (count,) + lost_ref.shape
+                )
     else:
         (o_ref,) = refs
 
@@ -41,8 +44,15 @@
             if mode == "image":
                 row = rows_ref[slot]
                 at = pl.multiple_of((row % blocks_piece) * vectors, vectors)
-                window = (row // blocks_piece, pl.ds(at, vectors), slice(None))
-                o_ref[window] = o_ref[window] + product
+                spot = row // blocks_piece
+                part_size = outs[0].shape[0]
+                for q, out_ref in enumerate(outs):
+                    window = (spot % part_size, pl.ds(at, vectors), slice(None))
+                    if len(outs) == 1:
+                        out_ref[window] = out_ref[window] + product
+                    else:
+                        mask = jnp.where(spot // part_size == q, 1.0, 0.0)
+                        out_ref[window] = out_ref[window] + product * mask
             else:
                 o_ref[g] = product[:, :128] + product[:, 128:]
 
@@ -64,8 +74,10 @@
         return (0, 0, jnp.minimum(i, nb_ref[0] - 1), 0, 0)
 
     if mode == "image":
-        out_shape = jax.ShapeDtypeStruct((owners, padded_rows, side), jnp.float32)
-        out_spec = pl.BlockSpec((owners, padded_rows, side), lambda i, *_: (0, 0, 0))
+        parts = 2 if owners % 2 == 0 else 1
+        part_shape = (owners // parts, padded_rows, side)
+        out_shape = [jax.ShapeDtypeStruct(part_shape, jnp.float32)] * parts
+        out_spec = [pl.BlockSpec(part_shape, lambda i, *_: (0, 0, 0))] * parts
     else:
         out_shape = jax.ShapeDtypeStruct((slots, vectors, 128), jnp.float32)
         out_spec = pl.BlockSpec((group_size, vectors, 128), lambda i, *_: (i, 0, 0))
@@ -202,16 +214,18 @@
         lost_dst = jnp.sum(payload[:, payload_rows, :vectors], axis=0)
         return payload, lost_dst
 
-    def reduce_rows(chunks):
+    def reduce_rows(outputs):
         n = src_count
         if n % 2 == 0:
             half = n // 2
-            part = chunks[:half] + lax.ppermute(chunks[half:], "src", [(i, i ^ 1) for i in range(n)])
+            keep, give = outputs
+            part = keep + lax.ppermute(give, "src", [(i, i ^ 1) for i in range(n)])
             total = part[0]
             for shift in range(1, half):
                 pairs = [(i, ((i // 2 + shift) % half) * 2 + i % 2) for i in range(n)]
                 total = total + lax.ppermute(part[shift], "src", pairs)
         else:
+            (chunks,) = outputs
             total = chunks[0]
             for shift in range(1, n):
                 pairs = [(i, (i + shift) % n) for i in range(n)]
@@ -328,13 +342,10 @@
     )
     block_scale = jnp.take(ratios_two, agg_of_block[block_ids.reshape(-1)], axis=1)
     block_scale = block_scale.T.reshape(groups, payload_rows, 1)
-    corrected_cols = jnp.concatenate(
-        [
-            gathered[:, :payload_rows, :] * block_scale,
-            jnp.zeros((groups, pad_rows, tile_side), jnp.float32),
-        ],
-        axis=1,
-    )
+    block_scale = jnp.concatenate(
+        [block_scale, jnp.zeros((groups, pad_rows, 1), jnp.float32)], axis=1
+    )
+    corrected_cols = gathered * block_scale
     lost_two = jnp.sum(lost_mass * ratios_two, axis=1)
 
     position = lax.axis_index(all_axes)

time: 155 us -> 158 us (1.019)
  starting transfers between devices: 46.4 us -> 57.2 us
  local copies, waits for them, and re-layouts: 15.5 us -> 10.9 us
  waiting for transfers between devices: 45.5 us -> 41.1 us
    ppermute x12, starting transfers between devices: 13.2 us -> 22.7 us  [reduce_rows(): total = total + lax.ppermute(part[shift], 'src', pairs)]
    slice x4 -> x0, local copies, waits for them, and re-layouts: 3.92 us -> none  [reduce_rows(): chunks[half:]]
    ppermute x12, waiting for transfers between devices: 24.6 us -> 21.8 us  [reduce_rows(): total = total + lax.ppermute(part[shift], 'src', pairs)]
    ppermute x12, waiting for transfers between devices: 7.81 us -> 5.87 us  [spread_columns(): lax.ppermute(payload, 'dst', [(i, i ^ v) for i in range(dst_count)])]
  transfers between devices with their start and end apart: 35 -> 35, of which waited for: 26 -> 21; matrix products, arithmetic and copies ran while one was open for 6% -> 6% of each run, Pallas kernels for 0% -> 0%
where the time goes in v7:
time: 158 us
  starting transfers between devices  57.2 us (36%)
  waiting for transfers between devices  41.1 us (26%)
  Pallas kernels  30.6 us (19%)
  other arithmetic  13.7 us (9%)
  local copies, waits for them, and re-layouts  10.9 us (7%)
  matrix products  3 us (2%)
  between operations  1.78 us (1%)
    pallas_call x5, Pallas kernels, tile_pass(): pl.pallas_call(functools.partial(tile_kernel, mode, blocks_piece, vectors...  30.6 us
    ppermute x12, starting transfers between devices, reduce_rows(): total = total + lax.ppermute(part[shift], 'src', pairs)  22.7 us
    ppermute x12, waiting for transfers between devices, reduce_rows(): total = total + lax.ppermute(part[shift], 'src', pairs)  21.8 us
    ppermute x12, starting transfers between devices, spread_columns(): lax.ppermute(payload, 'dst', [(i, i ^ v) for i in range(dst_count)])  15.2 us
    ppermute x4, starting transfers between devices, reduce_rows(): part = keep + lax.ppermute(give, 'src', [(i, i ^ 1) for i in range(n)])  9.46 us
    ppermute x3, starting transfers between devices, per_device(): pieces.append(lax.ppermute(shared, 'src', pairs))  6.19 us
    ppermute x12, waiting for transfers between devices, spread_columns(): lax.ppermute(payload, 'dst', [(i, i ^ v) for i in range(dst_count)])  5.87 us
    ppermute x4, waiting for transfers between devices, reduce_rows(): part = keep + lax.ppermute(give, 'src', [(i, i ^ 1) for i in range(n)])  4.84 us
  transfers between devices with their start and end apart: 35, of which 21 were waited for; matrix products, arithmetic and copies ran while one was open for 6% of the time, Pallas kernels for 0%

profile of v7, /device:TPU:0, one launch (start us, length us, event | category | flops | bytes accessed | tf_op | source)
XLA Modules:
  0.0 158.3 jit_solution(17119630264511872783)
XLA Ops:
  2.6 4.0 %collective-permute-start.2 = (f32[1,72,256]{2,1,0:T(8,128)S(1)}, f32[1,72,256]{2,1,0:T(8,128)S(1)}, u32[]{:S(2)}, u32[]{:S(2)}) collective-permute-start(f32[1,72,256]{2,1,0:T(8,128)S(1)} %fusion.43), channel_id=1, source_target_pairs={{0,3},{1,2},{2,1},{3,0},{4,7},{5,6},{6,5},{7,4},{8,11},{9,10},{10,... | collective-permute-start | bytes 221192 | tf_op jit(solution)/shard_map/ppermute | solution.py:208
  7.9 1.6 %gather_fusion = s32[128]{0:T(128)S(1)} fusion(s32[128]{0:T(128)} %param.29, s32[1024]{0:T(1024)S(1)} %pad_clamp_fusion.3), kind=kCustom, calls=%fused_computation | custom fusion | bytes 1536 | tf_op jit(solution)/shard_map/gather | solution.py:153
  12.8 6.1 %shard_map.95 = (f32[4,72,256]{2,1,0:T(8,128)}, f32[4,72,256]{2,1,0:T(8,128)}) custom-call(s32[128]{0:T(128)} %get-tuple-element.155.rows_ref, s32[128]{0:T(128)} %get-tuple-element.156.cols_ref, s32[128]{0:T(128)} %and_convert_fusion.live_ref, s32[1]{0:T(128)} %bitcast.5.nb_ref, f32[4,72,256]{2,1,0:T(8,128)} %copy-done.2, ...), custom_call_target="tpu_custom_call" | custom-call | tf_op jit(solution)/shard_map/pallas_call | solution.py:100
  18.9 2.5 %collective-permute-start.3 = (f32[4,72,256]{2,1,0:T(8,128)}, f32[4,72,256]{2,1,0:T(8,128)S(1)}, u32[]{:S(2)}, u32[]{:S(2)}) collective-permute-start(f32[4,72,256]{2,1,0:T(8,128)} %get-tuple-element.103), channel_id=1, source_target_pairs={{0,4},{4,0},{8,12},{12,8},{16,20},{20,16},{24,28},{28,24},{1,5},{5... | collective-permute-start | bytes 884744 | tf_op jit(solution)/shard_map/ppermute | solution.py:222
  23.8 5.2 %collective-permute-start.6 = (f32[72,256]{1,0:T(8,128)S(1)}, f32[72,256]{1,0:T(8,128)S(1)}, u32[]{:S(2)}, u32[]{:S(2)}) collective-permute-start(f32[72,256]{1,0:T(8,128)S(1)} %get-tuple-element.142), channel_id=1, source_target_pairs={{0,24},{4,28},{8,0},{12,4},{16,8},{20,12},{24,16},{28,20},{1,25},{... | collective-permute-start | bytes 221192 | tf_op jit(solution)/shard_map/ppermute | solution.py:226
  31.7 4.7 %collective-permute-done.5 = f32[72,256]{1,0:T(8,128)S(1)} collective-permute-done((f32[72,256]{1,0:T(8,128)S(1)}, f32[72,256]{1,0:T(8,128)S(1)}, u32[]{:S(2)}, u32[]{:S(2)}) %collective-permute-start.5) | collective-permute-done | bytes 73760 | tf_op jit(solution)/shard_map/ppermute | solution.py:226
  37.7 2.5 %collective-permute-start.7 = (f32[1,72,256]{2,1,0:T(8,128)S(1)}, f32[1,72,256]{2,1,0:T(8,128)S(1)}, u32[]{:S(2)}, u32[]{:S(2)}) collective-permute-start(f32[1,72,256]{2,1,0:T(8,128)S(1)} %fusion.39), channel_id=1, source_target_pairs={{0,1},{1,0},{2,3},{3,2},{4,5},{5,4},{6,7},{7,6},{8,9},{9,8},{10,11... | collective-permute-start | bytes 221192 | tf_op jit(solution)/shard_map/ppermute | solution.py:208
  40.2 2.3 %collective-permute-done.9 = f32[1,72,256]{2,1,0:T(8,128)S(1)} collective-permute-done((f32[1,72,256]{2,1,0:T(8,128)S(1)}, f32[1,72,256]{2,1,0:T(8,128)S(1)}, u32[]{:S(2)}, u32[]{:S(2)}) %collective-permute-start.9) | collective-permute-done | bytes 73760 | tf_op jit(solution)/shard_map/ppermute | solution.py:208
  43.5 6.0 %shard_map.96 = (f32[4,72,256]{2,1,0:T(8,128)}, f32[4,72,256]{2,1,0:T(8,128)}) custom-call(s32[128]{0:T(128)} %get-tuple-element.155.rows_ref, s32[128]{0:T(128)} %get-tuple-element.156.cols_ref, s32[128]{0:T(128)} %and_convert_fusion.live_ref, s32[1]{0:T(128)} %bitcast.5.nb_ref, f32[4,72,256]{2,1,0:T(8,128)} %copy-done.3, ...), custom_call_target="tpu_custom_call" | custom-call | tf_op jit(solution)/shard_map/pallas_call | solution.py:100
  49.5 2.3 %collective-permute-start.10 = (f32[4,72,256]{2,1,0:T(8,128)}, f32[4,72,256]{2,1,0:T(8,128)S(1)}, u32[]{:S(2)}, u32[]{:S(2)}) collective-permute-start(f32[4,72,256]{2,1,0:T(8,128)} %get-tuple-element.105), channel_id=1, source_target_pairs={{0,4},{4,0},{8,12},{12,8},{16,20},{20,16},{24,28},{28,24},{1,5},{5... | collective-permute-start | bytes 884744 | tf_op jit(solution)/shard_map/ppermute | solution.py:222
  54.3 3.0 %collective-permute-start.13 = (f32[72,256]{1,0:T(8,128)S(1)}, f32[72,256]{1,0:T(8,128)S(1)}, u32[]{:S(2)}, u32[]{:S(2)}) collective-permute-start(f32[72,256]{1,0:T(8,128)S(1)} %get-tuple-element.139), channel_id=1, source_target_pairs={{0,24},{4,28},{8,0},{12,4},{16,8},{20,12},{24,16},{28,20},{1,25},{... | collective-permute-start | bytes 221192 | tf_op jit(solution)/shard_map/ppermute | solution.py:226
  57.8 1.9 %collective-permute-start.11 = (f32[72,256]{1,0:T(8,128)S(1)}, f32[72,256]{1,0:T(8,128)S(1)}, u32[]{:S(2)}, u32[]{:S(2)}) collective-permute-start(f32[72,256]{1,0:T(8,128)S(1)} %get-tuple-element.138), channel_id=1, source_target_pairs={{0,8},{4,12},{8,16},{12,20},{16,24},{20,28},{24,0},{28,4},{1,9},{5... | collective-permute-start | bytes 221192 | tf_op jit(solution)/shard_map/ppermute | solution.py:226
  61.0 4.4 %collective-permute-done.12 = f32[72,256]{1,0:T(8,128)S(1)} collective-permute-done((f32[72,256]{1,0:T(8,128)S(1)}, f32[72,256]{1,0:T(8,128)S(1)}, u32[]{:S(2)}, u32[]{:S(2)}) %collective-permute-start.12) | collective-permute-done | bytes 73760 | tf_op jit(solution)/shard_map/ppermute | solution.py:226
  66.3 2.8 %collective-permute-start.14 = (f32[1,72,256]{2,1,0:T(8,128)S(1)}, f32[1,72,256]{2,1,0:T(8,128)S(1)}, u32[]{:S(2)}, u32[]{:S(2)}) collective-permute-start(f32[1,72,256]{2,1,0:T(8,128)S(1)} %maximum_bitcast_fusion), channel_id=1, source_target_pairs={{0,1},{1,0},{2,3},{3,2},{4,5},{5,4},{6,7},{7,6},{8,9},{9,8},{10,11... | collective-permute-start | bytes 221192 | tf_op jit(solution)/shard_map/ppermute | solution.py:208
  72.2 6.3 %shard_map.97 = f32[128,16,128]{2,1,0:T(8,128)} custom-call(s32[128]{0:T(128)} %clamp_bitcast_fusion.rows_ref, s32[128]{0:T(128)} %get-tuple-element.156.cols_ref, s32[128]{0:T(128)} %and_convert_fusion.live_ref, s32[1]{0:T(128)} %bitcast.5.nb_ref, f32[4,72,256]{2,1,0:T(8,128)} %pad_maximum_fusion.2.x_ref, bf16[1,1,128,256,256]{4,3,2,1,0:T(8,128)(2,1)} %t_ref.9), custom_call_target="tpu_custom_call" | custom-call | tf_op jit(solution)/shard_map/pallas_call | solution.py:100
  80.3 2.1 %collective-permute-start.17 = (f32[1,2440]{1,0:T(1,128)S(1)}, f32[1,2440]{1,0:T(1,128)S(1)}, u32[]{:S(2)}, u32[]{:S(2)}) collective-permute-start(f32[1,2440]{1,0:T(1,128)S(1)} %broadcast_in_dim.21), channel_id=1, source_target_pairs={{0,1},{1,0},{2,3},{3,2},{4,5},{5,4},{6,7},{7,6},{8,9},{9,8},{10,11... | collective-permute-start | bytes 29288 | tf_op jit(solution)/shard_map/ppermute | solution.py:284
  84.1 2.0 %collective-permute-done.18 = f32[1,2440]{1,0:T(1,128)S(1)} collective-permute-done((f32[1,2440]{1,0:T(1,128)S(1)}, f32[1,2440]{1,0:T(1,128)S(1)}, u32[]{:S(2)}, u32[]{:S(2)}) %collective-permute-start.18) | collective-permute-done | bytes 9792 | tf_op jit(solution)/shard_map/ppermute | solution.py:284
  89.1 3.3 %collective-permute-start.22 = (f32[8,2440]{1,0:T(8,128)S(1)}, f32[8,2440]{1,0:T(8,128)S(1)}, u32[]{:S(2)}, u32[]{:S(2)}) collective-permute-start(f32[8,2440]{1,0:T(8,128)S(1)} %concatenate.64), channel_id=1, source_target_pairs={{0,16},{4,20},{8,24},{12,28},{16,0},{20,4},{24,8},{28,12},{1,17},{... | collective-permute-start | bytes 234248 | tf_op jit(solution)/shard_map/ppermute | solution.py:296
  92.4 2.8 %collective-permute-start.23 = (f32[8,2440]{1,0:T(8,128)S(1)}, f32[8,2440]{1,0:T(8,128)S(1)}, u32[]{:S(2)}, u32[]{:S(2)}) collective-permute-start(f32[8,2440]{1,0:T(8,128)S(1)} %concatenate.64), channel_id=1, source_target_pairs={{0,24},{4,28},{8,0},{12,4},{16,8},{20,12},{24,16},{28,20},{1,25},{... | collective-permute-start | bytes 234248 | tf_op jit(solution)/shard_map/ppermute | solution.py:296
  95.5 3.4 %collective-permute-done.22 = f32[8,2440]{1,0:T(8,128)S(1)} collective-permute-done((f32[8,2440]{1,0:T(8,128)S(1)}, f32[8,2440]{1,0:T(8,128)S(1)}, u32[]{:S(2)}, u32[]{:S(2)}) %collective-permute-start.22) | collective-permute-done | bytes 78112 | tf_op jit(solution)/shard_map/ppermute | solution.py:296
  105.2 6.1 %shard_map.98 = (f32[4,72,256]{2,1,0:T(8,128)}, f32[4,72,256]{2,1,0:T(8,128)}) custom-call(s32[128]{0:T(128)} %get-tuple-element.155.rows_ref, s32[128]{0:T(128)} %get-tuple-element.156.cols_ref, s32[128]{0:T(128)} %and_convert_fusion.live_ref, s32[1]{0:T(128)} %bitcast.5.nb_ref, f32[4,72,256]{2,1,0:T(8,128)} %broadcast_multiply_fusion.x_ref, ...), custom_call_target="tpu_custom_call" | custom-call | tf_op jit(solution)/shard_map/pallas_call | solution.py:100
  111.3 2.6 %collective-permute-start.24 = (f32[4,72,256]{2,1,0:T(8,128)}, f32[4,72,256]{2,1,0:T(8,128)S(1)}, u32[]{:S(2)}, u32[]{:S(2)}) collective-permute-start(f32[4,72,256]{2,1,0:T(8,128)} %get-tuple-element.107), channel_id=1, source_target_pairs={{0,4},{4,0},{8,12},{12,8},{16,20},{20,16},{24,28},{28,24},{1,5},{5... | collective-permute-start | bytes 884744 | tf_op jit(solution)/shard_map/ppermute | solution.py:222
  116.4 5.0 %collective-permute-start.27 = (f32[72,256]{1,0:T(8,128)S(1)}, f32[72,256]{1,0:T(8,128)S(1)}, u32[]{:S(2)}, u32[]{:S(2)}) collective-permute-start(f32[72,256]{1,0:T(8,128)S(1)} %get-tuple-element.135), channel_id=1, source_target_pairs={{0,24},{4,28},{8,0},{12,4},{16,8},{20,12},{24,16},{28,20},{1,25},{... | collective-permute-start | bytes 221192 | tf_op jit(solution)/shard_map/ppermute | solution.py:226
  122.1 2.0 %collective-permute-done.27 = f32[72,256]{1,0:T(8,128)S(1)} collective-permute-done((f32[72,256]{1,0:T(8,128)S(1)}, f32[72,256]{1,0:T(8,128)S(1)}, u32[]{:S(2)}, u32[]{:S(2)}) %collective-permute-start.27) | collective-permute-done | bytes 73760 | tf_op jit(solution)/shard_map/ppermute | solution.py:226
  124.1 4.6 %collective-permute-done.26 = f32[72,256]{1,0:T(8,128)S(1)} collective-permute-done((f32[72,256]{1,0:T(8,128)S(1)}, f32[72,256]{1,0:T(8,128)S(1)}, u32[]{:S(2)}, u32[]{:S(2)}) %collective-permute-start.26) | collective-permute-done | bytes 73760 | tf_op jit(solution)/shard_map/ppermute | solution.py:226
  129.1 3.4 %collective-permute-start.28 = (f32[1,72,256]{2,1,0:T(8,128)S(1)}, f32[1,72,256]{2,1,0:T(8,128)S(1)}, u32[]{:S(2)}, u32[]{:S(2)}) collective-permute-start(f32[1,72,256]{2,1,0:T(8,128)S(1)} %fusion.35), channel_id=1, source_target_pairs={{0,1},{1,0},{2,3},{3,2},{4,5},{5,4},{6,7},{7,6},{8,9},{9,8},{10,11... | collective-permute-start | bytes 221192 | tf_op jit(solution)/shard_map/ppermute | solution.py:208
  132.5 2.4 %collective-permute-done.30 = f32[1,72,256]{2,1,0:T(8,128)S(1)} collective-permute-done((f32[1,72,256]{2,1,0:T(8,128)S(1)}, f32[1,72,256]{2,1,0:T(8,128)S(1)}, u32[]{:S(2)}, u32[]{:S(2)}) %collective-permute-start.30) | collective-permute-done | bytes 73760 | tf_op jit(solution)/shard_map/ppermute | solution.py:208
  135.6 6.0 %shard_map.99 = (f32[4,72,256]{2,1,0:T(8,128)}, f32[4,72,256]{2,1,0:T(8,128)}) custom-call(s32[128]{0:T(128)} %get-tuple-element.155.rows_ref, s32[128]{0:T(128)} %get-tuple-element.156.cols_ref, s32[128]{0:T(128)} %and_convert_fusion.live_ref, s32[1]{0:T(128)} %bitcast.5.nb_ref, f32[4,72,256]{2,1,0:T(8,128)} %copy-done.1, ...), custom_call_target="tpu_custom_call" | custom-call | tf_op jit(solution)/shard_map/pallas_call | solution.py:100
  141.7 2.0 %collective-permute-start.31 = (f32[4,72,256]{2,1,0:T(8,128)}, f32[4,72,256]{2,1,0:T(8,128)S(1)}, u32[]{:S(2)}, u32[]{:S(2)}) collective-permute-start(f32[4,72,256]{2,1,0:T(8,128)} %get-tuple-element.109), channel_id=1, source_target_pairs={{0,4},{4,0},{8,12},{12,8},{16,20},{20,16},{24,28},{28,24},{1,5},{5... | collective-permute-start | bytes 884744 | tf_op jit(solution)/shard_map/ppermute | solution.py:222
  146.1 3.4 %collective-permute-start.34 = (f32[72,256]{1,0:T(8,128)S(1)}, f32[72,256]{1,0:T(8,128)S(1)}, u32[]{:S(2)}, u32[]{:S(2)}) collective-permute-start(f32[72,256]{1,0:T(8,128)S(1)} %get-tuple-element.132), channel_id=1, source_target_pairs={{0,24},{4,28},{8,0},{12,4},{16,8},{20,12},{24,16},{28,20},{1,25},{... | collective-permute-start | bytes 221192 | tf_op jit(solution)/shard_map/ppermute | solution.py:226
  149.6 1.9 %collective-permute-start.32 = (f32[72,256]{1,0:T(8,128)S(1)}, f32[72,256]{1,0:T(8,128)S(1)}, u32[]{:S(2)}, u32[]{:S(2)}) collective-permute-start(f32[72,256]{1,0:T(8,128)S(1)} %get-tuple-element.131), channel_id=1, source_target_pairs={{0,8},{4,12},{8,16},{12,20},{16,24},{20,28},{24,0},{28,4},{1,9},{5... | collective-permute-start | bytes 221192 | tf_op jit(solution)/shard_map/ppermute | solution.py:226
  152.3 5.1 %collective-permute-done.33 = f32[72,256]{1,0:T(8,128)S(1)} collective-permute-done((f32[72,256]{1,0:T(8,128)S(1)}, f32[72,256]{1,0:T(8,128)S(1)}, u32[]{:S(2)}, u32[]{:S(2)}) %collective-permute-start.33) | collective-permute-done | bytes 73760 | tf_op jit(solution)/shard_map/ppermute | solution.py:226
  (163 shorter events, 42.6 us)
Async XLA Ops:
  2.6 9.4 %collective-permute-start.2 = (f32[1,72,256]{2,1,0:T(8,128)S(1)}, f32[1,72,256]{2,1,0:T(8,128)S(1)}, u32[]{:S(2)}, u32[]{:S(2)}) collective-permute-start(f32[1,72,256]{2,1,0:T(8,128)S(1)} %fusion.43), channel_id=1, source_target_pairs={{0,3},{1,2},{2,1},{3,0},{4,7},{5,6},{6,5},{7,4},{8,11},{9,10},{10,... | collective-permute-start | bytes 221192 | tf_op jit(solution)/shard_map/ppermute | solution.py:208
  6.6 5.4 %collective-permute-start.1 = (f32[1,72,256]{2,1,0:T(8,128)S(1)}, f32[1,72,256]{2,1,0:T(8,128)S(1)}, u32[]{:S(2)}, u32[]{:S(2)}) collective-permute-start(f32[1,72,256]{2,1,0:T(8,128)S(1)} %fusion.43), channel_id=1, source_target_pairs={{0,2},{1,3},{2,0},{3,1},{4,6},{5,7},{6,4},{7,5},{8,10},{9,11},{10,... | collective-permute-start | bytes 221192 | tf_op jit(solution)/shard_map/ppermute | solution.py:208
  7.1 4.9 %collective-permute-start = (f32[1,72,256]{2,1,0:T(8,128)S(1)}, f32[1,72,256]{2,1,0:T(8,128)S(1)}, u32[]{:S(2)}, u32[]{:S(2)}) collective-permute-start(f32[1,72,256]{2,1,0:T(8,128)S(1)} %fusion.43), channel_id=1, source_target_pairs={{0,1},{1,0},{2,3},{3,2},{4,5},{5,4},{6,7},{7,6},{8,9},{9,8},{10,11... | collective-permute-start | bytes 221192 | tf_op jit(solution)/shard_map/ppermute | solution.py:208
  18.9 3.9 %collective-permute-start.3 = (f32[4,72,256]{2,1,0:T(8,128)}, f32[4,72,256]{2,1,0:T(8,128)S(1)}, u32[]{:S(2)}, u32[]{:S(2)}) collective-permute-start(f32[4,72,256]{2,1,0:T(8,128)} %get-tuple-element.103), channel_id=1, source_target_pairs={{0,4},{4,0},{8,12},{12,8},{16,20},{20,16},{24,28},{28,24},{1,5},{5... | collective-permute-start | bytes 884744 | tf_op jit(solution)/shard_map/ppermute | solution.py:222
  23.8 7.8 %collective-permute-start.6 = (f32[72,256]{1,0:T(8,128)S(1)}, f32[72,256]{1,0:T(8,128)S(1)}, u32[]{:S(2)}, u32[]{:S(2)}) collective-permute-start(f32[72,256]{1,0:T(8,128)S(1)} %get-tuple-element.142), channel_id=1, source_target_pairs={{0,24},{4,28},{8,0},{12,4},{16,8},{20,12},{24,16},{28,20},{1,25},{... | collective-permute-start | bytes 221192 | tf_op jit(solution)/shard_map/ppermute | solution.py:226
  29.0 7.4 %collective-permute-start.5 = (f32[72,256]{1,0:T(8,128)S(1)}, f32[72,256]{1,0:T(8,128)S(1)}, u32[]{:S(2)}, u32[]{:S(2)}) collective-permute-start(f32[72,256]{1,0:T(8,128)S(1)} %get-tuple-element.143), channel_id=1, source_target_pairs={{0,16},{4,20},{8,24},{12,28},{16,0},{20,4},{24,8},{28,12},{1,17},{... | collective-permute-start | bytes 221192 | tf_op jit(solution)/shard_map/ppermute | solution.py:226
  29.0 7.4 %collective-permute-start.4 = (f32[72,256]{1,0:T(8,128)S(1)}, f32[72,256]{1,0:T(8,128)S(1)}, u32[]{:S(2)}, u32[]{:S(2)}) collective-permute-start(f32[72,256]{1,0:T(8,128)S(1)} %get-tuple-element.141), channel_id=1, source_target_pairs={{0,8},{4,12},{8,16},{12,20},{16,24},{20,28},{24,0},{28,4},{1,9},{5... | collective-permute-start | bytes 221192 | tf_op jit(solution)/shard_map/ppermute | solution.py:226
  36.6 5.8 %collective-permute-start.9 = (f32[1,72,256]{2,1,0:T(8,128)S(1)}, f32[1,72,256]{2,1,0:T(8,128)S(1)}, u32[]{:S(2)}, u32[]{:S(2)}) collective-permute-start(f32[1,72,256]{2,1,0:T(8,128)S(1)} %fusion.39), channel_id=1, source_target_pairs={{0,3},{1,2},{2,1},{3,0},{4,7},{5,6},{6,5},{7,4},{8,11},{9,10},{10,... | collective-permute-start | bytes 221192 | tf_op jit(solution)/shard_map/ppermute | solution.py:208
  36.7 5.8 %collective-permute-start.8 = (f32[1,72,256]{2,1,0:T(8,128)S(1)}, f32[1,72,256]{2,1,0:T(8,128)S(1)}, u32[]{:S(2)}, u32[]{:S(2)}) collective-permute-start(f32[1,72,256]{2,1,0:T(8,128)S(1)} %fusion.39), channel_id=1, source_target_pairs={{0,2},{1,3},{2,0},{3,1},{4,6},{5,7},{6,4},{7,5},{8,10},{9,11},{10,... | collective-permute-start | bytes 221192 | tf_op jit(solution)/shard_map/ppermute | solution.py:208
  37.7 5.0 %collective-permute-start.7 = (f32[1,72,256]{2,1,0:T(8,128)S(1)}, f32[1,72,256]{2,1,0:T(8,128)S(1)}, u32[]{:S(2)}, u32[]{:S(2)}) collective-permute-start(f32[1,72,256]{2,1,0:T(8,128)S(1)} %fusion.39), channel_id=1, source_target_pairs={{0,1},{1,0},{2,3},{3,2},{4,5},{5,4},{6,7},{7,6},{8,9},{9,8},{10,11... | collective-permute-start | bytes 221192 | tf_op jit(solution)/shard_map/ppermute | solution.py:208
  49.5 3.7 %collective-permute-start.10 = (f32[4,72,256]{2,1,0:T(8,128)}, f32[4,72,256]{2,1,0:T(8,128)S(1)}, u32[]{:S(2)}, u32[]{:S(2)}) collective-permute-start(f32[4,72,256]{2,1,0:T(8,128)} %get-tuple-element.105), channel_id=1, source_target_pairs={{0,4},{4,0},{8,12},{12,8},{16,20},{20,16},{24,28},{28,24},{1,5},{5... | collective-permute-start | bytes 884744 | tf_op jit(solution)/shard_map/ppermute | solution.py:222
  54.3 6.7 %collective-permute-start.13 = (f32[72,256]{1,0:T(8,128)S(1)}, f32[72,256]{1,0:T(8,128)S(1)}, u32[]{:S(2)}, u32[]{:S(2)}) collective-permute-start(f32[72,256]{1,0:T(8,128)S(1)} %get-tuple-element.139), channel_id=1, source_target_pairs={{0,24},{4,28},{8,0},{12,4},{16,8},{20,12},{24,16},{28,20},{1,25},{... | collective-permute-start | bytes 221192 | tf_op jit(solution)/shard_map/ppermute | solution.py:226
  57.3 8.1 %collective-permute-start.12 = (f32[72,256]{1,0:T(8,128)S(1)}, f32[72,256]{1,0:T(8,128)S(1)}, u32[]{:S(2)}, u32[]{:S(2)}) collective-permute-start(f32[72,256]{1,0:T(8,128)S(1)} %get-tuple-element.140), channel_id=1, source_target_pairs={{0,16},{4,20},{8,24},{12,28},{16,0},{20,4},{24,8},{28,12},{1,17},{... | collective-permute-start | bytes 221192 | tf_op jit(solution)/shard_map/ppermute | solution.py:226
  57.8 7.6 %collective-permute-start.11 = (f32[72,256]{1,0:T(8,128)S(1)}, f32[72,256]{1,0:T(8,128)S(1)}, u32[]{:S(2)}, u32[]{:S(2)}) collective-permute-start(f32[72,256]{1,0:T(8,128)S(1)} %get-tuple-element.138), channel_id=1, source_target_pairs={{0,8},{4,12},{8,16},{12,20},{16,24},{20,28},{24,0},{28,4},{1,9},{5... | collective-permute-start | bytes 221192 | tf_op jit(solution)/shard_map/ppermute | solution.py:226
  65.6 5.5 %collective-permute-start.16 = (f32[1,72,256]{2,1,0:T(8,128)S(1)}, f32[1,72,256]{2,1,0:T(8,128)S(1)}, u32[]{:S(2)}, u32[]{:S(2)}) collective-permute-start(f32[1,72,256]{2,1,0:T(8,128)S(1)} %maximum_bitcast_fusion), channel_id=1, source_target_pairs={{0,3},{1,2},{2,1},{3,0},{4,7},{5,6},{6,5},{7,4},{8,11},{9,10},{10,... | collective-permute-start | bytes 221192 | tf_op jit(solution)/shard_map/ppermute | solution.py:208
  65.7 5.4 %collective-permute-start.15 = (f32[1,72,256]{2,1,0:T(8,128)S(1)}, f32[1,72,256]{2,1,0:T(8,128)S(1)}, u32[]{:S(2)}, u32[]{:S(2)}) collective-permute-start(f32[1,72,256]{2,1,0:T(8,128)S(1)} %maximum_bitcast_fusion), channel_id=1, source_target_pairs={{0,2},{1,3},{2,0},{3,1},{4,6},{5,7},{6,4},{7,5},{8,10},{9,11},{10,... | collective-permute-start | bytes 221192 | tf_op jit(solution)/shard_map/ppermute | solution.py:208
  66.3 5.1 %collective-permute-start.14 = (f32[1,72,256]{2,1,0:T(8,128)S(1)}, f32[1,72,256]{2,1,0:T(8,128)S(1)}, u32[]{:S(2)}, u32[]{:S(2)}) collective-permute-start(f32[1,72,256]{2,1,0:T(8,128)S(1)} %maximum_bitcast_fusion), channel_id=1, source_target_pairs={{0,1},{1,0},{2,3},{3,2},{4,5},{5,4},{6,7},{7,6},{8,9},{9,8},{10,11... | collective-permute-start | bytes 221192 | tf_op jit(solution)/shard_map/ppermute | solution.py:208
  80.3 3.7 %collective-permute-start.17 = (f32[1,2440]{1,0:T(1,128)S(1)}, f32[1,2440]{1,0:T(1,128)S(1)}, u32[]{:S(2)}, u32[]{:S(2)}) collective-permute-start(f32[1,2440]{1,0:T(1,128)S(1)} %broadcast_in_dim.21), channel_id=1, source_target_pairs={{0,1},{1,0},{2,3},{3,2},{4,5},{5,4},{6,7},{7,6},{8,9},{9,8},{10,11... | collective-permute-start | bytes 29288 | tf_op jit(solution)/shard_map/ppermute | solution.py:284
  83.0 4.6 %collective-permute-start.19 = (f32[1,2440]{1,0:T(1,128)S(1)}, f32[1,2440]{1,0:T(1,128)S(1)}, u32[]{:S(2)}, u32[]{:S(2)}) collective-permute-start(f32[1,2440]{1,0:T(1,128)S(1)} %broadcast_in_dim.21), channel_id=1, source_target_pairs={{0,3},{1,2},{2,1},{3,0},{4,7},{5,6},{6,5},{7,4},{8,11},{9,10},{10,... | collective-permute-start | bytes 29288 | tf_op jit(solution)/shard_map/ppermute | solution.py:284
  89.0 6.5 %collective-permute-start.21 = (f32[8,2440]{1,0:T(8,128)S(1)}, f32[8,2440]{1,0:T(8,128)S(1)}, u32[]{:S(2)}, u32[]{:S(2)}) collective-permute-start(f32[8,2440]{1,0:T(8,128)S(1)} %concatenate.64), channel_id=1, source_target_pairs={{0,8},{4,12},{8,16},{12,20},{16,24},{20,28},{24,0},{28,4},{1,9},{5... | collective-permute-start | bytes 234248 | tf_op jit(solution)/shard_map/ppermute | solution.py:296
  89.1 9.9 %collective-permute-start.22 = (f32[8,2440]{1,0:T(8,128)S(1)}, f32[8,2440]{1,0:T(8,128)S(1)}, u32[]{:S(2)}, u32[]{:S(2)}) collective-permute-start(f32[8,2440]{1,0:T(8,128)S(1)} %concatenate.64), channel_id=1, source_target_pairs={{0,16},{4,20},{8,24},{12,28},{16,0},{20,4},{24,8},{28,12},{1,17},{... | collective-permute-start | bytes 234248 | tf_op jit(solution)/shard_map/ppermute | solution.py:296
  92.4 6.6 %collective-permute-start.23 = (f32[8,2440]{1,0:T(8,128)S(1)}, f32[8,2440]{1,0:T(8,128)S(1)}, u32[]{:S(2)}, u32[]{:S(2)}) collective-permute-start(f32[8,2440]{1,0:T(8,128)S(1)} %concatenate.64), channel_id=1, source_target_pairs={{0,24},{4,28},{8,0},{12,4},{16,8},{20,12},{24,16},{28,20},{1,25},{... | collective-permute-start | bytes 234248 | tf_op jit(solution)/shard_map/ppermute | solution.py:296
  111.3 4.1 %collective-permute-start.24 = (f32[4,72,256]{2,1,0:T(8,128)}, f32[4,72,256]{2,1,0:T(8,128)S(1)}, u32[]{:S(2)}, u32[]{:S(2)}) collective-permute-start(f32[4,72,256]{2,1,0:T(8,128)} %get-tuple-element.107), channel_id=1, source_target_pairs={{0,4},{4,0},{8,12},{12,8},{16,20},{20,16},{24,28},{28,24},{1,5},{5... | collective-permute-start | bytes 884744 | tf_op jit(solution)/shard_map/ppermute | solution.py:222
  116.4 7.6 %collective-permute-start.27 = (f32[72,256]{1,0:T(8,128)S(1)}, f32[72,256]{1,0:T(8,128)S(1)}, u32[]{:S(2)}, u32[]{:S(2)}) collective-permute-start(f32[72,256]{1,0:T(8,128)S(1)} %get-tuple-element.135), channel_id=1, source_target_pairs={{0,24},{4,28},{8,0},{12,4},{16,8},{20,12},{24,16},{28,20},{1,25},{... | collective-permute-start | bytes 221192 | tf_op jit(solution)/shard_map/ppermute | solution.py:226
  121.4 7.3 %collective-permute-start.26 = (f32[72,256]{1,0:T(8,128)S(1)}, f32[72,256]{1,0:T(8,128)S(1)}, u32[]{:S(2)}, u32[]{:S(2)}) collective-permute-start(f32[72,256]{1,0:T(8,128)S(1)} %get-tuple-element.136), channel_id=1, source_target_pairs={{0,16},{4,20},{8,24},{12,28},{16,0},{20,4},{24,8},{28,12},{1,17},{... | collective-permute-start | bytes 221192 | tf_op jit(solution)/shard_map/ppermute | solution.py:226
  121.4 7.3 %collective-permute-start.25 = (f32[72,256]{1,0:T(8,128)S(1)}, f32[72,256]{1,0:T(8,128)S(1)}, u32[]{:S(2)}, u32[]{:S(2)}) collective-permute-start(f32[72,256]{1,0:T(8,128)S(1)} %get-tuple-element.137), channel_id=1, source_target_pairs={{0,8},{4,12},{8,16},{12,20},{16,24},{20,28},{24,0},{28,4},{1,9},{5... | collective-permute-start | bytes 221192 | tf_op jit(solution)/shard_map/ppermute | solution.py:226
  129.0 5.9 %collective-permute-start.30 = (f32[1,72,256]{2,1,0:T(8,128)S(1)}, f32[1,72,256]{2,1,0:T(8,128)S(1)}, u32[]{:S(2)}, u32[]{:S(2)}) collective-permute-start(f32[1,72,256]{2,1,0:T(8,128)S(1)} %fusion.35), channel_id=1, source_target_pairs={{0,3},{1,2},{2,1},{3,0},{4,7},{5,6},{6,5},{7,4},{8,11},{9,10},{10,... | collective-permute-start | bytes 221192 | tf_op jit(solution)/shard_map/ppermute | solution.py:208
  129.0 5.9 %collective-permute-start.29 = (f32[1,72,256]{2,1,0:T(8,128)S(1)}, f32[1,72,256]{2,1,0:T(8,128)S(1)}, u32[]{:S(2)}, u32[]{:S(2)}) collective-permute-start(f32[1,72,256]{2,1,0:T(8,128)S(1)} %fusion.35), channel_id=1, source_target_pairs={{0,2},{1,3},{2,0},{3,1},{4,6},{5,7},{6,4},{7,5},{8,10},{9,11},{10,... | collective-permute-start | bytes 221192 | tf_op jit(solution)/shard_map/ppermute | solution.py:208
  129.1 5.8 %collective-permute-start.28 = (f32[1,72,256]{2,1,0:T(8,128)S(1)}, f32[1,72,256]{2,1,0:T(8,128)S(1)}, u32[]{:S(2)}, u32[]{:S(2)}) collective-permute-start(f32[1,72,256]{2,1,0:T(8,128)S(1)} %fusion.35), channel_id=1, source_target_pairs={{0,1},{1,0},{2,3},{3,2},{4,5},{5,4},{6,7},{7,6},{8,9},{9,8},{10,11... | collective-permute-start | bytes 221192 | tf_op jit(solution)/shard_map/ppermute | solution.py:208
  146.1 6.2 %collective-permute-start.34 = (f32[72,256]{1,0:T(8,128)S(1)}, f32[72,256]{1,0:T(8,128)S(1)}, u32[]{:S(2)}, u32[]{:S(2)}) collective-permute-start(f32[72,256]{1,0:T(8,128)S(1)} %get-tuple-element.132), channel_id=1, source_target_pairs={{0,24},{4,28},{8,0},{12,4},{16,8},{20,12},{24,16},{28,20},{1,25},{... | collective-permute-start | bytes 221192 | tf_op jit(solution)/shard_map/ppermute | solution.py:226
  149.5 7.9 %collective-permute-start.33 = (f32[72,256]{1,0:T(8,128)S(1)}, f32[72,256]{1,0:T(8,128)S(1)}, u32[]{:S(2)}, u32[]{:S(2)}) collective-permute-start(f32[72,256]{1,0:T(8,128)S(1)} %get-tuple-element.133), channel_id=1, source_target_pairs={{0,16},{4,20},{8,24},{12,28},{16,0},{20,4},{24,8},{28,12},{1,17},{... | collective-permute-start | bytes 221192 | tf_op jit(solution)/shard_map/ppermute | solution.py:226
  149.6 7.8 %collective-permute-start.32 = (f32[72,256]{1,0:T(8,128)S(1)}, f32[72,256]{1,0:T(8,128)S(1)}, u32[]{:S(2)}, u32[]{:S(2)}) collective-permute-start(f32[72,256]{1,0:T(8,128)S(1)} %get-tuple-element.131), channel_id=1, source_target_pairs={{0,8},{4,12},{8,16},{12,20},{16,24},{20,28},{24,0},{28,4},{1,9},{5... | collective-permute-start | bytes 221192 | tf_op jit(solution)/shard_map/ppermute | solution.py:226
  (10 other events, 160.1 us)

commit v8 on v7

--- a/solution.py
+++ b/solution.py
@@ -31,6 +31,10 @@
                 )
     else:
         (o_ref,) = refs
+
+        @pl.when(step == 0)
+        def _():
+            o_ref[...] = jnp.zeros_like(o_ref)
 
     @pl.when(step < nb_ref[0])
     def _():
@@ -54,13 +58,9 @@
                         mask = jnp.where(spot // part_size == q, 1.0, 0.0)
                         out_ref[window] = out_ref[window] + product * mask
             else:
-                o_ref[g] = product[:, :128] + product[:, 128:]
-
-    if mode == "entries":
-
-        @pl.when(step >= nb_ref[0])
-        def _():
-            o_ref[...] = jnp.zeros_like(o_ref)
+                row_sum = jnp.sum(product, axis=1, keepdims=True)
+                lane = lax.broadcasted_iota(jnp.int32, o_ref.shape, 1)
+                o_ref[...] = o_ref[...] + jnp.where(lane == slot, row_sum, 0.0)
 
 
 def tile_pass(mode, x_cols, tiles, rows, cols, live, block_count, row_blocks, vectors, lost=None):
@@ -79,8 +79,8 @@
         out_shape = [jax.ShapeDtypeStruct(part_shape, jnp.float32)] * parts
         out_spec = [pl.BlockSpec(part_shape, lambda i, *_: (0, 0, 0))] * parts
     else:
-        out_shape = jax.ShapeDtypeStruct((slots, vectors, 128), jnp.float32)
-        out_spec = pl.BlockSpec((group_size, vectors, 128), lambda i, *_: (i, 0, 0))
+        out_shape = jax.ShapeDtypeStruct((vectors, slots), jnp.float32)
+        out_spec = pl.BlockSpec((vectors, slots), lambda i, *_: (0, 0))
     in_specs = [
         pl.BlockSpec((groups, padded_rows, side), lambda i, *_: (0, 0, 0)),
         pl.BlockSpec((None, None, group_size, side, side), tile_index),
@@ -262,7 +262,7 @@
     entries = tile_pass(
         "entries", gathered, tiles, own_rows, kernel_cols, live_mask, block_count,
         row_blocks, vectors,
-    ).sum(axis=2)
+    ).T
     block_sums = jnp.sum(relaxed_two, axis=2)
     row_agg = agg_of_block[row_global]
     col_agg = agg_of_block[col_global]

time: 158 us -> 151 us (0.956); the launches traced: 158 us -> 149 us
  starting transfers between devices: 57.2 us -> 41.6 us
  waiting for transfers between devices: 41.1 us -> 49.3 us
  other arithmetic: 13.7 us -> 12.1 us
    ppermute x4, starting transfers between devices: 9.46 us -> 0.01 us  [reduce_rows(): part = keep + lax.ppermute(give, 'src', [(i, i ^ 1) for i in range(n)])]
    ppermute x12, starting transfers between devices: 22.7 us -> 13.3 us  [reduce_rows(): total = total + lax.ppermute(part[shift], 'src', pairs)]
    ppermute x12, waiting for transfers between devices: 5.87 us -> 11.5 us  [spread_columns(): lax.ppermute(payload, 'dst', [(i, i ^ v) for i in range(dst_count)])]
    ppermute x12, starting transfers between devices: 15.2 us -> 19.5 us  [spread_columns(): lax.ppermute(payload, 'dst', [(i, i ^ v) for i in range(dst_count)])]
  transfers between devices with their start and end apart: 35 -> 35, of which waited for: 21 -> 25; matrix products, arithmetic and copies ran while one was open for 6% -> 6% of each run, Pallas kernels for 0% -> 0%
where the time goes in v8:
time: 151 us; the launch traced here: 149 us
  waiting for transfers between devices  49.3 us (33%)
  starting transfers between devices  41.6 us (28%)
  Pallas kernels  29.9 us (20%)
  other arithmetic  12.1 us (8%)
  local copies, waits for them, and re-layouts  11.7 us (8%)
  matrix products  3 us (2%)
  between operations  1.76 us (1%)
    pallas_call x5, Pallas kernels, tile_pass(): pl.pallas_call(functools.partial(tile_kernel, mode, blocks_piece, vectors...  29.9 us
    ppermute x12, waiting for transfers between devices, reduce_rows(): total = total + lax.ppermute(part[shift], 'src', pairs)  23.3 us
    ppermute x12, starting transfers between devices, spread_columns(): lax.ppermute(payload, 'dst', [(i, i ^ v) for i in range(dst_count)])  19.5 us
    ppermute x12, starting transfers between devices, reduce_rows(): total = total + lax.ppermute(part[shift], 'src', pairs)  13.3 us
    ppermute x12, waiting for transfers between devices, spread_columns(): lax.ppermute(payload, 'dst', [(i, i ^ v) for i in range(dst_count)])  11.5 us
    ppermute x4, waiting for transfers between devices, reduce_rows(): part = keep + lax.ppermute(give, 'src', [(i, i ^ 1) for i in range(n)])  6.31 us
    ppermute x3, starting transfers between devices, per_device(): pieces.append(lax.ppermute(shared, 'src', pairs))  5.16 us
    ppermute x3, waiting for transfers between devices, per_device(): pieces.append(lax.ppermute(shared, 'src', pairs))  4.8 us
  transfers between devices with their start and end apart: 35, of which 25 were waited for; matrix products, arithmetic and copies ran while one was open for 6% of the time, Pallas kernels for 0%

profile of v8, /device:TPU:0, one launch (start us, length us, event | category | flops | bytes accessed | tf_op | source)
XLA Modules:
  0.0 149.3 jit_solution(4908661096956400434)
XLA Ops:
  2.6 4.0 %collective-permute-start.2 = (f32[1,72,256]{2,1,0:T(8,128)S(1)}, f32[1,72,256]{2,1,0:T(8,128)S(1)}, u32[]{:S(2)}, u32[]{:S(2)}) collective-permute-start(f32[1,72,256]{2,1,0:T(8,128)S(1)} %fusion.43), channel_id=1, source_target_pairs={{0,3},{1,2},{2,1},{3,0},{4,7},{5,6},{6,5},{7,4},{8,11},{9,10},{10,... | collective-permute-start | bytes 221192 | tf_op jit(solution)/shard_map/ppermute | solution.py:208
  12.8 6.1 %shard_map.95 = (f32[4,72,256]{2,1,0:T(8,128)}, f32[4,72,256]{2,1,0:T(8,128)}) custom-call(s32[128]{0:T(128)} %get-tuple-element.155.rows_ref, s32[128]{0:T(128)} %get-tuple-element.156.cols_ref, s32[128]{0:T(128)} %and_convert_fusion.live_ref, s32[1]{0:T(128)} %bitcast.5.nb_ref, f32[4,72,256]{2,1,0:T(8,128)} %copy-done.2, ...), custom_call_target="tpu_custom_call" | custom-call | tf_op jit(solution)/shard_map/pallas_call | solution.py:100
  19.0 1.7 %collective-permute-done.3 = f32[4,72,256]{2,1,0:T(8,128)S(1)} collective-permute-done((f32[4,72,256]{2,1,0:T(8,128)}, f32[4,72,256]{2,1,0:T(8,128)S(1)}, u32[]{:S(2)}, u32[]{:S(2)}) %collective-permute-start.3) | collective-permute-done | bytes 294944 | tf_op jit(solution)/shard_map/ppermute | solution.py:222
  21.7 4.1 %collective-permute-start.6 = (f32[72,256]{1,0:T(8,128)S(1)}, f32[72,256]{1,0:T(8,128)S(1)}, u32[]{:S(2)}, u32[]{:S(2)}) collective-permute-start(f32[72,256]{1,0:T(8,128)S(1)} %get-tuple-element.142), channel_id=1, source_target_pairs={{0,24},{4,28},{8,0},{12,4},{16,8},{20,12},{24,16},{28,20},{1,25},{... | collective-permute-start | bytes 221192 | tf_op jit(solution)/shard_map/ppermute | solution.py:226
  28.4 4.7 %collective-permute-done.5 = f32[72,256]{1,0:T(8,128)S(1)} collective-permute-done((f32[72,256]{1,0:T(8,128)S(1)}, f32[72,256]{1,0:T(8,128)S(1)}, u32[]{:S(2)}, u32[]{:S(2)}) %collective-permute-start.5) | collective-permute-done | bytes 73760 | tf_op jit(solution)/shard_map/ppermute | solution.py:226
  33.4 3.5 %collective-permute-start.9 = (f32[1,72,256]{2,1,0:T(8,128)S(1)}, f32[1,72,256]{2,1,0:T(8,128)S(1)}, u32[]{:S(2)}, u32[]{:S(2)}) collective-permute-start(f32[1,72,256]{2,1,0:T(8,128)S(1)} %fusion.39), channel_id=1, source_target_pairs={{0,3},{1,2},{2,1},{3,0},{4,7},{5,6},{6,5},{7,4},{8,11},{9,10},{10,... | collective-permute-start | bytes 221192 | tf_op jit(solution)/shard_map/ppermute | solution.py:208
  36.9 1.8 %collective-permute-start.8 = (f32[1,72,256]{2,1,0:T(8,128)S(1)}, f32[1,72,256]{2,1,0:T(8,128)S(1)}, u32[]{:S(2)}, u32[]{:S(2)}) collective-permute-start(f32[1,72,256]{2,1,0:T(8,128)S(1)} %fusion.39), channel_id=1, source_target_pairs={{0,2},{1,3},{2,0},{3,1},{4,6},{5,7},{6,4},{7,5},{8,10},{9,11},{10,... | collective-permute-start | bytes 221192 | tf_op jit(solution)/shard_map/ppermute | solution.py:208
  39.4 1.9 %collective-permute-done.8 = f32[1,72,256]{2,1,0:T(8,128)S(1)} collective-permute-done((f32[1,72,256]{2,1,0:T(8,128)S(1)}, f32[1,72,256]{2,1,0:T(8,128)S(1)}, u32[]{:S(2)}, u32[]{:S(2)}) %collective-permute-start.8) | collective-permute-done | bytes 73760 | tf_op jit(solution)/shard_map/ppermute | solution.py:208
  41.3 1.8 %collective-permute-done.7 = f32[1,72,256]{2,1,0:T(8,128)S(1)} collective-permute-done((f32[1,72,256]{2,1,0:T(8,128)S(1)}, f32[1,72,256]{2,1,0:T(8,128)S(1)}, u32[]{:S(2)}, u32[]{:S(2)}) %collective-permute-start.7) | collective-permute-done | bytes 73760 | tf_op jit(solution)/shard_map/ppermute | solution.py:208
  43.8 6.0 %shard_map.96 = (f32[4,72,256]{2,1,0:T(8,128)}, f32[4,72,256]{2,1,0:T(8,128)}) custom-call(s32[128]{0:T(128)} %get-tuple-element.155.rows_ref, s32[128]{0:T(128)} %get-tuple-element.156.cols_ref, s32[128]{0:T(128)} %and_convert_fusion.live_ref, s32[1]{0:T(128)} %bitcast.5.nb_ref, f32[4,72,256]{2,1,0:T(8,128)} %copy-done.3, ...), custom_call_target="tpu_custom_call" | custom-call | tf_op jit(solution)/shard_map/pallas_call | solution.py:100
  53.2 1.8 %collective-permute-start.11 = (f32[72,256]{1,0:T(8,128)S(1)}, f32[72,256]{1,0:T(8,128)S(1)}, u32[]{:S(2)}, u32[]{:S(2)}) collective-permute-start(f32[72,256]{1,0:T(8,128)S(1)} %get-tuple-element.138), channel_id=1, source_target_pairs={{0,8},{4,12},{8,16},{12,20},{16,24},{20,28},{24,0},{28,4},{1,9},{5... | collective-permute-start | bytes 221192 | tf_op jit(solution)/shard_map/ppermute | solution.py:226
  56.3 1.9 %collective-permute-done.13 = f32[72,256]{1,0:T(8,128)S(1)} collective-permute-done((f32[72,256]{1,0:T(8,128)S(1)}, f32[72,256]{1,0:T(8,128)S(1)}, u32[]{:S(2)}, u32[]{:S(2)}) %collective-permute-start.13) | collective-permute-done | bytes 73760 | tf_op jit(solution)/shard_map/ppermute | solution.py:226
  58.2 3.0 %collective-permute-done.12 = f32[72,256]{1,0:T(8,128)S(1)} collective-permute-done((f32[72,256]{1,0:T(8,128)S(1)}, f32[72,256]{1,0:T(8,128)S(1)}, u32[]{:S(2)}, u32[]{:S(2)}) %collective-permute-start.12) | collective-permute-done | bytes 73760 | tf_op jit(solution)/shard_map/ppermute | solution.py:226
  61.4 2.6 %collective-permute-start.16 = (f32[1,72,256]{2,1,0:T(8,128)S(1)}, f32[1,72,256]{2,1,0:T(8,128)S(1)}, u32[]{:S(2)}, u32[]{:S(2)}) collective-permute-start(f32[1,72,256]{2,1,0:T(8,128)S(1)} %maximum_bitcast_fusion), channel_id=1, source_target_pairs={{0,3},{1,2},{2,1},{3,0},{4,7},{5,6},{6,5},{7,4},{8,11},{9,10},{10,... | collective-permute-start | bytes 221192 | tf_op jit(solution)/shard_map/ppermute | solution.py:208
  70.6 5.6 %shard_map.97 = f32[16,128]{1,0:T(8,128)} custom-call(s32[128]{0:T(128)} %clamp_bitcast_fusion.rows_ref, s32[128]{0:T(128)} %get-tuple-element.156.cols_ref, s32[128]{0:T(128)} %and_convert_fusion.live_ref, s32[1]{0:T(128)} %bitcast.5.nb_ref, f32[4,72,256]{2,1,0:T(8,128)} %pad_maximum_fusion.2.x_ref, bf16[1,1,128,256,256]{4,3,2,1,0:T(8,128)(2,1)} %t_ref.9), custom_call_target="tpu_custom_call" | custom-call | tf_op jit(solution)/shard_map/pallas_call | solution.py:100
  78.3 2.4 %collective-permute-start.19 = (f32[1,2440]{1,0:T(1,128)S(1)}, f32[1,2440]{1,0:T(1,128)S(1)}, u32[]{:S(2)}, u32[]{:S(2)}) collective-permute-start(f32[1,2440]{1,0:T(1,128)S(1)} %broadcast_in_dim.21), channel_id=1, source_target_pairs={{0,3},{1,2},{2,1},{3,0},{4,7},{5,6},{6,5},{7,4},{8,11},{9,10},{10,... | collective-permute-start | bytes 29288 | tf_op jit(solution)/shard_map/ppermute | solution.py:284
  81.0 1.9 %collective-permute-done.19 = f32[1,2440]{1,0:T(1,128)S(1)} collective-permute-done((f32[1,2440]{1,0:T(1,128)S(1)}, f32[1,2440]{1,0:T(1,128)S(1)}, u32[]{:S(2)}, u32[]{:S(2)}) %collective-permute-start.19) | collective-permute-done | bytes 9792 | tf_op jit(solution)/shard_map/ppermute | solution.py:284
  86.6 2.8 %collective-permute-start.23 = (f32[8,2440]{1,0:T(8,128)S(1)}, f32[8,2440]{1,0:T(8,128)S(1)}, u32[]{:S(2)}, u32[]{:S(2)}) collective-permute-start(f32[8,2440]{1,0:T(8,128)S(1)} %concatenate.64), channel_id=1, source_target_pairs={{0,24},{4,28},{8,0},{12,4},{16,8},{20,12},{24,16},{28,20},{1,25},{... | collective-permute-start | bytes 234248 | tf_op jit(solution)/shard_map/ppermute | solution.py:296
  89.5 1.9 %collective-permute-done.21 = f32[8,2440]{1,0:T(8,128)S(1)} collective-permute-done((f32[8,2440]{1,0:T(8,128)S(1)}, f32[8,2440]{1,0:T(8,128)S(1)}, u32[]{:S(2)}, u32[]{:S(2)}) %collective-permute-start.21) | collective-permute-done | bytes 78112 | tf_op jit(solution)/shard_map/ppermute | solution.py:296
  91.4 2.9 %collective-permute-done.22 = f32[8,2440]{1,0:T(8,128)S(1)} collective-permute-done((f32[8,2440]{1,0:T(8,128)S(1)}, f32[8,2440]{1,0:T(8,128)S(1)}, u32[]{:S(2)}, u32[]{:S(2)}) %collective-permute-start.22) | collective-permute-done | bytes 78112 | tf_op jit(solution)/shard_map/ppermute | solution.py:296
  100.5 6.1 %shard_map.98 = (f32[4,72,256]{2,1,0:T(8,128)}, f32[4,72,256]{2,1,0:T(8,128)}) custom-call(s32[128]{0:T(128)} %get-tuple-element.155.rows_ref, s32[128]{0:T(128)} %get-tuple-element.156.cols_ref, s32[128]{0:T(128)} %and_convert_fusion.live_ref, s32[1]{0:T(128)} %bitcast.5.nb_ref, f32[4,72,256]{2,1,0:T(8,128)} %broadcast_multiply_fusion.x_ref, ...), custom_call_target="tpu_custom_call" | custom-call | tf_op jit(solution)/shard_map/pallas_call | solution.py:100
  106.7 1.8 %collective-permute-done.24 = f32[4,72,256]{2,1,0:T(8,128)S(1)} collective-permute-done((f32[4,72,256]{2,1,0:T(8,128)}, f32[4,72,256]{2,1,0:T(8,128)S(1)}, u32[]{:S(2)}, u32[]{:S(2)}) %collective-permute-start.24) | collective-permute-done | bytes 294944 | tf_op jit(solution)/shard_map/ppermute | solution.py:222
  109.5 3.2 %collective-permute-start.27 = (f32[72,256]{1,0:T(8,128)S(1)}, f32[72,256]{1,0:T(8,128)S(1)}, u32[]{:S(2)}, u32[]{:S(2)}) collective-permute-start(f32[72,256]{1,0:T(8,128)S(1)} %get-tuple-element.135), channel_id=1, source_target_pairs={{0,24},{4,28},{8,0},{12,4},{16,8},{20,12},{24,16},{28,20},{1,25},{... | collective-permute-start | bytes 221192 | tf_op jit(solution)/shard_map/ppermute | solution.py:226
  113.3 2.0 %collective-permute-done.27 = f32[72,256]{1,0:T(8,128)S(1)} collective-permute-done((f32[72,256]{1,0:T(8,128)S(1)}, f32[72,256]{1,0:T(8,128)S(1)}, u32[]{:S(2)}, u32[]{:S(2)}) %collective-permute-start.27) | collective-permute-done | bytes 73760 | tf_op jit(solution)/shard_map/ppermute | solution.py:226
  115.3 4.9 %collective-permute-done.26 = f32[72,256]{1,0:T(8,128)S(1)} collective-permute-done((f32[72,256]{1,0:T(8,128)S(1)}, f32[72,256]{1,0:T(8,128)S(1)}, u32[]{:S(2)}, u32[]{:S(2)}) %collective-permute-start.26) | collective-permute-done | bytes 73760 | tf_op jit(solution)/shard_map/ppermute | solution.py:226
  120.5 2.0 %collective-permute-start.30 = (f32[1,72,256]{2,1,0:T(8,128)S(1)}, f32[1,72,256]{2,1,0:T(8,128)S(1)}, u32[]{:S(2)}, u32[]{:S(2)}) collective-permute-start(f32[1,72,256]{2,1,0:T(8,128)S(1)} %fusion.35), channel_id=1, source_target_pairs={{0,3},{1,2},{2,1},{3,0},{4,7},{5,6},{6,5},{7,4},{8,11},{9,10},{10,... | collective-permute-start | bytes 221192 | tf_op jit(solution)/shard_map/ppermute | solution.py:208
  122.5 3.5 %collective-permute-start.29 = (f32[1,72,256]{2,1,0:T(8,128)S(1)}, f32[1,72,256]{2,1,0:T(8,128)S(1)}, u32[]{:S(2)}, u32[]{:S(2)}) collective-permute-start(f32[1,72,256]{2,1,0:T(8,128)S(1)} %fusion.35), channel_id=1, source_target_pairs={{0,2},{1,3},{2,0},{3,1},{4,6},{5,7},{6,4},{7,5},{8,10},{9,11},{10,... | collective-permute-start | bytes 221192 | tf_op jit(solution)/shard_map/ppermute | solution.py:208
  126.1 2.3 %collective-permute-done.29 = f32[1,72,256]{2,1,0:T(8,128)S(1)} collective-permute-done((f32[1,72,256]{2,1,0:T(8,128)S(1)}, f32[1,72,256]{2,1,0:T(8,128)S(1)}, u32[]{:S(2)}, u32[]{:S(2)}) %collective-permute-start.29) | collective-permute-done | bytes 73760 | tf_op jit(solution)/shard_map/ppermute | solution.py:208
  128.4 2.0 %collective-permute-done.28 = f32[1,72,256]{2,1,0:T(8,128)S(1)} collective-permute-done((f32[1,72,256]{2,1,0:T(8,128)S(1)}, f32[1,72,256]{2,1,0:T(8,128)S(1)}, u32[]{:S(2)}, u32[]{:S(2)}) %collective-permute-start.28) | collective-permute-done | bytes 73760 | tf_op jit(solution)/shard_map/ppermute | solution.py:208
  131.1 6.0 %shard_map.99 = (f32[4,72,256]{2,1,0:T(8,128)}, f32[4,72,256]{2,1,0:T(8,128)}) custom-call(s32[128]{0:T(128)} %get-tuple-element.155.rows_ref, s32[128]{0:T(128)} %get-tuple-element.156.cols_ref, s32[128]{0:T(128)} %and_convert_fusion.live_ref, s32[1]{0:T(128)} %bitcast.5.nb_ref, f32[4,72,256]{2,1,0:T(8,128)} %copy-done.1, ...), custom_call_target="tpu_custom_call" | custom-call | tf_op jit(solution)/shard_map/pallas_call | solution.py:100
  142.7 2.7 %collective-permute-done.34 = f32[72,256]{1,0:T(8,128)S(1)} collective-permute-done((f32[72,256]{1,0:T(8,128)S(1)}, f32[72,256]{1,0:T(8,128)S(1)}, u32[]{:S(2)}, u32[]{:S(2)}) %collective-permute-start.34) | collective-permute-done | bytes 73760 | tf_op jit(solution)/shard_map/ppermute | solution.py:226
  145.5 3.0 %collective-permute-done.33 = f32[72,256]{1,0:T(8,128)S(1)} collective-permute-done((f32[72,256]{1,0:T(8,128)S(1)}, f32[72,256]{1,0:T(8,128)S(1)}, u32[]{:S(2)}, u32[]{:S(2)}) %collective-permute-start.33) | collective-permute-done | bytes 73760 | tf_op jit(solution)/shard_map/ppermute | solution.py:226
  (163 shorter events, 45.6 us)
Async XLA Ops:
  2.6 9.4 %collective-permute-start.2 = (f32[1,72,256]{2,1,0:T(8,128)S(1)}, f32[1,72,256]{2,1,0:T(8,128)S(1)}, u32[]{:S(2)}, u32[]{:S(2)}) collective-permute-start(f32[1,72,256]{2,1,0:T(8,128)S(1)} %fusion.43), channel_id=1, source_target_pairs={{0,3},{1,2},{2,1},{3,0},{4,7},{5,6},{6,5},{7,4},{8,11},{9,10},{10,... | collective-permute-start | bytes 221192 | tf_op jit(solution)/shard_map/ppermute | solution.py:208
  6.6 5.4 %collective-permute-start.1 = (f32[1,72,256]{2,1,0:T(8,128)S(1)}, f32[1,72,256]{2,1,0:T(8,128)S(1)}, u32[]{:S(2)}, u32[]{:S(2)}) collective-permute-start(f32[1,72,256]{2,1,0:T(8,128)S(1)} %fusion.43), channel_id=1, source_target_pairs={{0,2},{1,3},{2,0},{3,1},{4,6},{5,7},{6,4},{7,5},{8,10},{9,11},{10,... | collective-permute-start | bytes 221192 | tf_op jit(solution)/shard_map/ppermute | solution.py:208
  7.1 4.9 %collective-permute-start = (f32[1,72,256]{2,1,0:T(8,128)S(1)}, f32[1,72,256]{2,1,0:T(8,128)S(1)}, u32[]{:S(2)}, u32[]{:S(2)}) collective-permute-start(f32[1,72,256]{2,1,0:T(8,128)S(1)} %fusion.43), channel_id=1, source_target_pairs={{0,1},{1,0},{2,3},{3,2},{4,5},{5,4},{6,7},{7,6},{8,9},{9,8},{10,11... | collective-permute-start | bytes 221192 | tf_op jit(solution)/shard_map/ppermute | solution.py:208
  18.9 1.8 %collective-permute-start.3 = (f32[4,72,256]{2,1,0:T(8,128)}, f32[4,72,256]{2,1,0:T(8,128)S(1)}, u32[]{:S(2)}, u32[]{:S(2)}) collective-permute-start(f32[4,72,256]{2,1,0:T(8,128)} %get-tuple-element.103), channel_id=1, source_target_pairs={{0,4},{4,0},{8,12},{12,8},{16,20},{20,16},{24,28},{28,24},{1,5},{5... | collective-permute-start | bytes 884744 | tf_op jit(solution)/shard_map/ppermute | solution.py:222
  21.7 6.7 %collective-permute-start.6 = (f32[72,256]{1,0:T(8,128)S(1)}, f32[72,256]{1,0:T(8,128)S(1)}, u32[]{:S(2)}, u32[]{:S(2)}) collective-permute-start(f32[72,256]{1,0:T(8,128)S(1)} %get-tuple-element.142), channel_id=1, source_target_pairs={{0,24},{4,28},{8,0},{12,4},{16,8},{20,12},{24,16},{28,20},{1,25},{... | collective-permute-start | bytes 221192 | tf_op jit(solution)/shard_map/ppermute | solution.py:226
  25.8 7.4 %collective-permute-start.5 = (f32[72,256]{1,0:T(8,128)S(1)}, f32[72,256]{1,0:T(8,128)S(1)}, u32[]{:S(2)}, u32[]{:S(2)}) collective-permute-start(f32[72,256]{1,0:T(8,128)S(1)} %get-tuple-element.143), channel_id=1, source_target_pairs={{0,16},{4,20},{8,24},{12,28},{16,0},{20,4},{24,8},{28,12},{1,17},{... | collective-permute-start | bytes 221192 | tf_op jit(solution)/shard_map/ppermute | solution.py:226
  25.8 7.4 %collective-permute-start.4 = (f32[72,256]{1,0:T(8,128)S(1)}, f32[72,256]{1,0:T(8,128)S(1)}, u32[]{:S(2)}, u32[]{:S(2)}) collective-permute-start(f32[72,256]{1,0:T(8,128)S(1)} %get-tuple-element.141), channel_id=1, source_target_pairs={{0,8},{4,12},{8,16},{12,20},{16,24},{20,28},{24,0},{28,4},{1,9},{5... | collective-permute-start | bytes 221192 | tf_op jit(solution)/shard_map/ppermute | solution.py:226
  33.4 5.9 %collective-permute-start.9 = (f32[1,72,256]{2,1,0:T(8,128)S(1)}, f32[1,72,256]{2,1,0:T(8,128)S(1)}, u32[]{:S(2)}, u32[]{:S(2)}) collective-permute-start(f32[1,72,256]{2,1,0:T(8,128)S(1)} %fusion.39), channel_id=1, source_target_pairs={{0,3},{1,2},{2,1},{3,0},{4,7},{5,6},{6,5},{7,4},{8,11},{9,10},{10,... | collective-permute-start | bytes 221192 | tf_op jit(solution)/shard_map/ppermute | solution.py:208
  36.9 4.4 %collective-permute-start.8 = (f32[1,72,256]{2,1,0:T(8,128)S(1)}, f32[1,72,256]{2,1,0:T(8,128)S(1)}, u32[]{:S(2)}, u32[]{:S(2)}) collective-permute-start(f32[1,72,256]{2,1,0:T(8,128)S(1)} %fusion.39), channel_id=1, source_target_pairs={{0,2},{1,3},{2,0},{3,1},{4,6},{5,7},{6,4},{7,5},{8,10},{9,11},{10,... | collective-permute-start | bytes 221192 | tf_op jit(solution)/shard_map/ppermute | solution.py:208
  38.7 4.4 %collective-permute-start.7 = (f32[1,72,256]{2,1,0:T(8,128)S(1)}, f32[1,72,256]{2,1,0:T(8,128)S(1)}, u32[]{:S(2)}, u32[]{:S(2)}) collective-permute-start(f32[1,72,256]{2,1,0:T(8,128)S(1)} %fusion.39), channel_id=1, source_target_pairs={{0,1},{1,0},{2,3},{3,2},{4,5},{5,4},{6,7},{7,6},{8,9},{9,8},{10,11... | collective-permute-start | bytes 221192 | tf_op jit(solution)/shard_map/ppermute | solution.py:208
  49.8 1.8 %collective-permute-start.10 = (f32[4,72,256]{2,1,0:T(8,128)}, f32[4,72,256]{2,1,0:T(8,128)S(1)}, u32[]{:S(2)}, u32[]{:S(2)}) collective-permute-start(f32[4,72,256]{2,1,0:T(8,128)} %get-tuple-element.105), channel_id=1, source_target_pairs={{0,4},{4,0},{8,12},{12,8},{16,20},{20,16},{24,28},{28,24},{1,5},{5... | collective-permute-start | bytes 884744 | tf_op jit(solution)/shard_map/ppermute | solution.py:222
  52.6 5.6 %collective-permute-start.13 = (f32[72,256]{1,0:T(8,128)S(1)}, f32[72,256]{1,0:T(8,128)S(1)}, u32[]{:S(2)}, u32[]{:S(2)}) collective-permute-start(f32[72,256]{1,0:T(8,128)S(1)} %get-tuple-element.139), channel_id=1, source_target_pairs={{0,24},{4,28},{8,0},{12,4},{16,8},{20,12},{24,16},{28,20},{1,25},{... | collective-permute-start | bytes 221192 | tf_op jit(solution)/shard_map/ppermute | solution.py:226
  52.7 8.5 %collective-permute-start.12 = (f32[72,256]{1,0:T(8,128)S(1)}, f32[72,256]{1,0:T(8,128)S(1)}, u32[]{:S(2)}, u32[]{:S(2)}) collective-permute-start(f32[72,256]{1,0:T(8,128)S(1)} %get-tuple-element.140), channel_id=1, source_target_pairs={{0,16},{4,20},{8,24},{12,28},{16,0},{20,4},{24,8},{28,12},{1,17},{... | collective-permute-start | bytes 221192 | tf_op jit(solution)/shard_map/ppermute | solution.py:226
  53.2 8.0 %collective-permute-start.11 = (f32[72,256]{1,0:T(8,128)S(1)}, f32[72,256]{1,0:T(8,128)S(1)}, u32[]{:S(2)}, u32[]{:S(2)}) collective-permute-start(f32[72,256]{1,0:T(8,128)S(1)} %get-tuple-element.138), channel_id=1, source_target_pairs={{0,8},{4,12},{8,16},{12,20},{16,24},{20,28},{24,0},{28,4},{1,9},{5... | collective-permute-start | bytes 221192 | tf_op jit(solution)/shard_map/ppermute | solution.py:226
  61.4 5.5 %collective-permute-start.16 = (f32[1,72,256]{2,1,0:T(8,128)S(1)}, f32[1,72,256]{2,1,0:T(8,128)S(1)}, u32[]{:S(2)}, u32[]{:S(2)}) collective-permute-start(f32[1,72,256]{2,1,0:T(8,128)S(1)} %maximum_bitcast_fusion), channel_id=1, source_target_pairs={{0,3},{1,2},{2,1},{3,0},{4,7},{5,6},{6,5},{7,4},{8,11},{9,10},{10,... | collective-permute-start | bytes 221192 | tf_op jit(solution)/shard_map/ppermute | solution.py:208
  64.0 4.4 %collective-permute-start.15 = (f32[1,72,256]{2,1,0:T(8,128)S(1)}, f32[1,72,256]{2,1,0:T(8,128)S(1)}, u32[]{:S(2)}, u32[]{:S(2)}) collective-permute-start(f32[1,72,256]{2,1,0:T(8,128)S(1)} %maximum_bitcast_fusion), channel_id=1, source_target_pairs={{0,2},{1,3},{2,0},{3,1},{4,6},{5,7},{6,4},{7,5},{8,10},{9,11},{10,... | collective-permute-start | bytes 221192 | tf_op jit(solution)/shard_map/ppermute | solution.py:208
  65.5 4.4 %collective-permute-start.14 = (f32[1,72,256]{2,1,0:T(8,128)S(1)}, f32[1,72,256]{2,1,0:T(8,128)S(1)}, u32[]{:S(2)}, u32[]{:S(2)}) collective-permute-start(f32[1,72,256]{2,1,0:T(8,128)S(1)} %maximum_bitcast_fusion), channel_id=1, source_target_pairs={{0,1},{1,0},{2,3},{3,2},{4,5},{5,4},{6,7},{7,6},{8,9},{9,8},{10,11... | collective-permute-start | bytes 221192 | tf_op jit(solution)/shard_map/ppermute | solution.py:208
  77.2 3.7 %collective-permute-start.17 = (f32[1,2440]{1,0:T(1,128)S(1)}, f32[1,2440]{1,0:T(1,128)S(1)}, u32[]{:S(2)}, u32[]{:S(2)}) collective-permute-start(f32[1,2440]{1,0:T(1,128)S(1)} %broadcast_in_dim.21), channel_id=1, source_target_pairs={{0,1},{1,0},{2,3},{3,2},{4,5},{5,4},{6,7},{7,6},{8,9},{9,8},{10,11... | collective-permute-start | bytes 29288 | tf_op jit(solution)/shard_map/ppermute | solution.py:284
  77.3 3.7 %collective-permute-start.18 = (f32[1,2440]{1,0:T(1,128)S(1)}, f32[1,2440]{1,0:T(1,128)S(1)}, u32[]{:S(2)}, u32[]{:S(2)}) collective-permute-start(f32[1,2440]{1,0:T(1,128)S(1)} %broadcast_in_dim.21), channel_id=1, source_target_pairs={{0,2},{1,3},{2,0},{3,1},{4,6},{5,7},{6,4},{7,5},{8,10},{9,11},{10,... | collective-permute-start | bytes 29288 | tf_op jit(solution)/shard_map/ppermute | solution.py:284
  78.3 4.6 %collective-permute-start.19 = (f32[1,2440]{1,0:T(1,128)S(1)}, f32[1,2440]{1,0:T(1,128)S(1)}, u32[]{:S(2)}, u32[]{:S(2)}) collective-permute-start(f32[1,2440]{1,0:T(1,128)S(1)} %broadcast_in_dim.21), channel_id=1, source_target_pairs={{0,3},{1,2},{2,1},{3,0},{4,7},{5,6},{6,5},{7,4},{8,11},{9,10},{10,... | collective-permute-start | bytes 29288 | tf_op jit(solution)/shard_map/ppermute | solution.py:284
  84.3 7.0 %collective-permute-start.21 = (f32[8,2440]{1,0:T(8,128)S(1)}, f32[8,2440]{1,0:T(8,128)S(1)}, u32[]{:S(2)}, u32[]{:S(2)}) collective-permute-start(f32[8,2440]{1,0:T(8,128)S(1)} %concatenate.64), channel_id=1, source_target_pairs={{0,8},{4,12},{8,16},{12,20},{16,24},{20,28},{24,0},{28,4},{1,9},{5... | collective-permute-start | bytes 234248 | tf_op jit(solution)/shard_map/ppermute | solution.py:296
  85.8 8.5 %collective-permute-start.22 = (f32[8,2440]{1,0:T(8,128)S(1)}, f32[8,2440]{1,0:T(8,128)S(1)}, u32[]{:S(2)}, u32[]{:S(2)}) collective-permute-start(f32[8,2440]{1,0:T(8,128)S(1)} %concatenate.64), channel_id=1, source_target_pairs={{0,16},{4,20},{8,24},{12,28},{16,0},{20,4},{24,8},{28,12},{1,17},{... | collective-permute-start | bytes 234248 | tf_op jit(solution)/shard_map/ppermute | solution.py:296
  86.6 7.7 %collective-permute-start.23 = (f32[8,2440]{1,0:T(8,128)S(1)}, f32[8,2440]{1,0:T(8,128)S(1)}, u32[]{:S(2)}, u32[]{:S(2)}) collective-permute-start(f32[8,2440]{1,0:T(8,128)S(1)} %concatenate.64), channel_id=1, source_target_pairs={{0,24},{4,28},{8,0},{12,4},{16,8},{20,12},{24,16},{28,20},{1,25},{... | collective-permute-start | bytes 234248 | tf_op jit(solution)/shard_map/ppermute | solution.py:296
  109.5 5.9 %collective-permute-start.27 = (f32[72,256]{1,0:T(8,128)S(1)}, f32[72,256]{1,0:T(8,128)S(1)}, u32[]{:S(2)}, u32[]{:S(2)}) collective-permute-start(f32[72,256]{1,0:T(8,128)S(1)} %get-tuple-element.135), channel_id=1, source_target_pairs={{0,24},{4,28},{8,0},{12,4},{16,8},{20,12},{24,16},{28,20},{1,25},{... | collective-permute-start | bytes 221192 | tf_op jit(solution)/shard_map/ppermute | solution.py:226
  112.7 7.6 %collective-permute-start.26 = (f32[72,256]{1,0:T(8,128)S(1)}, f32[72,256]{1,0:T(8,128)S(1)}, u32[]{:S(2)}, u32[]{:S(2)}) collective-permute-start(f32[72,256]{1,0:T(8,128)S(1)} %get-tuple-element.136), channel_id=1, source_target_pairs={{0,16},{4,20},{8,24},{12,28},{16,0},{20,4},{24,8},{28,12},{1,17},{... | collective-permute-start | bytes 221192 | tf_op jit(solution)/shard_map/ppermute | solution.py:226
  113.2 7.1 %collective-permute-start.25 = (f32[72,256]{1,0:T(8,128)S(1)}, f32[72,256]{1,0:T(8,128)S(1)}, u32[]{:S(2)}, u32[]{:S(2)}) collective-permute-start(f32[72,256]{1,0:T(8,128)S(1)} %get-tuple-element.137), channel_id=1, source_target_pairs={{0,8},{4,12},{8,16},{12,20},{16,24},{20,28},{24,0},{28,4},{1,9},{5... | collective-permute-start | bytes 221192 | tf_op jit(solution)/shard_map/ppermute | solution.py:226
  120.5 5.6 %collective-permute-start.30 = (f32[1,72,256]{2,1,0:T(8,128)S(1)}, f32[1,72,256]{2,1,0:T(8,128)S(1)}, u32[]{:S(2)}, u32[]{:S(2)}) collective-permute-start(f32[1,72,256]{2,1,0:T(8,128)S(1)} %fusion.35), channel_id=1, source_target_pairs={{0,3},{1,2},{2,1},{3,0},{4,7},{5,6},{6,5},{7,4},{8,11},{9,10},{10,... | collective-permute-start | bytes 221192 | tf_op jit(solution)/shard_map/ppermute | solution.py:208
  122.5 5.8 %collective-permute-start.29 = (f32[1,72,256]{2,1,0:T(8,128)S(1)}, f32[1,72,256]{2,1,0:T(8,128)S(1)}, u32[]{:S(2)}, u32[]{:S(2)}) collective-permute-start(f32[1,72,256]{2,1,0:T(8,128)S(1)} %fusion.35), channel_id=1, source_target_pairs={{0,2},{1,3},{2,0},{3,1},{4,6},{5,7},{6,4},{7,5},{8,10},{9,11},{10,... | collective-permute-start | bytes 221192 | tf_op jit(solution)/shard_map/ppermute | solution.py:208
  126.0 4.4 %collective-permute-start.28 = (f32[1,72,256]{2,1,0:T(8,128)S(1)}, f32[1,72,256]{2,1,0:T(8,128)S(1)}, u32[]{:S(2)}, u32[]{:S(2)}) collective-permute-start(f32[1,72,256]{2,1,0:T(8,128)S(1)} %fusion.35), channel_id=1, source_target_pairs={{0,1},{1,0},{2,3},{3,2},{4,5},{5,4},{6,7},{7,6},{8,9},{9,8},{10,11... | collective-permute-start | bytes 221192 | tf_op jit(solution)/shard_map/ppermute | solution.py:208
  139.9 5.6 %collective-permute-start.34 = (f32[72,256]{1,0:T(8,128)S(1)}, f32[72,256]{1,0:T(8,128)S(1)}, u32[]{:S(2)}, u32[]{:S(2)}) collective-permute-start(f32[72,256]{1,0:T(8,128)S(1)} %get-tuple-element.132), channel_id=1, source_target_pairs={{0,24},{4,28},{8,0},{12,4},{16,8},{20,12},{24,16},{28,20},{1,25},{... | collective-permute-start | bytes 221192 | tf_op jit(solution)/shard_map/ppermute | solution.py:226
  140.0 8.5 %collective-permute-start.33 = (f32[72,256]{1,0:T(8,128)S(1)}, f32[72,256]{1,0:T(8,128)S(1)}, u32[]{:S(2)}, u32[]{:S(2)}) collective-permute-start(f32[72,256]{1,0:T(8,128)S(1)} %get-tuple-element.133), channel_id=1, source_target_pairs={{0,16},{4,20},{8,24},{12,28},{16,0},{20,4},{24,8},{28,12},{1,17},{... | collective-permute-start | bytes 221192 | tf_op jit(solution)/shard_map/ppermute | solution.py:226
  140.4 8.0 %collective-permute-start.32 = (f32[72,256]{1,0:T(8,128)S(1)}, f32[72,256]{1,0:T(8,128)S(1)}, u32[]{:S(2)}, u32[]{:S(2)}) collective-permute-start(f32[72,256]{1,0:T(8,128)S(1)} %get-tuple-element.131), channel_id=1, source_target_pairs={{0,8},{4,12},{8,16},{12,20},{16,24},{20,28},{24,0},{28,4},{1,9},{5... | collective-permute-start | bytes 221192 | tf_op jit(solution)/shard_map/ppermute | solution.py:226
  (10 other events, 151.1 us)

commit v9 on v8

--- a/solution.py
+++ b/solution.py
@@ -262,21 +262,24 @@
     entries = tile_pass(
         "entries", gathered, tiles, own_rows, kernel_cols, live_mask, block_count,
         row_blocks, vectors,
-    ).T
+    )
     block_sums = jnp.sum(relaxed_two, axis=2)
     row_agg = agg_of_block[row_global]
     col_agg = agg_of_block[col_global]
-    fields = [
-        entries.reshape(-1),
-        row_agg.astype(jnp.float32),
-        col_agg.astype(jnp.float32),
+
+    def as_rows(values):
+        extra = -values.shape[0] % slots_total
+        return jnp.pad(values, (0, extra)).reshape(-1, slots_total)
+
+    small = [
         block_sums.reshape(-1),
         tele_sums.reshape(-1),
         piece_agg.astype(jnp.float32),
         piece_dangling,
     ]
-    sizes = [f.shape[0] for f in fields]
-    shared = jnp.concatenate(fields)[None]
+    small_rows = [as_rows(f) for f in small]
+    fields = [entries, row_agg.astype(jnp.float32)[None], col_agg.astype(jnp.float32)[None]]
+    shared = jnp.concatenate(fields + small_rows, axis=0)[None]
     if exchange and src_count % 2 == 0:
         shared = jnp.concatenate(
             [shared]
@@ -297,26 +300,26 @@
         shared = jnp.concatenate(pieces, axis=0)
     else:
         shared = lax.all_gather(shared[0], all_axes, axis=0, tiled=False)
-    offsets = [0]
-    for size in sizes:
-        offsets.append(offsets[-1] + size)
-    every = [shared[:, offsets[i]:offsets[i + 1]] for i in range(len(sizes))]
-    all_entries = every[0].reshape(-1, vectors)
-    all_row_hot = every[1].reshape(-1)[:, None] == agg_range[None, :].astype(jnp.float32)
-    all_col_hot = every[2].reshape(-1)[:, None] == agg_range[None, :].astype(jnp.float32)
-    all_row_hot = all_row_hot.astype(jnp.bfloat16)
-    all_col_hot = all_col_hot.astype(jnp.bfloat16)
-    all_block_sums = every[3].reshape(-1, vectors)
-    all_tele_sums = every[4].reshape(-1, vectors)
-    all_block_hot = (every[5].reshape(-1)[:, None] == agg_range[None, :].astype(jnp.float32))
-    all_block_hot = all_block_hot.astype(jnp.float32)
-    all_dangling = every[6].reshape(-1)
+    all_entries = shared[:, :vectors, :]
+    agg_float = agg_range.astype(jnp.float32)
+    all_row_hot = (shared[:, vectors, :, None] == agg_float).astype(jnp.bfloat16)
+    all_col_hot = (shared[:, vectors + 1, :, None] == agg_float).astype(jnp.bfloat16)
+    every = []
+    at = vectors + 2
+    for field, rows in zip(small, small_rows):
+        count = rows.shape[0]
+        every.append(shared[:, at:at + count, :].reshape(shared.shape[0], -1)[:, :field.shape[0]])
+        at += count
+    all_block_sums = every[0].reshape(-1, vectors)
+    all_tele_sums = every[1].reshape(-1, vectors)
+    all_block_hot = (every[2].reshape(-1)[:, None] == agg_float[None, :]).astype(jnp.float32)
+    all_dangling = every[3].reshape(-1)
     totals = jnp.einsum("bk,ba->ka", all_block_sums, all_block_hot, precision=highest)
     lost_mass = jnp.einsum(
         "bk,ba->ka", all_block_sums * all_dangling[:, None], all_block_hot, precision=highest
     )
     weight = jnp.einsum("bk,ba->ka", all_tele_sums, all_block_hot, precision=highest)
-    inflow_one = select_dot("tk,ta->ka", all_entries, all_row_hot)
+    inflow_one = select_dot("dkt,dta->ka", all_entries, all_row_hot)
 
     def coarse_sweep(inflow, ratios):
         carried = jnp.sum(lost_mass * ratios, axis=1)
@@ -327,8 +330,8 @@
 
     level_one = coarse_sweep(inflow_one, jnp.ones((vectors, agg_count), jnp.float32))
     ratios_one = level_one / totals
-    ratio_at_tile = select_dot("ka,ta->tk", ratios_one, all_col_hot)
-    inflow_two = select_dot("tk,ta->ka", all_entries * ratio_at_tile, all_row_hot)
+    ratio_at_tile = select_dot("ka,dta->dkt", ratios_one, all_col_hot)
+    inflow_two = select_dot("dkt,dta->ka", all_entries * ratio_at_tile, all_row_hot)
     level_two = coarse_sweep(inflow_two, ratios_one)
     ratios_two = level_two / totals
     groups = gathered.shape[0]

time: 151 us -> 160 us (1.060)
  starting transfers between devices: 41.6 us -> 47.4 us
  waiting for transfers between devices: 49.3 us -> 51.4 us
    ppermute x12, starting transfers between devices: 13.3 us -> 24.7 us  [reduce_rows(): total = total + lax.ppermute(part[shift], 'src', pairs)]
    ppermute x12, waiting for transfers between devices: 11.5 us -> 7.05 us  [spread_columns(): lax.ppermute(payload, 'dst', [(i, i ^ v) for i in range(dst_count)])]
    ppermute x12, starting transfers between devices: 19.5 us -> 15.2 us  [spread_columns(): lax.ppermute(payload, 'dst', [(i, i ^ v) for i in range(dst_count)])]
    ppermute x3, waiting for transfers between devices: 4.8 us -> 9.03 us  [per_device(): pieces.append(lax.ppermute(shared, 'src', pairs))]
  transfers between devices with their start and end apart: 35 -> 35, of which waited for: 25 -> 21; matrix products, arithmetic and copies ran while one was open for 6% -> 7% of each run, Pallas kernels for 0% -> 0%
where the time goes in v9:
time: 160 us; the launch traced here: 157 us
  waiting for transfers between devices  51.4 us (32%)
  starting transfers between devices  47.4 us (30%)
  Pallas kernels  29.8 us (19%)
  other arithmetic  13.5 us (8%)
  local copies, waits for them, and re-layouts  10.6 us (7%)
  matrix products  2.98 us (2%)
  between operations  1.78 us (1%)
    pallas_call x5, Pallas kernels, tile_pass(): pl.pallas_call(functools.partial(tile_kernel, mode, blocks_piece, vectors...  29.8 us
    ppermute x12, waiting for transfers between devices, reduce_rows(): total = total + lax.ppermute(part[shift], 'src', pairs)  24.8 us
    ppermute x12, starting transfers between devices, reduce_rows(): total = total + lax.ppermute(part[shift], 'src', pairs)  24.7 us
    ppermute x12, starting transfers between devices, spread_columns(): lax.ppermute(payload, 'dst', [(i, i ^ v) for i in range(dst_count)])  15.2 us
    ppermute x3, waiting for transfers between devices, per_device(): pieces.append(lax.ppermute(shared, 'src', pairs))  9.03 us
    ppermute x12, waiting for transfers between devices, spread_columns(): lax.ppermute(payload, 'dst', [(i, i ^ v) for i in range(dst_count)])  7.05 us
    ppermute x4, waiting for transfers between devices, reduce_rows(): part = keep + lax.ppermute(give, 'src', [(i, i ^ 1) for i in range(n)])  5.79 us
    add x4, other arithmetic, reduce_rows(): part = keep + lax.ppermute(give, 'src', [(i, i ^ 1) for i in range(n)])  4.01 us
  transfers between devices with their start and end apart: 35, of which 21 were waited for; matrix products, arithmetic and copies ran while one was open for 7% of the time, Pallas kernels for 0%

profile of v9, /device:TPU:0, one launch (start us, length us, event | category | flops | bytes accessed | tf_op | source)
XLA Modules:
  0.0 157.5 jit_solution(10723671064790804053)
XLA Ops:
  2.6 4.0 %collective-permute-start.2 = (f32[1,72,256]{2,1,0:T(8,128)S(1)}, f32[1,72,256]{2,1,0:T(8,128)S(1)}, u32[]{:S(2)}, u32[]{:S(2)}) collective-permute-start(f32[1,72,256]{2,1,0:T(8,128)S(1)} %fusion.51), channel_id=1, source_target_pairs={{0,3},{1,2},{2,1},{3,0},{4,7},{5,6},{6,5},{7,4},{8,11},{9,10},{10,... | collective-permute-start | bytes 221192 | tf_op jit(solution)/shard_map/ppermute | solution.py:208
  12.0 1.6 %gather_fusion = s32[128]{0:T(128)S(1)} fusion(s32[128]{0:T(128)} %param.29, s32[1024]{0:T(1024)S(1)} %get-tuple-element.164), kind=kCustom, calls=%fused_computation | custom fusion | bytes 1536 | tf_op jit(solution)/shard_map/gather | solution.py:153
  16.2 6.0 %shard_map.95 = (f32[4,72,256]{2,1,0:T(8,128)}, f32[4,72,256]{2,1,0:T(8,128)}) custom-call(s32[128]{0:T(128)} %get-tuple-element.165.rows_ref, s32[128]{0:T(128)} %get-tuple-element.166.cols_ref, s32[128]{0:T(128)} %and_convert_fusion.live_ref, s32[1]{0:T(128)} %bitcast.5.nb_ref, f32[4,72,256]{2,1,0:T(8,128)} %copy-done.2, ...), custom_call_target="tpu_custom_call" | custom-call | tf_op jit(solution)/shard_map/pallas_call | solution.py:100
  25.0 2.0 %collective-permute-start.4 = (f32[72,256]{1,0:T(8,128)S(1)}, f32[72,256]{1,0:T(8,128)S(1)}, u32[]{:S(2)}, u32[]{:S(2)}) collective-permute-start(f32[72,256]{1,0:T(8,128)S(1)} %get-tuple-element.144), channel_id=1, source_target_pairs={{0,8},{4,12},{8,16},{12,20},{16,24},{20,28},{24,0},{28,4},{1,9},{5... | collective-permute-start | bytes 221192 | tf_op jit(solution)/shard_map/ppermute | solution.py:226
  27.0 5.3 %collective-permute-start.6 = (f32[72,256]{1,0:T(8,128)S(1)}, f32[72,256]{1,0:T(8,128)S(1)}, u32[]{:S(2)}, u32[]{:S(2)}) collective-permute-start(f32[72,256]{1,0:T(8,128)S(1)} %get-tuple-element.145), channel_id=1, source_target_pairs={{0,24},{4,28},{8,0},{12,4},{16,8},{20,12},{24,16},{28,20},{1,25},{... | collective-permute-start | bytes 221192 | tf_op jit(solution)/shard_map/ppermute | solution.py:226
  35.0 4.6 %collective-permute-done.5 = f32[72,256]{1,0:T(8,128)S(1)} collective-permute-done((f32[72,256]{1,0:T(8,128)S(1)}, f32[72,256]{1,0:T(8,128)S(1)}, u32[]{:S(2)}, u32[]{:S(2)}) %collective-permute-start.5) | collective-permute-done | bytes 73760 | tf_op jit(solution)/shard_map/ppermute | solution.py:226
  40.0 3.4 %collective-permute-start.7 = (f32[1,72,256]{2,1,0:T(8,128)S(1)}, f32[1,72,256]{2,1,0:T(8,128)S(1)}, u32[]{:S(2)}, u32[]{:S(2)}) collective-permute-start(f32[1,72,256]{2,1,0:T(8,128)S(1)} %fusion.47), channel_id=1, source_target_pairs={{0,1},{1,0},{2,3},{3,2},{4,5},{5,4},{6,7},{7,6},{8,9},{9,8},{10,11... | collective-permute-start | bytes 221192 | tf_op jit(solution)/shard_map/ppermute | solution.py:208
  43.5 2.3 %collective-permute-done.9 = f32[1,72,256]{2,1,0:T(8,128)S(1)} collective-permute-done((f32[1,72,256]{2,1,0:T(8,128)S(1)}, f32[1,72,256]{2,1,0:T(8,128)S(1)}, u32[]{:S(2)}, u32[]{:S(2)}) %collective-permute-start.9) | collective-permute-done | bytes 73760 | tf_op jit(solution)/shard_map/ppermute | solution.py:208
  46.6 6.0 %shard_map.96 = (f32[4,72,256]{2,1,0:T(8,128)}, f32[4,72,256]{2,1,0:T(8,128)}) custom-call(s32[128]{0:T(128)} %get-tuple-element.165.rows_ref, s32[128]{0:T(128)} %get-tuple-element.166.cols_ref, s32[128]{0:T(128)} %and_convert_fusion.live_ref, s32[1]{0:T(128)} %bitcast.5.nb_ref, f32[4,72,256]{2,1,0:T(8,128)} %copy-done.3, ...), custom_call_target="tpu_custom_call" | custom-call | tf_op jit(solution)/shard_map/pallas_call | solution.py:100
  52.6 1.8 %collective-permute-done.10 = f32[4,72,256]{2,1,0:T(8,128)S(1)} collective-permute-done((f32[4,72,256]{2,1,0:T(8,128)}, f32[4,72,256]{2,1,0:T(8,128)S(1)}, u32[]{:S(2)}, u32[]{:S(2)}) %collective-permute-start.10) | collective-permute-done | bytes 294944 | tf_op jit(solution)/shard_map/ppermute | solution.py:222
  55.5 5.3 %collective-permute-start.13 = (f32[72,256]{1,0:T(8,128)S(1)}, f32[72,256]{1,0:T(8,128)S(1)}, u32[]{:S(2)}, u32[]{:S(2)}) collective-permute-start(f32[72,256]{1,0:T(8,128)S(1)} %get-tuple-element.142), channel_id=1, source_target_pairs={{0,24},{4,28},{8,0},{12,4},{16,8},{20,12},{24,16},{28,20},{1,25},{... | collective-permute-start | bytes 221192 | tf_op jit(solution)/shard_map/ppermute | solution.py:226
  61.2 2.1 %collective-permute-done.11 = f32[72,256]{1,0:T(8,128)S(1)} collective-permute-done((f32[72,256]{1,0:T(8,128)S(1)}, f32[72,256]{1,0:T(8,128)S(1)}, u32[]{:S(2)}, u32[]{:S(2)}) %collective-permute-start.11) | collective-permute-done | bytes 73760 | tf_op jit(solution)/shard_map/ppermute | solution.py:226
  63.4 4.6 %collective-permute-done.12 = f32[72,256]{1,0:T(8,128)S(1)} collective-permute-done((f32[72,256]{1,0:T(8,128)S(1)}, f32[72,256]{1,0:T(8,128)S(1)}, u32[]{:S(2)}, u32[]{:S(2)}) %collective-permute-start.12) | collective-permute-done | bytes 73760 | tf_op jit(solution)/shard_map/ppermute | solution.py:226
  69.2 2.6 %collective-permute-start.14 = (f32[1,72,256]{2,1,0:T(8,128)S(1)}, f32[1,72,256]{2,1,0:T(8,128)S(1)}, u32[]{:S(2)}, u32[]{:S(2)}) collective-permute-start(f32[1,72,256]{2,1,0:T(8,128)S(1)} %maximum_bitcast_fusion), channel_id=1, source_target_pairs={{0,1},{1,0},{2,3},{3,2},{4,5},{5,4},{6,7},{7,6},{8,9},{9,8},{10,11... | collective-permute-start | bytes 221192 | tf_op jit(solution)/shard_map/ppermute | solution.py:208
  71.8 2.3 %collective-permute-done.16 = f32[1,72,256]{2,1,0:T(8,128)S(1)} collective-permute-done((f32[1,72,256]{2,1,0:T(8,128)S(1)}, f32[1,72,256]{2,1,0:T(8,128)S(1)}, u32[]{:S(2)}, u32[]{:S(2)}) %collective-permute-start.16) | collective-permute-done | bytes 73760 | tf_op jit(solution)/shard_map/ppermute | solution.py:208
  74.9 5.6 %shard_map.97 = f32[16,128]{1,0:T(8,128)} custom-call(s32[128]{0:T(128)} %clamp_bitcast_fusion.rows_ref, s32[128]{0:T(128)} %get-tuple-element.166.cols_ref, s32[128]{0:T(128)} %and_convert_fusion.live_ref, s32[1]{0:T(128)} %bitcast.5.nb_ref, f32[4,72,256]{2,1,0:T(8,128)} %pad_maximum_fusion.2.x_ref, bf16[1,1,128,256,256]{4,3,2,1,0:T(8,128)(2,1)} %t_ref.9), custom_call_target="tpu_custom_call" | custom-call | tf_op jit(solution)/shard_map/pallas_call | solution.py:100
  82.7 2.0 %collective-permute-start.18 = (f32[1,22,128]{2,1,0:T(8,128)S(1)}, f32[1,22,128]{2,1,0:T(8,128)S(1)}, u32[]{:S(2)}, u32[]{:S(2)}) collective-permute-start(f32[1,22,128]{2,1,0:T(8,128)S(1)} %bitcast.288), channel_id=1, source_target_pairs={{0,2},{1,3},{2,0},{3,1},{4,6},{5,7},{6,4},{7,5},{8,10},{9,11},{10,... | collective-permute-start | bytes 33800 | tf_op jit(solution)/shard_map/ppermute | solution.py:287
  86.4 2.0 %collective-permute-done.17 = f32[1,22,128]{2,1,0:T(8,128)S(1)} collective-permute-done((f32[1,22,128]{2,1,0:T(8,128)S(1)}, f32[1,22,128]{2,1,0:T(8,128)S(1)}, u32[]{:S(2)}, u32[]{:S(2)}) %collective-permute-start.17) | collective-permute-done | bytes 11296 | tf_op jit(solution)/shard_map/ppermute | solution.py:287
  90.1 3.5 %collective-permute-start.23 = (f32[8,22,128]{2,1,0:T(8,128)S(1)}, f32[8,22,128]{2,1,0:T(8,128)S(1)}, u32[]{:S(2)}, u32[]{:S(2)}) collective-permute-start(f32[8,22,128]{2,1,0:T(8,128)S(1)} %get-tuple-element.147), channel_id=1, source_target_pairs={{0,24},{4,28},{8,0},{12,4},{16,8},{20,12},{24,16},{28,20},{1,25},{... | collective-permute-start | bytes 270344 | tf_op jit(solution)/shard_map/ppermute | solution.py:299
  93.6 3.7 %collective-permute-done.21 = f32[8,22,128]{2,1,0:T(8,128)S(1)} collective-permute-done((f32[8,22,128]{2,1,0:T(8,128)S(1)}, f32[8,22,128]{2,1,0:T(8,128)S(1)}, u32[]{:S(2)}, u32[]{:S(2)}) %collective-permute-start.21) | collective-permute-done | bytes 90144 | tf_op jit(solution)/shard_map/ppermute | solution.py:299
  97.2 5.4 %collective-permute-done.22 = f32[8,22,128]{2,1,0:T(8,128)S(1)} collective-permute-done((f32[8,22,128]{2,1,0:T(8,128)S(1)}, f32[8,22,128]{2,1,0:T(8,128)S(1)}, u32[]{:S(2)}, u32[]{:S(2)}) %collective-permute-start.22) | collective-permute-done | bytes 90144 | tf_op jit(solution)/shard_map/ppermute | solution.py:299
  107.4 6.1 %shard_map.98 = (f32[4,72,256]{2,1,0:T(8,128)}, f32[4,72,256]{2,1,0:T(8,128)}) custom-call(s32[128]{0:T(128)} %get-tuple-element.165.rows_ref, s32[128]{0:T(128)} %get-tuple-element.166.cols_ref, s32[128]{0:T(128)} %and_convert_fusion.live_ref, s32[1]{0:T(128)} %bitcast.5.nb_ref, f32[4,72,256]{2,1,0:T(8,128)} %broadcast_multiply_fusion.x_ref, ...), custom_call_target="tpu_custom_call" | custom-call | tf_op jit(solution)/shard_map/pallas_call | solution.py:100
  113.5 1.8 %collective-permute-done.24 = f32[4,72,256]{2,1,0:T(8,128)S(1)} collective-permute-done((f32[4,72,256]{2,1,0:T(8,128)}, f32[4,72,256]{2,1,0:T(8,128)S(1)}, u32[]{:S(2)}, u32[]{:S(2)}) %collective-permute-start.24) | collective-permute-done | bytes 294944 | tf_op jit(solution)/shard_map/ppermute | solution.py:222
  116.3 4.8 %collective-permute-start.27 = (f32[72,256]{1,0:T(8,128)S(1)}, f32[72,256]{1,0:T(8,128)S(1)}, u32[]{:S(2)}, u32[]{:S(2)}) collective-permute-start(f32[72,256]{1,0:T(8,128)S(1)} %get-tuple-element.138), channel_id=1, source_target_pairs={{0,24},{4,28},{8,0},{12,4},{16,8},{20,12},{24,16},{28,20},{1,25},{... | collective-permute-start | bytes 221192 | tf_op jit(solution)/shard_map/ppermute | solution.py:226
  121.8 2.0 %collective-permute-done.27 = f32[72,256]{1,0:T(8,128)S(1)} collective-permute-done((f32[72,256]{1,0:T(8,128)S(1)}, f32[72,256]{1,0:T(8,128)S(1)}, u32[]{:S(2)}, u32[]{:S(2)}) %collective-permute-start.27) | collective-permute-done | bytes 73760 | tf_op jit(solution)/shard_map/ppermute | solution.py:226
  123.8 4.6 %collective-permute-done.26 = f32[72,256]{1,0:T(8,128)S(1)} collective-permute-done((f32[72,256]{1,0:T(8,128)S(1)}, f32[72,256]{1,0:T(8,128)S(1)}, u32[]{:S(2)}, u32[]{:S(2)}) %collective-permute-start.26) | collective-permute-done | bytes 73760 | tf_op jit(solution)/shard_map/ppermute | solution.py:226
  129.4 2.8 %collective-permute-start.28 = (f32[1,72,256]{2,1,0:T(8,128)S(1)}, f32[1,72,256]{2,1,0:T(8,128)S(1)}, u32[]{:S(2)}, u32[]{:S(2)}) collective-permute-start(f32[1,72,256]{2,1,0:T(8,128)S(1)} %fusion.43), channel_id=1, source_target_pairs={{0,1},{1,0},{2,3},{3,2},{4,5},{5,4},{6,7},{7,6},{8,9},{9,8},{10,11... | collective-permute-start | bytes 221192 | tf_op jit(solution)/shard_map/ppermute | solution.py:208
  132.2 2.4 %collective-permute-done.30 = f32[1,72,256]{2,1,0:T(8,128)S(1)} collective-permute-done((f32[1,72,256]{2,1,0:T(8,128)S(1)}, f32[1,72,256]{2,1,0:T(8,128)S(1)}, u32[]{:S(2)}, u32[]{:S(2)}) %collective-permute-start.30) | collective-permute-done | bytes 73760 | tf_op jit(solution)/shard_map/ppermute | solution.py:208
  135.4 6.0 %shard_map.99 = (f32[4,72,256]{2,1,0:T(8,128)}, f32[4,72,256]{2,1,0:T(8,128)}) custom-call(s32[128]{0:T(128)} %get-tuple-element.165.rows_ref, s32[128]{0:T(128)} %get-tuple-element.166.cols_ref, s32[128]{0:T(128)} %and_convert_fusion.live_ref, s32[1]{0:T(128)} %bitcast.5.nb_ref, f32[4,72,256]{2,1,0:T(8,128)} %copy-done.1, ...), custom_call_target="tpu_custom_call" | custom-call | tf_op jit(solution)/shard_map/pallas_call | solution.py:100
  141.5 1.7 %collective-permute-done.31 = f32[4,72,256]{2,1,0:T(8,128)S(1)} collective-permute-done((f32[4,72,256]{2,1,0:T(8,128)}, f32[4,72,256]{2,1,0:T(8,128)S(1)}, u32[]{:S(2)}, u32[]{:S(2)}) %collective-permute-start.31) | collective-permute-done | bytes 294944 | tf_op jit(solution)/shard_map/ppermute | solution.py:222
  144.4 4.9 %collective-permute-start.34 = (f32[72,256]{1,0:T(8,128)S(1)}, f32[72,256]{1,0:T(8,128)S(1)}, u32[]{:S(2)}, u32[]{:S(2)}) collective-permute-start(f32[72,256]{1,0:T(8,128)S(1)} %get-tuple-element.135), channel_id=1, source_target_pairs={{0,24},{4,28},{8,0},{12,4},{16,8},{20,12},{24,16},{28,20},{1,25},{... | collective-permute-start | bytes 221192 | tf_op jit(solution)/shard_map/ppermute | solution.py:226
  152.0 4.6 %collective-permute-done.33 = f32[72,256]{1,0:T(8,128)S(1)} collective-permute-done((f32[72,256]{1,0:T(8,128)S(1)}, f32[72,256]{1,0:T(8,128)S(1)}, u32[]{:S(2)}, u32[]{:S(2)}) %collective-permute-start.33) | collective-permute-done | bytes 73760 | tf_op jit(solution)/shard_map/ppermute | solution.py:226
  (162 shorter events, 37.9 us)
Async XLA Ops:
  2.6 12.8 %collective-permute-start.2 = (f32[1,72,256]{2,1,0:T(8,128)S(1)}, f32[1,72,256]{2,1,0:T(8,128)S(1)}, u32[]{:S(2)}, u32[]{:S(2)}) collective-permute-start(f32[1,72,256]{2,1,0:T(8,128)S(1)} %fusion.51), channel_id=1, source_target_pairs={{0,3},{1,2},{2,1},{3,0},{4,7},{5,6},{6,5},{7,4},{8,11},{9,10},{10,... | collective-permute-start | bytes 221192 | tf_op jit(solution)/shard_map/ppermute | solution.py:208
  6.6 8.8 %collective-permute-start.1 = (f32[1,72,256]{2,1,0:T(8,128)S(1)}, f32[1,72,256]{2,1,0:T(8,128)S(1)}, u32[]{:S(2)}, u32[]{:S(2)}) collective-permute-start(f32[1,72,256]{2,1,0:T(8,128)S(1)} %fusion.51), channel_id=1, source_target_pairs={{0,2},{1,3},{2,0},{3,1},{4,6},{5,7},{6,4},{7,5},{8,10},{9,11},{10,... | collective-permute-start | bytes 221192 | tf_op jit(solution)/shard_map/ppermute | solution.py:208
  7.1 8.3 %collective-permute-start = (f32[1,72,256]{2,1,0:T(8,128)S(1)}, f32[1,72,256]{2,1,0:T(8,128)S(1)}, u32[]{:S(2)}, u32[]{:S(2)}) collective-permute-start(f32[1,72,256]{2,1,0:T(8,128)S(1)} %fusion.51), channel_id=1, source_target_pairs={{0,1},{1,0},{2,3},{3,2},{4,5},{5,4},{6,7},{7,6},{8,9},{9,8},{10,11... | collective-permute-start | bytes 221192 | tf_op jit(solution)/shard_map/ppermute | solution.py:208
  25.0 10.0 %collective-permute-start.4 = (f32[72,256]{1,0:T(8,128)S(1)}, f32[72,256]{1,0:T(8,128)S(1)}, u32[]{:S(2)}, u32[]{:S(2)}) collective-permute-start(f32[72,256]{1,0:T(8,128)S(1)} %get-tuple-element.144), channel_id=1, source_target_pairs={{0,8},{4,12},{8,16},{12,20},{16,24},{20,28},{24,0},{28,4},{1,9},{5... | collective-permute-start | bytes 221192 | tf_op jit(solution)/shard_map/ppermute | solution.py:226
  27.0 8.0 %collective-permute-start.6 = (f32[72,256]{1,0:T(8,128)S(1)}, f32[72,256]{1,0:T(8,128)S(1)}, u32[]{:S(2)}, u32[]{:S(2)}) collective-permute-start(f32[72,256]{1,0:T(8,128)S(1)} %get-tuple-element.145), channel_id=1, source_target_pairs={{0,24},{4,28},{8,0},{12,4},{16,8},{20,12},{24,16},{28,20},{1,25},{... | collective-permute-start | bytes 221192 | tf_op jit(solution)/shard_map/ppermute | solution.py:226
  32.3 7.2 %collective-permute-start.5 = (f32[72,256]{1,0:T(8,128)S(1)}, f32[72,256]{1,0:T(8,128)S(1)}, u32[]{:S(2)}, u32[]{:S(2)}) collective-permute-start(f32[72,256]{1,0:T(8,128)S(1)} %get-tuple-element.146), channel_id=1, source_target_pairs={{0,16},{4,20},{8,24},{12,28},{16,0},{20,4},{24,8},{28,12},{1,17},{... | collective-permute-start | bytes 221192 | tf_op jit(solution)/shard_map/ppermute | solution.py:226
  39.8 6.0 %collective-permute-start.9 = (f32[1,72,256]{2,1,0:T(8,128)S(1)}, f32[1,72,256]{2,1,0:T(8,128)S(1)}, u32[]{:S(2)}, u32[]{:S(2)}) collective-permute-start(f32[1,72,256]{2,1,0:T(8,128)S(1)} %fusion.47), channel_id=1, source_target_pairs={{0,3},{1,2},{2,1},{3,0},{4,7},{5,6},{6,5},{7,4},{8,11},{9,10},{10,... | collective-permute-start | bytes 221192 | tf_op jit(solution)/shard_map/ppermute | solution.py:208
  39.9 5.9 %collective-permute-start.8 = (f32[1,72,256]{2,1,0:T(8,128)S(1)}, f32[1,72,256]{2,1,0:T(8,128)S(1)}, u32[]{:S(2)}, u32[]{:S(2)}) collective-permute-start(f32[1,72,256]{2,1,0:T(8,128)S(1)} %fusion.47), channel_id=1, source_target_pairs={{0,2},{1,3},{2,0},{3,1},{4,6},{5,7},{6,4},{7,5},{8,10},{9,11},{10,... | collective-permute-start | bytes 221192 | tf_op jit(solution)/shard_map/ppermute | solution.py:208
  40.0 5.8 %collective-permute-start.7 = (f32[1,72,256]{2,1,0:T(8,128)S(1)}, f32[1,72,256]{2,1,0:T(8,128)S(1)}, u32[]{:S(2)}, u32[]{:S(2)}) collective-permute-start(f32[1,72,256]{2,1,0:T(8,128)S(1)} %fusion.47), channel_id=1, source_target_pairs={{0,1},{1,0},{2,3},{3,2},{4,5},{5,4},{6,7},{7,6},{8,9},{9,8},{10,11... | collective-permute-start | bytes 221192 | tf_op jit(solution)/shard_map/ppermute | solution.py:208
  52.6 1.8 %collective-permute-start.10 = (f32[4,72,256]{2,1,0:T(8,128)}, f32[4,72,256]{2,1,0:T(8,128)S(1)}, u32[]{:S(2)}, u32[]{:S(2)}) collective-permute-start(f32[4,72,256]{2,1,0:T(8,128)} %get-tuple-element.105), channel_id=1, source_target_pairs={{0,4},{4,0},{8,12},{12,8},{16,20},{20,16},{24,28},{28,24},{1,5},{5... | collective-permute-start | bytes 884744 | tf_op jit(solution)/shard_map/ppermute | solution.py:222
  55.4 8.0 %collective-permute-start.11 = (f32[72,256]{1,0:T(8,128)S(1)}, f32[72,256]{1,0:T(8,128)S(1)}, u32[]{:S(2)}, u32[]{:S(2)}) collective-permute-start(f32[72,256]{1,0:T(8,128)S(1)} %get-tuple-element.141), channel_id=1, source_target_pairs={{0,8},{4,12},{8,16},{12,20},{16,24},{20,28},{24,0},{28,4},{1,9},{5... | collective-permute-start | bytes 221192 | tf_op jit(solution)/shard_map/ppermute | solution.py:226
  55.5 8.0 %collective-permute-start.13 = (f32[72,256]{1,0:T(8,128)S(1)}, f32[72,256]{1,0:T(8,128)S(1)}, u32[]{:S(2)}, u32[]{:S(2)}) collective-permute-start(f32[72,256]{1,0:T(8,128)S(1)} %get-tuple-element.142), channel_id=1, source_target_pairs={{0,24},{4,28},{8,0},{12,4},{16,8},{20,12},{24,16},{28,20},{1,25},{... | collective-permute-start | bytes 221192 | tf_op jit(solution)/shard_map/ppermute | solution.py:226
  60.7 7.2 %collective-permute-start.12 = (f32[72,256]{1,0:T(8,128)S(1)}, f32[72,256]{1,0:T(8,128)S(1)}, u32[]{:S(2)}, u32[]{:S(2)}) collective-permute-start(f32[72,256]{1,0:T(8,128)S(1)} %get-tuple-element.143), channel_id=1, source_target_pairs={{0,16},{4,20},{8,24},{12,28},{16,0},{20,4},{24,8},{28,12},{1,17},{... | collective-permute-start | bytes 221192 | tf_op jit(solution)/shard_map/ppermute | solution.py:226
  68.2 6.0 %collective-permute-start.16 = (f32[1,72,256]{2,1,0:T(8,128)S(1)}, f32[1,72,256]{2,1,0:T(8,128)S(1)}, u32[]{:S(2)}, u32[]{:S(2)}) collective-permute-start(f32[1,72,256]{2,1,0:T(8,128)S(1)} %maximum_bitcast_fusion), channel_id=1, source_target_pairs={{0,3},{1,2},{2,1},{3,0},{4,7},{5,6},{6,5},{7,4},{8,11},{9,10},{10,... | collective-permute-start | bytes 221192 | tf_op jit(solution)/shard_map/ppermute | solution.py:208
  68.3 5.9 %collective-permute-start.15 = (f32[1,72,256]{2,1,0:T(8,128)S(1)}, f32[1,72,256]{2,1,0:T(8,128)S(1)}, u32[]{:S(2)}, u32[]{:S(2)}) collective-permute-start(f32[1,72,256]{2,1,0:T(8,128)S(1)} %maximum_bitcast_fusion), channel_id=1, source_target_pairs={{0,2},{1,3},{2,0},{3,1},{4,6},{5,7},{6,4},{7,5},{8,10},{9,11},{10,... | collective-permute-start | bytes 221192 | tf_op jit(solution)/shard_map/ppermute | solution.py:208
  69.2 5.0 %collective-permute-start.14 = (f32[1,72,256]{2,1,0:T(8,128)S(1)}, f32[1,72,256]{2,1,0:T(8,128)S(1)}, u32[]{:S(2)}, u32[]{:S(2)}) collective-permute-start(f32[1,72,256]{2,1,0:T(8,128)S(1)} %maximum_bitcast_fusion), channel_id=1, source_target_pairs={{0,1},{1,0},{2,3},{3,2},{4,5},{5,4},{6,7},{7,6},{8,9},{9,8},{10,11... | collective-permute-start | bytes 221192 | tf_op jit(solution)/shard_map/ppermute | solution.py:208
  81.3 4.7 %collective-permute-start.19 = (f32[1,22,128]{2,1,0:T(8,128)S(1)}, f32[1,22,128]{2,1,0:T(8,128)S(1)}, u32[]{:S(2)}, u32[]{:S(2)}) collective-permute-start(f32[1,22,128]{2,1,0:T(8,128)S(1)} %bitcast.287), channel_id=1, source_target_pairs={{0,3},{1,2},{2,1},{3,0},{4,7},{5,6},{6,5},{7,4},{8,11},{9,10},{10,... | collective-permute-start | bytes 33800 | tf_op jit(solution)/shard_map/ppermute | solution.py:287
  82.7 3.7 %collective-permute-start.18 = (f32[1,22,128]{2,1,0:T(8,128)S(1)}, f32[1,22,128]{2,1,0:T(8,128)S(1)}, u32[]{:S(2)}, u32[]{:S(2)}) collective-permute-start(f32[1,22,128]{2,1,0:T(8,128)S(1)} %bitcast.288), channel_id=1, source_target_pairs={{0,2},{1,3},{2,0},{3,1},{4,6},{5,7},{6,4},{7,5},{8,10},{9,11},{10,... | collective-permute-start | bytes 33800 | tf_op jit(solution)/shard_map/ppermute | solution.py:287
  84.7 3.7 %collective-permute-start.17 = (f32[1,22,128]{2,1,0:T(8,128)S(1)}, f32[1,22,128]{2,1,0:T(8,128)S(1)}, u32[]{:S(2)}, u32[]{:S(2)}) collective-permute-start(f32[1,22,128]{2,1,0:T(8,128)S(1)} %bitcast.289), channel_id=1, source_target_pairs={{0,1},{1,0},{2,3},{3,2},{4,5},{5,4},{6,7},{7,6},{8,9},{9,8},{10,11... | collective-permute-start | bytes 33800 | tf_op jit(solution)/shard_map/ppermute | solution.py:287
  89.7 7.5 %collective-permute-start.21 = (f32[8,22,128]{2,1,0:T(8,128)S(1)}, f32[8,22,128]{2,1,0:T(8,128)S(1)}, u32[]{:S(2)}, u32[]{:S(2)}) collective-permute-start(f32[8,22,128]{2,1,0:T(8,128)S(1)} %get-tuple-element.147), channel_id=1, source_target_pairs={{0,8},{4,12},{8,16},{12,20},{16,24},{20,28},{24,0},{28,4},{1,9},{5... | collective-permute-start | bytes 270344 | tf_op jit(solution)/shard_map/ppermute | solution.py:299
  90.1 12.5 %collective-permute-start.23 = (f32[8,22,128]{2,1,0:T(8,128)S(1)}, f32[8,22,128]{2,1,0:T(8,128)S(1)}, u32[]{:S(2)}, u32[]{:S(2)}) collective-permute-start(f32[8,22,128]{2,1,0:T(8,128)S(1)} %get-tuple-element.147), channel_id=1, source_target_pairs={{0,24},{4,28},{8,0},{12,4},{16,8},{20,12},{24,16},{28,20},{1,25},{... | collective-permute-start | bytes 270344 | tf_op jit(solution)/shard_map/ppermute | solution.py:299
  93.6 9.0 %collective-permute-start.22 = (f32[8,22,128]{2,1,0:T(8,128)S(1)}, f32[8,22,128]{2,1,0:T(8,128)S(1)}, u32[]{:S(2)}, u32[]{:S(2)}) collective-permute-start(f32[8,22,128]{2,1,0:T(8,128)S(1)} %get-tuple-element.147), channel_id=1, source_target_pairs={{0,16},{4,20},{8,24},{12,28},{16,0},{20,4},{24,8},{28,12},{1,17},{... | collective-permute-start | bytes 270344 | tf_op jit(solution)/shard_map/ppermute | solution.py:299
  116.3 7.4 %collective-permute-start.27 = (f32[72,256]{1,0:T(8,128)S(1)}, f32[72,256]{1,0:T(8,128)S(1)}, u32[]{:S(2)}, u32[]{:S(2)}) collective-permute-start(f32[72,256]{1,0:T(8,128)S(1)} %get-tuple-element.138), channel_id=1, source_target_pairs={{0,24},{4,28},{8,0},{12,4},{16,8},{20,12},{24,16},{28,20},{1,25},{... | collective-permute-start | bytes 221192 | tf_op jit(solution)/shard_map/ppermute | solution.py:226
  121.1 7.3 %collective-permute-start.26 = (f32[72,256]{1,0:T(8,128)S(1)}, f32[72,256]{1,0:T(8,128)S(1)}, u32[]{:S(2)}, u32[]{:S(2)}) collective-permute-start(f32[72,256]{1,0:T(8,128)S(1)} %get-tuple-element.139), channel_id=1, source_target_pairs={{0,16},{4,20},{8,24},{12,28},{16,0},{20,4},{24,8},{28,12},{1,17},{... | collective-permute-start | bytes 221192 | tf_op jit(solution)/shard_map/ppermute | solution.py:226
  121.1 7.3 %collective-permute-start.25 = (f32[72,256]{1,0:T(8,128)S(1)}, f32[72,256]{1,0:T(8,128)S(1)}, u32[]{:S(2)}, u32[]{:S(2)}) collective-permute-start(f32[72,256]{1,0:T(8,128)S(1)} %get-tuple-element.140), channel_id=1, source_target_pairs={{0,8},{4,12},{8,16},{12,20},{16,24},{20,28},{24,0},{28,4},{1,9},{5... | collective-permute-start | bytes 221192 | tf_op jit(solution)/shard_map/ppermute | solution.py:226
  128.7 5.9 %collective-permute-start.30 = (f32[1,72,256]{2,1,0:T(8,128)S(1)}, f32[1,72,256]{2,1,0:T(8,128)S(1)}, u32[]{:S(2)}, u32[]{:S(2)}) collective-permute-start(f32[1,72,256]{2,1,0:T(8,128)S(1)} %fusion.43), channel_id=1, source_target_pairs={{0,3},{1,2},{2,1},{3,0},{4,7},{5,6},{6,5},{7,4},{8,11},{9,10},{10,... | collective-permute-start | bytes 221192 | tf_op jit(solution)/shard_map/ppermute | solution.py:208
  128.7 5.9 %collective-permute-start.29 = (f32[1,72,256]{2,1,0:T(8,128)S(1)}, f32[1,72,256]{2,1,0:T(8,128)S(1)}, u32[]{:S(2)}, u32[]{:S(2)}) collective-permute-start(f32[1,72,256]{2,1,0:T(8,128)S(1)} %fusion.43), channel_id=1, source_target_pairs={{0,2},{1,3},{2,0},{3,1},{4,6},{5,7},{6,4},{7,5},{8,10},{9,11},{10,... | collective-permute-start | bytes 221192 | tf_op jit(solution)/shard_map/ppermute | solution.py:208
  129.4 5.2 %collective-permute-start.28 = (f32[1,72,256]{2,1,0:T(8,128)S(1)}, f32[1,72,256]{2,1,0:T(8,128)S(1)}, u32[]{:S(2)}, u32[]{:S(2)}) collective-permute-start(f32[1,72,256]{2,1,0:T(8,128)S(1)} %fusion.43), channel_id=1, source_target_pairs={{0,1},{1,0},{2,3},{3,2},{4,5},{5,4},{6,7},{7,6},{8,9},{9,8},{10,11... | collective-permute-start | bytes 221192 | tf_op jit(solution)/shard_map/ppermute | solution.py:208
  141.4 1.8 %collective-permute-start.31 = (f32[4,72,256]{2,1,0:T(8,128)}, f32[4,72,256]{2,1,0:T(8,128)S(1)}, u32[]{:S(2)}, u32[]{:S(2)}) collective-permute-start(f32[4,72,256]{2,1,0:T(8,128)} %get-tuple-element.109), channel_id=1, source_target_pairs={{0,4},{4,0},{8,12},{12,8},{16,20},{20,16},{24,28},{28,24},{1,5},{5... | collective-permute-start | bytes 884744 | tf_op jit(solution)/shard_map/ppermute | solution.py:222
  144.2 7.8 %collective-permute-start.32 = (f32[72,256]{1,0:T(8,128)S(1)}, f32[72,256]{1,0:T(8,128)S(1)}, u32[]{:S(2)}, u32[]{:S(2)}) collective-permute-start(f32[72,256]{1,0:T(8,128)S(1)} %get-tuple-element.134), channel_id=1, source_target_pairs={{0,8},{4,12},{8,16},{12,20},{16,24},{20,28},{24,0},{28,4},{1,9},{5... | collective-permute-start | bytes 221192 | tf_op jit(solution)/shard_map/ppermute | solution.py:226
  144.4 7.6 %collective-permute-start.34 = (f32[72,256]{1,0:T(8,128)S(1)}, f32[72,256]{1,0:T(8,128)S(1)}, u32[]{:S(2)}, u32[]{:S(2)}) collective-permute-start(f32[72,256]{1,0:T(8,128)S(1)} %get-tuple-element.135), channel_id=1, source_target_pairs={{0,24},{4,28},{8,0},{12,4},{16,8},{20,12},{24,16},{28,20},{1,25},{... | collective-permute-start | bytes 221192 | tf_op jit(solution)/shard_map/ppermute | solution.py:226
  149.3 7.2 %collective-permute-start.33 = (f32[72,256]{1,0:T(8,128)S(1)}, f32[72,256]{1,0:T(8,128)S(1)}, u32[]{:S(2)}, u32[]{:S(2)}) collective-permute-start(f32[72,256]{1,0:T(8,128)S(1)} %get-tuple-element.136), channel_id=1, source_target_pairs={{0,16},{4,20},{8,24},{12,28},{16,0},{20,4},{24,8},{28,12},{1,17},{... | collective-permute-start | bytes 221192 | tf_op jit(solution)/shard_map/ppermute | solution.py:226
  (9 other events, 109.1 us)

commit v10 on v8

--- a/solution.py
+++ b/solution.py
@@ -17,17 +17,19 @@
 ):
     step = pl.program_id(0)
     if mode == "image":
-        lost_ref = refs[0]
-        outs = refs[1:]
+        outs = refs
         body_rows = blocks_piece * vectors
 
         @pl.when(step == 0)
         def _():
+            lost_rows = x_ref[0, body_rows:, :]
+            for v in range(1, x_ref.shape[0]):
+                lost_rows = lost_rows + x_ref[v, body_rows:, :]
             for out_ref in outs:
                 count = out_ref.shape[0]
                 out_ref[:, :body_rows, :] = jnp.zeros((count, body_rows, out_ref.shape[2]), jnp.float32)
                 out_ref[:, body_rows:, :] = jnp.broadcast_to(
-                    lost_ref[...][None], (count,) + lost_ref.shape
+                    lost_rows[None], (count,) + lost_rows.shape
                 )
     else:
         (o_ref,) = refs
@@ -86,11 +88,6 @@
         pl.BlockSpec((None, None, group_size, side, side), tile_index),
     ]
     operands = [x_cols, tiles]
-    if mode == "image":
-        pad = padded_rows - blocks_piece * vectors
-        lost_block = jnp.zeros((pad, side), jnp.float32).at[0, :vectors].set(lost)
-        in_specs.append(pl.BlockSpec((pad, side), lambda i, *_: (0, 0)))
-        operands.append(lost_block)
     grid_spec = pltpu.PrefetchScalarGridSpec(
         num_scalar_prefetch=4,
         grid=(steps,),
@@ -238,12 +235,10 @@
 
     def relaxation(blocks, lost_sum=None, gathered=None):
         if gathered is None:
-            gathered, lost_dst = spread_columns(blocks, lost_partial(blocks))
-        else:
-            lost_dst = jnp.zeros((vectors,), jnp.float32)
+            gathered, _ = spread_columns(blocks, lost_partial(blocks))
         accumulated = tile_pass(
             "image", gathered, tiles, kernel_rows, kernel_cols, live_mask, block_count,
-            row_blocks, vectors, lost_dst,
+            row_blocks, vectors,
         )
         image, lost_total = reduce_rows(accumulated)
         if lost_sum is None:

time: 151 us -> 154 us (1.020)
  starting transfers between devices: 41.6 us -> 46.8 us
  waiting for transfers between devices: 49.3 us -> 46.8 us
  local copies, waits for them, and re-layouts: 11.7 us -> 9.59 us
  other arithmetic: 12.1 us -> 14 us
    ppermute x12, starting transfers between devices: 13.3 us -> 22.4 us  [reduce_rows(): total = total + lax.ppermute(part[shift], 'src', pairs)]
    ppermute x12, starting transfers between devices: 19.5 us -> 15.2 us  [spread_columns(): lax.ppermute(payload, 'dst', [(i, i ^ v) for i in range(dst_count)])]
    ppermute x12, waiting for transfers between devices: 11.5 us -> 7.47 us  [spread_columns(): lax.ppermute(payload, 'dst', [(i, i ^ v) for i in range(dst_count)])]
    ppermute x3, waiting for transfers between devices: 2.18 us -> 4.55 us  [per_device(): lax.ppermute(shared, 'dst', [(i, i ^ v) for i in range(dst_count)])]
    concatenate x4, other arithmetic: 0.82 us -> 2.94 us  [spread_columns(): payload = jnp.concatenate(pieces, axis=0)]
    scatter x4 -> x0, local copies, waits for them, and re-layouts: 2.02 us -> none  [the longest x3 2.02 us: tile_pass(): lost_block = jnp.zeros((pad, side), jnp.float32).at[0, :vectors].set(lost)]
    ppermute x12, waiting for transfers between devices: 23.3 us -> 21.3 us  [reduce_rows(): total = total + lax.ppermute(part[shift], 'src', pairs)]
    ppermute x3, starting transfers between devices: 3.55 us -> 5.21 us  [per_device(): lax.ppermute(shared, 'dst', [(i, i ^ v) for i in range(dst_count)])]
  transfers between devices with their start and end apart: 35 -> 35, of which waited for: 25 -> 20; matrix products, arithmetic and copies ran while one was open for 6% -> 6% of each run, Pallas kernels for 0% -> 0%
where the time goes in v10:
time: 154 us; the launch traced here: 152 us
  starting transfers between devices  46.8 us (30%)
  waiting for transfers between devices  46.8 us (30%)
  Pallas kernels  29.9 us (19%)
  other arithmetic  14 us (9%)
  local copies, waits for them, and re-layouts  9.59 us (6%)
  matrix products  3 us (2%)
  between operations  1.74 us (1%)
    pallas_call x5, Pallas kernels, tile_pass(): pl.pallas_call(functools.partial(tile_kernel, mode, blocks_piece, vectors...  29.9 us
    ppermute x12, starting transfers between devices, reduce_rows(): total = total + lax.ppermute(part[shift], 'src', pairs)  22.4 us
    ppermute x12, waiting for transfers between devices, reduce_rows(): total = total + lax.ppermute(part[shift], 'src', pairs)  21.3 us
    ppermute x12, starting transfers between devices, spread_columns(): lax.ppermute(payload, 'dst', [(i, i ^ v) for i in range(dst_count)])  15.2 us
    ppermute x12, waiting for transfers between devices, spread_columns(): lax.ppermute(payload, 'dst', [(i, i ^ v) for i in range(dst_count)])  7.47 us
    ppermute x4, waiting for transfers between devices, reduce_rows(): part = keep + lax.ppermute(give, 'src', [(i, i ^ 1) for i in range(n)])  6.31 us
    ppermute x3, waiting for transfers between devices, per_device(): pieces.append(lax.ppermute(shared, 'src', pairs))  5.95 us
    ppermute x3, starting transfers between devices, per_device(): lax.ppermute(shared, 'dst', [(i, i ^ v) for i in range(dst_count)])  5.21 us
  transfers between devices with their start and end apart: 35, of which 20 were waited for; matrix products, arithmetic and copies ran while one was open for 6% of the time, Pallas kernels for 0%

profile of v10, /device:TPU:0, one launch (start us, length us, event | category | flops | bytes accessed | tf_op | source)
XLA Modules:
  0.0 151.8 jit_solution(17050417637904625474)
XLA Ops:
  2.6 4.0 %collective-permute-start.2 = (f32[1,72,256]{2,1,0:T(8,128)S(1)}, f32[1,72,256]{2,1,0:T(8,128)S(1)}, u32[]{:S(2)}, u32[]{:S(2)}) collective-permute-start(f32[1,72,256]{2,1,0:T(8,128)S(1)} %fusion.44), channel_id=1, source_target_pairs={{0,3},{1,2},{2,1},{3,0},{4,7},{5,6},{6,5},{7,4},{8,11},{9,10},{10,... | collective-permute-start | bytes 221192 | tf_op jit(solution)/shard_map/ppermute | solution.py:205
  7.9 1.6 %gather_fusion = s32[128]{0:T(128)S(1)} fusion(s32[128]{0:T(128)} %param.21, s32[1024]{0:T(1024)S(1)} %pad_clamp_fusion.3), kind=kCustom, calls=%fused_computation | custom fusion | bytes 1536 | tf_op jit(solution)/shard_map/gather | solution.py:150
  12.7 6.1 %shard_map.95 = (f32[4,72,256]{2,1,0:T(8,128)}, f32[4,72,256]{2,1,0:T(8,128)}) custom-call(s32[128]{0:T(128)} %get-tuple-element.111.rows_ref, s32[128]{0:T(128)} %get-tuple-element.112.cols_ref, s32[128]{0:T(128)} %and_convert_fusion.live_ref, s32[1]{0:T(128)} %bitcast.5.nb_ref, f32[4,72,256]{2,1,0:T(8,128)} %pad_maximum_fusion.x_ref, ...), custom_call_target="tpu_custom_call" | custom-call | tf_op jit(solution)/shard_map/pallas_call | solution.py:97
  18.9 1.7 %collective-permute-done.3 = f32[4,72,256]{2,1,0:T(8,128)S(1)} collective-permute-done((f32[4,72,256]{2,1,0:T(8,128)}, f32[4,72,256]{2,1,0:T(8,128)S(1)}, u32[]{:S(2)}, u32[]{:S(2)}) %collective-permute-start.3) | collective-permute-done | bytes 294944 | tf_op jit(solution)/shard_map/ppermute | solution.py:219
  21.6 4.1 %collective-permute-start.6 = (f32[72,256]{1,0:T(8,128)S(1)}, f32[72,256]{1,0:T(8,128)S(1)}, u32[]{:S(2)}, u32[]{:S(2)}) collective-permute-start(f32[72,256]{1,0:T(8,128)S(1)} %get-tuple-element.98), channel_id=1, source_target_pairs={{0,24},{4,28},{8,0},{12,4},{16,8},{20,12},{24,16},{28,20},{1,25},{... | collective-permute-start | bytes 221192 | tf_op jit(solution)/shard_map/ppermute | solution.py:223
  29.2 5.1 %collective-permute-done.5 = f32[72,256]{1,0:T(8,128)S(1)} collective-permute-done((f32[72,256]{1,0:T(8,128)S(1)}, f32[72,256]{1,0:T(8,128)S(1)}, u32[]{:S(2)}, u32[]{:S(2)}) %collective-permute-start.5) | collective-permute-done | bytes 73760 | tf_op jit(solution)/shard_map/ppermute | solution.py:223
  34.5 2.3 %collective-permute-start.9 = (f32[1,72,256]{2,1,0:T(8,128)S(1)}, f32[1,72,256]{2,1,0:T(8,128)S(1)}, u32[]{:S(2)}, u32[]{:S(2)}) collective-permute-start(f32[1,72,256]{2,1,0:T(8,128)S(1)} %fusion.40), channel_id=1, source_target_pairs={{0,3},{1,2},{2,1},{3,0},{4,7},{5,6},{6,5},{7,4},{8,11},{9,10},{10,... | collective-permute-start | bytes 221192 | tf_op jit(solution)/shard_map/ppermute | solution.py:205
  38.1 2.4 %collective-permute-done.9 = f32[1,72,256]{2,1,0:T(8,128)S(1)} collective-permute-done((f32[1,72,256]{2,1,0:T(8,128)S(1)}, f32[1,72,256]{2,1,0:T(8,128)S(1)}, u32[]{:S(2)}, u32[]{:S(2)}) %collective-permute-start.9) | collective-permute-done | bytes 73760 | tf_op jit(solution)/shard_map/ppermute | solution.py:205
  42.0 6.0 %shard_map.96 = (f32[4,72,256]{2,1,0:T(8,128)}, f32[4,72,256]{2,1,0:T(8,128)}) custom-call(s32[128]{0:T(128)} %get-tuple-element.111.rows_ref, s32[128]{0:T(128)} %get-tuple-element.112.cols_ref, s32[128]{0:T(128)} %and_convert_fusion.live_ref, s32[1]{0:T(128)} %bitcast.5.nb_ref, f32[4,72,256]{2,1,0:T(8,128)} %pad_maximum_fusion.1.x_ref, ...), custom_call_target="tpu_custom_call" | custom-call | tf_op jit(solution)/shard_map/pallas_call | solution.py:97
  52.2 2.5 %collective-permute-start.12 = (f32[72,256]{1,0:T(8,128)S(1)}, f32[72,256]{1,0:T(8,128)S(1)}, u32[]{:S(2)}, u32[]{:S(2)}) collective-permute-start(f32[72,256]{1,0:T(8,128)S(1)} %get-tuple-element.96), channel_id=1, source_target_pairs={{0,16},{4,20},{8,24},{12,28},{16,0},{20,4},{24,8},{28,12},{1,17},{... | collective-permute-start | bytes 221192 | tf_op jit(solution)/shard_map/ppermute | solution.py:223
  54.8 1.9 %collective-permute-start.11 = (f32[72,256]{1,0:T(8,128)S(1)}, f32[72,256]{1,0:T(8,128)S(1)}, u32[]{:S(2)}, u32[]{:S(2)}) collective-permute-start(f32[72,256]{1,0:T(8,128)S(1)} %get-tuple-element.94), channel_id=1, source_target_pairs={{0,8},{4,12},{8,16},{12,20},{16,24},{20,28},{24,0},{28,4},{1,9},{5... | collective-permute-start | bytes 221192 | tf_op jit(solution)/shard_map/ppermute | solution.py:223
  57.9 4.3 %collective-permute-done.12 = f32[72,256]{1,0:T(8,128)S(1)} collective-permute-done((f32[72,256]{1,0:T(8,128)S(1)}, f32[72,256]{1,0:T(8,128)S(1)}, u32[]{:S(2)}, u32[]{:S(2)}) %collective-permute-start.12) | collective-permute-done | bytes 73760 | tf_op jit(solution)/shard_map/ppermute | solution.py:223
  62.4 2.5 %collective-permute-start.16 = (f32[1,72,256]{2,1,0:T(8,128)S(1)}, f32[1,72,256]{2,1,0:T(8,128)S(1)}, u32[]{:S(2)}, u32[]{:S(2)}) collective-permute-start(f32[1,72,256]{2,1,0:T(8,128)S(1)} %fusion.36), channel_id=1, source_target_pairs={{0,3},{1,2},{2,1},{3,0},{4,7},{5,6},{6,5},{7,4},{8,11},{9,10},{10,... | collective-permute-start | bytes 221192 | tf_op jit(solution)/shard_map/ppermute | solution.py:205
  70.1 5.6 %shard_map.97 = f32[16,128]{1,0:T(8,128)} custom-call(s32[128]{0:T(128)} %clamp_bitcast_fusion.rows_ref, s32[128]{0:T(128)} %get-tuple-element.112.cols_ref, s32[128]{0:T(128)} %and_convert_fusion.live_ref, s32[1]{0:T(128)} %bitcast.5.nb_ref, f32[4,72,256]{2,1,0:T(8,128)} %pad_maximum_fusion.2.x_ref, bf16[1,1,128,256,256]{4,3,2,1,0:T(8,128)(2,1)} %t_ref.9), custom_call_target="tpu_custom_call" | custom-call | tf_op jit(solution)/shard_map/pallas_call | solution.py:97
  77.8 4.1 %collective-permute-start.18 = (f32[1,2440]{1,0:T(1,128)S(1)}, f32[1,2440]{1,0:T(1,128)S(1)}, u32[]{:S(2)}, u32[]{:S(2)}) collective-permute-start(f32[1,2440]{1,0:T(1,128)S(1)} %broadcast_in_dim.21), channel_id=1, source_target_pairs={{0,2},{1,3},{2,0},{3,1},{4,6},{5,7},{6,4},{7,5},{8,10},{9,11},{10,... | collective-permute-start | bytes 29288 | tf_op jit(solution)/shard_map/ppermute | solution.py:279
  81.9 1.6 %collective-permute-done.18 = f32[1,2440]{1,0:T(1,128)S(1)} collective-permute-done((f32[1,2440]{1,0:T(1,128)S(1)}, f32[1,2440]{1,0:T(1,128)S(1)}, u32[]{:S(2)}, u32[]{:S(2)}) %collective-permute-start.18) | collective-permute-done | bytes 9792 | tf_op jit(solution)/shard_map/ppermute | solution.py:279
  83.5 2.9 %collective-permute-done.19 = f32[1,2440]{1,0:T(1,128)S(1)} collective-permute-done((f32[1,2440]{1,0:T(1,128)S(1)}, f32[1,2440]{1,0:T(1,128)S(1)}, u32[]{:S(2)}, u32[]{:S(2)}) %collective-permute-start.19) | collective-permute-done | bytes 9792 | tf_op jit(solution)/shard_map/ppermute | solution.py:279
  88.0 3.7 %collective-permute-start.23 = (f32[8,2440]{1,0:T(8,128)S(1)}, f32[8,2440]{1,0:T(8,128)S(1)}, u32[]{:S(2)}, u32[]{:S(2)}) collective-permute-start(f32[8,2440]{1,0:T(8,128)S(1)} %concatenate.57), channel_id=1, source_target_pairs={{0,24},{4,28},{8,0},{12,4},{16,8},{20,12},{24,16},{28,20},{1,25},{... | collective-permute-start | bytes 234248 | tf_op jit(solution)/shard_map/ppermute | solution.py:291
  91.8 3.4 %collective-permute-done.21 = f32[8,2440]{1,0:T(8,128)S(1)} collective-permute-done((f32[8,2440]{1,0:T(8,128)S(1)}, f32[8,2440]{1,0:T(8,128)S(1)}, u32[]{:S(2)}, u32[]{:S(2)}) %collective-permute-start.21) | collective-permute-done | bytes 78112 | tf_op jit(solution)/shard_map/ppermute | solution.py:291
  95.1 2.6 %collective-permute-done.22 = f32[8,2440]{1,0:T(8,128)S(1)} collective-permute-done((f32[8,2440]{1,0:T(8,128)S(1)}, f32[8,2440]{1,0:T(8,128)S(1)}, u32[]{:S(2)}, u32[]{:S(2)}) %collective-permute-start.22) | collective-permute-done | bytes 78112 | tf_op jit(solution)/shard_map/ppermute | solution.py:291
  103.9 6.1 %shard_map.98 = (f32[4,72,256]{2,1,0:T(8,128)}, f32[4,72,256]{2,1,0:T(8,128)}) custom-call(s32[128]{0:T(128)} %get-tuple-element.111.rows_ref, s32[128]{0:T(128)} %get-tuple-element.112.cols_ref, s32[128]{0:T(128)} %and_convert_fusion.live_ref, s32[1]{0:T(128)} %bitcast.5.nb_ref, f32[4,72,256]{2,1,0:T(8,128)} %broadcast_multiply_fusion.x_ref, ...), custom_call_target="tpu_custom_call" | custom-call | tf_op jit(solution)/shard_map/pallas_call | solution.py:97
  110.1 1.8 %collective-permute-done.24 = f32[4,72,256]{2,1,0:T(8,128)S(1)} collective-permute-done((f32[4,72,256]{2,1,0:T(8,128)}, f32[4,72,256]{2,1,0:T(8,128)S(1)}, u32[]{:S(2)}, u32[]{:S(2)}) %collective-permute-start.24) | collective-permute-done | bytes 294944 | tf_op jit(solution)/shard_map/ppermute | solution.py:219
  112.9 2.1 %collective-permute-start.27 = (f32[72,256]{1,0:T(8,128)S(1)}, f32[72,256]{1,0:T(8,128)S(1)}, u32[]{:S(2)}, u32[]{:S(2)}) collective-permute-start(f32[72,256]{1,0:T(8,128)S(1)} %get-tuple-element.91), channel_id=1, source_target_pairs={{0,24},{4,28},{8,0},{12,4},{16,8},{20,12},{24,16},{28,20},{1,25},{... | collective-permute-start | bytes 221192 | tf_op jit(solution)/shard_map/ppermute | solution.py:223
  115.0 3.1 %collective-permute-start.26 = (f32[72,256]{1,0:T(8,128)S(1)}, f32[72,256]{1,0:T(8,128)S(1)}, u32[]{:S(2)}, u32[]{:S(2)}) collective-permute-start(f32[72,256]{1,0:T(8,128)S(1)} %get-tuple-element.92), channel_id=1, source_target_pairs={{0,16},{4,20},{8,24},{12,28},{16,0},{20,4},{24,8},{28,12},{1,17},{... | collective-permute-start | bytes 221192 | tf_op jit(solution)/shard_map/ppermute | solution.py:223
  119.5 5.9 %collective-permute-done.26 = f32[72,256]{1,0:T(8,128)S(1)} collective-permute-done((f32[72,256]{1,0:T(8,128)S(1)}, f32[72,256]{1,0:T(8,128)S(1)}, u32[]{:S(2)}, u32[]{:S(2)}) %collective-permute-start.26) | collective-permute-done | bytes 73760 | tf_op jit(solution)/shard_map/ppermute | solution.py:223
  125.8 3.4 %collective-permute-start.28 = (f32[1,72,256]{2,1,0:T(8,128)S(1)}, f32[1,72,256]{2,1,0:T(8,128)S(1)}, u32[]{:S(2)}, u32[]{:S(2)}) collective-permute-start(f32[1,72,256]{2,1,0:T(8,128)S(1)} %fusion.35), channel_id=1, source_target_pairs={{0,1},{1,0},{2,3},{3,2},{4,5},{5,4},{6,7},{7,6},{8,9},{9,8},{10,11... | collective-permute-start | bytes 221192 | tf_op jit(solution)/shard_map/ppermute | solution.py:205
  129.2 1.9 %collective-permute-done.30 = f32[1,72,256]{2,1,0:T(8,128)S(1)} collective-permute-done((f32[1,72,256]{2,1,0:T(8,128)S(1)}, f32[1,72,256]{2,1,0:T(8,128)S(1)}, u32[]{:S(2)}, u32[]{:S(2)}) %collective-permute-start.30) | collective-permute-done | bytes 73760 | tf_op jit(solution)/shard_map/ppermute | solution.py:205
  132.2 6.0 %shard_map.99 = (f32[4,72,256]{2,1,0:T(8,128)}, f32[4,72,256]{2,1,0:T(8,128)}) custom-call(s32[128]{0:T(128)} %get-tuple-element.111.rows_ref, s32[128]{0:T(128)} %get-tuple-element.112.cols_ref, s32[128]{0:T(128)} %and_convert_fusion.live_ref, s32[1]{0:T(128)} %bitcast.5.nb_ref, f32[4,72,256]{2,1,0:T(8,128)} %pad_maximum_fusion.3.x_ref, ...), custom_call_target="tpu_custom_call" | custom-call | tf_op jit(solution)/shard_map/pallas_call | solution.py:97
  138.3 1.7 %collective-permute-done.31 = f32[4,72,256]{2,1,0:T(8,128)S(1)} collective-permute-done((f32[4,72,256]{2,1,0:T(8,128)}, f32[4,72,256]{2,1,0:T(8,128)S(1)}, u32[]{:S(2)}, u32[]{:S(2)}) %collective-permute-start.31) | collective-permute-done | bytes 294944 | tf_op jit(solution)/shard_map/ppermute | solution.py:219
  141.1 2.3 %collective-permute-start.33 = (f32[72,256]{1,0:T(8,128)S(1)}, f32[72,256]{1,0:T(8,128)S(1)}, u32[]{:S(2)}, u32[]{:S(2)}) collective-permute-start(f32[72,256]{1,0:T(8,128)S(1)} %get-tuple-element.89), channel_id=1, source_target_pairs={{0,16},{4,20},{8,24},{12,28},{16,0},{20,4},{24,8},{28,12},{1,17},{... | collective-permute-start | bytes 221192 | tf_op jit(solution)/shard_map/ppermute | solution.py:223
  143.5 1.9 %collective-permute-start.32 = (f32[72,256]{1,0:T(8,128)S(1)}, f32[72,256]{1,0:T(8,128)S(1)}, u32[]{:S(2)}, u32[]{:S(2)}) collective-permute-start(f32[72,256]{1,0:T(8,128)S(1)} %get-tuple-element.87), channel_id=1, source_target_pairs={{0,8},{4,12},{8,16},{12,20},{16,24},{20,28},{24,0},{28,4},{1,9},{5... | collective-permute-start | bytes 221192 | tf_op jit(solution)/shard_map/ppermute | solution.py:223
  146.2 4.7 %collective-permute-done.33 = f32[72,256]{1,0:T(8,128)S(1)} collective-permute-done((f32[72,256]{1,0:T(8,128)S(1)}, f32[72,256]{1,0:T(8,128)S(1)}, u32[]{:S(2)}, u32[]{:S(2)}) %collective-permute-start.33) | collective-permute-done | bytes 73760 | tf_op jit(solution)/shard_map/ppermute | solution.py:223
  (148 shorter events, 40.4 us)
Async XLA Ops:
  2.6 9.3 %collective-permute-start.2 = (f32[1,72,256]{2,1,0:T(8,128)S(1)}, f32[1,72,256]{2,1,0:T(8,128)S(1)}, u32[]{:S(2)}, u32[]{:S(2)}) collective-permute-start(f32[1,72,256]{2,1,0:T(8,128)S(1)} %fusion.44), channel_id=1, source_target_pairs={{0,3},{1,2},{2,1},{3,0},{4,7},{5,6},{6,5},{7,4},{8,11},{9,10},{10,... | collective-permute-start | bytes 221192 | tf_op jit(solution)/shard_map/ppermute | solution.py:205
  6.6 5.4 %collective-permute-start.1 = (f32[1,72,256]{2,1,0:T(8,128)S(1)}, f32[1,72,256]{2,1,0:T(8,128)S(1)}, u32[]{:S(2)}, u32[]{:S(2)}) collective-permute-start(f32[1,72,256]{2,1,0:T(8,128)S(1)} %fusion.44), channel_id=1, source_target_pairs={{0,2},{1,3},{2,0},{3,1},{4,6},{5,7},{6,4},{7,5},{8,10},{9,11},{10,... | collective-permute-start | bytes 221192 | tf_op jit(solution)/shard_map/ppermute | solution.py:205
  7.1 4.9 %collective-permute-start = (f32[1,72,256]{2,1,0:T(8,128)S(1)}, f32[1,72,256]{2,1,0:T(8,128)S(1)}, u32[]{:S(2)}, u32[]{:S(2)}) collective-permute-start(f32[1,72,256]{2,1,0:T(8,128)S(1)} %fusion.44), channel_id=1, source_target_pairs={{0,1},{1,0},{2,3},{3,2},{4,5},{5,4},{6,7},{7,6},{8,9},{9,8},{10,11... | collective-permute-start | bytes 221192 | tf_op jit(solution)/shard_map/ppermute | solution.py:205
  18.8 1.8 %collective-permute-start.3 = (f32[4,72,256]{2,1,0:T(8,128)}, f32[4,72,256]{2,1,0:T(8,128)S(1)}, u32[]{:S(2)}, u32[]{:S(2)}) collective-permute-start(f32[4,72,256]{2,1,0:T(8,128)} %get-tuple-element.59), channel_id=1, source_target_pairs={{0,4},{4,0},{8,12},{12,8},{16,20},{20,16},{24,28},{28,24},{1,5},{5... | collective-permute-start | bytes 884744 | tf_op jit(solution)/shard_map/ppermute | solution.py:219
  21.6 7.5 %collective-permute-start.6 = (f32[72,256]{1,0:T(8,128)S(1)}, f32[72,256]{1,0:T(8,128)S(1)}, u32[]{:S(2)}, u32[]{:S(2)}) collective-permute-start(f32[72,256]{1,0:T(8,128)S(1)} %get-tuple-element.98), channel_id=1, source_target_pairs={{0,24},{4,28},{8,0},{12,4},{16,8},{20,12},{24,16},{28,20},{1,25},{... | collective-permute-start | bytes 221192 | tf_op jit(solution)/shard_map/ppermute | solution.py:223
  25.7 8.5 %collective-permute-start.5 = (f32[72,256]{1,0:T(8,128)S(1)}, f32[72,256]{1,0:T(8,128)S(1)}, u32[]{:S(2)}, u32[]{:S(2)}) collective-permute-start(f32[72,256]{1,0:T(8,128)S(1)} %get-tuple-element.99), channel_id=1, source_target_pairs={{0,16},{4,20},{8,24},{12,28},{16,0},{20,4},{24,8},{28,12},{1,17},{... | collective-permute-start | bytes 221192 | tf_op jit(solution)/shard_map/ppermute | solution.py:223
  27.0 7.2 %collective-permute-start.4 = (f32[72,256]{1,0:T(8,128)S(1)}, f32[72,256]{1,0:T(8,128)S(1)}, u32[]{:S(2)}, u32[]{:S(2)}) collective-permute-start(f32[72,256]{1,0:T(8,128)S(1)} %get-tuple-element.97), channel_id=1, source_target_pairs={{0,8},{4,12},{8,16},{12,20},{16,24},{20,28},{24,0},{28,4},{1,9},{5... | collective-permute-start | bytes 221192 | tf_op jit(solution)/shard_map/ppermute | solution.py:223
  34.5 6.0 %collective-permute-start.9 = (f32[1,72,256]{2,1,0:T(8,128)S(1)}, f32[1,72,256]{2,1,0:T(8,128)S(1)}, u32[]{:S(2)}, u32[]{:S(2)}) collective-permute-start(f32[1,72,256]{2,1,0:T(8,128)S(1)} %fusion.40), channel_id=1, source_target_pairs={{0,3},{1,2},{2,1},{3,0},{4,7},{5,6},{6,5},{7,4},{8,11},{9,10},{10,... | collective-permute-start | bytes 221192 | tf_op jit(solution)/shard_map/ppermute | solution.py:205
  36.8 4.4 %collective-permute-start.8 = (f32[1,72,256]{2,1,0:T(8,128)S(1)}, f32[1,72,256]{2,1,0:T(8,128)S(1)}, u32[]{:S(2)}, u32[]{:S(2)}) collective-permute-start(f32[1,72,256]{2,1,0:T(8,128)S(1)} %fusion.40), channel_id=1, source_target_pairs={{0,2},{1,3},{2,0},{3,1},{4,6},{5,7},{6,4},{7,5},{8,10},{9,11},{10,... | collective-permute-start | bytes 221192 | tf_op jit(solution)/shard_map/ppermute | solution.py:205
  36.9 4.4 %collective-permute-start.7 = (f32[1,72,256]{2,1,0:T(8,128)S(1)}, f32[1,72,256]{2,1,0:T(8,128)S(1)}, u32[]{:S(2)}, u32[]{:S(2)}) collective-permute-start(f32[1,72,256]{2,1,0:T(8,128)S(1)} %fusion.40), channel_id=1, source_target_pairs={{0,1},{1,0},{2,3},{3,2},{4,5},{5,4},{6,7},{7,6},{8,9},{9,8},{10,11... | collective-permute-start | bytes 221192 | tf_op jit(solution)/shard_map/ppermute | solution.py:205
  48.0 1.8 %collective-permute-start.10 = (f32[4,72,256]{2,1,0:T(8,128)}, f32[4,72,256]{2,1,0:T(8,128)S(1)}, u32[]{:S(2)}, u32[]{:S(2)}) collective-permute-start(f32[4,72,256]{2,1,0:T(8,128)} %get-tuple-element.61), channel_id=1, source_target_pairs={{0,4},{4,0},{8,12},{12,8},{16,20},{20,16},{24,28},{28,24},{1,5},{5... | collective-permute-start | bytes 884744 | tf_op jit(solution)/shard_map/ppermute | solution.py:219
  50.8 7.1 %collective-permute-start.13 = (f32[72,256]{1,0:T(8,128)S(1)}, f32[72,256]{1,0:T(8,128)S(1)}, u32[]{:S(2)}, u32[]{:S(2)}) collective-permute-start(f32[72,256]{1,0:T(8,128)S(1)} %get-tuple-element.95), channel_id=1, source_target_pairs={{0,24},{4,28},{8,0},{12,4},{16,8},{20,12},{24,16},{28,20},{1,25},{... | collective-permute-start | bytes 221192 | tf_op jit(solution)/shard_map/ppermute | solution.py:223
  52.2 10.0 %collective-permute-start.12 = (f32[72,256]{1,0:T(8,128)S(1)}, f32[72,256]{1,0:T(8,128)S(1)}, u32[]{:S(2)}, u32[]{:S(2)}) collective-permute-start(f32[72,256]{1,0:T(8,128)S(1)} %get-tuple-element.96), channel_id=1, source_target_pairs={{0,16},{4,20},{8,24},{12,28},{16,0},{20,4},{24,8},{28,12},{1,17},{... | collective-permute-start | bytes 221192 | tf_op jit(solution)/shard_map/ppermute | solution.py:223
  54.8 7.5 %collective-permute-start.11 = (f32[72,256]{1,0:T(8,128)S(1)}, f32[72,256]{1,0:T(8,128)S(1)}, u32[]{:S(2)}, u32[]{:S(2)}) collective-permute-start(f32[72,256]{1,0:T(8,128)S(1)} %get-tuple-element.94), channel_id=1, source_target_pairs={{0,8},{4,12},{8,16},{12,20},{16,24},{20,28},{24,0},{28,4},{1,9},{5... | collective-permute-start | bytes 221192 | tf_op jit(solution)/shard_map/ppermute | solution.py:223
  62.4 5.9 %collective-permute-start.16 = (f32[1,72,256]{2,1,0:T(8,128)S(1)}, f32[1,72,256]{2,1,0:T(8,128)S(1)}, u32[]{:S(2)}, u32[]{:S(2)}) collective-permute-start(f32[1,72,256]{2,1,0:T(8,128)S(1)} %fusion.36), channel_id=1, source_target_pairs={{0,3},{1,2},{2,1},{3,0},{4,7},{5,6},{6,5},{7,4},{8,11},{9,10},{10,... | collective-permute-start | bytes 221192 | tf_op jit(solution)/shard_map/ppermute | solution.py:205
  65.0 4.4 %collective-permute-start.15 = (f32[1,72,256]{2,1,0:T(8,128)S(1)}, f32[1,72,256]{2,1,0:T(8,128)S(1)}, u32[]{:S(2)}, u32[]{:S(2)}) collective-permute-start(f32[1,72,256]{2,1,0:T(8,128)S(1)} %fusion.36), channel_id=1, source_target_pairs={{0,2},{1,3},{2,0},{3,1},{4,6},{5,7},{6,4},{7,5},{8,10},{9,11},{10,... | collective-permute-start | bytes 221192 | tf_op jit(solution)/shard_map/ppermute | solution.py:205
  65.0 4.4 %collective-permute-start.14 = (f32[1,72,256]{2,1,0:T(8,128)S(1)}, f32[1,72,256]{2,1,0:T(8,128)S(1)}, u32[]{:S(2)}, u32[]{:S(2)}) collective-permute-start(f32[1,72,256]{2,1,0:T(8,128)S(1)} %fusion.36), channel_id=1, source_target_pairs={{0,1},{1,0},{2,3},{3,2},{4,5},{5,4},{6,7},{7,6},{8,9},{9,8},{10,11... | collective-permute-start | bytes 221192 | tf_op jit(solution)/shard_map/ppermute | solution.py:205
  76.7 5.2 %collective-permute-start.17 = (f32[1,2440]{1,0:T(1,128)S(1)}, f32[1,2440]{1,0:T(1,128)S(1)}, u32[]{:S(2)}, u32[]{:S(2)}) collective-permute-start(f32[1,2440]{1,0:T(1,128)S(1)} %broadcast_in_dim.21), channel_id=1, source_target_pairs={{0,1},{1,0},{2,3},{3,2},{4,5},{5,4},{6,7},{7,6},{8,9},{9,8},{10,11... | collective-permute-start | bytes 29288 | tf_op jit(solution)/shard_map/ppermute | solution.py:279
  77.8 5.8 %collective-permute-start.18 = (f32[1,2440]{1,0:T(1,128)S(1)}, f32[1,2440]{1,0:T(1,128)S(1)}, u32[]{:S(2)}, u32[]{:S(2)}) collective-permute-start(f32[1,2440]{1,0:T(1,128)S(1)} %broadcast_in_dim.21), channel_id=1, source_target_pairs={{0,2},{1,3},{2,0},{3,1},{4,6},{5,7},{6,4},{7,5},{8,10},{9,11},{10,... | collective-permute-start | bytes 29288 | tf_op jit(solution)/shard_map/ppermute | solution.py:279
  81.9 4.6 %collective-permute-start.19 = (f32[1,2440]{1,0:T(1,128)S(1)}, f32[1,2440]{1,0:T(1,128)S(1)}, u32[]{:S(2)}, u32[]{:S(2)}) collective-permute-start(f32[1,2440]{1,0:T(1,128)S(1)} %broadcast_in_dim.21), channel_id=1, source_target_pairs={{0,3},{1,2},{2,1},{3,0},{4,7},{5,6},{6,5},{7,4},{8,11},{9,10},{10,... | collective-permute-start | bytes 29288 | tf_op jit(solution)/shard_map/ppermute | solution.py:279
  87.9 7.2 %collective-permute-start.21 = (f32[8,2440]{1,0:T(8,128)S(1)}, f32[8,2440]{1,0:T(8,128)S(1)}, u32[]{:S(2)}, u32[]{:S(2)}) collective-permute-start(f32[8,2440]{1,0:T(8,128)S(1)} %concatenate.57), channel_id=1, source_target_pairs={{0,8},{4,12},{8,16},{12,20},{16,24},{20,28},{24,0},{28,4},{1,9},{5... | collective-permute-start | bytes 234248 | tf_op jit(solution)/shard_map/ppermute | solution.py:291
  88.0 9.8 %collective-permute-start.22 = (f32[8,2440]{1,0:T(8,128)S(1)}, f32[8,2440]{1,0:T(8,128)S(1)}, u32[]{:S(2)}, u32[]{:S(2)}) collective-permute-start(f32[8,2440]{1,0:T(8,128)S(1)} %concatenate.57), channel_id=1, source_target_pairs={{0,16},{4,20},{8,24},{12,28},{16,0},{20,4},{24,8},{28,12},{1,17},{... | collective-permute-start | bytes 234248 | tf_op jit(solution)/shard_map/ppermute | solution.py:291
  88.0 9.7 %collective-permute-start.23 = (f32[8,2440]{1,0:T(8,128)S(1)}, f32[8,2440]{1,0:T(8,128)S(1)}, u32[]{:S(2)}, u32[]{:S(2)}) collective-permute-start(f32[8,2440]{1,0:T(8,128)S(1)} %concatenate.57), channel_id=1, source_target_pairs={{0,24},{4,28},{8,0},{12,4},{16,8},{20,12},{24,16},{28,20},{1,25},{... | collective-permute-start | bytes 234248 | tf_op jit(solution)/shard_map/ppermute | solution.py:291
  112.9 6.6 %collective-permute-start.27 = (f32[72,256]{1,0:T(8,128)S(1)}, f32[72,256]{1,0:T(8,128)S(1)}, u32[]{:S(2)}, u32[]{:S(2)}) collective-permute-start(f32[72,256]{1,0:T(8,128)S(1)} %get-tuple-element.91), channel_id=1, source_target_pairs={{0,24},{4,28},{8,0},{12,4},{16,8},{20,12},{24,16},{28,20},{1,25},{... | collective-permute-start | bytes 221192 | tf_op jit(solution)/shard_map/ppermute | solution.py:223
  115.0 10.4 %collective-permute-start.26 = (f32[72,256]{1,0:T(8,128)S(1)}, f32[72,256]{1,0:T(8,128)S(1)}, u32[]{:S(2)}, u32[]{:S(2)}) collective-permute-start(f32[72,256]{1,0:T(8,128)S(1)} %get-tuple-element.92), channel_id=1, source_target_pairs={{0,16},{4,20},{8,24},{12,28},{16,0},{20,4},{24,8},{28,12},{1,17},{... | collective-permute-start | bytes 221192 | tf_op jit(solution)/shard_map/ppermute | solution.py:223
  118.1 7.2 %collective-permute-start.25 = (f32[72,256]{1,0:T(8,128)S(1)}, f32[72,256]{1,0:T(8,128)S(1)}, u32[]{:S(2)}, u32[]{:S(2)}) collective-permute-start(f32[72,256]{1,0:T(8,128)S(1)} %get-tuple-element.93), channel_id=1, source_target_pairs={{0,8},{4,12},{8,16},{12,20},{16,24},{20,28},{24,0},{28,4},{1,9},{5... | collective-permute-start | bytes 221192 | tf_op jit(solution)/shard_map/ppermute | solution.py:223
  125.6 5.5 %collective-permute-start.30 = (f32[1,72,256]{2,1,0:T(8,128)S(1)}, f32[1,72,256]{2,1,0:T(8,128)S(1)}, u32[]{:S(2)}, u32[]{:S(2)}) collective-permute-start(f32[1,72,256]{2,1,0:T(8,128)S(1)} %fusion.35), channel_id=1, source_target_pairs={{0,3},{1,2},{2,1},{3,0},{4,7},{5,6},{6,5},{7,4},{8,11},{9,10},{10,... | collective-permute-start | bytes 221192 | tf_op jit(solution)/shard_map/ppermute | solution.py:205
  125.7 5.4 %collective-permute-start.29 = (f32[1,72,256]{2,1,0:T(8,128)S(1)}, f32[1,72,256]{2,1,0:T(8,128)S(1)}, u32[]{:S(2)}, u32[]{:S(2)}) collective-permute-start(f32[1,72,256]{2,1,0:T(8,128)S(1)} %fusion.35), channel_id=1, source_target_pairs={{0,2},{1,3},{2,0},{3,1},{4,6},{5,7},{6,4},{7,5},{8,10},{9,11},{10,... | collective-permute-start | bytes 221192 | tf_op jit(solution)/shard_map/ppermute | solution.py:205
  125.8 5.7 %collective-permute-start.28 = (f32[1,72,256]{2,1,0:T(8,128)S(1)}, f32[1,72,256]{2,1,0:T(8,128)S(1)}, u32[]{:S(2)}, u32[]{:S(2)}) collective-permute-start(f32[1,72,256]{2,1,0:T(8,128)S(1)} %fusion.35), channel_id=1, source_target_pairs={{0,1},{1,0},{2,3},{3,2},{4,5},{5,4},{6,7},{7,6},{8,9},{9,8},{10,11... | collective-permute-start | bytes 221192 | tf_op jit(solution)/shard_map/ppermute | solution.py:205
  141.0 5.1 %collective-permute-start.34 = (f32[72,256]{1,0:T(8,128)S(1)}, f32[72,256]{1,0:T(8,128)S(1)}, u32[]{:S(2)}, u32[]{:S(2)}) collective-permute-start(f32[72,256]{1,0:T(8,128)S(1)} %get-tuple-element.88), channel_id=1, source_target_pairs={{0,24},{4,28},{8,0},{12,4},{16,8},{20,12},{24,16},{28,20},{1,25},{... | collective-permute-start | bytes 221192 | tf_op jit(solution)/shard_map/ppermute | solution.py:223
  141.1 9.8 %collective-permute-start.33 = (f32[72,256]{1,0:T(8,128)S(1)}, f32[72,256]{1,0:T(8,128)S(1)}, u32[]{:S(2)}, u32[]{:S(2)}) collective-permute-start(f32[72,256]{1,0:T(8,128)S(1)} %get-tuple-element.89), channel_id=1, source_target_pairs={{0,16},{4,20},{8,24},{12,28},{16,0},{20,4},{24,8},{28,12},{1,17},{... | collective-permute-start | bytes 221192 | tf_op jit(solution)/shard_map/ppermute | solution.py:223
  143.5 7.5 %collective-permute-start.32 = (f32[72,256]{1,0:T(8,128)S(1)}, f32[72,256]{1,0:T(8,128)S(1)}, u32[]{:S(2)}, u32[]{:S(2)}) collective-permute-start(f32[72,256]{1,0:T(8,128)S(1)} %get-tuple-element.87), channel_id=1, source_target_pairs={{0,8},{4,12},{8,16},{12,20},{16,24},{20,28},{24,0},{28,4},{1,9},{5... | collective-permute-start | bytes 221192 | tf_op jit(solution)/shard_map/ppermute | solution.py:223
  (6 other events, 102.4 us)

commit v11 on v10

--- a/solution.py
+++ b/solution.py
@@ -8,7 +8,7 @@
 from jax.sharding import PartitionSpec as P
 
 damping = 0.85
-group_size = 32
+group_size = 64
 highest = lax.Precision.HIGHEST
 
 

time: 154 us -> 152 us (0.987); the launches traced: 152 us -> 152 us
  waiting for transfers between devices: 46.8 us -> 43.2 us
  Pallas kernels: 29.9 us -> 32.7 us
    pallas_call x5, Pallas kernels: 29.9 us -> 32.7 us  [tile_pass(): pl.pallas_call(functools.partial(tile_kernel, mode, blocks_piece, vectors...]
    ppermute x12, waiting for transfers between devices: 21.3 us -> 18.9 us  [reduce_rows(): total = total + lax.ppermute(part[shift], 'src', pairs)]
    ppermute x12, waiting for transfers between devices: 7.47 us -> 9.51 us  [spread_columns(): lax.ppermute(payload, 'dst', [(i, i ^ v) for i in range(dst_count)])]
    ppermute x3, waiting for transfers between devices: 4.55 us -> 2.69 us  [per_device(): lax.ppermute(shared, 'dst', [(i, i ^ v) for i in range(dst_count)])]
    ppermute x3, starting transfers between devices: 5.21 us -> 3.55 us  [per_device(): lax.ppermute(shared, 'dst', [(i, i ^ v) for i in range(dst_count)])]
  transfers between devices with their start and end apart: 35 -> 35, of which waited for: 20 -> 23; matrix products, arithmetic and copies ran while one was open for 6% -> 6% of each run, Pallas kernels for 0% -> 0%
where the time goes in v11:
time: 152 us
  starting transfers between devices  48 us (32%)
  waiting for transfers between devices  43.2 us (28%)
  Pallas kernels  32.7 us (22%)
  other arithmetic  14 us (9%)
  local copies, waits for them, and re-layouts  9.59 us (6%)
  matrix products  3 us (2%)
  between operations  1.71 us (1%)
    pallas_call x5, Pallas kernels, tile_pass(): pl.pallas_call(functools.partial(tile_kernel, mode, blocks_piece, vectors...  32.7 us
    ppermute x12, starting transfers between devices, reduce_rows(): total = total + lax.ppermute(part[shift], 'src', pairs)  23 us
    ppermute x12, waiting for transfers between devices, reduce_rows(): total = total + lax.ppermute(part[shift], 'src', pairs)  18.9 us
    ppermute x12, starting transfers between devices, spread_columns(): lax.ppermute(payload, 'dst', [(i, i ^ v) for i in range(dst_count)])  16 us
    ppermute x12, waiting for transfers between devices, spread_columns(): lax.ppermute(payload, 'dst', [(i, i ^ v) for i in range(dst_count)])  9.51 us
    ppermute x4, waiting for transfers between devices, reduce_rows(): part = keep + lax.ppermute(give, 'src', [(i, i ^ 1) for i in range(n)])  6.31 us
    ppermute x3, starting transfers between devices, per_device(): pieces.append(lax.ppermute(shared, 'src', pairs))  5.39 us
    ppermute x3, waiting for transfers between devices, per_device(): pieces.append(lax.ppermute(shared, 'src', pairs))  4.57 us
  transfers between devices with their start and end apart: 35, of which 23 were waited for; matrix products, arithmetic and copies ran while one was open for 6% of the time, Pallas kernels for 0%

profile of v11, /device:TPU:0, one launch (start us, length us, event | category | flops | bytes accessed | tf_op | source)
XLA Modules:
  0.0 152.2 jit_solution(16634710037907049866)
XLA Ops:
  2.6 4.0 %collective-permute-start.2 = (f32[1,72,256]{2,1,0:T(8,128)S(1)}, f32[1,72,256]{2,1,0:T(8,128)S(1)}, u32[]{:S(2)}, u32[]{:S(2)}) collective-permute-start(f32[1,72,256]{2,1,0:T(8,128)S(1)} %fusion.44), channel_id=1, source_target_pairs={{0,3},{1,2},{2,1},{3,0},{4,7},{5,6},{6,5},{7,4},{8,11},{9,10},{10,... | collective-permute-start | bytes 221192 | tf_op jit(solution)/shard_map/ppermute | solution.py:205
  12.7 6.8 %shard_map.95 = (f32[4,72,256]{2,1,0:T(8,128)}, f32[4,72,256]{2,1,0:T(8,128)}) custom-call(s32[128]{0:T(128)} %get-tuple-element.111.rows_ref, s32[128]{0:T(128)} %get-tuple-element.112.cols_ref, s32[128]{0:T(128)} %and_convert_fusion.live_ref, s32[1]{0:T(128)} %bitcast.5.nb_ref, f32[4,72,256]{2,1,0:T(8,128)} %pad_maximum_fusion.x_ref, ...), custom_call_target="tpu_custom_call" | custom-call | tf_op jit(solution)/shard_map/pallas_call | solution.py:97
  19.5 1.7 %collective-permute-done.3 = f32[4,72,256]{2,1,0:T(8,128)S(1)} collective-permute-done((f32[4,72,256]{2,1,0:T(8,128)}, f32[4,72,256]{2,1,0:T(8,128)S(1)}, u32[]{:S(2)}, u32[]{:S(2)}) %collective-permute-start.3) | collective-permute-done | bytes 294944 | tf_op jit(solution)/shard_map/ppermute | solution.py:219
  22.3 4.1 %collective-permute-start.6 = (f32[72,256]{1,0:T(8,128)S(1)}, f32[72,256]{1,0:T(8,128)S(1)}, u32[]{:S(2)}, u32[]{:S(2)}) collective-permute-start(f32[72,256]{1,0:T(8,128)S(1)} %get-tuple-element.98), channel_id=1, source_target_pairs={{0,24},{4,28},{8,0},{12,4},{16,8},{20,12},{24,16},{28,20},{1,25},{... | collective-permute-start | bytes 221192 | tf_op jit(solution)/shard_map/ppermute | solution.py:223
  27.8 1.9 %collective-permute-start.4 = (f32[72,256]{1,0:T(8,128)S(1)}, f32[72,256]{1,0:T(8,128)S(1)}, u32[]{:S(2)}, u32[]{:S(2)}) collective-permute-start(f32[72,256]{1,0:T(8,128)S(1)} %get-tuple-element.97), channel_id=1, source_target_pairs={{0,8},{4,12},{8,16},{12,20},{16,24},{20,28},{24,0},{28,4},{1,9},{5... | collective-permute-start | bytes 221192 | tf_op jit(solution)/shard_map/ppermute | solution.py:223
  30.4 4.7 %collective-permute-done.5 = f32[72,256]{1,0:T(8,128)S(1)} collective-permute-done((f32[72,256]{1,0:T(8,128)S(1)}, f32[72,256]{1,0:T(8,128)S(1)}, u32[]{:S(2)}, u32[]{:S(2)}) %collective-permute-start.5) | collective-permute-done | bytes 73760 | tf_op jit(solution)/shard_map/ppermute | solution.py:223
  36.8 1.7 %collective-permute-start.8 = (f32[1,72,256]{2,1,0:T(8,128)S(1)}, f32[1,72,256]{2,1,0:T(8,128)S(1)}, u32[]{:S(2)}, u32[]{:S(2)}) collective-permute-start(f32[1,72,256]{2,1,0:T(8,128)S(1)} %fusion.40), channel_id=1, source_target_pairs={{0,2},{1,3},{2,0},{3,1},{4,6},{5,7},{6,4},{7,5},{8,10},{9,11},{10,... | collective-permute-start | bytes 221192 | tf_op jit(solution)/shard_map/ppermute | solution.py:205
  38.8 2.2 %collective-permute-done.9 = f32[1,72,256]{2,1,0:T(8,128)S(1)} collective-permute-done((f32[1,72,256]{2,1,0:T(8,128)S(1)}, f32[1,72,256]{2,1,0:T(8,128)S(1)}, u32[]{:S(2)}, u32[]{:S(2)}) %collective-permute-start.9) | collective-permute-done | bytes 73760 | tf_op jit(solution)/shard_map/ppermute | solution.py:205
  43.6 6.6 %shard_map.96 = (f32[4,72,256]{2,1,0:T(8,128)}, f32[4,72,256]{2,1,0:T(8,128)}) custom-call(s32[128]{0:T(128)} %get-tuple-element.111.rows_ref, s32[128]{0:T(128)} %get-tuple-element.112.cols_ref, s32[128]{0:T(128)} %and_convert_fusion.live_ref, s32[1]{0:T(128)} %bitcast.5.nb_ref, f32[4,72,256]{2,1,0:T(8,128)} %pad_maximum_fusion.1.x_ref, ...), custom_call_target="tpu_custom_call" | custom-call | tf_op jit(solution)/shard_map/pallas_call | solution.py:97
  53.5 2.6 %collective-permute-start.12 = (f32[72,256]{1,0:T(8,128)S(1)}, f32[72,256]{1,0:T(8,128)S(1)}, u32[]{:S(2)}, u32[]{:S(2)}) collective-permute-start(f32[72,256]{1,0:T(8,128)S(1)} %get-tuple-element.96), channel_id=1, source_target_pairs={{0,16},{4,20},{8,24},{12,28},{16,0},{20,4},{24,8},{28,12},{1,17},{... | collective-permute-start | bytes 221192 | tf_op jit(solution)/shard_map/ppermute | solution.py:223
  56.1 1.9 %collective-permute-start.11 = (f32[72,256]{1,0:T(8,128)S(1)}, f32[72,256]{1,0:T(8,128)S(1)}, u32[]{:S(2)}, u32[]{:S(2)}) collective-permute-start(f32[72,256]{1,0:T(8,128)S(1)} %get-tuple-element.94), channel_id=1, source_target_pairs={{0,8},{4,12},{8,16},{12,20},{16,24},{20,28},{24,0},{28,4},{1,9},{5... | collective-permute-start | bytes 221192 | tf_op jit(solution)/shard_map/ppermute | solution.py:223
  59.2 4.0 %collective-permute-done.12 = f32[72,256]{1,0:T(8,128)S(1)} collective-permute-done((f32[72,256]{1,0:T(8,128)S(1)}, f32[72,256]{1,0:T(8,128)S(1)}, u32[]{:S(2)}, u32[]{:S(2)}) %collective-permute-start.12) | collective-permute-done | bytes 73760 | tf_op jit(solution)/shard_map/ppermute | solution.py:223
  63.6 1.9 %collective-permute-start.15 = (f32[1,72,256]{2,1,0:T(8,128)S(1)}, f32[1,72,256]{2,1,0:T(8,128)S(1)}, u32[]{:S(2)}, u32[]{:S(2)}) collective-permute-start(f32[1,72,256]{2,1,0:T(8,128)S(1)} %fusion.36), channel_id=1, source_target_pairs={{0,2},{1,3},{2,0},{3,1},{4,6},{5,7},{6,4},{7,5},{8,10},{9,11},{10,... | collective-permute-start | bytes 221192 | tf_op jit(solution)/shard_map/ppermute | solution.py:205
  70.5 6.0 %shard_map.97 = f32[16,128]{1,0:T(8,128)} custom-call(s32[128]{0:T(128)} %clamp_bitcast_fusion.rows_ref, s32[128]{0:T(128)} %get-tuple-element.112.cols_ref, s32[128]{0:T(128)} %and_convert_fusion.live_ref, s32[1]{0:T(128)} %bitcast.5.nb_ref, f32[4,72,256]{2,1,0:T(8,128)} %pad_maximum_fusion.2.x_ref, bf16[1,1,128,256,256]{4,3,2,1,0:T(8,128)(2,1)} %t_ref.9), custom_call_target="tpu_custom_call" | custom-call | tf_op jit(solution)/shard_map/pallas_call | solution.py:97
  77.5 1.7 %collective-permute-start.17 = (f32[1,2440]{1,0:T(1,128)S(1)}, f32[1,2440]{1,0:T(1,128)S(1)}, u32[]{:S(2)}, u32[]{:S(2)}) collective-permute-start(f32[1,2440]{1,0:T(1,128)S(1)} %broadcast_in_dim.21), channel_id=1, source_target_pairs={{0,1},{1,0},{2,3},{3,2},{4,5},{5,4},{6,7},{7,6},{8,9},{9,8},{10,11... | collective-permute-start | bytes 29288 | tf_op jit(solution)/shard_map/ppermute | solution.py:279
  79.2 1.9 %collective-permute-start.19 = (f32[1,2440]{1,0:T(1,128)S(1)}, f32[1,2440]{1,0:T(1,128)S(1)}, u32[]{:S(2)}, u32[]{:S(2)}) collective-permute-start(f32[1,2440]{1,0:T(1,128)S(1)} %broadcast_in_dim.21), channel_id=1, source_target_pairs={{0,3},{1,2},{2,1},{3,0},{4,7},{5,6},{6,5},{7,4},{8,11},{9,10},{10,... | collective-permute-start | bytes 29288 | tf_op jit(solution)/shard_map/ppermute | solution.py:279
  85.2 1.9 %collective-permute-start.21 = (f32[8,2440]{1,0:T(8,128)S(1)}, f32[8,2440]{1,0:T(8,128)S(1)}, u32[]{:S(2)}, u32[]{:S(2)}) collective-permute-start(f32[8,2440]{1,0:T(8,128)S(1)} %concatenate.57), channel_id=1, source_target_pairs={{0,8},{4,12},{8,16},{12,20},{16,24},{20,28},{24,0},{28,4},{1,9},{5... | collective-permute-start | bytes 234248 | tf_op jit(solution)/shard_map/ppermute | solution.py:291
  87.7 2.8 %collective-permute-start.23 = (f32[8,2440]{1,0:T(8,128)S(1)}, f32[8,2440]{1,0:T(8,128)S(1)}, u32[]{:S(2)}, u32[]{:S(2)}) collective-permute-start(f32[8,2440]{1,0:T(8,128)S(1)} %concatenate.57), channel_id=1, source_target_pairs={{0,24},{4,28},{8,0},{12,4},{16,8},{20,12},{24,16},{28,20},{1,25},{... | collective-permute-start | bytes 234248 | tf_op jit(solution)/shard_map/ppermute | solution.py:291
  92.2 2.9 %collective-permute-done.22 = f32[8,2440]{1,0:T(8,128)S(1)} collective-permute-done((f32[8,2440]{1,0:T(8,128)S(1)}, f32[8,2440]{1,0:T(8,128)S(1)}, u32[]{:S(2)}, u32[]{:S(2)}) %collective-permute-start.22) | collective-permute-done | bytes 78112 | tf_op jit(solution)/shard_map/ppermute | solution.py:291
  101.4 6.8 %shard_map.98 = (f32[4,72,256]{2,1,0:T(8,128)}, f32[4,72,256]{2,1,0:T(8,128)}) custom-call(s32[128]{0:T(128)} %get-tuple-element.111.rows_ref, s32[128]{0:T(128)} %get-tuple-element.112.cols_ref, s32[128]{0:T(128)} %and_convert_fusion.live_ref, s32[1]{0:T(128)} %bitcast.5.nb_ref, f32[4,72,256]{2,1,0:T(8,128)} %broadcast_multiply_fusion.x_ref, ...), custom_call_target="tpu_custom_call" | custom-call | tf_op jit(solution)/shard_map/pallas_call | solution.py:97
  108.1 1.8 %collective-permute-done.24 = f32[4,72,256]{2,1,0:T(8,128)S(1)} collective-permute-done((f32[4,72,256]{2,1,0:T(8,128)}, f32[4,72,256]{2,1,0:T(8,128)S(1)}, u32[]{:S(2)}, u32[]{:S(2)}) %collective-permute-start.24) | collective-permute-done | bytes 294944 | tf_op jit(solution)/shard_map/ppermute | solution.py:219
  110.9 3.2 %collective-permute-start.27 = (f32[72,256]{1,0:T(8,128)S(1)}, f32[72,256]{1,0:T(8,128)S(1)}, u32[]{:S(2)}, u32[]{:S(2)}) collective-permute-start(f32[72,256]{1,0:T(8,128)S(1)} %get-tuple-element.91), channel_id=1, source_target_pairs={{0,24},{4,28},{8,0},{12,4},{16,8},{20,12},{24,16},{28,20},{1,25},{... | collective-permute-start | bytes 221192 | tf_op jit(solution)/shard_map/ppermute | solution.py:223
  114.7 1.9 %collective-permute-start.25 = (f32[72,256]{1,0:T(8,128)S(1)}, f32[72,256]{1,0:T(8,128)S(1)}, u32[]{:S(2)}, u32[]{:S(2)}) collective-permute-start(f32[72,256]{1,0:T(8,128)S(1)} %get-tuple-element.93), channel_id=1, source_target_pairs={{0,8},{4,12},{8,16},{12,20},{16,24},{20,28},{24,0},{28,4},{1,9},{5... | collective-permute-start | bytes 221192 | tf_op jit(solution)/shard_map/ppermute | solution.py:223
  116.8 5.4 %collective-permute-done.26 = f32[72,256]{1,0:T(8,128)S(1)} collective-permute-done((f32[72,256]{1,0:T(8,128)S(1)}, f32[72,256]{1,0:T(8,128)S(1)}, u32[]{:S(2)}, u32[]{:S(2)}) %collective-permute-start.26) | collective-permute-done | bytes 73760 | tf_op jit(solution)/shard_map/ppermute | solution.py:223
  122.5 3.7 %collective-permute-start.30 = (f32[1,72,256]{2,1,0:T(8,128)S(1)}, f32[1,72,256]{2,1,0:T(8,128)S(1)}, u32[]{:S(2)}, u32[]{:S(2)}) collective-permute-start(f32[1,72,256]{2,1,0:T(8,128)S(1)} %fusion.35), channel_id=1, source_target_pairs={{0,3},{1,2},{2,1},{3,0},{4,7},{5,6},{6,5},{7,4},{8,11},{9,10},{10,... | collective-permute-start | bytes 221192 | tf_op jit(solution)/shard_map/ppermute | solution.py:205
  126.8 1.7 %collective-permute-done.30 = f32[1,72,256]{2,1,0:T(8,128)S(1)} collective-permute-done((f32[1,72,256]{2,1,0:T(8,128)S(1)}, f32[1,72,256]{2,1,0:T(8,128)S(1)}, u32[]{:S(2)}, u32[]{:S(2)}) %collective-permute-start.30) | collective-permute-done | bytes 73760 | tf_op jit(solution)/shard_map/ppermute | solution.py:205
  128.5 2.0 %collective-permute-done.29 = f32[1,72,256]{2,1,0:T(8,128)S(1)} collective-permute-done((f32[1,72,256]{2,1,0:T(8,128)S(1)}, f32[1,72,256]{2,1,0:T(8,128)S(1)}, u32[]{:S(2)}, u32[]{:S(2)}) %collective-permute-start.29) | collective-permute-done | bytes 73760 | tf_op jit(solution)/shard_map/ppermute | solution.py:205
  131.7 6.6 %shard_map.99 = (f32[4,72,256]{2,1,0:T(8,128)}, f32[4,72,256]{2,1,0:T(8,128)}) custom-call(s32[128]{0:T(128)} %get-tuple-element.111.rows_ref, s32[128]{0:T(128)} %get-tuple-element.112.cols_ref, s32[128]{0:T(128)} %and_convert_fusion.live_ref, s32[1]{0:T(128)} %bitcast.5.nb_ref, f32[4,72,256]{2,1,0:T(8,128)} %pad_maximum_fusion.3.x_ref, ...), custom_call_target="tpu_custom_call" | custom-call | tf_op jit(solution)/shard_map/pallas_call | solution.py:97
  138.4 1.7 %collective-permute-done.31 = f32[4,72,256]{2,1,0:T(8,128)S(1)} collective-permute-done((f32[4,72,256]{2,1,0:T(8,128)}, f32[4,72,256]{2,1,0:T(8,128)S(1)}, u32[]{:S(2)}, u32[]{:S(2)}) %collective-permute-start.31) | collective-permute-done | bytes 294944 | tf_op jit(solution)/shard_map/ppermute | solution.py:219
  141.3 2.8 %collective-permute-start.33 = (f32[72,256]{1,0:T(8,128)S(1)}, f32[72,256]{1,0:T(8,128)S(1)}, u32[]{:S(2)}, u32[]{:S(2)}) collective-permute-start(f32[72,256]{1,0:T(8,128)S(1)} %get-tuple-element.89), channel_id=1, source_target_pairs={{0,16},{4,20},{8,24},{12,28},{16,0},{20,4},{24,8},{28,12},{1,17},{... | collective-permute-start | bytes 221192 | tf_op jit(solution)/shard_map/ppermute | solution.py:223
  144.1 1.9 %collective-permute-start.32 = (f32[72,256]{1,0:T(8,128)S(1)}, f32[72,256]{1,0:T(8,128)S(1)}, u32[]{:S(2)}, u32[]{:S(2)}) collective-permute-start(f32[72,256]{1,0:T(8,128)S(1)} %get-tuple-element.87), channel_id=1, source_target_pairs={{0,8},{4,12},{8,16},{12,20},{16,24},{20,28},{24,0},{28,4},{1,9},{5... | collective-permute-start | bytes 221192 | tf_op jit(solution)/shard_map/ppermute | solution.py:223
  146.8 4.5 %collective-permute-done.33 = f32[72,256]{1,0:T(8,128)S(1)} collective-permute-done((f32[72,256]{1,0:T(8,128)S(1)}, f32[72,256]{1,0:T(8,128)S(1)}, u32[]{:S(2)}, u32[]{:S(2)}) %collective-permute-start.33) | collective-permute-done | bytes 73760 | tf_op jit(solution)/shard_map/ppermute | solution.py:223
  (148 shorter events, 45.3 us)
Async XLA Ops:
  2.6 9.3 %collective-permute-start.2 = (f32[1,72,256]{2,1,0:T(8,128)S(1)}, f32[1,72,256]{2,1,0:T(8,128)S(1)}, u32[]{:S(2)}, u32[]{:S(2)}) collective-permute-start(f32[1,72,256]{2,1,0:T(8,128)S(1)} %fusion.44), channel_id=1, source_target_pairs={{0,3},{1,2},{2,1},{3,0},{4,7},{5,6},{6,5},{7,4},{8,11},{9,10},{10,... | collective-permute-start | bytes 221192 | tf_op jit(solution)/shard_map/ppermute | solution.py:205
  6.6 5.4 %collective-permute-start.1 = (f32[1,72,256]{2,1,0:T(8,128)S(1)}, f32[1,72,256]{2,1,0:T(8,128)S(1)}, u32[]{:S(2)}, u32[]{:S(2)}) collective-permute-start(f32[1,72,256]{2,1,0:T(8,128)S(1)} %fusion.44), channel_id=1, source_target_pairs={{0,2},{1,3},{2,0},{3,1},{4,6},{5,7},{6,4},{7,5},{8,10},{9,11},{10,... | collective-permute-start | bytes 221192 | tf_op jit(solution)/shard_map/ppermute | solution.py:205
  7.1 4.9 %collective-permute-start = (f32[1,72,256]{2,1,0:T(8,128)S(1)}, f32[1,72,256]{2,1,0:T(8,128)S(1)}, u32[]{:S(2)}, u32[]{:S(2)}) collective-permute-start(f32[1,72,256]{2,1,0:T(8,128)S(1)} %fusion.44), channel_id=1, source_target_pairs={{0,1},{1,0},{2,3},{3,2},{4,5},{5,4},{6,7},{7,6},{8,9},{9,8},{10,11... | collective-permute-start | bytes 221192 | tf_op jit(solution)/shard_map/ppermute | solution.py:205
  19.5 1.8 %collective-permute-start.3 = (f32[4,72,256]{2,1,0:T(8,128)}, f32[4,72,256]{2,1,0:T(8,128)S(1)}, u32[]{:S(2)}, u32[]{:S(2)}) collective-permute-start(f32[4,72,256]{2,1,0:T(8,128)} %get-tuple-element.59), channel_id=1, source_target_pairs={{0,4},{4,0},{8,12},{12,8},{16,20},{20,16},{24,28},{28,24},{1,5},{5... | collective-permute-start | bytes 884744 | tf_op jit(solution)/shard_map/ppermute | solution.py:219
  22.3 8.1 %collective-permute-start.6 = (f32[72,256]{1,0:T(8,128)S(1)}, f32[72,256]{1,0:T(8,128)S(1)}, u32[]{:S(2)}, u32[]{:S(2)}) collective-permute-start(f32[72,256]{1,0:T(8,128)S(1)} %get-tuple-element.98), channel_id=1, source_target_pairs={{0,24},{4,28},{8,0},{12,4},{16,8},{20,12},{24,16},{28,20},{1,25},{... | collective-permute-start | bytes 221192 | tf_op jit(solution)/shard_map/ppermute | solution.py:223
  26.3 8.7 %collective-permute-start.5 = (f32[72,256]{1,0:T(8,128)S(1)}, f32[72,256]{1,0:T(8,128)S(1)}, u32[]{:S(2)}, u32[]{:S(2)}) collective-permute-start(f32[72,256]{1,0:T(8,128)S(1)} %get-tuple-element.99), channel_id=1, source_target_pairs={{0,16},{4,20},{8,24},{12,28},{16,0},{20,4},{24,8},{28,12},{1,17},{... | collective-permute-start | bytes 221192 | tf_op jit(solution)/shard_map/ppermute | solution.py:223
  27.8 7.2 %collective-permute-start.4 = (f32[72,256]{1,0:T(8,128)S(1)}, f32[72,256]{1,0:T(8,128)S(1)}, u32[]{:S(2)}, u32[]{:S(2)}) collective-permute-start(f32[72,256]{1,0:T(8,128)S(1)} %get-tuple-element.97), channel_id=1, source_target_pairs={{0,8},{4,12},{8,16},{12,20},{16,24},{20,28},{24,0},{28,4},{1,9},{5... | collective-permute-start | bytes 221192 | tf_op jit(solution)/shard_map/ppermute | solution.py:223
  35.3 5.7 %collective-permute-start.9 = (f32[1,72,256]{2,1,0:T(8,128)S(1)}, f32[1,72,256]{2,1,0:T(8,128)S(1)}, u32[]{:S(2)}, u32[]{:S(2)}) collective-permute-start(f32[1,72,256]{2,1,0:T(8,128)S(1)} %fusion.40), channel_id=1, source_target_pairs={{0,3},{1,2},{2,1},{3,0},{4,7},{5,6},{6,5},{7,4},{8,11},{9,10},{10,... | collective-permute-start | bytes 221192 | tf_op jit(solution)/shard_map/ppermute | solution.py:205
  36.8 4.7 %collective-permute-start.8 = (f32[1,72,256]{2,1,0:T(8,128)S(1)}, f32[1,72,256]{2,1,0:T(8,128)S(1)}, u32[]{:S(2)}, u32[]{:S(2)}) collective-permute-start(f32[1,72,256]{2,1,0:T(8,128)S(1)} %fusion.40), channel_id=1, source_target_pairs={{0,2},{1,3},{2,0},{3,1},{4,6},{5,7},{6,4},{7,5},{8,10},{9,11},{10,... | collective-permute-start | bytes 221192 | tf_op jit(solution)/shard_map/ppermute | solution.py:205
  38.5 4.4 %collective-permute-start.7 = (f32[1,72,256]{2,1,0:T(8,128)S(1)}, f32[1,72,256]{2,1,0:T(8,128)S(1)}, u32[]{:S(2)}, u32[]{:S(2)}) collective-permute-start(f32[1,72,256]{2,1,0:T(8,128)S(1)} %fusion.40), channel_id=1, source_target_pairs={{0,1},{1,0},{2,3},{3,2},{4,5},{5,4},{6,7},{7,6},{8,9},{9,8},{10,11... | collective-permute-start | bytes 221192 | tf_op jit(solution)/shard_map/ppermute | solution.py:205
  50.2 1.8 %collective-permute-start.10 = (f32[4,72,256]{2,1,0:T(8,128)}, f32[4,72,256]{2,1,0:T(8,128)S(1)}, u32[]{:S(2)}, u32[]{:S(2)}) collective-permute-start(f32[4,72,256]{2,1,0:T(8,128)} %get-tuple-element.61), channel_id=1, source_target_pairs={{0,4},{4,0},{8,12},{12,8},{16,20},{20,16},{24,28},{28,24},{1,5},{5... | collective-permute-start | bytes 884744 | tf_op jit(solution)/shard_map/ppermute | solution.py:219
  53.0 6.2 %collective-permute-start.13 = (f32[72,256]{1,0:T(8,128)S(1)}, f32[72,256]{1,0:T(8,128)S(1)}, u32[]{:S(2)}, u32[]{:S(2)}) collective-permute-start(f32[72,256]{1,0:T(8,128)S(1)} %get-tuple-element.95), channel_id=1, source_target_pairs={{0,24},{4,28},{8,0},{12,4},{16,8},{20,12},{24,16},{28,20},{1,25},{... | collective-permute-start | bytes 221192 | tf_op jit(solution)/shard_map/ppermute | solution.py:223
  53.5 9.8 %collective-permute-start.12 = (f32[72,256]{1,0:T(8,128)S(1)}, f32[72,256]{1,0:T(8,128)S(1)}, u32[]{:S(2)}, u32[]{:S(2)}) collective-permute-start(f32[72,256]{1,0:T(8,128)S(1)} %get-tuple-element.96), channel_id=1, source_target_pairs={{0,16},{4,20},{8,24},{12,28},{16,0},{20,4},{24,8},{28,12},{1,17},{... | collective-permute-start | bytes 221192 | tf_op jit(solution)/shard_map/ppermute | solution.py:223
  56.1 7.2 %collective-permute-start.11 = (f32[72,256]{1,0:T(8,128)S(1)}, f32[72,256]{1,0:T(8,128)S(1)}, u32[]{:S(2)}, u32[]{:S(2)}) collective-permute-start(f32[72,256]{1,0:T(8,128)S(1)} %get-tuple-element.94), channel_id=1, source_target_pairs={{0,8},{4,12},{8,16},{12,20},{16,24},{20,28},{24,0},{28,4},{1,9},{5... | collective-permute-start | bytes 221192 | tf_op jit(solution)/shard_map/ppermute | solution.py:223
  63.5 5.3 %collective-permute-start.16 = (f32[1,72,256]{2,1,0:T(8,128)S(1)}, f32[1,72,256]{2,1,0:T(8,128)S(1)}, u32[]{:S(2)}, u32[]{:S(2)}) collective-permute-start(f32[1,72,256]{2,1,0:T(8,128)S(1)} %fusion.36), channel_id=1, source_target_pairs={{0,3},{1,2},{2,1},{3,0},{4,7},{5,6},{6,5},{7,4},{8,11},{9,10},{10,... | collective-permute-start | bytes 221192 | tf_op jit(solution)/shard_map/ppermute | solution.py:205
  63.6 5.2 %collective-permute-start.15 = (f32[1,72,256]{2,1,0:T(8,128)S(1)}, f32[1,72,256]{2,1,0:T(8,128)S(1)}, u32[]{:S(2)}, u32[]{:S(2)}) collective-permute-start(f32[1,72,256]{2,1,0:T(8,128)S(1)} %fusion.36), channel_id=1, source_target_pairs={{0,2},{1,3},{2,0},{3,1},{4,6},{5,7},{6,4},{7,5},{8,10},{9,11},{10,... | collective-permute-start | bytes 221192 | tf_op jit(solution)/shard_map/ppermute | solution.py:205
  65.5 4.4 %collective-permute-start.14 = (f32[1,72,256]{2,1,0:T(8,128)S(1)}, f32[1,72,256]{2,1,0:T(8,128)S(1)}, u32[]{:S(2)}, u32[]{:S(2)}) collective-permute-start(f32[1,72,256]{2,1,0:T(8,128)S(1)} %fusion.36), channel_id=1, source_target_pairs={{0,1},{1,0},{2,3},{3,2},{4,5},{5,4},{6,7},{7,6},{8,9},{9,8},{10,11... | collective-permute-start | bytes 221192 | tf_op jit(solution)/shard_map/ppermute | solution.py:205
  77.5 3.7 %collective-permute-start.17 = (f32[1,2440]{1,0:T(1,128)S(1)}, f32[1,2440]{1,0:T(1,128)S(1)}, u32[]{:S(2)}, u32[]{:S(2)}) collective-permute-start(f32[1,2440]{1,0:T(1,128)S(1)} %broadcast_in_dim.21), channel_id=1, source_target_pairs={{0,1},{1,0},{2,3},{3,2},{4,5},{5,4},{6,7},{7,6},{8,9},{9,8},{10,11... | collective-permute-start | bytes 29288 | tf_op jit(solution)/shard_map/ppermute | solution.py:279
  79.2 3.7 %collective-permute-start.18 = (f32[1,2440]{1,0:T(1,128)S(1)}, f32[1,2440]{1,0:T(1,128)S(1)}, u32[]{:S(2)}, u32[]{:S(2)}) collective-permute-start(f32[1,2440]{1,0:T(1,128)S(1)} %broadcast_in_dim.21), channel_id=1, source_target_pairs={{0,2},{1,3},{2,0},{3,1},{4,6},{5,7},{6,4},{7,5},{8,10},{9,11},{10,... | collective-permute-start | bytes 29288 | tf_op jit(solution)/shard_map/ppermute | solution.py:279
  79.2 4.6 %collective-permute-start.19 = (f32[1,2440]{1,0:T(1,128)S(1)}, f32[1,2440]{1,0:T(1,128)S(1)}, u32[]{:S(2)}, u32[]{:S(2)}) collective-permute-start(f32[1,2440]{1,0:T(1,128)S(1)} %broadcast_in_dim.21), channel_id=1, source_target_pairs={{0,3},{1,2},{2,1},{3,0},{4,7},{5,6},{6,5},{7,4},{8,11},{9,10},{10,... | collective-permute-start | bytes 29288 | tf_op jit(solution)/shard_map/ppermute | solution.py:279
  85.2 7.1 %collective-permute-start.21 = (f32[8,2440]{1,0:T(8,128)S(1)}, f32[8,2440]{1,0:T(8,128)S(1)}, u32[]{:S(2)}, u32[]{:S(2)}) collective-permute-start(f32[8,2440]{1,0:T(8,128)S(1)} %concatenate.57), channel_id=1, source_target_pairs={{0,8},{4,12},{8,16},{12,20},{16,24},{20,28},{24,0},{28,4},{1,9},{5... | collective-permute-start | bytes 234248 | tf_op jit(solution)/shard_map/ppermute | solution.py:291
  87.1 8.1 %collective-permute-start.22 = (f32[8,2440]{1,0:T(8,128)S(1)}, f32[8,2440]{1,0:T(8,128)S(1)}, u32[]{:S(2)}, u32[]{:S(2)}) collective-permute-start(f32[8,2440]{1,0:T(8,128)S(1)} %concatenate.57), channel_id=1, source_target_pairs={{0,16},{4,20},{8,24},{12,28},{16,0},{20,4},{24,8},{28,12},{1,17},{... | collective-permute-start | bytes 234248 | tf_op jit(solution)/shard_map/ppermute | solution.py:291
  87.7 7.4 %collective-permute-start.23 = (f32[8,2440]{1,0:T(8,128)S(1)}, f32[8,2440]{1,0:T(8,128)S(1)}, u32[]{:S(2)}, u32[]{:S(2)}) collective-permute-start(f32[8,2440]{1,0:T(8,128)S(1)} %concatenate.57), channel_id=1, source_target_pairs={{0,24},{4,28},{8,0},{12,4},{16,8},{20,12},{24,16},{28,20},{1,25},{... | collective-permute-start | bytes 234248 | tf_op jit(solution)/shard_map/ppermute | solution.py:291
  110.9 5.9 %collective-permute-start.27 = (f32[72,256]{1,0:T(8,128)S(1)}, f32[72,256]{1,0:T(8,128)S(1)}, u32[]{:S(2)}, u32[]{:S(2)}) collective-permute-start(f32[72,256]{1,0:T(8,128)S(1)} %get-tuple-element.91), channel_id=1, source_target_pairs={{0,24},{4,28},{8,0},{12,4},{16,8},{20,12},{24,16},{28,20},{1,25},{... | collective-permute-start | bytes 221192 | tf_op jit(solution)/shard_map/ppermute | solution.py:223
  114.2 8.1 %collective-permute-start.26 = (f32[72,256]{1,0:T(8,128)S(1)}, f32[72,256]{1,0:T(8,128)S(1)}, u32[]{:S(2)}, u32[]{:S(2)}) collective-permute-start(f32[72,256]{1,0:T(8,128)S(1)} %get-tuple-element.92), channel_id=1, source_target_pairs={{0,16},{4,20},{8,24},{12,28},{16,0},{20,4},{24,8},{28,12},{1,17},{... | collective-permute-start | bytes 221192 | tf_op jit(solution)/shard_map/ppermute | solution.py:223
  114.7 7.6 %collective-permute-start.25 = (f32[72,256]{1,0:T(8,128)S(1)}, f32[72,256]{1,0:T(8,128)S(1)}, u32[]{:S(2)}, u32[]{:S(2)}) collective-permute-start(f32[72,256]{1,0:T(8,128)S(1)} %get-tuple-element.93), channel_id=1, source_target_pairs={{0,8},{4,12},{8,16},{12,20},{16,24},{20,28},{24,0},{28,4},{1,9},{5... | collective-permute-start | bytes 221192 | tf_op jit(solution)/shard_map/ppermute | solution.py:223
  122.5 6.0 %collective-permute-start.30 = (f32[1,72,256]{2,1,0:T(8,128)S(1)}, f32[1,72,256]{2,1,0:T(8,128)S(1)}, u32[]{:S(2)}, u32[]{:S(2)}) collective-permute-start(f32[1,72,256]{2,1,0:T(8,128)S(1)} %fusion.35), channel_id=1, source_target_pairs={{0,3},{1,2},{2,1},{3,0},{4,7},{5,6},{6,5},{7,4},{8,11},{9,10},{10,... | collective-permute-start | bytes 221192 | tf_op jit(solution)/shard_map/ppermute | solution.py:205
  126.1 4.4 %collective-permute-start.29 = (f32[1,72,256]{2,1,0:T(8,128)S(1)}, f32[1,72,256]{2,1,0:T(8,128)S(1)}, u32[]{:S(2)}, u32[]{:S(2)}) collective-permute-start(f32[1,72,256]{2,1,0:T(8,128)S(1)} %fusion.35), channel_id=1, source_target_pairs={{0,2},{1,3},{2,0},{3,1},{4,6},{5,7},{6,4},{7,5},{8,10},{9,11},{10,... | collective-permute-start | bytes 221192 | tf_op jit(solution)/shard_map/ppermute | solution.py:205
  126.6 4.4 %collective-permute-start.28 = (f32[1,72,256]{2,1,0:T(8,128)S(1)}, f32[1,72,256]{2,1,0:T(8,128)S(1)}, u32[]{:S(2)}, u32[]{:S(2)}) collective-permute-start(f32[1,72,256]{2,1,0:T(8,128)S(1)} %fusion.35), channel_id=1, source_target_pairs={{0,1},{1,0},{2,3},{3,2},{4,5},{5,4},{6,7},{7,6},{8,9},{9,8},{10,11... | collective-permute-start | bytes 221192 | tf_op jit(solution)/shard_map/ppermute | solution.py:205
  141.2 5.6 %collective-permute-start.34 = (f32[72,256]{1,0:T(8,128)S(1)}, f32[72,256]{1,0:T(8,128)S(1)}, u32[]{:S(2)}, u32[]{:S(2)}) collective-permute-start(f32[72,256]{1,0:T(8,128)S(1)} %get-tuple-element.88), channel_id=1, source_target_pairs={{0,24},{4,28},{8,0},{12,4},{16,8},{20,12},{24,16},{28,20},{1,25},{... | collective-permute-start | bytes 221192 | tf_op jit(solution)/shard_map/ppermute | solution.py:223
  141.3 10.0 %collective-permute-start.33 = (f32[72,256]{1,0:T(8,128)S(1)}, f32[72,256]{1,0:T(8,128)S(1)}, u32[]{:S(2)}, u32[]{:S(2)}) collective-permute-start(f32[72,256]{1,0:T(8,128)S(1)} %get-tuple-element.89), channel_id=1, source_target_pairs={{0,16},{4,20},{8,24},{12,28},{16,0},{20,4},{24,8},{28,12},{1,17},{... | collective-permute-start | bytes 221192 | tf_op jit(solution)/shard_map/ppermute | solution.py:223
  144.1 7.2 %collective-permute-start.32 = (f32[72,256]{1,0:T(8,128)S(1)}, f32[72,256]{1,0:T(8,128)S(1)}, u32[]{:S(2)}, u32[]{:S(2)}) collective-permute-start(f32[72,256]{1,0:T(8,128)S(1)} %get-tuple-element.87), channel_id=1, source_target_pairs={{0,8},{4,12},{8,16},{12,20},{16,24},{20,28},{24,0},{28,4},{1,9},{5... | collective-permute-start | bytes 221192 | tf_op jit(solution)/shard_map/ppermute | solution.py:223
  (6 other events, 108.5 us)
